TPU v7x, 32 devices: a whole 2x2x4 slice. The times are simulated.
32 devices in a mesh: snp: 8 (over z, y), samp: 4 (over x, core).
Axes of the slice: x: 2, y: 2, z: 4, core: 2. Of those that a mesh axis runs over, the one named last changes fastest.
Arguments:
- genotypes: bfloat16 [1536, 5120], P('samp', 'snp'), may hold values from -0.076171875 to 0.076171875
- responses: float32 [3072, 1536], P('snp', 'samp'), may hold values from -6 to 6
- weights: float32 [1024, 64, 128], P('snp'), may hold values from -6 to 6
- pattern: int32 [1024, 2], P('snp'), may hold values from 0 to 45, as said below
- entry_count: int32 [8], P('snp'), may hold values from 64 to 128, as said below
- tile_slot: int32 [46], replicated, may hold values from 0 to 47, as said below
- penalty: float32 [46], replicated, may hold values from 0.5 to 5
Outputs:
- new_weights: float32 [1024, 64, 128], P('snp')
Inputs may be any that keep to these rules, and one draw needn't show every extreme that they name: `pattern`: column 0 is a block below 5, column 1 a tile below 46; within one segment's 128 rows no (block, tile) pair repeats. `entry_count`: some segment has all 128 entries live. `tile_slot`: distinct slots.
All inputs are finite; a program needn't handle non-finite values.
Results may differ from a plain program's by a relative error of at most 0.0032.
Values may be sent and summed in bfloat16 or wider, within the bound.
No kernel may reach another device: no remote copies, remote signals or barrier semaphores. Data moves between devices by JAX's collectives and lax.ppermute only.
A program may use at most 128 MiB of HBM per device.

v0:
```python
import jax
import jax.numpy as jnp
from jax import lax
from jax.sharding import PartitionSpec as P

ITERS = 2


step_scale = 0.3


def shrink_soft(current, gradient, cutoff, active):
    shifted = current + step_scale * gradient
    shrunk = jnp.sign(shifted) * jnp.maximum(jnp.abs(shifted) - cutoff, jnp.float32(0.0))
    return jnp.where(active[:, None, None], shrunk, jnp.float32(0.0))


def per_device(genotypes, responses, weights, pattern, entry_count, tile_slot, penalty):
    sample_count = genotypes.shape[0]
    entries = weights.shape[0]
    tile_width = weights.shape[1]
    block_width = weights.shape[2]
    block_count = genotypes.shape[1] // block_width
    own_rows = responses.shape[0]
    slot_total = lax.axis_size("snp") * (own_rows // tile_width)
    geno_blocks = genotypes.reshape(sample_count, block_count, block_width)
    block_hot = (pattern[:, 0:1] == jnp.arange(block_count, dtype=jnp.int32)[None, :]).astype(
        jnp.bfloat16
    )
    geno_sel = jnp.einsum(
        "eb,sbk->esk", block_hot, geno_blocks, preferred_element_type=jnp.float32
    ).astype(jnp.bfloat16)
    tile_hot = pattern[:, 1:2] == jnp.arange(penalty.shape[0], dtype=jnp.int32)[None, :]
    slot_ids = jnp.sum(jnp.where(tile_hot, tile_slot[None, :], 0), axis=1)
    per_entry = jnp.dot(tile_hot.astype(jnp.float32), penalty, precision=lax.Precision.HIGHEST)
    cutoff = step_scale * per_entry[:, None, None]
    slot_hot = (slot_ids[:, None] == jnp.arange(slot_total, dtype=jnp.int32)[None, :]).astype(
        jnp.float32
    )
    active = jnp.arange(entries, dtype=jnp.int32) < entry_count[0]
    current = jnp.where(active[:, None, None], weights, jnp.float32(0.0))
    for sweep in range(ITERS):
        weight_bf = current.astype(jnp.bfloat16)
        products = jnp.einsum(
            "esk,epk->eps", geno_sel, weight_bf, preferred_element_type=jnp.float32
        )
        summed = jnp.einsum("ej,eps->jps", slot_hot, products, precision=lax.Precision.HIGHEST)
        rounded = summed.reshape(
            own_rows * lax.axis_size("snp") // tile_width * tile_width, sample_count
        ).astype(jnp.bfloat16)
        prediction = lax.psum_scatter(
            lax.optimization_barrier(rounded).astype(jnp.float32),
            "snp",
            scatter_dimension=0,
            tiled=True,
        )
        residual = (responses - prediction).astype(jnp.bfloat16)
        shard_rows = lax.all_gather(residual, "snp", axis=0, tiled=True)
        slot_span = shard_rows.shape[0] // tile_width
        pick_slot_part = slot_hot.astype(jnp.bfloat16)
        blocks = shard_rows.reshape(slot_span, tile_width, sample_count)
        picked = jnp.einsum(
            "ej,jps->eps", pick_slot_part, blocks, preferred_element_type=jnp.float32
        )
        local_gradient = jnp.einsum(
            "eps,esk->epk",
            picked.astype(jnp.bfloat16),
            geno_sel,
            preferred_element_type=jnp.float32,
        )
        gradient = lax.psum(local_gradient, "samp")
        current = shrink_soft(current, gradient, cutoff, active)
    return current


def solution(mesh):
    in_specs = (
        P("samp", "snp"),
        P("snp", "samp"),
        P("snp", None, None),
        P("snp", None),
        P("snp"),
        P(),
        P(),
    )
    out_specs = P("snp", None, None)
    return jax.shard_map(
        per_device, mesh=mesh, in_specs=in_specs, out_specs=out_specs, check_vma=False
    )
```

profile of v0, /device:TPU:0, one launch (start us, length us, event | category | flops | bytes accessed | tf_op | source)
XLA Modules:
  0.0 690.2 jit_solution(5242019085507732894)
XLA Ops:
  7.2 0.8 slice_bitcast_fusion.1
  8.0 1.3 copy.28
  9.3 0.5 copy.29
  9.8 0.7 select_reduce_fusion
  10.5 6.7 convolution_convert_fusion
  17.2 37.1 %fusion.10 = f32[128,64,384]{2,1,0:T(8,128)} fusion(bf16[128,384,128]{2,0,1:T(8,128)(2,1)} %convolution_convert_fusion, f32[128,64,128]{2,1,0:T(8,128)} %param.9, pred[128]{0:T(512)(128)(4,1)S(1)} %iota_compare_fusion.4), kind=kOutput, calls=%fused_computation.10 | convolution fusion | flops 806354944 | bytes 29360256 | tf_op jit(solution)/shard_map/esk,epk->eps/dot_general | solution.py:44
  54.3 16.0 %fusion.19 = bf16[48,64,384]{2,0,1:T(8,128)(2,1)S(1)} fusion(f32[128,64,384]{2,1,0:T(8,128)} %fusion.10, s32[128]{0:T(128)S(1)} %select_reduce_fusion), kind=kOutput, calls=%fused_computation.25 | convolution fusion | flops 1813125120 | bytes 14942720 | tf_op jit(solution)/shard_map/ej,eps->jps/dot_general | solution.py:47
  70.3 0.6 copy.32
  70.9 2.4 convert_element_type.54
  73.3 0.0 all-gather.3.cloned.1.call-start
  73.4 98.1 %reduce-scatter.3.cloned.1.call-done = f32[384,384]{1,0:T(8,128)} async-done(((f32[3072,384]{1,0:T(8,128)}), f32[384,384]{1,0:T(8,128)}) %reduce-scatter.3.cloned.1.call-update) | async-done | bytes 589840 | tf_op jit(solution)/shard_map/reduce_scatter | solution.py:51
  171.5 1.8 subtract_convert_fusion.1
  173.3 0.4 all-reduce.3.cloned.1.call-start
  173.8 51.7 %all-gather.3.cloned.1.call-done = bf16[3072,384]{1,0:T(8,128)(2,1)} async-done(((bf16[384,384]{1,0:T(8,128)(2,1)}), bf16[3072,384]{1,0:T(8,128)(2,1)}) %all-gather.3.cloned.1.call-update) | async-done | bytes 2359312 | tf_op jit(solution)/shard_map/all_gather | solution.py:58
  225.5 4.4 convolution_convert_fusion.2
  229.9 33.9 %fusion.8 = f32[128,64,128]{2,1,0:T(8,128)} fusion(bf16[128,384,128]{2,0,1:T(8,128)(2,1)} %convolution_convert_fusion, bf16[128,64,384]{2,0,1:T(8,128)(2,1)S(1)} %convolution_convert_fusion.2), kind=kOutput, calls=%fused_computation.8 | convolution fusion | flops 805306368 | bytes 23068672 | tf_op jit(solution)/shard_map/eps,esk->epk/dot_general | solution.py:65
  263.8 0.0 reduce-scatter.5.cloned.1.call-start
  263.9 0.1 fusion.25
  264.0 84.0 %all-reduce.3.cloned.1.call-done = f32[128,64,128]{2,1,0:T(8,128)} async-done(((f32[128,64,128]{2,1,0:T(8,128)}), f32[128,64,128]{2,1,0:T(8,128)}) %all-reduce.3.cloned.1.call-update) | async-done | bytes 4194320 | tf_op jit(solution)/shard_map/psum | solution.py:71
  348.0 34.3 %fusion.6 = f32[128,64,384]{2,1,0:T(8,128)} fusion(bf16[128,384,128]{2,0,1:T(8,128)(2,1)} %convolution_convert_fusion, f32[128,64,128]{2,1,0:T(8,128)} %all-reduce.3.cloned.1.call-done, f32[128,64,128]{2,1,0:T(8,128)} %param.9, f32[128]{0:T(128)S(1)} %fusion.25, pred[128]{0:T(512)(128)(4,1)S(1)} %iota_compare_fusion.4), kind=kOutput, calls=%fused_computation.6 | convolution fusion | flops 815792128 | bytes 33555072 | tf_op jit(solution)/shard_map/esk,epk->eps/dot_general | solution.py:44
  382.4 16.0 %fusion.22 = bf16[48,64,384]{2,0,1:T(8,128)(2,1)S(1)} fusion(f32[128,64,384]{2,1,0:T(8,128)} %fusion.6, s32[128]{0:T(128)S(1)} %select_reduce_fusion), kind=kOutput, calls=%fused_computation.26 | convolution fusion | flops 1813125120 | bytes 14942720 | tf_op jit(solution)/shard_map/ej,eps->jps/dot_general | solution.py:47
  398.4 0.6 copy.38
  399.0 2.4 convert_element_type.60
  401.4 0.0 all-gather.5.cloned.1.call-start
  401.4 95.5 %reduce-scatter.5.cloned.1.call-done = f32[384,384]{1,0:T(8,128)} async-done(((f32[3072,384]{1,0:T(8,128)}), f32[384,384]{1,0:T(8,128)}) %reduce-scatter.5.cloned.1.call-update) | async-done | bytes 589840 | tf_op jit(solution)/shard_map/reduce_scatter | solution.py:51
  496.9 1.8 subtract_convert_fusion
  498.8 0.3 all-reduce.5.cloned.1.call-start
  499.1 52.0 %all-gather.5.cloned.1.call-done = bf16[3072,384]{1,0:T(8,128)(2,1)} async-done(((bf16[384,384]{1,0:T(8,128)(2,1)}), bf16[3072,384]{1,0:T(8,128)(2,1)}) %all-gather.5.cloned.1.call-update) | async-done | bytes 2359312 | tf_op jit(solution)/shard_map/all_gather | solution.py:58
  551.1 4.4 convolution_convert_fusion.1
  555.5 34.3 %fusion.4 = f32[128,64,128]{2,1,0:T(8,128)} fusion(bf16[128,384,128]{2,0,1:T(8,128)(2,1)} %convolution_convert_fusion, bf16[128,64,384]{2,0,1:T(8,128)(2,1)S(1)} %convolution_convert_fusion.1), kind=kOutput, calls=%fused_computation.4 | convolution fusion | flops 805306368 | bytes 23068672 | tf_op jit(solution)/shard_map/eps,esk->epk/dot_general | solution.py:65
  589.8 84.2 %all-reduce.5.cloned.1.call-done = f32[128,64,128]{2,1,0:T(8,128)} async-done(((f32[128,64,128]{2,1,0:T(8,128)}), f32[128,64,128]{2,1,0:T(8,128)}) %all-reduce.5.cloned.1.call-update) | async-done | bytes 4194320 | tf_op jit(solution)/shard_map/psum | solution.py:71
  674.0 9.2 %multiply_select_fusion = f32[128,64,128]{2,1,0:T(8,128)} fusion(f32[128,64,128]{2,1,0:T(8,128)} %all-reduce.5.cloned.1.call-done, f32[128]{0:T(128)S(1)} %fusion.25, pred[128]{0:T(512)(128)(4,1)S(1)} %iota_compare_fusion.4, f32[128,64,128]{2,1,0:T(8,128)} %all-reduce.3.cloned.1.call-done, f32[128,64,128]{2,1,0:T(8,128)} %param.9), kind=kLoop, calls=%fused_computation.15 | loop fusion | flops 17825792 | bytes 16777856 | tf_op jit(solution)/shard_map/jit(_where)/select_n | solution.py:15
  (14 shorter events, 0.1 us)
Async XLA Ops:
  6.5 257.3 %copy-start = (f32[46]{0:T(128)S(1)}, f32[46]{0:T(128)}, u32[]{:S(2)}) copy-start(f32[46]{0:T(128)} %param.13) | copy-start | bytes 556
  6.5 164.9 %reduce-scatter.3.cloned.1.call-start = ((), (), s32[]{:S(2)}) async-start(), calls=%async_computation.2 | async-start | bytes 5308416 | tf_op jit(solution)/shard_map/reduce_scatter | solution.py:51
  70.9 100.6 %copy-start.2 = (f32[384,384]{1,0:T(8,128)S(1)}, f32[384,384]{1,0:T(8,128)}, u32[]{:S(2)}) copy-start(f32[384,384]{1,0:T(8,128)} %param.8) | copy-start | bytes 1769476
  73.3 152.2 %all-gather.3.cloned.1.call-start = ((), (), s32[]{:S(2)}) async-start(), calls=%async_computation.3 | async-start | bytes 2654208 | tf_op jit(solution)/shard_map/all_gather | solution.py:58
  173.3 174.7 %all-reduce.3.cloned.1.call-start = ((), (), s32[]{:S(2)}) async-start(), calls=%async_computation.4 | async-start | bytes 8388608 | tf_op jit(solution)/shard_map/psum | solution.py:71
  263.8 233.1 %reduce-scatter.5.cloned.1.call-start = ((), (), s32[]{:S(2)}) async-start(), calls=%async_computation.5 | async-start | bytes 5308416 | tf_op jit(solution)/shard_map/reduce_scatter | solution.py:51
  401.4 149.7 %all-gather.5.cloned.1.call-start = ((), (), s32[]{:S(2)}) async-start(), calls=%async_computation.6 | async-start | bytes 2654208 | tf_op jit(solution)/shard_map/all_gather | solution.py:58
  498.8 175.2 %all-reduce.5.cloned.1.call-start = ((), (), s32[]{:S(2)}) async-start(), calls=%async_computation.7 | async-start | bytes 8388608 | tf_op jit(solution)/shard_map/psum | solution.py:71
  674.0 9.2 %copy-start.1 = (f32[46]{0:T(128)S(1)}, f32[46]{0:T(128)}, u32[]{:S(2)}) copy-start(f32[46]{0:T(128)} %param.13) | copy-start | bytes 556
Sparse Core Ops, SparseCore 0:
  73.4 97.9 reduce-scatter.2
  173.6 51.8 all-gather.2
  263.9 84.0 all-reduce.2
  401.5 95.3 reduce-scatter.4
  499.2 51.8 all-gather.4
  589.9 84.0 all-reduce.4
where the time goes:
time: 693 us; the launch traced here: 690 us
  waiting for transfers between devices  466 us (67%)
  matrix products  187 us (27%)
  other arithmetic  18.4 us (3%)
  between operations  14.4 us (2%)
    reduce_scatter x2, waiting for transfers between devices, per_device(): lax.psum_scatter(lax.optimization_barrier(rounded).astype(jnp.float32), '...  194 us
    psum x2, waiting for transfers between devices, per_device(): gradient = lax.psum(local_gradient, 'samp')  168 us
    all_gather x2, waiting for transfers between devices, per_device(): shard_rows = lax.all_gather(residual, 'snp', axis=0, tiled=True)  104 us
    dot_general x2, matrix products, per_device(): jnp.einsum('esk,epk->eps', geno_sel, weight_bf, preferred_element_type=jn...  71.4 us
    dot_general x2, matrix products, per_device(): jnp.einsum('eps,esk->epk', picked.astype(jnp.bfloat16), geno_sel, preferr...  68.1 us
    dot_general x2, matrix products, per_device(): jnp.einsum('ej,eps->jps', slot_hot, products, precision=lax.Precision.HIG...  32 us
  transfers between devices with their start and end apart: 6, of which 6 were waited for; matrix products, arithmetic and copies ran while one was open for 0% of the time, Pallas kernels for 0%

commit v1 on v0

v1 whole, which is shorter than its diff:
```python
import jax
import jax.numpy as jnp
from jax import lax
from jax.sharding import PartitionSpec as P

ITERS = 2


step_scale = 0.3


def shrink_soft(current, gradient, cutoff, active):
    shifted = current + step_scale * gradient
    shrunk = jnp.sign(shifted) * jnp.maximum(jnp.abs(shifted) - cutoff, jnp.float32(0.0))
    return jnp.where(active[:, None, None], shrunk, jnp.float32(0.0))


def per_device(genotypes, responses, weights, pattern, entry_count, tile_slot, penalty):
    sample_count = genotypes.shape[0]
    entries, tile_width, block_width = weights.shape
    block_count = genotypes.shape[1] // block_width
    own_rows = responses.shape[0]
    owners = lax.axis_size("snp")
    own_slots = own_rows // tile_width
    slot_total = owners * own_slots
    cells = slot_total * block_count

    geno_blocks = genotypes.reshape(sample_count, block_count, block_width)
    blk = pattern[:, 0]
    tile = pattern[:, 1]
    tile_hot = tile[:, None] == jnp.arange(penalty.shape[0], dtype=jnp.int32)[None, :]
    slot_ids = jnp.sum(jnp.where(tile_hot, tile_slot[None, :], 0), axis=1)
    per_entry = jnp.sum(jnp.where(tile_hot, penalty[None, :], jnp.float32(0.0)), axis=1)
    cutoff = step_scale * per_entry[:, None, None]
    cell = slot_ids * block_count + blk
    cell_hot = (cell[:, None] == jnp.arange(cells, dtype=jnp.int32)[None, :]).astype(jnp.bfloat16)
    active = jnp.arange(entries, dtype=jnp.int32) < entry_count[0]
    current = jnp.where(active[:, None, None], weights, jnp.float32(0.0))
    for sweep in range(ITERS):
        weight_bf = current.astype(jnp.bfloat16)
        dense = jnp.einsum(
            "ec,epk->cpk", cell_hot, weight_bf, preferred_element_type=jnp.float32
        ).astype(jnp.bfloat16)
        dense = dense.reshape(slot_total, block_count, tile_width, block_width)
        partial = jnp.einsum(
            "jbpk,sbk->jps", dense, geno_blocks, preferred_element_type=jnp.float32
        ).astype(jnp.bfloat16)
        partial = partial.reshape(owners, own_rows, sample_count)
        gathered = lax.all_to_all(partial, "snp", 0, 0, tiled=False)
        prediction = jnp.sum(gathered.astype(jnp.float32), axis=0)
        residual = (responses - prediction).astype(jnp.bfloat16)
        shard_rows = lax.all_gather(residual, "snp", axis=0, tiled=True)
        blocks = shard_rows.reshape(slot_total, tile_width, sample_count)
        full = jnp.einsum(
            "jps,sbk->jbpk", blocks, geno_blocks, preferred_element_type=jnp.float32
        ).reshape(cells, tile_width, block_width)
        local_gradient = jnp.take(full, cell, axis=0, mode="clip")
        gradient = lax.psum(local_gradient, "samp")
        current = shrink_soft(current, gradient, cutoff, active)
    return current


def solution(mesh):
    in_specs = (
        P("samp", "snp"),
        P("snp", "samp"),
        P("snp", None, None),
        P("snp", None),
        P("snp"),
        P(),
        P(),
    )
    out_specs = P("snp", None, None)
    return jax.shard_map(
        per_device, mesh=mesh, in_specs=in_specs, out_specs=out_specs, check_vma=False
    )
```

time: 693 us -> 465 us (0.67)
  waiting for transfers between devices: 466 us -> 269 us
  matrix products: 187 us -> 23.6 us
  blocking collectives: 0 us -> 120 us
  local copies, waits for them, and re-layouts: 3.76 us -> 16.5 us
    reduce_scatter x2 -> x0, waiting for transfers between devices: 194 us -> none  [per_device(): lax.psum_scatter(lax.optimization_barrier(rounded).astype(jnp.float32), '...]
    dot_general x10 -> x6, matrix products: 187 us -> 23.6 us  [the longest x2 14.3 us: per_device(): jnp.einsum('jps,sbk->jbpk', blocks, geno_blocks, preferred_element_type=j...]
    all_to_all x0 -> x2, blocking collectives: none -> 120 us  [per_device(): gathered = lax.all_to_all(partial, 'snp', 0, 0, tiled=False)]
    gather x0 -> x2, local copies, waits for them, and re-layouts: none -> 12.1 us  [per_device(): local_gradient = jnp.take(full, cell, axis=0, mode='clip')]
  transfers between devices with their start and end apart: 6 -> 4, of which waited for: 6 -> 4; matrix products, arithmetic and copies ran while one was open for 0% -> 0% of each run, Pallas kernels for 0% -> 0%
where the time goes in v1:
time: 465 us; the launch traced here: 464 us
  waiting for transfers between devices  269 us (58%)
  blocking collectives  120 us (26%)
  matrix products  23.6 us (5%)
  other arithmetic  20.2 us (4%)
  local copies, waits for them, and re-layouts  16.5 us (4%)
  between operations  13.9 us (3%)
    psum x2, waiting for transfers between devices, per_device(): gradient = lax.psum(local_gradient, 'samp')  168 us
    all_to_all x2, blocking collectives, per_device(): gathered = lax.all_to_all(partial, 'snp', 0, 0, tiled=False)  120 us
    all_gather x2, waiting for transfers between devices, per_device(): shard_rows = lax.all_gather(residual, 'snp', axis=0, tiled=True)  102 us
    dot_general x2, matrix products, per_device(): jnp.einsum('jps,sbk->jbpk', blocks, geno_blocks, preferred_element_type=j...  14.3 us
    gather x2, local copies, waits for them, and re-layouts, per_device(): local_gradient = jnp.take(full, cell, axis=0, mode='clip')  12.1 us
  transfers between devices with their start and end apart: 4, of which 4 were waited for; matrix products, arithmetic and copies ran while one was open for 0% of the time, Pallas kernels for 0%

profile of v1, /device:TPU:0, one launch (start us, length us, event | category | flops | bytes accessed | tf_op | source)
XLA Modules:
  0.0 464.2 jit_solution(16346456032483803781)
XLA Ops:
  7.2 0.7 slice_bitcast_fusion
  7.9 0.7 select_reduce_fusion.1
  8.6 0.7 fusion.7
  9.3 1.3 copy.27
  10.6 2.6 select_convert_fusion
  13.2 2.0 convolution_convert_fusion.1
  15.3 1.0 copy.26
  16.3 2.6 bitcast_convert_fusion.1
  18.9 61.1 %all_to_all.10 = bf16[8,384,384]{2,1,0:T(8,128)(2,1)S(1)} all-to-all(bf16[8,384,384]{2,1,0:T(8,128)(2,1)S(1)} %bitcast.62), channel_id=1, replica_groups=mesh['snp'=8,'samp'=4] {'snp'}, dimensions={0} | all-to-all | bytes 4718592 | tf_op jit(solution)/shard_map/all_to_all | solution.py:49
  80.0 0.3 convert_reduce_fusion.1
  80.4 0.8 subtract_convert_fusion.1
  81.2 0.0 all-reduce.3.cloned.1.call-start
  81.2 51.2 %all-gather.3.cloned.1.call-done = bf16[3072,384]{1,0:T(8,128)(2,1)} async-done(((bf16[384,384]{1,0:T(8,128)(2,1)}), bf16[3072,384]{1,0:T(8,128)(2,1)}) %all-gather.3.cloned.1.call-update) | async-done | bytes 2359312 | tf_op jit(solution)/shard_map/all_gather | solution.py:52
  132.4 7.2 %fusion.9 = f32[48,64,5,128]{3,1,2,0:T(8,128)} fusion(bf16[48,64,384,1]{2,1,3,0:T(8,128)(2,1)} %bitcast.64, bf16[384,5,128,1]{0,2,1,3:T(8,128)(2,1)S(1)} %bitcast.57), kind=kOutput, calls=%fused_computation.29 | convolution fusion | flops 1509949440 | bytes 10715136 | tf_op jit(solution)/shard_map/jps,sbk->jbpk/dot_general | solution.py:54
  139.6 6.1 %gather_fusion = f32[128,64,128]{2,1,0:T(8,128)} fusion(f32[240,64,128]{2,1,0:T(8,128)} %bitcast.55, s32[1024]{0:T(1024)S(1)} %pad_clamp_fusion), kind=kCustom, calls=%fused_computation | custom fusion | bytes 8389120 | tf_op jit(solution)/shard_map/jit(_take)/gather | solution.py:57
  145.7 0.2 all-gather.5.cloned.1.call-start
  145.9 0.4 copy-done.1
  146.3 0.1 select_reduce_fusion
  146.4 83.4 %all-reduce.3.cloned.1.call-done = f32[128,64,128]{2,1,0:T(8,128)} async-done(((f32[128,64,128]{2,1,0:T(8,128)}), f32[128,64,128]{2,1,0:T(8,128)}) %all-reduce.3.cloned.1.call-update) | async-done | bytes 4194320 | tf_op jit(solution)/shard_map/psum | solution.py:58
  229.8 4.7 %fusion.8 = bf16[128,64,128]{2,1,0:T(8,128)(2,1)S(1)} fusion(f32[128]{0:T(128)S(1)} %broadcast_multiply_fusion, f32[128,64,128]{2,1,0:T(8,128)} %all-reduce.3.cloned.1.call-done, f32[128,64,128]{2,1,0:T(8,128)} %param.9, pred[128]{0:T(512)(128)(4,1)S(1)} %iota_compare_fusion.2), kind=kLoop, calls=%fused_computation.28 | loop fusion | flops 10485760 | bytes 10486400 | tf_op jit(solution)/shard_map/convert_element_type | solution.py:40
  234.6 2.0 convolution_convert_fusion
  236.6 1.0 copy.31
  237.6 2.6 bitcast_convert_fusion
  240.3 59.1 %all_to_all.11 = bf16[8,384,384]{2,1,0:T(8,128)(2,1)S(1)} all-to-all(bf16[8,384,384]{2,1,0:T(8,128)(2,1)S(1)} %bitcast.63), channel_id=1, replica_groups=mesh['snp'=8,'samp'=4] {'snp'}, dimensions={0} | all-to-all | bytes 4718592 | tf_op jit(solution)/shard_map/all_to_all | solution.py:49
  299.4 0.3 convert_reduce_fusion
  299.7 0.8 subtract_convert_fusion
  300.5 0.0 all-reduce.5.cloned.1.call-start
  300.6 50.6 %all-gather.5.cloned.1.call-done = bf16[3072,384]{1,0:T(8,128)(2,1)} async-done(((bf16[384,384]{1,0:T(8,128)(2,1)}), bf16[3072,384]{1,0:T(8,128)(2,1)}) %all-gather.5.cloned.1.call-update) | async-done | bytes 2359312 | tf_op jit(solution)/shard_map/all_gather | solution.py:52
  351.2 7.2 %fusion.10 = f32[48,64,5,128]{3,1,2,0:T(8,128)} fusion(bf16[48,64,384,1]{2,1,3,0:T(8,128)(2,1)} %bitcast.65, bf16[384,5,128,1]{0,2,1,3:T(8,128)(2,1)S(1)} %bitcast.59), kind=kOutput, calls=%fused_computation.30 | convolution fusion | flops 1509949440 | bytes 10715136 | tf_op jit(solution)/shard_map/jps,sbk->jbpk/dot_general | solution.py:54
  358.4 6.1 %gather_fusion.1 = f32[128,64,128]{2,1,0:T(8,128)} fusion(f32[240,64,128]{2,1,0:T(8,128)} %bitcast.54, s32[1024]{0:T(1024)S(1)} %pad_clamp_fusion), kind=kCustom, calls=%fused_computation.1 | custom fusion | bytes 8389120 | tf_op jit(solution)/shard_map/jit(_take)/gather | solution.py:57
  364.5 84.2 %all-reduce.5.cloned.1.call-done = f32[128,64,128]{2,1,0:T(8,128)} async-done(((f32[128,64,128]{2,1,0:T(8,128)}), f32[128,64,128]{2,1,0:T(8,128)}) %all-reduce.5.cloned.1.call-update) | async-done | bytes 4194320 | tf_op jit(solution)/shard_map/psum | solution.py:58
  448.6 9.1 %multiply_select_fusion = f32[128,64,128]{2,1,0:T(8,128)} fusion(f32[128,64,128]{2,1,0:T(8,128)} %all-reduce.5.cloned.1.call-done, f32[128]{0:T(128)S(1)} %broadcast_multiply_fusion, pred[128]{0:T(512)(128)(4,1)S(1)} %iota_compare_fusion.2, f32[128,64,128]{2,1,0:T(8,128)} %all-reduce.3.cloned.1.call-done, f32[128,64,128]{2,1,0:T(8,128)} %param.9), kind=kLoop, calls=%fused_computation.6 | loop fusion | flops 17825792 | bytes 16777856 | tf_op jit(solution)/shard_map/jit(_where)/select_n | solution.py:15
  (11 shorter events, 0.1 us)
Async XLA Ops:
  6.5 125.9 %all-gather.3.cloned.1.call-start = ((), (), s32[]{:S(2)}) async-start(), calls=%async_computation.2 | async-start | bytes 2654208 | tf_op jit(solution)/shard_map/all_gather | solution.py:52
  18.9 61.4 %copy-start = (f32[384,384]{1,0:T(8,128)S(1)}, f32[384,384]{1,0:T(8,128)}, u32[]{:S(2)}) copy-start(f32[384,384]{1,0:T(8,128)} %param.8) | copy-start | bytes 1769476
  81.2 148.7 %all-reduce.3.cloned.1.call-start = ((), (), s32[]{:S(2)}) async-start(), calls=%async_computation.3 | async-start | bytes 8388608 | tf_op jit(solution)/shard_map/psum | solution.py:58
  145.7 0.7 copy-start.1
  145.7 205.5 %all-gather.5.cloned.1.call-start = ((), (), s32[]{:S(2)}) async-start(), calls=%async_computation.4 | async-start | bytes 2654208 | tf_op jit(solution)/shard_map/all_gather | solution.py:52
  300.5 148.1 %all-reduce.5.cloned.1.call-start = ((), (), s32[]{:S(2)}) async-start(), calls=%async_computation.5 | async-start | bytes 8388608 | tf_op jit(solution)/shard_map/psum | solution.py:58
Sparse Core Ops, SparseCore 0:
  81.3 51.0 all-gather.2
  145.8 83.9 all-reduce.2
  300.7 50.4 all-gather.4
  364.6 84.0 all-reduce.4

commit v2 on v1

--- a/solution.py
+++ b/solution.py
@@ -55,15 +55,29 @@
             "jps,sbk->jbpk", blocks, geno_blocks, preferred_element_type=jnp.float32
         ).reshape(cells, tile_width, block_width)
         local_gradient = jnp.take(full, cell, axis=0, mode="clip")
-        gradient = lax.psum(local_gradient, "samp")
+        if SPLIT_SAMP:
+            part = lax.psum_scatter(local_gradient, "sc", scatter_dimension=0, tiled=True)
+            part = lax.psum(part, "sx")
+            gradient = lax.all_gather(part, "sc", axis=0, tiled=True)
+        else:
+            gradient = lax.psum(local_gradient, "samp")
         current = shrink_soft(current, gradient, cutoff, active)
     return current
 
 
+SPLIT_SAMP = True
+
+
 def solution(mesh):
+    snp_size, samp_size = mesh.devices.shape
+    samp = "samp"
+    if SPLIT_SAMP:
+        devices = mesh.devices.reshape(snp_size, 2, samp_size // 2)
+        mesh = jax.sharding.Mesh(devices, ("snp", "sx", "sc"))
+        samp = ("sx", "sc")
     in_specs = (
-        P("samp", "snp"),
-        P("snp", "samp"),
+        P(samp, "snp"),
+        P("snp", samp),
         P("snp", None, None),
         P("snp", None),
         P("snp"),

time: 465 us -> 483 us (1.039)
  waiting for transfers between devices: 269 us -> 287 us
    psum x2, waiting for transfers between devices: 168 us -> 133 us  [per_device(): part = lax.psum(part, 'sx')]
    all_gather x0 -> x2, waiting for transfers between devices: none -> 30 us  [per_device(): gradient = lax.all_gather(part, 'sc', axis=0, tiled=True)]
    reduce_scatter x0 -> x2, waiting for transfers between devices: none -> 21.4 us  [per_device(): lax.psum_scatter(local_gradient, 'sc', scatter_dimension=0, tiled=True)]
  transfers between devices with their start and end apart: 4 -> 8, of which waited for: 4 -> 8; matrix products, arithmetic and copies ran while one was open for 0% -> 0% of each run, Pallas kernels for 0% -> 0%
where the time goes in v2:
time: 483 us
  waiting for transfers between devices  287 us (59%)
  blocking collectives  121 us (25%)
  matrix products  23.6 us (5%)
  other arithmetic  20.2 us (4%)
  local copies, waits for them, and re-layouts  16.1 us (3%)
  between operations  14.3 us (3%)
    psum x2, waiting for transfers between devices, per_device(): part = lax.psum(part, 'sx')  133 us
    all_to_all x2, blocking collectives, per_device(): gathered = lax.all_to_all(partial, 'snp', 0, 0, tiled=False)  121 us
    all_gather x2, waiting for transfers between devices, per_device(): shard_rows = lax.all_gather(residual, 'snp', axis=0, tiled=True)  102 us
    all_gather x2, waiting for transfers between devices, per_device(): gradient = lax.all_gather(part, 'sc', axis=0, tiled=True)  30 us
    reduce_scatter x2, waiting for transfers between devices, per_device(): lax.psum_scatter(local_gradient, 'sc', scatter_dimension=0, tiled=True)  21.4 us
    dot_general x2, matrix products, per_device(): jnp.einsum('jps,sbk->jbpk', blocks, geno_blocks, preferred_element_type=j...  14.3 us
    gather x2, local copies, waits for them, and re-layouts, per_device(): local_gradient = jnp.take(full, cell, axis=0, mode='clip')  12.1 us
  transfers between devices with their start and end apart: 8, of which 8 were waited for; matrix products, arithmetic and copies ran while one was open for 0% of the time, Pallas kernels for 0%

profile of v2, /device:TPU:0, one launch (start us, length us, event | category | flops | bytes accessed | tf_op | source)
XLA Modules:
  0.0 482.6 jit_solution(14898244865369778887)
XLA Ops:
  7.2 0.7 slice_bitcast_fusion
  7.9 0.7 select_reduce_fusion.1
  8.6 0.7 fusion.7
  9.3 1.3 copy.36
  10.6 2.6 select_convert_fusion
  13.2 2.0 convolution_convert_fusion.1
  15.3 1.0 copy.35
  16.3 2.6 bitcast_convert_fusion.1
  18.9 61.1 %all_to_all.10 = bf16[8,384,384]{2,1,0:T(8,128)(2,1)S(1)} all-to-all(bf16[8,384,384]{2,1,0:T(8,128)(2,1)S(1)} %bitcast.62), channel_id=1, replica_groups=mesh['snp'=8,'sx'=2,'sc'=2] {'snp'}, dimensions={0} | all-to-all | bytes 4718592 | tf_op jit(solution)/shard_map/all_to_all | solution.py:49
  80.0 0.3 convert_reduce_fusion.1
  80.4 0.8 subtract_convert_fusion.1
  81.2 51.2 %all-gather.5.cloned.1.call-done = bf16[3072,384]{1,0:T(8,128)(2,1)} async-done(((bf16[384,384]{1,0:T(8,128)(2,1)}), bf16[3072,384]{1,0:T(8,128)(2,1)}) %all-gather.5.cloned.1.call-update) | async-done | bytes 2359312 | tf_op jit(solution)/shard_map/all_gather | solution.py:52
  132.4 7.2 %fusion.9 = f32[48,64,5,128]{3,1,2,0:T(8,128)} fusion(bf16[48,64,384,1]{2,1,3,0:T(8,128)(2,1)} %bitcast.64, bf16[384,5,128,1]{0,2,1,3:T(8,128)(2,1)S(1)} %bitcast.57), kind=kOutput, calls=%fused_computation.29 | convolution fusion | flops 1509949440 | bytes 10715136 | tf_op jit(solution)/shard_map/jps,sbk->jbpk/dot_general | solution.py:54
  139.6 6.1 %gather_fusion = f32[128,64,128]{2,1,0:T(8,128)} fusion(f32[240,64,128]{2,1,0:T(8,128)} %bitcast.55, s32[1024]{0:T(1024)S(1)} %pad_clamp_fusion), kind=kCustom, calls=%fused_computation | custom fusion | bytes 8389120 | tf_op jit(solution)/shard_map/jit(_take)/gather | solution.py:57
  145.7 10.7 %reduce-scatter.3.cloned.1.call-done = f32[64,64,128]{2,1,0:T(8,128)} async-done(((f32[128,64,128]{2,1,0:T(8,128)}), f32[64,64,128]{2,1,0:T(8,128)}) %reduce-scatter.3.cloned.1.call-update) | async-done | bytes 2097168 | tf_op jit(solution)/shard_map/reduce_scatter | solution.py:59
  156.5 66.6 %all-reduce.3.cloned.1.call-done = f32[64,64,128]{2,1,0:T(8,128)} async-done(((f32[64,64,128]{2,1,0:T(8,128)}), f32[64,64,128]{2,1,0:T(8,128)}) %all-reduce.3.cloned.1.call-update) | async-done | bytes 2097168 | tf_op jit(solution)/shard_map/psum | solution.py:60
  223.1 0.2 all-gather.9.cloned.1.call-start
  223.4 14.7 %all-gather.7.cloned.1.call-done = f32[128,64,128]{2,1,0:T(8,128)} async-done(((f32[64,64,128]{2,1,0:T(8,128)}), f32[128,64,128]{2,1,0:T(8,128)}) %all-gather.7.cloned.1.call-update) | async-done | bytes 4194320 | tf_op jit(solution)/shard_map/all_gather | solution.py:61
  238.1 4.7 fusion.8
  242.9 2.0 convolution_convert_fusion
  244.9 1.0 copy.40
  245.9 2.6 bitcast_convert_fusion
  248.6 59.8 %all_to_all.11 = bf16[8,384,384]{2,1,0:T(8,128)(2,1)S(1)} all-to-all(bf16[8,384,384]{2,1,0:T(8,128)(2,1)S(1)} %bitcast.63), channel_id=1, replica_groups=mesh['snp'=8,'sx'=2,'sc'=2] {'snp'}, dimensions={0} | all-to-all | bytes 4718592 | tf_op jit(solution)/shard_map/all_to_all | solution.py:49
  308.4 0.3 convert_reduce_fusion
  308.7 0.8 subtract_convert_fusion
  309.6 51.2 %all-gather.9.cloned.1.call-done = bf16[3072,384]{1,0:T(8,128)(2,1)} async-done(((bf16[384,384]{1,0:T(8,128)(2,1)}), bf16[3072,384]{1,0:T(8,128)(2,1)}) %all-gather.9.cloned.1.call-update) | async-done | bytes 2359312 | tf_op jit(solution)/shard_map/all_gather | solution.py:52
  360.8 7.2 %fusion.10 = f32[48,64,5,128]{3,1,2,0:T(8,128)} fusion(bf16[48,64,384,1]{2,1,3,0:T(8,128)(2,1)} %bitcast.65, bf16[384,5,128,1]{0,2,1,3:T(8,128)(2,1)S(1)} %bitcast.59), kind=kOutput, calls=%fused_computation.30 | convolution fusion | flops 1509949440 | bytes 10715136 | tf_op jit(solution)/shard_map/jps,sbk->jbpk/dot_general | solution.py:54
  368.0 6.1 %gather_fusion.1 = f32[128,64,128]{2,1,0:T(8,128)} fusion(f32[240,64,128]{2,1,0:T(8,128)} %bitcast.54, s32[1024]{0:T(1024)S(1)} %pad_clamp_fusion), kind=kCustom, calls=%fused_computation.1 | custom fusion | bytes 8389120 | tf_op jit(solution)/shard_map/jit(_take)/gather | solution.py:57
  374.1 10.7 %reduce-scatter.5.cloned.1.call-done = f32[64,64,128]{2,1,0:T(8,128)} async-done(((f32[128,64,128]{2,1,0:T(8,128)}), f32[64,64,128]{2,1,0:T(8,128)}) %reduce-scatter.5.cloned.1.call-update) | async-done | bytes 2097168 | tf_op jit(solution)/shard_map/reduce_scatter | solution.py:59
  384.9 66.5 %all-reduce.5.cloned.1.call-done = f32[64,64,128]{2,1,0:T(8,128)} async-done(((f32[64,64,128]{2,1,0:T(8,128)}), f32[64,64,128]{2,1,0:T(8,128)}) %all-reduce.5.cloned.1.call-update) | async-done | bytes 2097168 | tf_op jit(solution)/shard_map/psum | solution.py:60
  451.5 15.2 %all-gather.11.cloned.1.call-done = f32[128,64,128]{2,1,0:T(8,128)} async-done(((f32[64,64,128]{2,1,0:T(8,128)}), f32[128,64,128]{2,1,0:T(8,128)}) %all-gather.11.cloned.1.call-update) | async-done | bytes 4194320 | tf_op jit(solution)/shard_map/all_gather | solution.py:61
  466.7 9.1 %multiply_select_fusion = f32[128,64,128]{2,1,0:T(8,128)} fusion(f32[128,64,128]{2,1,0:T(8,128)} %all-gather.11.cloned.1.call-done, f32[128]{0:T(128)S(1)} %broadcast_multiply_fusion, pred[128]{0:T(512)(128)(4,1)S(1)} %iota_compare_fusion.2, f32[128,64,128]{2,1,0:T(8,128)} %all-gather.7.cloned.1.call-done, f32[128,64,128]{2,1,0:T(8,128)} %param.9), kind=kLoop, calls=%fused_computation.6 | loop fusion | flops 17825792 | bytes 16777856 | tf_op jit(solution)/shard_map/jit(_where)/select_n | solution.py:15
  (23 shorter events, 0.5 us)
Async XLA Ops:
  6.5 125.9 %all-gather.5.cloned.1.call-start = ((), (), s32[]{:S(2)}) async-start(), calls=%async_computation.4 | async-start | bytes 2654208 | tf_op jit(solution)/shard_map/all_gather | solution.py:52
  18.9 61.4 %copy-start = (f32[384,384]{1,0:T(8,128)S(1)}, f32[384,384]{1,0:T(8,128)}, u32[]{:S(2)}) copy-start(f32[384,384]{1,0:T(8,128)} %param.8) | copy-start | bytes 1769476
  81.2 75.2 %reduce-scatter.3.cloned.1.call-start = ((), (), s32[]{:S(2)}) async-start(), calls=%async_computation.5 | async-start | bytes 6291456 | tf_op jit(solution)/shard_map/reduce_scatter | solution.py:59
  145.6 77.6 %copy-start.1 = (f32[46]{0:T(128)S(1)}, f32[46]{0:T(128)}, u32[]{:S(2)}) copy-start(f32[46]{0:T(128)} %param.13) | copy-start | bytes 556
  145.7 77.4 %all-reduce.3.cloned.1.call-start = ((), (), s32[]{:S(2)}) async-start(), calls=%async_computation.6 | async-start | bytes 4194304 | tf_op jit(solution)/shard_map/psum | solution.py:60
  156.4 81.7 %all-gather.7.cloned.1.call-start = ((), (), s32[]{:S(2)}) async-start(), calls=%async_computation.7 | async-start | bytes 6291456 | tf_op jit(solution)/shard_map/all_gather | solution.py:61
  223.1 137.8 %all-gather.9.cloned.1.call-start = ((), (), s32[]{:S(2)}) async-start(), calls=%async_computation.8 | async-start | bytes 2654208 | tf_op jit(solution)/shard_map/all_gather | solution.py:52
  309.6 75.3 %reduce-scatter.5.cloned.1.call-start = ((), (), s32[]{:S(2)}) async-start(), calls=%async_computation.9 | async-start | bytes 6291456 | tf_op jit(solution)/shard_map/reduce_scatter | solution.py:59
  374.1 77.3 %all-reduce.5.cloned.1.call-start = ((), (), s32[]{:S(2)}) async-start(), calls=%async_computation.10 | async-start | bytes 4194304 | tf_op jit(solution)/shard_map/psum | solution.py:60
  384.9 81.8 %all-gather.11.cloned.1.call-start = ((), (), s32[]{:S(2)}) async-start(), calls=%async_computation.11 | async-start | bytes 6291456 | tf_op jit(solution)/shard_map/all_gather | solution.py:61
Sparse Core Ops, SparseCore 0:
  81.3 51.0 all-gather.4
  145.8 10.5 reduce-scatter.2
  158.8 64.1 all-reduce.2
  224.4 13.6 all-gather.6
  309.7 51.1 all-gather.8
  374.2 10.5 reduce-scatter.4
  387.2 64.1 all-reduce.4
  453.0 13.6 all-gather.10

commit v3 on v1

--- a/solution.py
+++ b/solution.py
@@ -55,7 +55,7 @@
             "jps,sbk->jbpk", blocks, geno_blocks, preferred_element_type=jnp.float32
         ).reshape(cells, tile_width, block_width)
         local_gradient = jnp.take(full, cell, axis=0, mode="clip")
-        gradient = lax.psum(local_gradient, "samp")
+        gradient = lax.psum(local_gradient.astype(jnp.bfloat16), "samp").astype(jnp.float32)
         current = shrink_soft(current, gradient, cutoff, active)
     return current
 

time: 465 us -> 390 us (0.84)
  waiting for transfers between devices: 269 us -> 202 us
    psum x2, waiting for transfers between devices: 168 us -> 99.8 us  [per_device(): lax.psum(local_gradient.astype(jnp.bfloat16), 'samp').astype(jnp.float32)]
where the time goes in v3:
time: 390 us; the launch traced here: 389 us
  waiting for transfers between devices  202 us (52%)
  blocking collectives  120 us (31%)
  matrix products  21.3 us (5%)
  other arithmetic  19.3 us (5%)
  between operations  13.9 us (4%)
  local copies, waits for them, and re-layouts  12.7 us (3%)
    all_to_all x2, blocking collectives, per_device(): gathered = lax.all_to_all(partial, 'snp', 0, 0, tiled=False)  120 us
    all_gather x2, waiting for transfers between devices, per_device(): shard_rows = lax.all_gather(residual, 'snp', axis=0, tiled=True)  102 us
    psum x2, waiting for transfers between devices, per_device(): lax.psum(local_gradient.astype(jnp.bfloat16), 'samp').astype(jnp.float32)  99.8 us
    dot_general x2, matrix products, per_device(): jnp.einsum('jps,sbk->jbpk', blocks, geno_blocks, preferred_element_type=j...  12 us
    gather x2, local copies, waits for them, and re-layouts, per_device(): local_gradient = jnp.take(full, cell, axis=0, mode='clip')  8.64 us
    select_n x1, other arithmetic, shrink_soft(): return jnp.where(active[:, None, None], shrunk, jnp.float32(0.0))  8.37 us
  transfers between devices with their start and end apart: 4, of which 4 were waited for; matrix products, arithmetic and copies ran while one was open for 0% of the time, Pallas kernels for 0%

profile of v3, /device:TPU:0, one launch (start us, length us, event | category | flops | bytes accessed | tf_op | source)
XLA Modules:
  0.0 389.2 jit_solution(18349182942142321295)
XLA Ops:
  7.2 0.7 slice_bitcast_fusion
  7.9 0.7 select_reduce_fusion.1
  8.6 0.7 fusion.7
  9.3 1.3 copy.27
  10.6 2.6 select_convert_fusion
  13.2 2.0 convolution_convert_fusion.1
  15.3 1.0 copy.26
  16.3 2.6 bitcast_convert_fusion.1
  18.9 61.1 %all_to_all.10 = bf16[8,384,384]{2,1,0:T(8,128)(2,1)S(1)} all-to-all(bf16[8,384,384]{2,1,0:T(8,128)(2,1)S(1)} %bitcast.56), channel_id=1, replica_groups=mesh['snp'=8,'samp'=4] {'snp'}, dimensions={0} | all-to-all | bytes 4718592 | tf_op jit(solution)/shard_map/all_to_all | solution.py:49
  80.0 0.3 convert_reduce_fusion.1
  80.4 0.8 subtract_convert_fusion.1
  81.2 0.0 all-reduce.3.cloned.1.call-start
  81.2 51.2 %all-gather.3.cloned.1.call-done = bf16[3072,384]{1,0:T(8,128)(2,1)} async-done(((bf16[384,384]{1,0:T(8,128)(2,1)}), bf16[3072,384]{1,0:T(8,128)(2,1)}) %all-gather.3.cloned.1.call-update) | async-done | bytes 2359312 | tf_op jit(solution)/shard_map/all_gather | solution.py:52
  132.4 6.0 %fusion.9 = bf16[48,64,5,128]{3,1,2,0:T(8,128)(2,1)} fusion(bf16[48,64,384,1]{2,1,3,0:T(8,128)(2,1)} %bitcast.64, bf16[384,5,128,1]{0,2,1,3:T(8,128)(2,1)S(1)} %bitcast.61), kind=kOutput, calls=%fused_computation.29 | convolution fusion | flops 1509949440 | bytes 6782976 | tf_op jit(solution)/shard_map/jps,sbk->jbpk/dot_general | solution.py:54
  138.4 4.2 %gather_fusion = bf16[128,64,128]{2,1,0:T(8,128)(2,1)} fusion(bf16[240,64,128]{2,1,0:T(8,128)(2,1)} %bitcast.59, s32[1024]{0:T(1024)S(1)} %pad_clamp_fusion), kind=kCustom, calls=%fused_computation | custom fusion | bytes 4194816 | tf_op jit(solution)/shard_map/jit(_take)/gather | solution.py:57
  142.7 0.0 all-reduce.3.cloned.1.call-update
  142.7 0.2 all-gather.5.cloned.1.call-start
  142.9 0.1 select_reduce_fusion
  143.0 49.8 %all-reduce.3.cloned.1.call-done = bf16[128,64,128]{2,1,0:T(8,128)(2,1)} async-done(((bf16[128,64,128]{2,1,0:T(8,128)(2,1)}), bf16[128,64,128]{2,1,0:T(8,128)(2,1)}) %all-reduce.3.cloned.1.call-update) | async-done | bytes 2097168 | tf_op jit(solution)/shard_map/psum | solution.py:58
  192.8 4.5 %fusion.8 = bf16[128,64,128]{2,1,0:T(8,128)(2,1)S(1)} fusion(f32[128]{0:T(128)S(1)} %broadcast_multiply_fusion, bf16[128,64,128]{2,1,0:T(8,128)(2,1)} %all-reduce.3.cloned.1.call-done, f32[128,64,128]{2,1,0:T(8,128)} %param.9, pred[128]{0:T(512)(128)(4,1)S(1)} %iota_compare_fusion.2), kind=kLoop, calls=%fused_computation.28 | loop fusion | flops 11534336 | bytes 8389248 | tf_op jit(solution)/shard_map/convert_element_type | solution.py:40
  197.3 2.0 convolution_convert_fusion
  199.4 1.0 copy.31
  200.4 2.6 bitcast_convert_fusion
  203.0 59.1 %all_to_all.11 = bf16[8,384,384]{2,1,0:T(8,128)(2,1)S(1)} all-to-all(bf16[8,384,384]{2,1,0:T(8,128)(2,1)S(1)} %bitcast.57), channel_id=1, replica_groups=mesh['snp'=8,'samp'=4] {'snp'}, dimensions={0} | all-to-all | bytes 4718592 | tf_op jit(solution)/shard_map/all_to_all | solution.py:49
  262.1 0.3 convert_reduce_fusion
  262.5 0.8 subtract_convert_fusion
  263.3 0.0 all-reduce.5.cloned.1.call-start
  263.3 50.5 %all-gather.5.cloned.1.call-done = bf16[3072,384]{1,0:T(8,128)(2,1)} async-done(((bf16[384,384]{1,0:T(8,128)(2,1)}), bf16[3072,384]{1,0:T(8,128)(2,1)}) %all-gather.5.cloned.1.call-update) | async-done | bytes 2359312 | tf_op jit(solution)/shard_map/all_gather | solution.py:52
  313.8 6.0 %fusion.10 = bf16[48,64,5,128]{3,1,2,0:T(8,128)(2,1)} fusion(bf16[48,64,384,1]{2,1,3,0:T(8,128)(2,1)} %bitcast.65, bf16[384,5,128,1]{0,2,1,3:T(8,128)(2,1)S(1)} %bitcast.63), kind=kOutput, calls=%fused_computation.30 | convolution fusion | flops 1509949440 | bytes 6782976 | tf_op jit(solution)/shard_map/jps,sbk->jbpk/dot_general | solution.py:54
  319.8 4.4 %gather_fusion.1 = bf16[128,64,128]{2,1,0:T(8,128)(2,1)} fusion(bf16[240,64,128]{2,1,0:T(8,128)(2,1)} %bitcast.58, s32[1024]{0:T(1024)S(1)} %pad_clamp_fusion), kind=kCustom, calls=%fused_computation.1 | custom fusion | bytes 4194816 | tf_op jit(solution)/shard_map/jit(_take)/gather | solution.py:57
  324.3 50.1 %all-reduce.5.cloned.1.call-done = bf16[128,64,128]{2,1,0:T(8,128)(2,1)} async-done(((bf16[128,64,128]{2,1,0:T(8,128)(2,1)}), bf16[128,64,128]{2,1,0:T(8,128)(2,1)}) %all-reduce.5.cloned.1.call-update) | async-done | bytes 2097168 | tf_op jit(solution)/shard_map/psum | solution.py:58
  374.3 8.4 %multiply_select_fusion = f32[128,64,128]{2,1,0:T(8,128)} fusion(bf16[128,64,128]{2,1,0:T(8,128)(2,1)} %all-reduce.5.cloned.1.call-done, f32[128]{0:T(128)S(1)} %broadcast_multiply_fusion, pred[128]{0:T(512)(128)(4,1)S(1)} %iota_compare_fusion.2, bf16[128,64,128]{2,1,0:T(8,128)(2,1)S(1)} %copy-done, f32[128,64,128]{2,1,0:T(8,128)} %param.9), kind=kLoop, calls=%fused_computation.6 | loop fusion | flops 19922944 | bytes 12583552 | tf_op jit(solution)/shard_map/jit(_where)/select_n | solution.py:15
  (13 shorter events, 0.1 us)
Async XLA Ops:
  6.5 125.9 %all-gather.3.cloned.1.call-start = ((), (), s32[]{:S(2)}) async-start(), calls=%async_computation.2 | async-start | bytes 2654208 | tf_op jit(solution)/shard_map/all_gather | solution.py:52
  18.9 61.4 %copy-start.1 = (f32[384,384]{1,0:T(8,128)S(1)}, f32[384,384]{1,0:T(8,128)}, u32[]{:S(2)}) copy-start(f32[384,384]{1,0:T(8,128)} %param.8) | copy-start | bytes 1769476
  81.2 111.6 %all-reduce.3.cloned.1.call-start = ((), (), s32[]{:S(2)}) async-start(), calls=%async_computation.3 | async-start | bytes 4194304 | tf_op jit(solution)/shard_map/psum | solution.py:58
  138.4 4.5 %copy-start.2 = (f32[46]{0:T(128)S(1)}, f32[46]{0:T(128)}, u32[]{:S(2)}) copy-start(f32[46]{0:T(128)} %param.13) | copy-start | bytes 556
  142.7 171.1 %all-gather.5.cloned.1.call-start = ((), (), s32[]{:S(2)}) async-start(), calls=%async_computation.4 | async-start | bytes 2654208 | tf_op jit(solution)/shard_map/all_gather | solution.py:52
  263.3 111.0 %all-reduce.5.cloned.1.call-start = ((), (), s32[]{:S(2)}) async-start(), calls=%async_computation.5 | async-start | bytes 4194304 | tf_op jit(solution)/shard_map/psum | solution.py:58
  319.8 54.5 %copy-start = (bf16[128,64,128]{2,1,0:T(8,128)(2,1)S(1)}, bf16[128,64,128]{2,1,0:T(8,128)(2,1)}, u32[]{:S(2)}) copy-start(bf16[128,64,128]{2,1,0:T(8,128)(2,1)} %all-reduce.3.cloned.1.call-done) | copy-start | bytes 6291460
Sparse Core Ops, SparseCore 0:
  81.3 51.0 all-gather.2
  142.8 49.9 all-reduce.2
  263.4 50.3 all-gather.4
  324.4 49.8 all-reduce.4

commit v4 on v3

--- a/solution.py
+++ b/solution.py
@@ -36,8 +36,13 @@
     cell_hot = (cell[:, None] == jnp.arange(cells, dtype=jnp.int32)[None, :]).astype(jnp.bfloat16)
     active = jnp.arange(entries, dtype=jnp.int32) < entry_count[0]
     current = jnp.where(active[:, None, None], weights, jnp.float32(0.0))
+    weight_bf = current.astype(jnp.bfloat16)
+    share = entries // lax.axis_size("samp")
+    start = lax.axis_index("samp") * share
+    own = lax.dynamic_slice_in_dim(current, start, share, 0)
+    own_cutoff = lax.dynamic_slice_in_dim(cutoff, start, share, 0)
+    own_active = lax.dynamic_slice_in_dim(active, start, share, 0)
     for sweep in range(ITERS):
-        weight_bf = current.astype(jnp.bfloat16)
         dense = jnp.einsum(
             "ec,epk->cpk", cell_hot, weight_bf, preferred_element_type=jnp.float32
         ).astype(jnp.bfloat16)
@@ -55,9 +60,11 @@
             "jps,sbk->jbpk", blocks, geno_blocks, preferred_element_type=jnp.float32
         ).reshape(cells, tile_width, block_width)
         local_gradient = jnp.take(full, cell, axis=0, mode="clip")
-        gradient = lax.psum(local_gradient.astype(jnp.bfloat16), "samp").astype(jnp.float32)
-        current = shrink_soft(current, gradient, cutoff, active)
-    return current
+        own_gradient = lax.psum_scatter(local_gradient, "samp", scatter_dimension=0, tiled=True)
+        own = shrink_soft(own, own_gradient, own_cutoff, own_active)
+        if sweep + 1 < ITERS:
+            weight_bf = lax.all_gather(own.astype(jnp.bfloat16), "samp", axis=0, tiled=True)
+    return lax.all_gather(own, "samp", axis=0, tiled=True)
 
 
 def solution(mesh):

time: 390 us -> 457 us (1.17)
  waiting for transfers between devices: 202 us -> 244 us
  local copies, waits for them, and re-layouts: 12.7 us -> 38.5 us
    psum x2 -> x0, waiting for transfers between devices: 99.8 us -> none  [per_device(): lax.psum(local_gradient.astype(jnp.bfloat16), 'samp').astype(jnp.float32)]
    reduce_scatter x0 -> x2, waiting for transfers between devices: none -> 85.5 us  [per_device(): lax.psum_scatter(local_gradient, 'samp', scatter_dimension=0, tiled=True)]
    all_gather x0 -> x2, waiting for transfers between devices: none -> 57.4 us  [the longest x1 34.6 us: per_device(): return lax.all_gather(own, 'samp', axis=0, tiled=True)]
    gather x2 -> x4, local copies, waits for them, and re-layouts: 8.64 us -> 25.2 us  [per_device(): local_gradient = jnp.take(full, cell, axis=0, mode='clip')]
    all_gather x0 -> x1, local copies, waits for them, and re-layouts: none -> 6.63 us  [per_device(): return lax.all_gather(own, 'samp', axis=0, tiled=True)]
    select_n x0 -> x1, other arithmetic: none -> 4.89 us  [per_device(): current = jnp.where(active[:, None, None], weights, jnp.float32(0.0))]
    select_n x1, other arithmetic: 8.37 us -> 3.49 us  [shrink_soft(): return jnp.where(active[:, None, None], shrunk, jnp.float32(0.0))]
  transfers between devices with their start and end apart: 4 -> 6, of which waited for: 4 -> 6; matrix products, arithmetic and copies ran while one was open for 0% -> 0% of each run, Pallas kernels for 0% -> 0%
where the time goes in v4:
time: 457 us
  waiting for transfers between devices  244 us (53%)
  blocking collectives  121 us (26%)
  local copies, waits for them, and re-layouts  38.5 us (8%)
  matrix products  23.5 us (5%)
  other arithmetic  15 us (3%)
  between operations  14.2 us (3%)
    all_to_all x2, blocking collectives, per_device(): gathered = lax.all_to_all(partial, 'snp', 0, 0, tiled=False)  121 us
    all_gather x2, waiting for transfers between devices, per_device(): shard_rows = lax.all_gather(residual, 'snp', axis=0, tiled=True)  101 us
    reduce_scatter x2, waiting for transfers between devices, per_device(): lax.psum_scatter(local_gradient, 'samp', scatter_dimension=0, tiled=True)  85.5 us
    all_gather x1, waiting for transfers between devices, per_device(): return lax.all_gather(own, 'samp', axis=0, tiled=True)  34.6 us
    gather x4, local copies, waits for them, and re-layouts, per_device(): local_gradient = jnp.take(full, cell, axis=0, mode='clip')  25.2 us
    all_gather x1, waiting for transfers between devices, per_device(): lax.all_gather(own.astype(jnp.bfloat16), 'samp', axis=0, tiled=True)  22.7 us
    dot_general x2, matrix products, per_device(): jnp.einsum('jps,sbk->jbpk', blocks, geno_blocks, preferred_element_type=j...  14.3 us
  transfers between devices with their start and end apart: 6, of which 6 were waited for; matrix products, arithmetic and copies ran while one was open for 0% of the time, Pallas kernels for 0%

profile of v4, /device:TPU:0, one launch (start us, length us, event | category | flops | bytes accessed | tf_op | source)
XLA Modules:
  0.0 456.5 jit_solution(1614173949414493424)
XLA Ops:
  7.2 0.7 slice_bitcast_fusion
  7.9 0.7 select_reduce_fusion.1
  8.6 0.7 fusion.6
  9.3 1.3 copy.29
  10.6 4.9 %copy_select_fusion = f32[128,64,128]{2,0,1:T(8,128)S(1)} fusion(f32[128,64,128]{2,1,0:T(8,128)} %param.9, pred[128]{0:T(512)(128)(4,1)S(1)} %iota_compare_fusion.2), kind=kLoop, calls=%fused_computation.6 | loop fusion | flops 1048576 | bytes 8388736 | tf_op jit(solution)/shard_map/jit(_where)/select_n | solution.py:38
  15.5 2.0 copy-done
  17.5 1.2 convolution_convert_fusion.1
  18.7 1.0 copy.28
  19.7 2.6 bitcast_convert_fusion.1
  22.3 61.1 %all_to_all.10 = bf16[8,384,384]{2,1,0:T(8,128)(2,1)S(1)} all-to-all(bf16[8,384,384]{2,1,0:T(8,128)(2,1)S(1)} %bitcast.63), channel_id=1, replica_groups=mesh['snp'=8,'samp'=4] {'snp'}, dimensions={0} | all-to-all | bytes 4718592 | tf_op jit(solution)/shard_map/all_to_all | solution.py:54
  83.8 0.8 subtract_convert_fusion.1
  84.8 51.0 %all-gather.5.cloned.1.call-done = bf16[3072,384]{1,0:T(8,128)(2,1)} async-done(((bf16[384,384]{1,0:T(8,128)(2,1)}), bf16[3072,384]{1,0:T(8,128)(2,1)}) %all-gather.5.cloned.1.call-update) | async-done | bytes 2359312 | tf_op jit(solution)/shard_map/all_gather | solution.py:57
  135.8 7.2 %fusion.8 = f32[48,64,5,128]{3,1,2,0:T(8,128)} fusion(bf16[48,64,384,1]{2,1,3,0:T(8,128)(2,1)} %bitcast.65, bf16[384,5,128,1]{0,2,1,3:T(8,128)(2,1)S(1)} %bitcast.58), kind=kOutput, calls=%fused_computation.28 | convolution fusion | flops 1509949440 | bytes 10715136 | tf_op jit(solution)/shard_map/jps,sbk->jbpk/dot_general | solution.py:59
  143.0 6.1 %gather_fusion = f32[128,64,128]{2,1,0:T(8,128)} fusion(f32[240,64,128]{2,1,0:T(8,128)} %bitcast.56, s32[1024]{0:T(1024)S(1)} %pad_clamp_fusion), kind=kCustom, calls=%fused_computation | custom fusion | bytes 8389120 | tf_op jit(solution)/shard_map/jit(_take)/gather | solution.py:62
  149.0 6.6 %copy.32 = f32[128,64,128]{2,0,1:T(8,128)} copy(f32[128,64,128]{2,1,0:T(8,128)} %gather_fusion) | data formatting | bytes 8388608 | tf_op jit(solution)/shard_map/jit(_take)/gather | solution.py:62
  155.8 0.5 copy-done.3
  156.4 42.4 %reduce-scatter.3.cloned.1.call-done = f32[32,64,128]{2,0,1:T(8,128)} async-done(((f32[128,64,128]{2,0,1:T(8,128)}), f32[32,64,128]{2,0,1:T(8,128)}) %reduce-scatter.3.cloned.1.call-update) | async-done | bytes 1048592 | tf_op jit(solution)/shard_map/reduce_scatter | solution.py:63
  198.8 2.9 fusion.7
  201.7 22.7 %all-gather.7.cloned.1.call-done = bf16[128,64,128]{2,0,1:T(8,128)(2,1)} async-done(((bf16[32,64,128]{2,0,1:T(8,128)(2,1)}), bf16[128,64,128]{2,0,1:T(8,128)(2,1)}) %all-gather.7.cloned.1.call-update) | async-done | bytes 2097168 | tf_op jit(solution)/shard_map/all_gather | solution.py:66
  224.4 2.8 convolution_convert_fusion
  227.2 1.0 copy.33
  228.2 2.6 bitcast_convert_fusion
  230.8 59.5 %all_to_all.11 = bf16[8,384,384]{2,1,0:T(8,128)(2,1)S(1)} all-to-all(bf16[8,384,384]{2,1,0:T(8,128)(2,1)S(1)} %bitcast.64), channel_id=1, replica_groups=mesh['snp'=8,'samp'=4] {'snp'}, dimensions={0} | all-to-all | bytes 4718592 | tf_op jit(solution)/shard_map/all_to_all | solution.py:54
  290.7 0.8 subtract_convert_fusion
  291.8 50.1 %all-gather.9.cloned.1.call-done = bf16[3072,384]{1,0:T(8,128)(2,1)} async-done(((bf16[384,384]{1,0:T(8,128)(2,1)}), bf16[3072,384]{1,0:T(8,128)(2,1)}) %all-gather.9.cloned.1.call-update) | async-done | bytes 2359312 | tf_op jit(solution)/shard_map/all_gather | solution.py:57
  341.9 7.2 %fusion.9 = f32[48,64,5,128]{3,1,2,0:T(8,128)} fusion(bf16[48,64,384,1]{2,1,3,0:T(8,128)(2,1)} %bitcast.66, bf16[384,5,128,1]{0,2,1,3:T(8,128)(2,1)S(1)} %bitcast.60), kind=kOutput, calls=%fused_computation.29 | convolution fusion | flops 1509949440 | bytes 10715136 | tf_op jit(solution)/shard_map/jps,sbk->jbpk/dot_general | solution.py:59
  349.1 6.1 %gather_fusion.1 = f32[128,64,128]{2,1,0:T(8,128)} fusion(f32[240,64,128]{2,1,0:T(8,128)} %bitcast.55, s32[1024]{0:T(1024)S(1)} %pad_clamp_fusion), kind=kCustom, calls=%fused_computation.1 | custom fusion | bytes 8389120 | tf_op jit(solution)/shard_map/jit(_take)/gather | solution.py:62
  355.1 6.6 %copy.36 = f32[128,64,128]{2,0,1:T(8,128)} copy(f32[128,64,128]{2,1,0:T(8,128)} %gather_fusion.1) | data formatting | bytes 8388608 | tf_op jit(solution)/shard_map/jit(_take)/gather | solution.py:62
  361.7 43.1 %reduce-scatter.5.cloned.1.call-done = f32[32,64,128]{2,0,1:T(8,128)} async-done(((f32[128,64,128]{2,0,1:T(8,128)}), f32[32,64,128]{2,0,1:T(8,128)}) %reduce-scatter.5.cloned.1.call-update) | async-done | bytes 1048592 | tf_op jit(solution)/shard_map/reduce_scatter | solution.py:63
  404.9 3.5 multiply_select_fusion
  408.4 34.6 %all-gather.11.cloned.1.call-done = f32[128,64,128]{2,0,1:T(8,128)} async-done(((f32[32,64,128]{2,0,1:T(8,128)}), f32[128,64,128]{2,0,1:T(8,128)}) %all-gather.11.cloned.1.call-update) | async-done | bytes 4194320 | tf_op jit(solution)/shard_map/all_gather | solution.py:67
  443.1 6.6 %copy.37 = f32[128,64,128]{2,1,0:T(8,128)} copy(f32[128,64,128]{2,0,1:T(8,128)} %all-gather.11.cloned.1.call-done) | data formatting | bytes 8388608 | tf_op jit(solution)/shard_map/all_gather | solution.py:67
  (26 shorter events, 1.6 us)
Async XLA Ops:
  6.5 129.3 %all-gather.5.cloned.1.call-start = ((), (), s32[]{:S(2)}) async-start(), calls=%async_computation.4 | async-start | bytes 2654208 | tf_op jit(solution)/shard_map/all_gather | solution.py:57
  15.5 2.0 copy-start
  22.3 61.4 %copy-start.2 = (f32[384,384]{1,0:T(8,128)S(1)}, f32[384,384]{1,0:T(8,128)}, u32[]{:S(2)}) copy-start(f32[384,384]{1,0:T(8,128)} %param.8) | copy-start | bytes 1769476
  84.6 114.2 %reduce-scatter.3.cloned.1.call-start = ((), (), s32[]{:S(2)}) async-start(), calls=%async_computation.5 | async-start | bytes 5242880 | tf_op jit(solution)/shard_map/reduce_scatter | solution.py:63
  155.6 0.7 copy-start.3
  155.6 68.8 %all-gather.7.cloned.1.call-start = ((), (), s32[]{:S(2)}) async-start(), calls=%async_computation.6 | async-start | bytes 2621440 | tf_op jit(solution)/shard_map/all_gather | solution.py:66
  201.7 140.2 %all-gather.9.cloned.1.call-start = ((), (), s32[]{:S(2)}) async-start(), calls=%async_computation.7 | async-start | bytes 2654208 | tf_op jit(solution)/shard_map/all_gather | solution.py:57
  291.5 113.3 %reduce-scatter.5.cloned.1.call-start = ((), (), s32[]{:S(2)}) async-start(), calls=%async_computation.8 | async-start | bytes 5242880 | tf_op jit(solution)/shard_map/reduce_scatter | solution.py:63
  361.7 43.2 %copy-start.1 = (f32[32,64,128]{2,0,1:T(8,128)S(1)}, f32[32,64,128]{2,0,1:T(8,128)}, u32[]{:S(2)}) copy-start(f32[32,64,128]{2,0,1:T(8,128)} %reduce-scatter.3.cloned.1.call-done) | copy-start | bytes 3145732
  361.7 81.4 %all-gather.11.cloned.1.call-start = ((), (), s32[]{:S(2)}) async-start(), calls=%async_computation.9 | async-start | bytes 5242880 | tf_op jit(solution)/shard_map/all_gather | solution.py:67
Sparse Core Ops, SparseCore 0:
  84.7 51.0 all-gather.4
  155.7 43.0 reduce-scatter.2
  201.8 22.5 all-gather.6
  291.7 50.1 all-gather.8
  361.8 43.0 reduce-scatter.4
  408.5 34.4 all-gather.10

commit v5 on v4

--- a/solution.py
+++ b/solution.py
@@ -60,11 +60,15 @@
             "jps,sbk->jbpk", blocks, geno_blocks, preferred_element_type=jnp.float32
         ).reshape(cells, tile_width, block_width)
         local_gradient = jnp.take(full, cell, axis=0, mode="clip")
-        own_gradient = lax.psum_scatter(local_gradient, "samp", scatter_dimension=0, tiled=True)
+        rows = local_gradient.reshape(entries * tile_width, block_width)
+        mine = lax.psum_scatter(rows, "samp", scatter_dimension=0, tiled=True)
+        own_gradient = mine.reshape(share, tile_width, block_width)
         own = shrink_soft(own, own_gradient, own_cutoff, own_active)
         if sweep + 1 < ITERS:
-            weight_bf = lax.all_gather(own.astype(jnp.bfloat16), "samp", axis=0, tiled=True)
-    return lax.all_gather(own, "samp", axis=0, tiled=True)
+            flat = own.astype(jnp.bfloat16).reshape(share * tile_width, block_width)
+            weight_bf = lax.all_gather(flat, "samp", axis=0, tiled=True).reshape(weights.shape)
+    flat = own.reshape(share * tile_width, block_width)
+    return lax.all_gather(flat, "samp", axis=0, tiled=True).reshape(weights.shape)
 
 
 def solution(mesh):

time: 457 us -> 444 us (0.972)
  local copies, waits for them, and re-layouts: 38.5 us -> 21.6 us
    gather x4 -> x2, local copies, waits for them, and re-layouts: 25.2 us -> 12.1 us  [per_device(): local_gradient = jnp.take(full, cell, axis=0, mode='clip')]
    all_gather x1 -> x0, local copies, waits for them, and re-layouts: 6.63 us -> none  [per_device(): return lax.all_gather(own, 'samp', axis=0, tiled=True)]
    select_n x1 -> x0, other arithmetic: 4.89 us -> none  [per_device(): current = jnp.where(active[:, None, None], weights, jnp.float32(0.0))]
where the time goes in v5:
time: 444 us; the launch traced here: 443 us
  waiting for transfers between devices  244 us (55%)
  blocking collectives  121 us (27%)
  matrix products  25.2 us (6%)
  local copies, waits for them, and re-layouts  21.6 us (5%)
  other arithmetic  16.9 us (4%)
  between operations  14.2 us (3%)
    all_to_all x2, blocking collectives, per_device(): gathered = lax.all_to_all(partial, 'snp', 0, 0, tiled=False)  121 us
    all_gather x2, waiting for transfers between devices, per_device(): shard_rows = lax.all_gather(residual, 'snp', axis=0, tiled=True)  101 us
    reduce_scatter x2, waiting for transfers between devices, per_device(): mine = lax.psum_scatter(rows, 'samp', scatter_dimension=0, tiled=True)  85.5 us
    all_gather x2, waiting for transfers between devices, per_device(): lax.all_gather(flat, 'samp', axis=0, tiled=True).reshape(weights.shape)  57.2 us
    dot_general x2, matrix products, per_device(): jnp.einsum('jps,sbk->jbpk', blocks, geno_blocks, preferred_element_type=j...  14.3 us
    gather x2, local copies, waits for them, and re-layouts, per_device(): local_gradient = jnp.take(full, cell, axis=0, mode='clip')  12.1 us
  transfers between devices with their start and end apart: 6, of which 6 were waited for; matrix products, arithmetic and copies ran while one was open for 0% of the time, Pallas kernels for 0%

profile of v5, /device:TPU:0, one launch (start us, length us, event | category | flops | bytes accessed | tf_op | source)
XLA Modules:
  0.0 443.1 jit_solution(6692212059129603375)
XLA Ops:
  7.2 0.7 slice_bitcast_fusion
  7.9 0.7 select_reduce_fusion.1
  8.6 0.7 fusion.7
  9.3 1.3 copy.26
  10.6 4.8 %fusion.9 = (bf16[128,64,128]{2,1,0:T(8,128)(2,1)S(1)}, f32[128,64,128]{2,1,0:T(8,128)}) fusion(f32[128,64,128]{2,1,0:T(8,128)} %param.9, pred[128]{0:T(512)(128)(4,1)S(1)} %iota_compare_fusion.2), kind=kLoop, calls=%fused_computation.31 | loop fusion | flops 2097152 | bytes 10485888 | tf_op jit(solution)/shard_map/convert_element_type | solution.py:39
  15.4 2.0 convolution_convert_fusion.1
  17.4 1.0 copy.25
  18.5 2.6 bitcast_convert_fusion.1
  21.1 61.1 %all_to_all.10 = bf16[8,384,384]{2,1,0:T(8,128)(2,1)S(1)} all-to-all(bf16[8,384,384]{2,1,0:T(8,128)(2,1)S(1)} %bitcast.77), channel_id=1, replica_groups=mesh['snp'=8,'samp'=4] {'snp'}, dimensions={0} | all-to-all | bytes 4718592 | tf_op jit(solution)/shard_map/all_to_all | solution.py:54
  82.2 0.3 convert_reduce_fusion.1
  82.5 0.8 subtract_convert_fusion.1
  83.4 51.2 %all-gather.5.cloned.1.call-done = bf16[3072,384]{1,0:T(8,128)(2,1)} async-done(((bf16[384,384]{1,0:T(8,128)(2,1)}), bf16[3072,384]{1,0:T(8,128)(2,1)}) %all-gather.5.cloned.1.call-update) | async-done | bytes 2359312 | tf_op jit(solution)/shard_map/all_gather | solution.py:57
  134.6 7.2 %fusion.10 = f32[48,64,5,128]{3,1,2,0:T(8,128)} fusion(bf16[48,64,384,1]{2,1,3,0:T(8,128)(2,1)} %bitcast.79, bf16[384,5,128,1]{0,2,1,3:T(8,128)(2,1)S(1)} %bitcast.69), kind=kOutput, calls=%fused_computation.32 | convolution fusion | flops 1509949440 | bytes 10715136 | tf_op jit(solution)/shard_map/jps,sbk->jbpk/dot_general | solution.py:59
  141.7 6.1 %gather_fusion = f32[128,64,128]{2,1,0:T(8,128)} fusion(f32[240,64,128]{2,1,0:T(8,128)} %bitcast.63, s32[1024]{0:T(1024)S(1)} %pad_clamp_fusion), kind=kCustom, calls=%fused_computation | custom fusion | bytes 8389120 | tf_op jit(solution)/shard_map/jit(_take)/gather | solution.py:62
  148.0 0.5 copy-done.1
  148.6 42.4 %reduce-scatter.3.cloned.1.call-done = f32[2048,128]{1,0:T(8,128)} async-done(((f32[8192,128]{1,0:T(8,128)}), f32[2048,128]{1,0:T(8,128)}) %reduce-scatter.3.cloned.1.call-update) | async-done | bytes 1048592 | tf_op jit(solution)/shard_map/reduce_scatter | solution.py:64
  191.0 1.3 broadcast_multiply_fusion.1
  192.3 2.5 fusion.8
  195.1 22.5 %all-gather.7.cloned.1.call-done = bf16[8192,128]{1,0:T(8,128)(2,1)} async-done(((bf16[2048,128]{1,0:T(8,128)(2,1)}), bf16[8192,128]{1,0:T(8,128)(2,1)}) %all-gather.7.cloned.1.call-update) | async-done | bytes 2097168 | tf_op jit(solution)/shard_map/all_gather | solution.py:69
  217.7 3.6 convolution_convert_fusion
  221.3 1.0 copy.30
  222.3 2.6 bitcast_convert_fusion
  224.9 59.5 %all_to_all.11 = bf16[8,384,384]{2,1,0:T(8,128)(2,1)S(1)} all-to-all(bf16[8,384,384]{2,1,0:T(8,128)(2,1)S(1)} %bitcast.78), channel_id=1, replica_groups=mesh['snp'=8,'samp'=4] {'snp'}, dimensions={0} | all-to-all | bytes 4718592 | tf_op jit(solution)/shard_map/all_to_all | solution.py:54
  284.8 0.8 subtract_convert_fusion
  285.6 50.3 %all-gather.9.cloned.1.call-done = bf16[3072,384]{1,0:T(8,128)(2,1)} async-done(((bf16[384,384]{1,0:T(8,128)(2,1)}), bf16[3072,384]{1,0:T(8,128)(2,1)}) %all-gather.9.cloned.1.call-update) | async-done | bytes 2359312 | tf_op jit(solution)/shard_map/all_gather | solution.py:57
  336.0 7.2 %fusion.11 = f32[48,64,5,128]{3,1,2,0:T(8,128)} fusion(bf16[48,64,384,1]{2,1,3,0:T(8,128)(2,1)} %bitcast.80, bf16[384,5,128,1]{0,2,1,3:T(8,128)(2,1)S(1)} %bitcast.71), kind=kOutput, calls=%fused_computation.33 | convolution fusion | flops 1509949440 | bytes 10715136 | tf_op jit(solution)/shard_map/jps,sbk->jbpk/dot_general | solution.py:59
  343.1 6.1 %gather_fusion.1 = f32[128,64,128]{2,1,0:T(8,128)} fusion(f32[240,64,128]{2,1,0:T(8,128)} %bitcast.62, s32[1024]{0:T(1024)S(1)} %pad_clamp_fusion), kind=kCustom, calls=%fused_computation.1 | custom fusion | bytes 8389120 | tf_op jit(solution)/shard_map/jit(_take)/gather | solution.py:62
  349.3 43.1 %reduce-scatter.5.cloned.1.call-done = f32[2048,128]{1,0:T(8,128)} async-done(((f32[8192,128]{1,0:T(8,128)}), f32[2048,128]{1,0:T(8,128)}) %reduce-scatter.5.cloned.1.call-update) | async-done | bytes 1048592 | tf_op jit(solution)/shard_map/reduce_scatter | solution.py:64
  392.4 1.3 broadcast_multiply_fusion
  393.7 3.1 multiply_select_fusion
  396.9 34.6 %all-gather.11.cloned.1.call-done = f32[8192,128]{1,0:T(8,128)} async-done(((f32[2048,128]{1,0:T(8,128)}), f32[8192,128]{1,0:T(8,128)}) %all-gather.11.cloned.1.call-update) | async-done | bytes 4194320 | tf_op jit(solution)/shard_map/all_gather | solution.py:71
  431.5 4.8 %copy.51 = f32[128,64,128]{2,1,0:T(8,128)} copy(f32[128,64,128]{2,1,0:T(8,128)} %bitcast.74) | data formatting | bytes 8388608
  (22 shorter events, 1.1 us)
Async XLA Ops:
  6.5 128.1 %all-gather.5.cloned.1.call-start = ((), (), s32[]{:S(2)}) async-start(), calls=%async_computation.4 | async-start | bytes 2654208 | tf_op jit(solution)/shard_map/all_gather | solution.py:57
  21.1 61.4 %copy-start = (f32[384,384]{1,0:T(8,128)S(1)}, f32[384,384]{1,0:T(8,128)}, u32[]{:S(2)}) copy-start(f32[384,384]{1,0:T(8,128)} %param.8) | copy-start | bytes 1769476
  83.4 107.7 %reduce-scatter.3.cloned.1.call-start = ((), (), s32[]{:S(2)}) async-start(), calls=%async_computation.5 | async-start | bytes 5242880 | tf_op jit(solution)/shard_map/reduce_scatter | solution.py:64
  147.8 0.7 copy-start.1
  147.8 69.8 %all-gather.7.cloned.1.call-start = ((), (), s32[]{:S(2)}) async-start(), calls=%async_computation.6 | async-start | bytes 2621440 | tf_op jit(solution)/shard_map/all_gather | solution.py:69
  194.9 141.1 %all-gather.9.cloned.1.call-start = ((), (), s32[]{:S(2)}) async-start(), calls=%async_computation.7 | async-start | bytes 2654208 | tf_op jit(solution)/shard_map/all_gather | solution.py:57
  285.6 106.8 %reduce-scatter.5.cloned.1.call-start = ((), (), s32[]{:S(2)}) async-start(), calls=%async_computation.8 | async-start | bytes 5242880 | tf_op jit(solution)/shard_map/reduce_scatter | solution.py:64
  349.2 82.3 %all-gather.11.cloned.1.call-start = ((), (), s32[]{:S(2)}) async-start(), calls=%async_computation.9 | async-start | bytes 5242880 | tf_op jit(solution)/shard_map/all_gather | solution.py:71
Sparse Core Ops, SparseCore 0:
  83.5 51.0 all-gather.4
  148.0 43.0 reduce-scatter.2
  195.0 22.5 all-gather.6
  285.7 50.1 all-gather.8
  349.3 43.0 reduce-scatter.4
  397.0 34.4 all-gather.10

commit v6 on v3

v6 whole, which is shorter than its diff:
```python
import jax
import jax.numpy as jnp
from jax import lax
from jax.sharding import PartitionSpec as P

ITERS = 2


step_scale = 0.3


def shrink_soft(current, gradient, cutoff, active):
    shifted = current + step_scale * gradient
    shrunk = jnp.sign(shifted) * jnp.maximum(jnp.abs(shifted) - cutoff, jnp.float32(0.0))
    return jnp.where(active[:, None, None], shrunk, jnp.float32(0.0))


def per_device(genotypes, responses, weights, pattern, entry_count, tile_slot, penalty):
    quarter = genotypes.shape[0]
    entries, tile_width, block_width = weights.shape
    block_count = genotypes.shape[1] // block_width
    own_rows = responses.shape[0]
    owners = lax.axis_size("snp")
    own_slots = own_rows // tile_width
    slot_total = owners * own_slots
    cells = slot_total * block_count
    halves = lax.axis_size("sx")
    cores = lax.axis_size("sc")
    half_p = tile_width // halves
    x = lax.axis_index("sx")
    c = lax.axis_index("sc")

    geno = lax.all_gather(genotypes, "sx", axis=0, tiled=True)
    sample_count = geno.shape[0]
    geno_blocks = geno.reshape(sample_count, block_count, block_width)
    resp = responses.reshape(own_slots, halves, half_p, quarter)
    resp = jnp.moveaxis(resp, 1, 0)
    resp = lax.all_to_all(resp, "sx", 0, 0, tiled=False)
    resp = jnp.moveaxis(resp, 0, 2).reshape(own_slots * half_p, halves * quarter)

    blk = pattern[:, 0]
    tile = pattern[:, 1]
    tile_hot = tile[:, None] == jnp.arange(penalty.shape[0], dtype=jnp.int32)[None, :]
    slot_ids = jnp.sum(jnp.where(tile_hot, tile_slot[None, :], 0), axis=1)
    per_entry = jnp.sum(jnp.where(tile_hot, penalty[None, :], jnp.float32(0.0)), axis=1)
    cutoff = step_scale * per_entry[:, None, None]
    cell = slot_ids * block_count + blk
    cell_hot = (cell[:, None] == jnp.arange(cells, dtype=jnp.int32)[None, :]).astype(jnp.bfloat16)
    active = jnp.arange(entries, dtype=jnp.int32) < entry_count[0]
    w_half = lax.dynamic_slice_in_dim(weights, x * half_p, half_p, 1)
    weight_bf = jnp.where(active[:, None, None], w_half, jnp.float32(0.0)).astype(jnp.bfloat16)
    share = entries // cores
    start = c * share
    own_active = lax.dynamic_slice_in_dim(active, start, share, 0)
    own_cutoff = lax.dynamic_slice_in_dim(cutoff, start, share, 0)
    own = jnp.where(
        own_active[:, None, None],
        lax.dynamic_slice_in_dim(w_half, start, share, 0),
        jnp.float32(0.0),
    )
    for sweep in range(ITERS):
        dense = jnp.einsum(
            "ec,epk->cpk", cell_hot, weight_bf, preferred_element_type=jnp.float32
        ).astype(jnp.bfloat16)
        dense = dense.reshape(slot_total, block_count, half_p, block_width)
        partial = jnp.einsum(
            "jbpk,sbk->jps", dense, geno_blocks, preferred_element_type=jnp.float32
        ).astype(jnp.bfloat16)
        partial = partial.reshape(owners, own_slots * half_p, sample_count)
        gathered = lax.all_to_all(partial, "snp", 0, 0, tiled=False)
        prediction = jnp.sum(gathered.astype(jnp.float32), axis=0)
        residual = (resp - prediction).astype(jnp.bfloat16)
        shard_rows = lax.all_gather(residual, "snp", axis=0, tiled=True)
        blocks = shard_rows.reshape(slot_total, half_p, sample_count)
        full = jnp.einsum(
            "jps,sbk->jbpk", blocks, geno_blocks, preferred_element_type=jnp.float32
        ).reshape(cells, half_p, block_width)
        local_gradient = jnp.take(full, cell, axis=0, mode="clip")
        rows = local_gradient.reshape(entries * half_p, block_width)
        mine = lax.psum_scatter(rows, "sc", scatter_dimension=0, tiled=True)
        own_gradient = mine.reshape(share, half_p, block_width)
        own = shrink_soft(own, own_gradient, own_cutoff, own_active)
        if sweep + 1 < ITERS:
            flat = own.astype(jnp.bfloat16).reshape(share * half_p, block_width)
            weight_bf = lax.all_gather(flat, "sc", axis=0, tiled=True).reshape(
                entries, half_p, block_width
            )
    both = lax.all_gather(own, "sx", axis=1, tiled=True)
    flat = both.reshape(share * tile_width, block_width)
    return lax.all_gather(flat, "sc", axis=0, tiled=True).reshape(weights.shape)


def solution(mesh):
    snp_size, samp_size = mesh.devices.shape
    devices = mesh.devices.reshape(snp_size, 2, samp_size // 2)
    mesh = jax.sharding.Mesh(devices, ("snp", "sx", "sc"))
    samp = ("sx", "sc")
    in_specs = (
        P(samp, "snp"),
        P("snp", samp),
        P("snp", None, None),
        P("snp", None),
        P("snp"),
        P(),
        P(),
    )
    out_specs = P("snp", None, None)
    return jax.shard_map(
        per_device, mesh=mesh, in_specs=in_specs, out_specs=out_specs, check_vma=False
    )
```

time: 390 us -> 387 us (level)
  blocking collectives: 120 us -> 78.8 us
  waiting for transfers between devices: 202 us -> 230 us
  starting transfers between devices: 0.31 us -> 10.8 us
  local copies, waits for them, and re-layouts: 12.7 us -> 17.6 us
  other arithmetic: 19.3 us -> 15.4 us
    psum x2 -> x0, waiting for transfers between devices: 99.8 us -> none  [per_device(): lax.psum(local_gradient.astype(jnp.bfloat16), 'samp').astype(jnp.float32)]
    all_to_all x2 -> x1, blocking collectives: 120 us -> 59.8 us  [per_device(): gathered = lax.all_to_all(partial, 'snp', 0, 0, tiled=False)]
    all_gather x0 -> x3, waiting for transfers between devices: none -> 59.8 us  [the longest x1 34.3 us: per_device(): both = lax.all_gather(own, 'sx', axis=1, tiled=True)]
    all_to_all x0 -> x2, waiting for transfers between devices: none -> 52.4 us  [the longest x1 52.4 us: per_device(): gathered = lax.all_to_all(partial, 'snp', 0, 0, tiled=False)]
    all_gather x0 -> x1, blocking collectives: none -> 18.9 us  [per_device(): geno = lax.all_gather(genotypes, 'sx', axis=0, tiled=True)]
    reduce_scatter x0 -> x2, waiting for transfers between devices: none -> 16.2 us  [per_device(): mine = lax.psum_scatter(rows, 'sc', scatter_dimension=0, tiled=True)]
    all_to_all x0 -> x2, starting transfers between devices: none -> 10.3 us  [the longest x1 6.09 us: per_device(): gathered = lax.all_to_all(partial, 'snp', 0, 0, tiled=False)]
    unnamed x7 -> x15, local copies, waits for them, and re-layouts: 1.3 us -> 5.79 us
  transfers between devices with their start and end apart: 4 -> 9, of which waited for: 4 -> 8; matrix products, arithmetic and copies ran while one was open for 0% -> 2% of each run, Pallas kernels for 0% -> 0%
where the time goes in v6:
time: 387 us; the launch traced here: 386 us
  waiting for transfers between devices  230 us (59%)
  blocking collectives  78.8 us (20%)
  matrix products  19.6 us (5%)
  local copies, waits for them, and re-layouts  17.6 us (5%)
  other arithmetic  15.4 us (4%)
  between operations  14.3 us (4%)
  starting transfers between devices  10.8 us (3%)
    all_gather x2, waiting for transfers between devices, per_device(): shard_rows = lax.all_gather(residual, 'snp', axis=0, tiled=True)  101 us
    all_to_all x1, blocking collectives, per_device(): gathered = lax.all_to_all(partial, 'snp', 0, 0, tiled=False)  59.8 us
    all_to_all x1, waiting for transfers between devices, per_device(): gathered = lax.all_to_all(partial, 'snp', 0, 0, tiled=False)  52.4 us
    all_gather x1, waiting for transfers between devices, per_device(): both = lax.all_gather(own, 'sx', axis=1, tiled=True)  34.3 us
    all_gather x1, blocking collectives, per_device(): geno = lax.all_gather(genotypes, 'sx', axis=0, tiled=True)  18.9 us
    reduce_scatter x2, waiting for transfers between devices, per_device(): mine = lax.psum_scatter(rows, 'sc', scatter_dimension=0, tiled=True)  16.2 us
    all_gather x1, waiting for transfers between devices, per_device(): return lax.all_gather(flat, 'sc', axis=0, tiled=True).reshape(weights.shape)  15.2 us
    dot_general x2, matrix products, per_device(): jnp.einsum('jps,sbk->jbpk', blocks, geno_blocks, preferred_element_type=j...  11.5 us
  transfers between devices with their start and end apart: 9, of which 8 were waited for; matrix products, arithmetic and copies ran while one was open for 2% of the time, Pallas kernels for 0%

profile of v6, /device:TPU:0, one launch (start us, length us, event | category | flops | bytes accessed | tf_op | source)
XLA Modules:
  0.0 386.4 jit_solution(10831247109943534280)
XLA Ops:
  6.5 2.0 copy.42
  8.5 4.2 %all-to-all-start = ((f32[2,6,32,384]{3,2,1,0:T(8,128)}), f32[2,6,32,384]{3,2,1,0:T(8,128)S(1)}, u32[]{:S(2)}, u32[]{:S(2)}) async-start(f32[2,6,32,384]{3,2,1,0:T(8,128)} %copy.42), calls=%async_computation | async-start | bytes 1179648 | tf_op jit(solution)/shard_map/all_to_all | solution.py:38
  13.8 18.9 %all_gather.18 = bf16[768,640]{0,1:T(8,128)(2,1)S(1)} all-gather(bf16[384,640]{0,1:T(8,128)(2,1)S(1)} %copy.46), channel_id=1, replica_groups=mesh['snp'=8,'sx'=2,'sc'=2] {'sx'}, dimensions={0}, use_global_device_ids=true | all-gather | bytes 1474560 | tf_op jit(solution)/shard_map/all_gather | solution.py:33
  32.7 2.2 select_convert_fusion
  34.9 0.7 convolution_convert_fusion.1
  35.6 0.5 copy.45
  36.2 3.2 bitcast_convert_fusion.1
  39.4 6.1 %all-to-all-start.1 = ((bf16[8,192,768]{2,1,0:T(8,128)(2,1)}), bf16[8,192,768]{2,1,0:T(8,128)(2,1)S(1)}, u32[]{:S(2)}, u32[]{:S(2)}) async-start(bf16[8,192,768]{2,1,0:T(8,128)(2,1)} %bitcast.77), calls=%async_computation.1 | async-start | bytes 4718592 | tf_op jit(solution)/shard_map/all_to_all | solution.py:70
  46.1 52.4 %all-to-all-done.1 = bf16[8,192,768]{2,1,0:T(8,128)(2,1)S(1)} async-done(((bf16[8,192,768]{2,1,0:T(8,128)(2,1)}), bf16[8,192,768]{2,1,0:T(8,128)(2,1)S(1)}, u32[]{:S(2)}, u32[]{:S(2)}) %all-to-all-start.1) | async-done | bytes 2359328 | tf_op jit(solution)/shard_map/all_to_all | solution.py:70
  98.8 0.8 subtract_convert_fusion.1
  99.7 50.3 %all-gather.6.cloned.1.call-done = bf16[1536,768]{1,0:T(8,128)(2,1)} async-done(((bf16[192,768]{1,0:T(8,128)(2,1)}), bf16[1536,768]{1,0:T(8,128)(2,1)}) %all-gather.6.cloned.1.call-update) | async-done | bytes 2359312 | tf_op jit(solution)/shard_map/all_gather | solution.py:73
  150.0 5.9 %fusion.9 = f32[48,32,5,128]{3,1,2,0:T(8,128)} fusion(bf16[48,32,768,1]{2,1,3,0:T(8,128)(2,1)} %bitcast.93, bf16[768,5,128,1]{0,2,1,3:T(8,128)(2,1)} %bitcast.89), kind=kOutput, calls=%fused_computation.31 | convolution fusion | flops 1509949440 | bytes 7274496 | tf_op jit(solution)/shard_map/jps,sbk->jbpk/dot_general | solution.py:75
  155.9 4.1 %gather_fusion = f32[128,32,128]{2,1,0:T(8,128)} fusion(f32[240,32,128]{2,1,0:T(8,128)} %bitcast.86, s32[1024]{0:T(1024)S(1)} %pad_clamp_fusion), kind=kCustom, calls=%fused_computation | custom fusion | bytes 4194816 | tf_op jit(solution)/shard_map/jit(_take)/gather | solution.py:78
  160.3 8.0 %reduce-scatter.3.cloned.1.call-done = f32[2048,128]{1,0:T(8,128)} async-done(((f32[4096,128]{1,0:T(8,128)}), f32[2048,128]{1,0:T(8,128)}) %reduce-scatter.3.cloned.1.call-update) | async-done | bytes 1048592 | tf_op jit(solution)/shard_map/reduce_scatter | solution.py:80
  168.3 1.3 broadcast_multiply_fusion.1
  169.6 3.6 fusion.8
  173.3 10.2 %all-gather.8.cloned.1.call-done = bf16[4096,128]{1,0:T(8,128)(2,1)} async-done(((bf16[2048,128]{1,0:T(8,128)(2,1)}), bf16[4096,128]{1,0:T(8,128)(2,1)}) %all-gather.8.cloned.1.call-update) | async-done | bytes 1048592 | tf_op jit(solution)/shard_map/all_gather | solution.py:85
  183.5 1.9 convolution_convert_fusion
  185.5 0.5 copy.50
  186.0 0.7 copy-done.1
  186.7 2.2 bitcast_convert_fusion
  188.9 59.8 %all_to_all.15 = bf16[8,192,768]{2,1,0:T(8,128)(2,1)S(1)} all-to-all(bf16[8,192,768]{2,1,0:T(8,128)(2,1)S(1)} %bitcast.78), channel_id=1, replica_groups=mesh['snp'=8,'sx'=2,'sc'=2] {'snp'}, dimensions={0} | all-to-all | bytes 4718592 | tf_op jit(solution)/shard_map/all_to_all | solution.py:70
  249.1 0.8 subtract_convert_fusion
  250.1 51.0 %all-gather.10.cloned.1.call-done = bf16[1536,768]{1,0:T(8,128)(2,1)} async-done(((bf16[192,768]{1,0:T(8,128)(2,1)}), bf16[1536,768]{1,0:T(8,128)(2,1)}) %all-gather.10.cloned.1.call-update) | async-done | bytes 2359312 | tf_op jit(solution)/shard_map/all_gather | solution.py:73
  301.1 5.6 %fusion.10 = f32[48,32,5,128]{3,1,2,0:T(8,128)} fusion(bf16[48,32,768,1]{2,1,3,0:T(8,128)(2,1)} %bitcast.94, bf16[768,5,128,1]{0,2,1,3:T(8,128)(2,1)S(1)} %bitcast.91), kind=kOutput, calls=%fused_computation.32 | convolution fusion | flops 1509949440 | bytes 7274496 | tf_op jit(solution)/shard_map/jps,sbk->jbpk/dot_general | solution.py:75
  306.8 4.1 %gather_fusion.1 = f32[128,32,128]{2,1,0:T(8,128)} fusion(f32[240,32,128]{2,1,0:T(8,128)} %bitcast.85, s32[1024]{0:T(1024)S(1)} %pad_clamp_fusion), kind=kCustom, calls=%fused_computation.1 | custom fusion | bytes 4194816 | tf_op jit(solution)/shard_map/jit(_take)/gather | solution.py:78
  310.9 8.2 %reduce-scatter.5.cloned.1.call-done = f32[2048,128]{1,0:T(8,128)} async-done(((f32[4096,128]{1,0:T(8,128)}), f32[2048,128]{1,0:T(8,128)}) %reduce-scatter.5.cloned.1.call-update) | async-done | bytes 1048592 | tf_op jit(solution)/shard_map/reduce_scatter | solution.py:80
  319.2 1.3 broadcast_multiply_fusion
  320.5 4.6 %multiply_select_fusion = f32[64,32,128]{2,1,0:T(8,128)} fusion(f32[64,32,128]{2,1,0:T(8,128)S(1)} %bitcast.76, f32[64]{0:T(128)S(1)} %dynamic_slice.16, pred[64]{0:T(512)(128)(4,1)S(1)} %dynamic_slice.13, f32[64,32,128]{2,1,0:T(8,128)S(1)} %bitcast.70, f32[128,64,128]{2,1,0:T(8,128)} %param.9, s32[]{:T(128)S(6)} %select_n.35, s32[]{:T(128)S(6)} %select_n.37), kind=kLoop, calls=%fused_computation.11 | loop fusion | flops 3932160 | bytes 4194632 | tf_op jit(solution)/shard_map/jit(_where)/select_n | solution.py:15
  325.2 34.3 %all-gather.12.cloned.1.call-done = f32[64,64,128]{2,1,0:T(8,128)} async-done(((f32[64,32,128]{2,1,0:T(8,128)}), f32[64,64,128]{2,1,0:T(8,128)}) %all-gather.12.cloned.1.call-update) | async-done | bytes 2097168 | tf_op jit(solution)/shard_map/all_gather | solution.py:88
  359.5 15.2 %all-gather.14.cloned.1.call-done = f32[8192,128]{1,0:T(8,128)} async-done(((f32[4096,128]{1,0:T(8,128)}), f32[8192,128]{1,0:T(8,128)}) %all-gather.14.cloned.1.call-update) | async-done | bytes 4194320 | tf_op jit(solution)/shard_map/all_gather | solution.py:90
  374.7 4.8 %copy.72 = f32[128,64,128]{2,1,0:T(8,128)} copy(f32[128,64,128]{2,1,0:T(8,128)} %bitcast.75) | data formatting | bytes 8388608
  (40 shorter events, 2.4 us)
Async XLA Ops:
  6.5 6.9 %copy-start.3 = (s32[128,2]{0,1:T(2,128)S(1)}, s32[128,2]{0,1:T(2,128)}, u32[]{:S(2)}) copy-start(s32[128,2]{0,1:T(2,128)} %param.10) | copy-start | bytes 3076
  6.5 6.9 %copy-start.4 = (s32[46]{0:T(128)S(1)}, s32[46]{0:T(128)}, u32[]{:S(2)}) copy-start(s32[46]{0:T(128)} %param.12) | copy-start | bytes 556
  6.5 7.0 %copy-start.2 = (bf16[384,640]{1,0:T(8,128)(2,1)S(1)}, bf16[384,640]{1,0:T(8,128)(2,1)}, u32[]{:S(2)}) copy-start(bf16[384,640]{1,0:T(8,128)(2,1)} %param.7) | copy-start | bytes 1474564
  8.5 30.9 %all-to-all-start = ((f32[2,6,32,384]{3,2,1,0:T(8,128)}), f32[2,6,32,384]{3,2,1,0:T(8,128)S(1)}, u32[]{:S(2)}, u32[]{:S(2)}) async-start(f32[2,6,32,384]{3,2,1,0:T(8,128)} %copy.42), calls=%async_computation | async-start | bytes 1179648 | tf_op jit(solution)/shard_map/all_to_all | solution.py:38
  32.7 3.5 copy-start
  39.4 59.1 %all-to-all-start.1 = ((bf16[8,192,768]{2,1,0:T(8,128)(2,1)}), bf16[8,192,768]{2,1,0:T(8,128)(2,1)S(1)}, u32[]{:S(2)}, u32[]{:S(2)}) async-start(bf16[8,192,768]{2,1,0:T(8,128)(2,1)} %bitcast.77), calls=%async_computation.1 | async-start | bytes 4718592 | tf_op jit(solution)/shard_map/all_to_all | solution.py:70
  45.5 104.5 %all-gather.6.cloned.1.call-start = ((), (), s32[]{:S(2)}) async-start(), calls=%async_computation.5 | async-start | bytes 2654208 | tf_op jit(solution)/shard_map/all_gather | solution.py:73
  99.6 68.7 %reduce-scatter.3.cloned.1.call-start = ((), (), s32[]{:S(2)}) async-start(), calls=%async_computation.6 | async-start | bytes 3145728 | tf_op jit(solution)/shard_map/reduce_scatter | solution.py:80
  155.9 4.3 %copy-start.5 = (f32[46]{0:T(128)S(1)}, f32[46]{0:T(128)}, u32[]{:S(2)}) copy-start(f32[46]{0:T(128)} %param.13) | copy-start | bytes 556
  160.0 23.5 %all-gather.8.cloned.1.call-start = ((), (), s32[]{:S(2)}) async-start(), calls=%async_computation.7 | async-start | bytes 1572864 | tf_op jit(solution)/shard_map/all_gather | solution.py:85
  173.3 127.9 %all-gather.10.cloned.1.call-start = ((), (), s32[]{:S(2)}) async-start(), calls=%async_computation.8 | async-start | bytes 2654208 | tf_op jit(solution)/shard_map/all_gather | solution.py:73
  185.5 1.2 copy-start.1
  249.9 69.3 %reduce-scatter.5.cloned.1.call-start = ((), (), s32[]{:S(2)}) async-start(), calls=%async_computation.9 | async-start | bytes 3145728 | tf_op jit(solution)/shard_map/reduce_scatter | solution.py:80
  310.9 48.6 %all-gather.12.cloned.1.call-start = ((), (), s32[]{:S(2)}) async-start(), calls=%async_computation.10 | async-start | bytes 3145728 | tf_op jit(solution)/shard_map/all_gather | solution.py:88
  325.1 49.6 %all-gather.14.cloned.1.call-start = ((), (), s32[]{:S(2)}) async-start(), calls=%async_computation.11 | async-start | bytes 6291456 | tf_op jit(solution)/shard_map/all_gather | solution.py:90
Sparse Core Ops, SparseCore 0:
  99.7 50.2 all-gather.5
  160.1 8.1 reduce-scatter.2
  173.4 10.1 all-gather.7
  250.0 51.0 all-gather.9
  311.0 8.1 reduce-scatter.4
  325.2 34.1 all-gather.11
  361.0 13.6 all-gather.13

commit v7 on v6

--- a/solution.py
+++ b/solution.py
@@ -30,13 +30,17 @@
     x = lax.axis_index("sx")
     c = lax.axis_index("sc")
 
-    geno = lax.all_gather(genotypes, "sx", axis=0, tiled=True)
+    swap = [(0, 1), (1, 0)]
+    geno_peer = lax.ppermute(genotypes, "sx", swap)
+    geno = jnp.concatenate([genotypes, geno_peer], axis=0)
     sample_count = geno.shape[0]
     geno_blocks = geno.reshape(sample_count, block_count, block_width)
-    resp = responses.reshape(own_slots, halves, half_p, quarter)
-    resp = jnp.moveaxis(resp, 1, 0)
-    resp = lax.all_to_all(resp, "sx", 0, 0, tiled=False)
-    resp = jnp.moveaxis(resp, 0, 2).reshape(own_slots * half_p, halves * quarter)
+    resp4 = responses.reshape(own_slots, halves, half_p, quarter)
+    resp_own = lax.dynamic_slice_in_dim(resp4, x, 1, 1)[:, 0]
+    resp_peer = lax.ppermute(lax.dynamic_slice_in_dim(resp4, 1 - x, 1, 1)[:, 0], "sx", swap)
+    resp = jnp.concatenate([resp_own, resp_peer], axis=2).reshape(
+        own_slots * half_p, halves * quarter
+    )
 
     blk = pattern[:, 0]
     tile = pattern[:, 1]
@@ -63,12 +67,23 @@
             "ec,epk->cpk", cell_hot, weight_bf, preferred_element_type=jnp.float32
         ).astype(jnp.bfloat16)
         dense = dense.reshape(slot_total, block_count, half_p, block_width)
-        partial = jnp.einsum(
-            "jbpk,sbk->jps", dense, geno_blocks, preferred_element_type=jnp.float32
-        ).astype(jnp.bfloat16)
-        partial = partial.reshape(owners, own_slots * half_p, sample_count)
-        gathered = lax.all_to_all(partial, "snp", 0, 0, tiled=False)
-        prediction = jnp.sum(gathered.astype(jnp.float32), axis=0)
+
+        def predict(samples):
+            count = samples.shape[0]
+            partial = jnp.einsum(
+                "jbpk,sbk->jps",
+                dense,
+                samples.reshape(count, block_count, block_width),
+                preferred_element_type=jnp.float32,
+            ).astype(jnp.bfloat16)
+            partial = partial.reshape(owners, own_slots * half_p, count)
+            gathered = lax.all_to_all(partial, "snp", 0, 0, tiled=False)
+            return jnp.sum(gathered.astype(jnp.float32), axis=0)
+
+        if sweep == 0:
+            prediction = jnp.concatenate([predict(genotypes), predict(geno_peer)], axis=1)
+        else:
+            prediction = predict(geno)
         residual = (resp - prediction).astype(jnp.bfloat16)
         shard_rows = lax.all_gather(residual, "snp", axis=0, tiled=True)
         blocks = shard_rows.reshape(slot_total, half_p, sample_count)

time: 387 us -> 378 us (0.977)
  blocking collectives: 78.8 us -> 59.8 us
  local copies, waits for them, and re-layouts: 17.6 us -> 23.5 us
    all_gather x1 -> x0, blocking collectives: 18.9 us -> none  [per_device(): geno = lax.all_gather(genotypes, 'sx', axis=0, tiled=True)]
    all_to_all x2, waiting for transfers between devices: 52.4 us -> 38.2 us  [predict(): gathered = lax.all_to_all(partial, 'snp', 0, 0, tiled=False)]
    ppermute x0 -> x2, waiting for transfers between devices: none -> 11.4 us  [the longest x1 11.4 us: per_device(): geno_peer = lax.ppermute(genotypes, 'sx', swap)]
  transfers between devices with their start and end apart: 9 -> 11, of which waited for: 8 -> 10; matrix products, arithmetic and copies ran while one was open for 2% -> 1% of each run, Pallas kernels for 0% -> 0%
where the time goes in v7:
time: 378 us; the launch traced here: 377 us
  waiting for transfers between devices  227 us (60%)
  blocking collectives  59.8 us (16%)
  local copies, waits for them, and re-layouts  23.5 us (6%)
  other arithmetic  19.2 us (5%)
  matrix products  19.2 us (5%)
  starting transfers between devices  14.4 us (4%)
  between operations  14.3 us (4%)
    all_gather x2, waiting for transfers between devices, per_device(): shard_rows = lax.all_gather(residual, 'snp', axis=0, tiled=True)  101 us
    all_to_all x1, blocking collectives, predict(): gathered = lax.all_to_all(partial, 'snp', 0, 0, tiled=False)  59.8 us
    all_to_all x2, waiting for transfers between devices, predict(): gathered = lax.all_to_all(partial, 'snp', 0, 0, tiled=False)  38.2 us
    all_gather x1, waiting for transfers between devices, per_device(): both = lax.all_gather(own, 'sx', axis=1, tiled=True)  34.3 us
    reduce_scatter x2, waiting for transfers between devices, per_device(): mine = lax.psum_scatter(rows, 'sc', scatter_dimension=0, tiled=True)  16.2 us
    all_gather x1, waiting for transfers between devices, per_device(): return lax.all_gather(flat, 'sc', axis=0, tiled=True).reshape(weights.shape)  15.2 us
    ppermute x1, waiting for transfers between devices, per_device(): geno_peer = lax.ppermute(genotypes, 'sx', swap)  11.4 us
    all_to_all x2, starting transfers between devices, predict(): gathered = lax.all_to_all(partial, 'snp', 0, 0, tiled=False)  10.9 us
  transfers between devices with their start and end apart: 11, of which 10 were waited for; matrix products, arithmetic and copies ran while one was open for 1% of the time, Pallas kernels for 0%

profile of v7, /device:TPU:0, one launch (start us, length us, event | category | flops | bytes accessed | tf_op | source)
XLA Modules:
  0.0 377.3 jit_solution(7424947359191635115)
XLA Ops:
  9.3 1.9 select_convert_fusion
  13.2 2.3 bitcast_convert_fusion.2
  15.5 7.3 %all-to-all-start = ((bf16[8,192,384]{2,1,0:T(8,128)(2,1)}), bf16[8,192,384]{2,1,0:T(8,128)(2,1)S(1)}, u32[]{:S(2)}, u32[]{:S(2)}) async-start(bf16[8,192,384]{2,1,0:T(8,128)(2,1)} %bitcast.100), calls=%async_computation | async-start | bytes 2359296 | tf_op jit(solution)/shard_map/all_to_all | solution.py:80
  22.8 1.5 collective-permute-start
  24.3 11.4 %collective-permute-done = bf16[384,640]{0,1:T(8,128)(2,1)S(1)} collective-permute-done((bf16[384,640]{0,1:T(8,128)(2,1)}, bf16[384,640]{0,1:T(8,128)(2,1)S(1)}, u32[]{:S(2)}, u32[]{:S(2)}) %collective-permute-start) | collective-permute-done | bytes 491552 | tf_op jit(solution)/shard_map/ppermute | solution.py:34
  36.5 2.3 bitcast_convert_fusion.1
  38.8 12.6 %all-to-all-done = bf16[8,192,384]{2,1,0:T(8,128)(2,1)S(1)} async-done(((bf16[8,192,384]{2,1,0:T(8,128)(2,1)}), bf16[8,192,384]{2,1,0:T(8,128)(2,1)S(1)}, u32[]{:S(2)}, u32[]{:S(2)}) %all-to-all-start) | async-done | bytes 1179680 | tf_op jit(solution)/shard_map/all_to_all | solution.py:80
  51.4 3.6 all-to-all-start.1
  55.8 1.5 collective-permute-start.1
  58.2 25.6 %all-to-all-done.1 = bf16[8,192,384]{2,1,0:T(8,128)(2,1)S(1)} async-done(((bf16[8,192,384]{2,1,0:T(8,128)(2,1)}), bf16[8,192,384]{2,1,0:T(8,128)(2,1)S(1)}, u32[]{:S(2)}, u32[]{:S(2)}) %all-to-all-start.1) | async-done | bytes 1179680 | tf_op jit(solution)/shard_map/all_to_all | solution.py:80
  83.9 1.7 fusion.14
  86.9 50.1 %all-gather.6.cloned.1.call-done = bf16[1536,768]{1,0:T(8,128)(2,1)} async-done(((bf16[192,768]{1,0:T(8,128)(2,1)}), bf16[1536,768]{1,0:T(8,128)(2,1)}) %all-gather.6.cloned.1.call-update) | async-done | bytes 2359312 | tf_op jit(solution)/shard_map/all_gather | solution.py:88
  137.0 4.9 %fusion.6 = f32[48,5,32,128]{3,0,2,1:T(8,128)S(1)} fusion(bf16[768,5,128,1]{0,2,3,1:T(8,128)(2,1)S(1)} %bitcast.104, bf16[48,32,768]{2,1,0:T(8,128)(2,1)} %bitcast.109), kind=kOutput, calls=%fused_computation.15 | convolution fusion | flops 1509949440 | bytes 7274496 | tf_op jit(solution)/shard_map/jps,sbk->jbpk/dot_general | solution.py:90
  141.9 3.1 copy.40
  145.0 4.1 %gather_fusion = f32[128,32,128]{2,1,0:T(8,128)} fusion(f32[240,32,128]{2,1,0:T(8,128)} %bitcast.85, s32[1024]{0:T(1024)S(1)} %pad_clamp_fusion), kind=kCustom, calls=%fused_computation | custom fusion | bytes 4194816 | tf_op jit(solution)/shard_map/jit(_take)/gather | solution.py:93
  149.5 8.0 %reduce-scatter.3.cloned.1.call-done = f32[2048,128]{1,0:T(8,128)} async-done(((f32[4096,128]{1,0:T(8,128)}), f32[2048,128]{1,0:T(8,128)}) %reduce-scatter.3.cloned.1.call-update) | async-done | bytes 1048592 | tf_op jit(solution)/shard_map/reduce_scatter | solution.py:95
  157.4 1.3 broadcast_multiply_fusion.1
  158.8 3.6 fusion.21
  162.6 10.1 %all-gather.8.cloned.1.call-done = bf16[4096,128]{1,0:T(8,128)(2,1)} async-done(((bf16[2048,128]{1,0:T(8,128)(2,1)}), bf16[4096,128]{1,0:T(8,128)(2,1)}) %all-gather.8.cloned.1.call-update) | async-done | bytes 1048592 | tf_op jit(solution)/shard_map/all_gather | solution.py:100
  172.7 1.9 convolution_convert_fusion
  175.1 2.2 bitcast_convert_fusion
  177.3 59.8 %all_to_all.15 = bf16[8,192,768]{2,1,0:T(8,128)(2,1)S(1)} all-to-all(bf16[8,192,768]{2,1,0:T(8,128)(2,1)S(1)} %bitcast.92), channel_id=1, replica_groups=mesh['snp'=8,'sx'=2,'sc'=2] {'snp'}, dimensions={0} | all-to-all | bytes 4718592 | tf_op jit(solution)/shard_map/all_to_all | solution.py:80
  238.4 51.2 %all-gather.10.cloned.1.call-done = bf16[1536,768]{1,0:T(8,128)(2,1)} async-done(((bf16[192,768]{1,0:T(8,128)(2,1)}), bf16[1536,768]{1,0:T(8,128)(2,1)}) %all-gather.10.cloned.1.call-update) | async-done | bytes 2359312 | tf_op jit(solution)/shard_map/all_gather | solution.py:88
  289.6 4.9 %fusion.9 = f32[48,5,32,128]{3,0,2,1:T(8,128)S(1)} fusion(bf16[768,5,128,1]{0,2,3,1:T(8,128)(2,1)S(1)} %bitcast.106, bf16[48,32,768]{2,1,0:T(8,128)(2,1)} %bitcast.110), kind=kOutput, calls=%fused_computation.16 | convolution fusion | flops 1509949440 | bytes 7274496 | tf_op jit(solution)/shard_map/jps,sbk->jbpk/dot_general | solution.py:90
  294.5 3.1 copy.46
  297.6 4.1 %gather_fusion.1 = f32[128,32,128]{2,1,0:T(8,128)} fusion(f32[240,32,128]{2,1,0:T(8,128)} %bitcast.84, s32[1024]{0:T(1024)S(1)} %pad_clamp_fusion), kind=kCustom, calls=%fused_computation.1 | custom fusion | bytes 4194816 | tf_op jit(solution)/shard_map/jit(_take)/gather | solution.py:93
  301.8 8.2 %reduce-scatter.5.cloned.1.call-done = f32[2048,128]{1,0:T(8,128)} async-done(((f32[4096,128]{1,0:T(8,128)}), f32[2048,128]{1,0:T(8,128)}) %reduce-scatter.5.cloned.1.call-update) | async-done | bytes 1048592 | tf_op jit(solution)/shard_map/reduce_scatter | solution.py:95
  310.1 1.3 broadcast_multiply_fusion
  311.4 4.6 %multiply_select_fusion = f32[64,32,128]{2,1,0:T(8,128)} fusion(f32[64,32,128]{2,1,0:T(8,128)S(1)} %bitcast.89, f32[64]{0:T(128)S(1)} %dynamic_slice.24, pred[64]{0:T(512)(128)(4,1)S(1)} %dynamic_slice.19, f32[64,32,128]{2,1,0:T(8,128)S(1)} %bitcast.83, f32[128,64,128]{2,1,0:T(8,128)} %param.9, s32[]{:T(128)S(6)} %select_n.41, s32[]{:T(128)S(6)} %select_n.43), kind=kLoop, calls=%fused_computation.21 | loop fusion | flops 3932160 | bytes 4194632 | tf_op jit(solution)/shard_map/jit(_where)/select_n | solution.py:15
  316.1 34.3 %all-gather.12.cloned.1.call-done = f32[64,64,128]{2,1,0:T(8,128)} async-done(((f32[64,32,128]{2,1,0:T(8,128)}), f32[64,64,128]{2,1,0:T(8,128)}) %all-gather.12.cloned.1.call-update) | async-done | bytes 2097168 | tf_op jit(solution)/shard_map/all_gather | solution.py:103
  350.4 15.2 %all-gather.14.cloned.1.call-done = f32[8192,128]{1,0:T(8,128)} async-done(((f32[4096,128]{1,0:T(8,128)}), f32[8192,128]{1,0:T(8,128)}) %all-gather.14.cloned.1.call-update) | async-done | bytes 4194320 | tf_op jit(solution)/shard_map/all_gather | solution.py:105
  365.6 4.8 %copy.81 = f32[128,64,128]{2,1,0:T(8,128)} copy(f32[128,64,128]{2,1,0:T(8,128)} %bitcast.88) | data formatting | bytes 8388608
  (46 shorter events, 10.3 us)
Async XLA Ops:
  11.9 1.0 copy-start.3
  13.2 2.3 copy-start
  15.5 35.9 %all-to-all-start = ((bf16[8,192,384]{2,1,0:T(8,128)(2,1)}), bf16[8,192,384]{2,1,0:T(8,128)(2,1)S(1)}, u32[]{:S(2)}, u32[]{:S(2)}) async-start(bf16[8,192,384]{2,1,0:T(8,128)(2,1)} %bitcast.100), calls=%async_computation | async-start | bytes 2359296 | tf_op jit(solution)/shard_map/all_to_all | solution.py:80
  22.8 12.9 %collective-permute-start = (bf16[384,640]{0,1:T(8,128)(2,1)}, bf16[384,640]{0,1:T(8,128)(2,1)S(1)}, u32[]{:S(2)}, u32[]{:S(2)}) collective-permute-start(bf16[384,640]{0,1:T(8,128)(2,1)} %copy-done), channel_id=1, source_target_pairs={{0,2},{2,0},{1,3},{3,1},{4,6},{6,4},{5,7},{7,5},{8,10},{10,8},{9,1... | collective-permute-start | bytes 1474568 | tf_op jit(solution)/shard_map/ppermute | solution.py:34
  35.7 0.8 copy-start.4
  38.8 16.3 %copy-start.2 = (f32[384,384]{1,0:T(8,128)S(1)}, f32[384,384]{1,0:T(8,128)}, u32[]{:S(2)}) copy-start(f32[384,384]{1,0:T(8,128)} %param.8) | copy-start | bytes 1769476
  51.4 32.4 %all-to-all-start.1 = ((bf16[8,192,384]{2,1,0:T(8,128)(2,1)}), bf16[8,192,384]{2,1,0:T(8,128)(2,1)S(1)}, u32[]{:S(2)}, u32[]{:S(2)}) async-start(bf16[8,192,384]{2,1,0:T(8,128)(2,1)} %bitcast.99), calls=%async_computation.1 | async-start | bytes 2359296 | tf_op jit(solution)/shard_map/all_to_all | solution.py:80
  55.0 82.0 %all-gather.6.cloned.1.call-start = ((), (), s32[]{:S(2)}) async-start(), calls=%async_computation.5 | async-start | bytes 2654208 | tf_op jit(solution)/shard_map/all_gather | solution.py:88
  55.8 29.9 %copy-start.1 = (bf16[384,640]{0,1:T(8,128)(2,1)S(1)}, bf16[384,640]{0,1:T(8,128)(2,1)}, u32[]{:S(2)}) copy-start(bf16[384,640]{0,1:T(8,128)(2,1)} %copy-done) | copy-start | bytes 1474564
  55.8 28.1 %collective-permute-start.1 = (f32[6,32,384]{2,1,0:T(8,128)}, f32[6,32,384]{2,1,0:T(8,128)S(1)}, u32[]{:S(2)}, u32[]{:S(2)}) collective-permute-start(f32[6,32,384]{2,1,0:T(8,128)} %get-tuple-element.6), channel_id=1, source_target_pairs={{0,2},{2,0},{1,3},{3,1},{4,6},{6,4},{5,7},{7,5},{8,10},{10,8},{9,1... | collective-permute-start | bytes 884744 | tf_op jit(solution)/shard_map/ppermute | solution.py:40
  85.7 71.7 %reduce-scatter.3.cloned.1.call-start = ((), (), s32[]{:S(2)}) async-start(), calls=%async_computation.6 | async-start | bytes 3145728 | tf_op jit(solution)/shard_map/reduce_scatter | solution.py:95
  145.0 4.3 %copy-start.5 = (f32[46]{0:T(128)S(1)}, f32[46]{0:T(128)}, u32[]{:S(2)}) copy-start(f32[46]{0:T(128)} %param.13) | copy-start | bytes 556
  149.2 23.5 %all-gather.8.cloned.1.call-start = ((), (), s32[]{:S(2)}) async-start(), calls=%async_computation.7 | async-start | bytes 1572864 | tf_op jit(solution)/shard_map/all_gather | solution.py:100
  162.4 127.2 %all-gather.10.cloned.1.call-start = ((), (), s32[]{:S(2)}) async-start(), calls=%async_computation.8 | async-start | bytes 2654208 | tf_op jit(solution)/shard_map/all_gather | solution.py:88
  238.4 71.7 %reduce-scatter.5.cloned.1.call-start = ((), (), s32[]{:S(2)}) async-start(), calls=%async_computation.9 | async-start | bytes 3145728 | tf_op jit(solution)/shard_map/reduce_scatter | solution.py:95
  301.8 48.6 %all-gather.12.cloned.1.call-start = ((), (), s32[]{:S(2)}) async-start(), calls=%async_computation.10 | async-start | bytes 3145728 | tf_op jit(solution)/shard_map/all_gather | solution.py:103
  316.0 49.6 %all-gather.14.cloned.1.call-start = ((), (), s32[]{:S(2)}) async-start(), calls=%async_computation.11 | async-start | bytes 6291456 | tf_op jit(solution)/shard_map/all_gather | solution.py:105
Sparse Core Ops, SparseCore 0:
  85.8 51.1 all-gather.5
  149.3 8.1 reduce-scatter.2
  162.5 10.1 all-gather.7
  238.5 51.0 all-gather.9
  301.9 8.1 reduce-scatter.4
  316.1 34.2 all-gather.11
  351.9 13.6 all-gather.13

commit v8 on v7

--- a/solution.py
+++ b/solution.py
@@ -100,9 +100,18 @@
             weight_bf = lax.all_gather(flat, "sc", axis=0, tiled=True).reshape(
                 entries, half_p, block_width
             )
-    both = lax.all_gather(own, "sx", axis=1, tiled=True)
-    flat = both.reshape(share * tile_width, block_width)
-    return lax.all_gather(flat, "sc", axis=0, tiled=True).reshape(weights.shape)
+    other_half = lax.ppermute(own, "sx", swap)
+    mine = jnp.where(
+        x == 0,
+        jnp.concatenate([own, other_half], axis=1),
+        jnp.concatenate([other_half, own], axis=1),
+    )
+    other_entries = lax.ppermute(mine, "sc", swap)
+    return jnp.where(
+        c == 0,
+        jnp.concatenate([mine, other_entries], axis=0),
+        jnp.concatenate([other_entries, mine], axis=0),
+    )
 
 
 def solution(mesh):

time: 378 us -> 359 us (0.950)
  waiting for transfers between devices: 227 us -> 205 us
  other arithmetic: 19.2 us -> 25.4 us
  local copies, waits for them, and re-layouts: 23.5 us -> 19.2 us
    all_gather x2 -> x0, waiting for transfers between devices: 49.6 us -> none  [the longest x1 34.3 us: per_device(): both = lax.all_gather(own, 'sx', axis=1, tiled=True)]
    ppermute x0 -> x2, waiting for transfers between devices: none -> 28 us  [the longest x1 23.7 us: per_device(): other_half = lax.ppermute(own, 'sx', swap)]
    select_n x0 -> x2, other arithmetic: none -> 7.12 us  [the longest x1 5.19 us: per_device(): jnp.where(c == 0, jnp.concatenate([mine, other_entries], axis=0), jnp.con...]
    unnamed x14 -> x13, local copies, waits for them, and re-layouts: 6.36 us -> 2.07 us
  transfers between devices with their start and end apart: 11 -> 11, of which waited for: 10 -> 10; matrix products, arithmetic and copies ran while one was open for 1% -> 2% of each run, Pallas kernels for 0% -> 0%
where the time goes in v8:
time: 359 us
  waiting for transfers between devices  205 us (57%)
  blocking collectives  59.8 us (17%)
  other arithmetic  25.4 us (7%)
  local copies, waits for them, and re-layouts  19.2 us (5%)
  matrix products  19.2 us (5%)
  starting transfers between devices  16.1 us (4%)
  between operations  14 us (4%)
    all_gather x2, waiting for transfers between devices, per_device(): shard_rows = lax.all_gather(residual, 'snp', axis=0, tiled=True)  101 us
    all_to_all x1, blocking collectives, predict(): gathered = lax.all_to_all(partial, 'snp', 0, 0, tiled=False)  59.8 us
    all_to_all x2, waiting for transfers between devices, predict(): gathered = lax.all_to_all(partial, 'snp', 0, 0, tiled=False)  38.2 us
    ppermute x1, waiting for transfers between devices, per_device(): other_half = lax.ppermute(own, 'sx', swap)  23.7 us
    reduce_scatter x2, waiting for transfers between devices, per_device(): mine = lax.psum_scatter(rows, 'sc', scatter_dimension=0, tiled=True)  15.8 us
    ppermute x1, waiting for transfers between devices, per_device(): geno_peer = lax.ppermute(genotypes, 'sx', swap)  11.4 us
    all_to_all x2, starting transfers between devices, predict(): gathered = lax.all_to_all(partial, 'snp', 0, 0, tiled=False)  10.9 us
    all_gather x1, waiting for transfers between devices, per_device(): lax.all_gather(flat, 'sc', axis=0, tiled=True)  10 us
  transfers between devices with their start and end apart: 11, of which 10 were waited for; matrix products, arithmetic and copies ran while one was open for 2% of the time, Pallas kernels for 0%

profile of v8, /device:TPU:0, one launch (start us, length us, event | category | flops | bytes accessed | tf_op | source)
XLA Modules:
  0.0 358.5 jit_solution(8053249686498767552)
XLA Ops:
  9.3 1.9 select_convert_fusion
  13.2 2.3 bitcast_convert_fusion.2
  15.5 7.3 %all-to-all-start = ((bf16[8,192,384]{2,1,0:T(8,128)(2,1)}), bf16[8,192,384]{2,1,0:T(8,128)(2,1)S(1)}, u32[]{:S(2)}, u32[]{:S(2)}) async-start(bf16[8,192,384]{2,1,0:T(8,128)(2,1)} %bitcast.96), calls=%async_computation | async-start | bytes 2359296 | tf_op jit(solution)/shard_map/all_to_all | solution.py:80
  22.8 1.5 collective-permute-start
  24.3 11.4 %collective-permute-done = bf16[384,640]{0,1:T(8,128)(2,1)S(1)} collective-permute-done((bf16[384,640]{0,1:T(8,128)(2,1)}, bf16[384,640]{0,1:T(8,128)(2,1)S(1)}, u32[]{:S(2)}, u32[]{:S(2)}) %collective-permute-start) | collective-permute-done | bytes 491552 | tf_op jit(solution)/shard_map/ppermute | solution.py:34
  36.5 2.3 bitcast_convert_fusion.1
  38.8 12.6 %all-to-all-done = bf16[8,192,384]{2,1,0:T(8,128)(2,1)S(1)} async-done(((bf16[8,192,384]{2,1,0:T(8,128)(2,1)}), bf16[8,192,384]{2,1,0:T(8,128)(2,1)S(1)}, u32[]{:S(2)}, u32[]{:S(2)}) %all-to-all-start) | async-done | bytes 1179680 | tf_op jit(solution)/shard_map/all_to_all | solution.py:80
  51.4 3.6 %all-to-all-start.1 = ((bf16[8,192,384]{2,1,0:T(8,128)(2,1)}), bf16[8,192,384]{2,1,0:T(8,128)(2,1)S(1)}, u32[]{:S(2)}, u32[]{:S(2)}) async-start(bf16[8,192,384]{2,1,0:T(8,128)(2,1)} %bitcast.95), calls=%async_computation.1 | async-start | bytes 2359296 | tf_op jit(solution)/shard_map/all_to_all | solution.py:80
  55.8 1.5 collective-permute-start.1
  58.2 25.6 %all-to-all-done.1 = bf16[8,192,384]{2,1,0:T(8,128)(2,1)S(1)} async-done(((bf16[8,192,384]{2,1,0:T(8,128)(2,1)}), bf16[8,192,384]{2,1,0:T(8,128)(2,1)S(1)}, u32[]{:S(2)}, u32[]{:S(2)}) %all-to-all-start.1) | async-done | bytes 1179680 | tf_op jit(solution)/shard_map/all_to_all | solution.py:80
  83.9 1.7 fusion.14
  86.9 50.1 %all-gather.4.cloned.1.call-done = bf16[1536,768]{1,0:T(8,128)(2,1)} async-done(((bf16[192,768]{1,0:T(8,128)(2,1)}), bf16[1536,768]{1,0:T(8,128)(2,1)}) %all-gather.4.cloned.1.call-update) | async-done | bytes 2359312 | tf_op jit(solution)/shard_map/all_gather | solution.py:88
  137.0 4.9 %fusion.6 = f32[48,5,32,128]{3,0,2,1:T(8,128)S(1)} fusion(bf16[768,5,128,1]{0,2,3,1:T(8,128)(2,1)S(1)} %bitcast.100, bf16[48,32,768]{2,1,0:T(8,128)(2,1)} %bitcast.105), kind=kOutput, calls=%fused_computation.17 | convolution fusion | flops 1509949440 | bytes 7274496 | tf_op jit(solution)/shard_map/jps,sbk->jbpk/dot_general | solution.py:90
  141.9 3.1 copy.40
  145.0 4.1 %gather_fusion = f32[128,32,128]{2,1,0:T(8,128)} fusion(f32[240,32,128]{2,1,0:T(8,128)} %bitcast.83, s32[1024]{0:T(1024)S(1)} %pad_clamp_fusion), kind=kCustom, calls=%fused_computation | custom fusion | bytes 4194816 | tf_op jit(solution)/shard_map/jit(_take)/gather | solution.py:93
  150.0 7.5 %reduce-scatter.3.cloned.1.call-done = f32[2048,128]{1,0:T(8,128)} async-done(((f32[4096,128]{1,0:T(8,128)}), f32[2048,128]{1,0:T(8,128)}) %reduce-scatter.3.cloned.1.call-update) | async-done | bytes 1048592 | tf_op jit(solution)/shard_map/reduce_scatter | solution.py:95
  158.8 3.6 %fusion.21 = bf16[64,32,128]{2,1,0:T(8,128)(2,1)} fusion(f32[64]{0:T(128)S(1)} %dynamic_slice.24, f32[64,32,128]{2,1,0:T(8,128)S(1)} %bitcast.80, f32[128,64,128]{2,1,0:T(8,128)} %param.9, s32[]{:T(128)S(6)} %select_n.59, s32[]{:T(128)S(6)} %select_n.61, pred[64]{0:T(512)(128)(4,1)S(1)} %dynamic_slice.19), kind=kLoop, calls=%fused_computation.47 | loop fusion | flops 2359296 | bytes 2621768 | tf_op jit(solution)/shard_map/convert_element_type | solution.py:99
  162.6 10.0 %all-gather.6.cloned.1.call-done = bf16[4096,128]{1,0:T(8,128)(2,1)} async-done(((bf16[2048,128]{1,0:T(8,128)(2,1)}), bf16[4096,128]{1,0:T(8,128)(2,1)}) %all-gather.6.cloned.1.call-update) | async-done | bytes 1048592 | tf_op jit(solution)/shard_map/all_gather | solution.py:100
  172.7 1.9 convolution_convert_fusion
  175.1 2.2 bitcast_convert_fusion
  177.3 59.8 %all_to_all.15 = bf16[8,192,768]{2,1,0:T(8,128)(2,1)S(1)} all-to-all(bf16[8,192,768]{2,1,0:T(8,128)(2,1)S(1)} %bitcast.89), channel_id=1, replica_groups=mesh['snp'=8,'sx'=2,'sc'=2] {'snp'}, dimensions={0} | all-to-all | bytes 4718592 | tf_op jit(solution)/shard_map/all_to_all | solution.py:80
  238.4 51.2 %all-gather.8.cloned.1.call-done = bf16[1536,768]{1,0:T(8,128)(2,1)} async-done(((bf16[192,768]{1,0:T(8,128)(2,1)}), bf16[1536,768]{1,0:T(8,128)(2,1)}) %all-gather.8.cloned.1.call-update) | async-done | bytes 2359312 | tf_op jit(solution)/shard_map/all_gather | solution.py:88
  289.6 4.9 %fusion.9 = f32[48,5,32,128]{3,0,2,1:T(8,128)S(1)} fusion(bf16[768,5,128,1]{0,2,3,1:T(8,128)(2,1)S(1)} %bitcast.102, bf16[48,32,768]{2,1,0:T(8,128)(2,1)} %bitcast.106), kind=kOutput, calls=%fused_computation.18 | convolution fusion | flops 1509949440 | bytes 7274496 | tf_op jit(solution)/shard_map/jps,sbk->jbpk/dot_general | solution.py:90
  294.5 3.1 copy.46
  297.6 4.1 %gather_fusion.1 = f32[128,32,128]{2,1,0:T(8,128)} fusion(f32[240,32,128]{2,1,0:T(8,128)} %bitcast.82, s32[1024]{0:T(1024)S(1)} %pad_clamp_fusion), kind=kCustom, calls=%fused_computation.1 | custom fusion | bytes 4194816 | tf_op jit(solution)/shard_map/jit(_take)/gather | solution.py:93
  301.8 8.3 %reduce-scatter.5.cloned.1.call-done = f32[2048,128]{1,0:T(8,128)} async-done(((f32[4096,128]{1,0:T(8,128)}), f32[2048,128]{1,0:T(8,128)}) %reduce-scatter.5.cloned.1.call-update) | async-done | bytes 1048592 | tf_op jit(solution)/shard_map/reduce_scatter | solution.py:95
  311.4 3.6 %multiply_select_fusion = f32[64,32,128]{2,1,0:T(8,128)S(1)} fusion(f32[64,32,128]{2,1,0:T(8,128)S(1)} %bitcast.86, f32[64]{0:T(128)S(1)} %dynamic_slice.24, pred[64]{0:T(512)(128)(4,1)S(1)} %dynamic_slice.19, f32[64,32,128]{2,1,0:T(8,128)S(1)} %bitcast.81, f32[128,64,128]{2,1,0:T(8,128)} %param.9, s32[]{:T(128)S(6)} %select_n.59, s32[]{:T(128)S(6)} %select_n.61), kind=kLoop, calls=%fused_computation.23 | loop fusion | flops 3932160 | bytes 4194632 | tf_op jit(solution)/shard_map/jit(_where)/select_n | solution.py:15
  315.0 1.7 collective-permute-start.2
  316.7 23.7 %collective-permute-done.2 = f32[64,32,128]{2,1,0:T(8,128)} collective-permute-done((f32[64,32,128]{2,1,0:T(8,128)S(1)}, f32[64,32,128]{2,1,0:T(8,128)}, u32[]{:S(2)}, u32[]{:S(2)}) %collective-permute-start.2) | collective-permute-done | bytes 1048608 | tf_op jit(solution)/shard_map/ppermute | solution.py:103
  340.5 1.9 maximum_select_fusion.1
  342.5 4.3 %collective-permute-done.3 = f32[64,64,128]{2,1,0:T(8,128)} collective-permute-done((f32[64,64,128]{2,1,0:T(8,128)S(1)}, f32[64,64,128]{2,1,0:T(8,128)}, u32[]{:S(2)}, u32[]{:S(2)}) %collective-permute-start.3) | collective-permute-done | bytes 2097184 | tf_op jit(solution)/shard_map/ppermute | solution.py:109
  346.8 5.2 %maximum_select_fusion = f32[128,64,128]{2,1,0:T(8,128)} fusion(f32[64,64,128]{2,1,0:T(8,128)} %collective-permute-done.3, f32[64,64,128]{2,1,0:T(8,128)S(1)} %maximum_select_fusion.1, pred[]{:T(512)S(6)} %eq.36), kind=kLoop, calls=%fused_computation.4 | loop fusion | flops 3145728 | bytes 8388609 | tf_op jit(solution)/shard_map/jit(_where)/select_n | solution.py:110
  (45 shorter events, 13.4 us)
Async XLA Ops:
  11.9 1.0 copy-start.3
  13.2 2.3 copy-start
  15.5 35.9 %all-to-all-start = ((bf16[8,192,384]{2,1,0:T(8,128)(2,1)}), bf16[8,192,384]{2,1,0:T(8,128)(2,1)S(1)}, u32[]{:S(2)}, u32[]{:S(2)}) async-start(bf16[8,192,384]{2,1,0:T(8,128)(2,1)} %bitcast.96), calls=%async_computation | async-start | bytes 2359296 | tf_op jit(solution)/shard_map/all_to_all | solution.py:80
  22.8 12.9 %collective-permute-start = (bf16[384,640]{0,1:T(8,128)(2,1)}, bf16[384,640]{0,1:T(8,128)(2,1)S(1)}, u32[]{:S(2)}, u32[]{:S(2)}) collective-permute-start(bf16[384,640]{0,1:T(8,128)(2,1)} %copy-done), channel_id=1, source_target_pairs={{0,2},{2,0},{1,3},{3,1},{4,6},{6,4},{5,7},{7,5},{8,10},{10,8},{9,1... | collective-permute-start | bytes 1474568 | tf_op jit(solution)/shard_map/ppermute | solution.py:34
  35.7 0.8 copy-start.4
  38.8 16.3 %copy-start.2 = (f32[384,384]{1,0:T(8,128)S(1)}, f32[384,384]{1,0:T(8,128)}, u32[]{:S(2)}) copy-start(f32[384,384]{1,0:T(8,128)} %param.8) | copy-start | bytes 1769476
  51.4 32.4 %all-to-all-start.1 = ((bf16[8,192,384]{2,1,0:T(8,128)(2,1)}), bf16[8,192,384]{2,1,0:T(8,128)(2,1)S(1)}, u32[]{:S(2)}, u32[]{:S(2)}) async-start(bf16[8,192,384]{2,1,0:T(8,128)(2,1)} %bitcast.95), calls=%async_computation.1 | async-start | bytes 2359296 | tf_op jit(solution)/shard_map/all_to_all | solution.py:80
  55.0 82.0 %all-gather.4.cloned.1.call-start = ((), (), s32[]{:S(2)}) async-start(), calls=%async_computation.5 | async-start | bytes 2654208 | tf_op jit(solution)/shard_map/all_gather | solution.py:88
  55.8 29.9 %copy-start.1 = (bf16[384,640]{0,1:T(8,128)(2,1)S(1)}, bf16[384,640]{0,1:T(8,128)(2,1)}, u32[]{:S(2)}) copy-start(bf16[384,640]{0,1:T(8,128)(2,1)} %copy-done) | copy-start | bytes 1474564
  55.8 28.1 %collective-permute-start.1 = (f32[6,32,384]{2,1,0:T(8,128)}, f32[6,32,384]{2,1,0:T(8,128)S(1)}, u32[]{:S(2)}, u32[]{:S(2)}) collective-permute-start(f32[6,32,384]{2,1,0:T(8,128)} %get-tuple-element.6), channel_id=1, source_target_pairs={{0,2},{2,0},{1,3},{3,1},{4,6},{6,4},{5,7},{7,5},{8,10},{10,8},{9,1... | collective-permute-start | bytes 884744 | tf_op jit(solution)/shard_map/ppermute | solution.py:40
  85.7 71.8 %reduce-scatter.3.cloned.1.call-start = ((), (), s32[]{:S(2)}) async-start(), calls=%async_computation.6 | async-start | bytes 3145728 | tf_op jit(solution)/shard_map/reduce_scatter | solution.py:95
  149.1 0.7 copy-start.5
  149.2 23.5 %all-gather.6.cloned.1.call-start = ((), (), s32[]{:S(2)}) async-start(), calls=%async_computation.7 | async-start | bytes 1572864 | tf_op jit(solution)/shard_map/all_gather | solution.py:100
  162.4 127.2 %all-gather.8.cloned.1.call-start = ((), (), s32[]{:S(2)}) async-start(), calls=%async_computation.8 | async-start | bytes 2654208 | tf_op jit(solution)/shard_map/all_gather | solution.py:88
  238.3 71.7 %reduce-scatter.5.cloned.1.call-start = ((), (), s32[]{:S(2)}) async-start(), calls=%async_computation.9 | async-start | bytes 3145728 | tf_op jit(solution)/shard_map/reduce_scatter | solution.py:95
  315.0 25.5 %collective-permute-start.2 = (f32[64,32,128]{2,1,0:T(8,128)S(1)}, f32[64,32,128]{2,1,0:T(8,128)}, u32[]{:S(2)}, u32[]{:S(2)}) collective-permute-start(f32[64,32,128]{2,1,0:T(8,128)S(1)} %multiply_select_fusion), channel_id=1, source_target_pairs={{0,2},{2,0},{1,3},{3,1},{4,6},{6,4},{5,7},{7,5},{8,10},{10,8},{9,1... | collective-permute-start | bytes 3145736 | tf_op jit(solution)/shard_map/ppermute | solution.py:103
  342.4 4.4 %collective-permute-start.3 = (f32[64,64,128]{2,1,0:T(8,128)S(1)}, f32[64,64,128]{2,1,0:T(8,128)}, u32[]{:S(2)}, u32[]{:S(2)}) collective-permute-start(f32[64,64,128]{2,1,0:T(8,128)S(1)} %maximum_select_fusion.1), channel_id=1, source_target_pairs={{0,1},{1,0},{2,3},{3,2},{4,5},{5,4},{6,7},{7,6},{8,9},{9,8},{10,11... | collective-permute-start | bytes 6291464 | tf_op jit(solution)/shard_map/ppermute | solution.py:109
Sparse Core Ops, SparseCore 0:
  85.8 51.1 all-gather.3
  149.3 8.1 reduce-scatter.2
  162.5 10.1 all-gather.5
  238.5 51.1 all-gather.7
  301.9 8.1 reduce-scatter.4

commit v9 on v8

--- a/solution.py
+++ b/solution.py
@@ -91,14 +91,18 @@
             "jps,sbk->jbpk", blocks, geno_blocks, preferred_element_type=jnp.float32
         ).reshape(cells, half_p, block_width)
         local_gradient = jnp.take(full, cell, axis=0, mode="clip")
-        rows = local_gradient.reshape(entries * half_p, block_width)
-        mine = lax.psum_scatter(rows, "sc", scatter_dimension=0, tiled=True)
-        own_gradient = mine.reshape(share, half_p, block_width)
+        split = local_gradient.reshape(cores, share, half_p, block_width)
+        keep = lax.dynamic_index_in_dim(split, c, 0, keepdims=False)
+        give = lax.dynamic_index_in_dim(split, 1 - c, 0, keepdims=False)
+        own_gradient = keep + lax.ppermute(give, "sc", swap)
         own = shrink_soft(own, own_gradient, own_cutoff, own_active)
         if sweep + 1 < ITERS:
-            flat = own.astype(jnp.bfloat16).reshape(share * half_p, block_width)
-            weight_bf = lax.all_gather(flat, "sc", axis=0, tiled=True).reshape(
-                entries, half_p, block_width
+            own_bf = own.astype(jnp.bfloat16)
+            other_bf = lax.ppermute(own_bf, "sc", swap)
+            weight_bf = jnp.where(
+                c == 0,
+                jnp.concatenate([own_bf, other_bf], axis=0),
+                jnp.concatenate([other_bf, own_bf], axis=0),
             )
     other_half = lax.ppermute(own, "sx", swap)
     mine = jnp.where(

time: 359 us -> 326 us (0.908)
  waiting for transfers between devices: 205 us -> 186 us
  other arithmetic: 25.4 us -> 16.1 us
    reduce_scatter x2 -> x0, waiting for transfers between devices: 15.8 us -> none  [per_device(): mine = lax.psum_scatter(rows, 'sc', scatter_dimension=0, tiled=True)]
    all_gather x1 -> x0, waiting for transfers between devices: 10 us -> none  [per_device(): lax.all_gather(flat, 'sc', axis=0, tiled=True)]
    ppermute x0 -> x3, waiting for transfers between devices: none -> 7.16 us  [the longest x2 5.39 us: per_device(): own_gradient = keep + lax.ppermute(give, 'sc', swap)]
where the time goes in v9:
time: 326 us; the launch traced here: 325 us
  waiting for transfers between devices  186 us (57%)
  blocking collectives  57 us (17%)
  matrix products  18 us (6%)
  local copies, waits for them, and re-layouts  17.8 us (5%)
  other arithmetic  16.1 us (5%)
  starting transfers between devices  16 us (5%)
  between operations  14.3 us (4%)
    all_gather x2, waiting for transfers between devices, per_device(): shard_rows = lax.all_gather(residual, 'snp', axis=0, tiled=True)  101 us
    all_to_all x1, blocking collectives, predict(): gathered = lax.all_to_all(partial, 'snp', 0, 0, tiled=False)  57 us
    all_to_all x2, waiting for transfers between devices, predict(): gathered = lax.all_to_all(partial, 'snp', 0, 0, tiled=False)  38.2 us
    ppermute x1, waiting for transfers between devices, per_device(): other_half = lax.ppermute(own, 'sx', swap)  23.7 us
    ppermute x1, waiting for transfers between devices, per_device(): geno_peer = lax.ppermute(genotypes, 'sx', swap)  11.4 us
    all_to_all x2, starting transfers between devices, predict(): gathered = lax.all_to_all(partial, 'snp', 0, 0, tiled=False)  10.9 us
    dot_general x2, matrix products, per_device(): jnp.einsum('jps,sbk->jbpk', blocks, geno_blocks, preferred_element_type=j...  9.76 us
    dot_general x3, matrix products, predict(): jnp.einsum('jbpk,sbk->jps', dense, samples.reshape(count, block_count, bl...  6.82 us
  transfers between devices with their start and end apart: 11, of which 10 were waited for; matrix products, arithmetic and copies ran while one was open for 2% of the time, Pallas kernels for 0%

profile of v9, /device:TPU:0, one launch (start us, length us, event | category | flops | bytes accessed | tf_op | source)
XLA Modules:
  0.0 325.0 jit_solution(14168658846296310999)
XLA Ops:
  9.3 1.9 select_convert_fusion
  13.2 2.3 bitcast_convert_fusion.2
  15.5 7.3 %all-to-all-start = ((bf16[8,192,384]{2,1,0:T(8,128)(2,1)}), bf16[8,192,384]{2,1,0:T(8,128)(2,1)S(1)}, u32[]{:S(2)}, u32[]{:S(2)}) async-start(bf16[8,192,384]{2,1,0:T(8,128)(2,1)} %bitcast.111), calls=%async_computation | async-start | bytes 2359296 | tf_op jit(solution)/shard_map/all_to_all | solution.py:80
  22.8 1.5 collective-permute-start
  24.3 11.4 %collective-permute-done = bf16[384,640]{0,1:T(8,128)(2,1)S(1)} collective-permute-done((bf16[384,640]{0,1:T(8,128)(2,1)}, bf16[384,640]{0,1:T(8,128)(2,1)S(1)}, u32[]{:S(2)}, u32[]{:S(2)}) %collective-permute-start) | collective-permute-done | bytes 491552 | tf_op jit(solution)/shard_map/ppermute | solution.py:34
  36.5 2.3 bitcast_convert_fusion.1
  38.8 12.6 %all-to-all-done = bf16[8,192,384]{2,1,0:T(8,128)(2,1)S(1)} async-done(((bf16[8,192,384]{2,1,0:T(8,128)(2,1)}), bf16[8,192,384]{2,1,0:T(8,128)(2,1)S(1)}, u32[]{:S(2)}, u32[]{:S(2)}) %all-to-all-start) | async-done | bytes 1179680 | tf_op jit(solution)/shard_map/all_to_all | solution.py:80
  51.4 3.6 %all-to-all-start.1 = ((bf16[8,192,384]{2,1,0:T(8,128)(2,1)}), bf16[8,192,384]{2,1,0:T(8,128)(2,1)S(1)}, u32[]{:S(2)}, u32[]{:S(2)}) async-start(bf16[8,192,384]{2,1,0:T(8,128)(2,1)} %bitcast.110), calls=%async_computation.1 | async-start | bytes 2359296 | tf_op jit(solution)/shard_map/all_to_all | solution.py:80
  55.8 1.5 collective-permute-start.1
  57.3 0.9 convert_reduce_fusion.2
  58.2 25.6 %all-to-all-done.1 = bf16[8,192,384]{2,1,0:T(8,128)(2,1)S(1)} async-done(((bf16[8,192,384]{2,1,0:T(8,128)(2,1)}), bf16[8,192,384]{2,1,0:T(8,128)(2,1)S(1)}, u32[]{:S(2)}, u32[]{:S(2)}) %all-to-all-start.1) | async-done | bytes 1179680 | tf_op jit(solution)/shard_map/all_to_all | solution.py:80
  83.9 1.7 fusion.18
  86.0 1.1 pad_maximum_fusion
  87.1 49.9 %all-gather.3.cloned.1.call-done = bf16[1536,768]{1,0:T(8,128)(2,1)} async-done(((bf16[192,768]{1,0:T(8,128)(2,1)}), bf16[1536,768]{1,0:T(8,128)(2,1)}) %all-gather.3.cloned.1.call-update) | async-done | bytes 2359312 | tf_op jit(solution)/shard_map/all_gather | solution.py:88
  137.0 4.9 %fusion.6 = f32[48,5,32,128]{3,0,2,1:T(8,128)S(1)} fusion(bf16[768,5,128,1]{0,2,3,1:T(8,128)(2,1)S(1)} %bitcast.114, bf16[48,32,768]{2,1,0:T(8,128)(2,1)} %bitcast.119), kind=kOutput, calls=%fused_computation.17 | convolution fusion | flops 1509949440 | bytes 7274496 | tf_op jit(solution)/shard_map/jps,sbk->jbpk/dot_general | solution.py:90
  141.9 3.1 copy.41
  145.0 2.8 gather_fusion
  147.8 1.0 dynamic-slice_bitcast_fusion.1
  149.1 2.7 collective-permute-done.2
  151.9 4.1 %fusion.25 = (bf16[64,32,128]{2,1,0:T(8,128)(2,1)S(1)}, f32[64,32,128]{2,1,0:T(8,128)}) fusion(f32[64]{0:T(128)S(1)} %dynamic_slice.39, f32[64,32,128]{2,1,0:T(8,128)} %collective-permute-done.2, f32[2,64,32,128]{3,2,1,0:T(8,128)S(1)} %bitcast.102, s32[]{:T(128)S(6)} %select_n.84, f32[128,64,128]{2,1,0:T(8,128)} %param.9, s32[]{:T(128)S(6)} %select_n.76, ...), kind=kLoop, calls=%fused_computation.54 | loop fusion | flops 2883584 | bytes 4718924 | tf_op jit(solution)/shard_map/convert_element_type | solution.py:100
  156.1 1.8 collective-permute-done.3
  160.0 2.2 bitcast_convert_fusion
  162.2 57.0 %all_to_all.15 = bf16[8,192,768]{2,1,0:T(8,128)(2,1)S(1)} all-to-all(bf16[8,192,768]{2,1,0:T(8,128)(2,1)S(1)} %bitcast.105), channel_id=1, replica_groups=mesh['snp'=8,'sx'=2,'sc'=2] {'snp'}, dimensions={0} | all-to-all | bytes 4718592 | tf_op jit(solution)/shard_map/all_to_all | solution.py:80
  220.4 51.2 %all-gather.5.cloned.1.call-done = bf16[1536,768]{1,0:T(8,128)(2,1)} async-done(((bf16[192,768]{1,0:T(8,128)(2,1)}), bf16[1536,768]{1,0:T(8,128)(2,1)}) %all-gather.5.cloned.1.call-update) | async-done | bytes 2359312 | tf_op jit(solution)/shard_map/all_gather | solution.py:88
  271.6 4.9 %fusion.9 = f32[48,5,32,128]{3,0,2,1:T(8,128)S(1)} fusion(bf16[768,5,128,1]{0,2,3,1:T(8,128)(2,1)S(1)} %bitcast.116, bf16[48,32,768]{2,1,0:T(8,128)(2,1)} %bitcast.120), kind=kOutput, calls=%fused_computation.18 | convolution fusion | flops 1509949440 | bytes 7274496 | tf_op jit(solution)/shard_map/jps,sbk->jbpk/dot_general | solution.py:90
  276.5 3.1 copy.47
  279.6 2.8 gather_fusion.1
  282.6 2.6 collective-permute-done.4
  285.8 1.5 collective-permute-start.5
  287.3 23.7 %collective-permute-done.5 = f32[64,32,128]{2,1,0:T(8,128)S(1)} collective-permute-done((f32[64,32,128]{2,1,0:T(8,128)S(1)}, f32[64,32,128]{2,1,0:T(8,128)S(1)}, u32[]{:S(2)}, u32[]{:S(2)}) %collective-permute-start.5) | collective-permute-done | bytes 1048608 | tf_op jit(solution)/shard_map/ppermute | solution.py:107
  311.5 4.1 %collective-permute-done.6 = f32[64,64,128]{2,1,0:T(8,128)S(1)} collective-permute-done((f32[64,64,128]{2,1,0:T(8,128)S(1)}, f32[64,64,128]{2,1,0:T(8,128)S(1)}, u32[]{:S(2)}, u32[]{:S(2)}) %collective-permute-start.6) | collective-permute-done | bytes 2097184 | tf_op jit(solution)/shard_map/ppermute | solution.py:113
  315.7 2.5 maximum_select_fusion
  (49 shorter events, 10.9 us)
Async XLA Ops:
  11.9 1.0 copy-start.6
  13.2 2.3 copy-start.1
  15.5 35.9 %all-to-all-start = ((bf16[8,192,384]{2,1,0:T(8,128)(2,1)}), bf16[8,192,384]{2,1,0:T(8,128)(2,1)S(1)}, u32[]{:S(2)}, u32[]{:S(2)}) async-start(bf16[8,192,384]{2,1,0:T(8,128)(2,1)} %bitcast.111), calls=%async_computation | async-start | bytes 2359296 | tf_op jit(solution)/shard_map/all_to_all | solution.py:80
  22.8 12.9 %collective-permute-start = (bf16[384,640]{0,1:T(8,128)(2,1)}, bf16[384,640]{0,1:T(8,128)(2,1)S(1)}, u32[]{:S(2)}, u32[]{:S(2)}) collective-permute-start(bf16[384,640]{0,1:T(8,128)(2,1)} %copy-done.1), channel_id=1, source_target_pairs={{0,2},{2,0},{1,3},{3,1},{4,6},{6,4},{5,7},{7,5},{8,10},{10,8},{9,1... | collective-permute-start | bytes 1474568 | tf_op jit(solution)/shard_map/ppermute | solution.py:34
  35.7 0.8 copy-start.7
  38.8 16.3 %copy-start.5 = (f32[384,384]{1,0:T(8,128)S(1)}, f32[384,384]{1,0:T(8,128)}, u32[]{:S(2)}) copy-start(f32[384,384]{1,0:T(8,128)} %param.8) | copy-start | bytes 1769476
  51.4 32.4 %all-to-all-start.1 = ((bf16[8,192,384]{2,1,0:T(8,128)(2,1)}), bf16[8,192,384]{2,1,0:T(8,128)(2,1)S(1)}, u32[]{:S(2)}, u32[]{:S(2)}) async-start(bf16[8,192,384]{2,1,0:T(8,128)(2,1)} %bitcast.110), calls=%async_computation.1 | async-start | bytes 2359296 | tf_op jit(solution)/shard_map/all_to_all | solution.py:80
  55.0 82.0 %all-gather.3.cloned.1.call-start = ((), (), s32[]{:S(2)}) async-start(), calls=%async_computation.3 | async-start | bytes 2654208 | tf_op jit(solution)/shard_map/all_gather | solution.py:88
  55.8 30.1 %copy-start.2 = (bf16[384,640]{0,1:T(8,128)(2,1)S(1)}, bf16[384,640]{0,1:T(8,128)(2,1)}, u32[]{:S(2)}) copy-start(bf16[384,640]{0,1:T(8,128)(2,1)} %copy-done.1) | copy-start | bytes 1474564
  55.8 28.1 %collective-permute-start.1 = (f32[6,32,384]{2,1,0:T(8,128)}, f32[6,32,384]{2,1,0:T(8,128)S(1)}, u32[]{:S(2)}, u32[]{:S(2)}) collective-permute-start(f32[6,32,384]{2,1,0:T(8,128)} %get-tuple-element.8), channel_id=1, source_target_pairs={{0,2},{2,0},{1,3},{3,1},{4,6},{6,4},{5,7},{7,5},{8,10},{10,8},{9,1... | collective-permute-start | bytes 884744 | tf_op jit(solution)/shard_map/ppermute | solution.py:40
  85.7 185.9 %all-gather.5.cloned.1.call-start = ((), (), s32[]{:S(2)}) async-start(), calls=%async_computation.4 | async-start | bytes 2654208 | tf_op jit(solution)/shard_map/all_gather | solution.py:88
  87.1 54.8 %copy-start.3 = (bf16[768,640]{0,1:T(8,128)(2,1)}, bf16[768,640]{0,1:T(8,128)(2,1)S(1)}, u32[]{:S(2)}) copy-start(bf16[768,640]{0,1:T(8,128)(2,1)S(1)} %pad_maximum_fusion) | copy-start | bytes 2949124
  147.8 1.1 copy-start.8
  148.9 3.0 collective-permute-start.2
  156.0 1.9 collective-permute-start.3
  158.8 1.2 copy-start.4
  282.4 2.8 copy-start
  282.5 2.7 collective-permute-start.4
  285.8 25.3 %collective-permute-start.5 = (f32[64,32,128]{2,1,0:T(8,128)S(1)}, f32[64,32,128]{2,1,0:T(8,128)S(1)}, u32[]{:S(2)}, u32[]{:S(2)}) collective-permute-start(f32[64,32,128]{2,1,0:T(8,128)S(1)} %multiply_select_fusion), channel_id=1, source_target_pairs={{0,2},{2,0},{1,3},{3,1},{4,6},{6,4},{5,7},{7,5},{8,10},{10,8},{9,1... | collective-permute-start | bytes 3145736 | tf_op jit(solution)/shard_map/ppermute | solution.py:107
  311.5 4.2 %collective-permute-start.6 = (f32[64,64,128]{2,1,0:T(8,128)S(1)}, f32[64,64,128]{2,1,0:T(8,128)S(1)}, u32[]{:S(2)}, u32[]{:S(2)}) collective-permute-start(f32[64,64,128]{2,1,0:T(8,128)S(1)} %maximum_select_fusion.1), channel_id=1, source_target_pairs={{0,1},{1,0},{2,3},{3,2},{4,5},{5,4},{6,7},{7,6},{8,9},{9,8},{10,11... | collective-permute-start | bytes 6291464 | tf_op jit(solution)/shard_map/ppermute | solution.py:113
Sparse Core Ops, SparseCore 0:
  85.8 51.1 all-gather.2
  220.5 51.0 all-gather.4

commit v10 on v9

--- a/solution.py
+++ b/solution.py
@@ -50,6 +50,17 @@
     cutoff = step_scale * per_entry[:, None, None]
     cell = slot_ids * block_count + blk
     cell_hot = (cell[:, None] == jnp.arange(cells, dtype=jnp.int32)[None, :]).astype(jnp.bfloat16)
+    ring = list(range(0, owners, 2)) + list(range(owners - 1, 0, -2))
+    ring_pos = [0] * owners
+    for k, dev in enumerate(ring):
+        ring_pos[dev] = k
+    forward = [(ring[k], ring[(k + 1) % owners]) for k in range(owners)]
+    backward = [(ring[k], ring[(k - 1) % owners]) for k in range(owners)]
+    forward_steps = owners // 2
+    ring_table = jnp.asarray(ring_pos, dtype=jnp.int32)
+    here = ring_table[lax.axis_index("snp")]
+    rel_owner = (ring_table[slot_ids // own_slots] - here) % owners
+    ring_cell = (rel_owner * own_slots + slot_ids % own_slots) * block_count + blk
     active = jnp.arange(entries, dtype=jnp.int32) < entry_count[0]
     w_half = lax.dynamic_slice_in_dim(weights, x * half_p, half_p, 1)
     weight_bf = jnp.where(active[:, None, None], w_half, jnp.float32(0.0)).astype(jnp.bfloat16)
@@ -85,12 +96,21 @@
         else:
             prediction = predict(geno)
         residual = (resp - prediction).astype(jnp.bfloat16)
-        shard_rows = lax.all_gather(residual, "snp", axis=0, tiled=True)
+        received = {0: residual}
+        moving = residual
+        for step in range(1, forward_steps + 1):
+            moving = lax.ppermute(moving, "snp", forward)
+            received[owners - step] = moving
+        moving = residual
+        for step in range(1, owners - forward_steps):
+            moving = lax.ppermute(moving, "snp", backward)
+            received[step] = moving
+        shard_rows = jnp.stack([received[d] for d in range(owners)])
         blocks = shard_rows.reshape(slot_total, half_p, sample_count)
         full = jnp.einsum(
             "jps,sbk->jbpk", blocks, geno_blocks, preferred_element_type=jnp.float32
         ).reshape(cells, half_p, block_width)
-        local_gradient = jnp.take(full, cell, axis=0, mode="clip")
+        local_gradient = jnp.take(full, ring_cell, axis=0, mode="clip")
         split = local_gradient.reshape(cores, share, half_p, block_width)
         keep = lax.dynamic_index_in_dim(split, c, 0, keepdims=False)
         give = lax.dynamic_index_in_dim(split, 1 - c, 0, keepdims=False)

time: 326 us -> 269 us (0.83)
  waiting for transfers between devices: 186 us -> 128 us
  starting transfers between devices: 16 us -> 31.3 us
  between operations: 14.3 us -> 1.03 us
  matrix products: 18 us -> 14.7 us
    all_gather x2 -> x0, waiting for transfers between devices: 101 us -> none  [per_device(): shard_rows = lax.all_gather(residual, 'snp', axis=0, tiled=True)]
    ppermute x0 -> x14, waiting for transfers between devices: none -> 42.6 us  [the longest x8 42.1 us: per_device(): moving = lax.ppermute(moving, 'snp', forward)]
    ppermute x0 -> x14, starting transfers between devices: none -> 14.5 us  [the longest x6 8.53 us: per_device(): moving = lax.ppermute(moving, 'snp', backward)]
    dot_general x2, matrix products: 9.76 us -> 6.48 us  [per_device(): jnp.einsum('jps,sbk->jbpk', blocks, geno_blocks, preferred_element_type=j...]
  transfers between devices with their start and end apart: 11 -> 23, of which waited for: 10 -> 18; matrix products, arithmetic and copies ran while one was open for 2% -> 2% of each run, Pallas kernels for 0% -> 0%
where the time goes in v10:
time: 269 us; the launch traced here: 268 us
  waiting for transfers between devices  128 us (48%)
  blocking collectives  59.7 us (22%)
  starting transfers between devices  31.3 us (12%)
  local copies, waits for them, and re-layouts  18.7 us (7%)
  other arithmetic  15.1 us (6%)
  matrix products  14.7 us (5%)
    all_to_all x1, blocking collectives, predict(): gathered = lax.all_to_all(partial, 'snp', 0, 0, tiled=False)  59.7 us
    ppermute x8, waiting for transfers between devices, per_device(): moving = lax.ppermute(moving, 'snp', forward)  42.1 us
    all_to_all x2, waiting for transfers between devices, predict(): gathered = lax.all_to_all(partial, 'snp', 0, 0, tiled=False)  39.1 us
    ppermute x1, waiting for transfers between devices, per_device(): other_half = lax.ppermute(own, 'sx', swap)  23.5 us
    all_to_all x2, starting transfers between devices, predict(): gathered = lax.all_to_all(partial, 'snp', 0, 0, tiled=False)  11.5 us
    ppermute x1, waiting for transfers between devices, per_device(): geno_peer = lax.ppermute(genotypes, 'sx', swap)  11.4 us
    ppermute x6, starting transfers between devices, per_device(): moving = lax.ppermute(moving, 'snp', backward)  8.53 us
    dot_general x3, matrix products, predict(): jnp.einsum('jbpk,sbk->jps', dense, samples.reshape(count, block_count, bl...  6.83 us
  transfers between devices with their start and end apart: 23, of which 18 were waited for; matrix products, arithmetic and copies ran while one was open for 2% of the time, Pallas kernels for 0%

profile of v10, /device:TPU:0, one launch (start us, length us, event | category | flops | bytes accessed | tf_op | source)
XLA Modules:
  0.0 268.5 jit_solution(10093578097872487232)
XLA Ops:
  8.6 2.3 bitcast_convert_fusion.2
  10.9 7.3 %all-to-all-start = ((bf16[8,192,384]{2,1,0:T(8,128)(2,1)}), bf16[8,192,384]{2,1,0:T(8,128)(2,1)S(1)}, u32[]{:S(2)}, u32[]{:S(2)}) async-start(bf16[8,192,384]{2,1,0:T(8,128)(2,1)} %bitcast.207), calls=%async_computation | async-start | bytes 2359296 | tf_op jit(solution)/shard_map/all_to_all | solution.py:91
  19.7 11.4 %collective-permute-done = bf16[384,640]{0,1:T(8,128)(2,1)S(1)} collective-permute-done((bf16[384,640]{0,1:T(8,128)(2,1)}, bf16[384,640]{0,1:T(8,128)(2,1)S(1)}, u32[]{:S(2)}, u32[]{:S(2)}) %collective-permute-start) | collective-permute-done | bytes 491552 | tf_op jit(solution)/shard_map/ppermute | solution.py:34
  31.9 2.3 bitcast_convert_fusion.1
  34.2 12.6 %all-to-all-done = bf16[8,192,384]{2,1,0:T(8,128)(2,1)S(1)} async-done(((bf16[8,192,384]{2,1,0:T(8,128)(2,1)}), bf16[8,192,384]{2,1,0:T(8,128)(2,1)S(1)}, u32[]{:S(2)}, u32[]{:S(2)}) %all-to-all-start) | async-done | bytes 1179680 | tf_op jit(solution)/shard_map/all_to_all | solution.py:91
  46.8 4.3 %all-to-all-start.1 = ((bf16[8,192,384]{2,1,0:T(8,128)(2,1)}), bf16[8,192,384]{2,1,0:T(8,128)(2,1)}, u32[]{:S(2)}, u32[]{:S(2)}) async-start(bf16[8,192,384]{2,1,0:T(8,128)(2,1)} %bitcast.206), calls=%async_computation.1 | async-start | bytes 2359296 | tf_op jit(solution)/shard_map/all_to_all | solution.py:91
  52.8 26.5 %all-to-all-done.1 = bf16[8,192,384]{2,1,0:T(8,128)(2,1)} async-done(((bf16[8,192,384]{2,1,0:T(8,128)(2,1)}), bf16[8,192,384]{2,1,0:T(8,128)(2,1)}, u32[]{:S(2)}, u32[]{:S(2)}) %all-to-all-start.1) | async-done | bytes 1179680 | tf_op jit(solution)/shard_map/all_to_all | solution.py:91
  81.0 2.0 collective-permute-start.2
  83.0 5.5 %collective-permute-done.5 = bf16[192,768]{1,0:T(8,128)(2,1)S(1)} collective-permute-done((bf16[192,768]{1,0:T(8,128)(2,1)S(1)}, bf16[192,768]{1,0:T(8,128)(2,1)S(1)}, u32[]{:S(2)}, u32[]{:S(2)}) %collective-permute-start.5) | collective-permute-done | bytes 294944 | tf_op jit(solution)/shard_map/ppermute | solution.py:102
  88.5 2.0 collective-permute-start.3
  91.7 4.0 %collective-permute-done.6 = bf16[192,768]{1,0:T(8,128)(2,1)S(1)} collective-permute-done((bf16[192,768]{1,0:T(8,128)(2,1)S(1)}, bf16[192,768]{1,0:T(8,128)(2,1)S(1)}, u32[]{:S(2)}, u32[]{:S(2)}) %collective-permute-start.6) | collective-permute-done | bytes 294944 | tf_op jit(solution)/shard_map/ppermute | solution.py:102
  97.9 4.6 %collective-permute-done.7 = bf16[192,768]{1,0:T(8,128)(2,1)S(1)} collective-permute-done((bf16[192,768]{1,0:T(8,128)(2,1)S(1)}, bf16[192,768]{1,0:T(8,128)(2,1)S(1)}, u32[]{:S(2)}, u32[]{:S(2)}) %collective-permute-start.7) | collective-permute-done | bytes 294944 | tf_op jit(solution)/shard_map/ppermute | solution.py:102
  103.2 6.4 %collective-permute-done.8 = bf16[192,768]{1,0:T(8,128)(2,1)S(1)} collective-permute-done((bf16[192,768]{1,0:T(8,128)(2,1)S(1)}, bf16[192,768]{1,0:T(8,128)(2,1)S(1)}, u32[]{:S(2)}, u32[]{:S(2)}) %collective-permute-start.8) | collective-permute-done | bytes 294944 | tf_op jit(solution)/shard_map/ppermute | solution.py:102
  109.7 3.2 %fusion.6 = f32[48,5,32,128]{3,0,2,1:T(8,128)S(1)} fusion(bf16[768,5,128,1]{0,2,3,1:T(8,128)(2,1)S(1)} %bitcast.208, bf16[48,32,768]{2,1,0:T(8,128)(2,1)S(1)} %bitcast.214), kind=kOutput, calls=%fused_computation.17 | convolution fusion | flops 1509949440 | bytes 7274496 | tf_op jit(solution)/shard_map/jps,sbk->jbpk/dot_general | solution.py:110
  113.0 3.1 %copy.42 = f32[48,5,32,128]{3,2,1,0:T(8,128)} copy(f32[48,5,32,128]{3,0,2,1:T(8,128)S(1)} %fusion.6) | data formatting | bytes 7864320 | tf_op jit(solution)/shard_map/jps,sbk->jbpk/transpose | solution.py:110
  116.1 2.8 %gather_fusion = f32[128,32,128]{2,1,0:T(8,128)S(1)} fusion(f32[240,32,128]{2,1,0:T(8,128)} %bitcast.186, s32[1024]{0:T(1024)S(1)} %pad_clamp_fusion), kind=kCustom, calls=%fused_computation | custom fusion | bytes 4194816 | tf_op jit(solution)/shard_map/jit(_take)/gather | solution.py:113
  120.2 2.7 %collective-permute-done.9 = f32[64,32,128]{2,1,0:T(8,128)} collective-permute-done((f32[64,32,128]{2,1,0:T(8,128)}, f32[64,32,128]{2,1,0:T(8,128)}, u32[]{:S(2)}, u32[]{:S(2)}) %collective-permute-start.9) | collective-permute-done | bytes 1048608 | tf_op jit(solution)/shard_map/ppermute | solution.py:117
  123.0 4.1 %fusion.36 = (bf16[64,32,128]{2,1,0:T(8,128)(2,1)S(1)}, f32[64,32,128]{2,1,0:T(8,128)}) fusion(f32[64]{0:T(128)S(1)} %dynamic_slice.43, f32[64,32,128]{2,1,0:T(8,128)} %collective-permute-done.9, f32[2,64,32,128]{3,2,1,0:T(8,128)S(1)} %bitcast.190, s32[]{:T(128)S(6)} %select_n.139, f32[128,64,128]{2,1,0:T(8,128)} %param.10, s32[]{:T(128)S(6)} %select_n.126, ...), kind=kLoop, calls=%fused_computation.96 | loop fusion | flops 2883584 | bytes 4718924 | tf_op jit(solution)/shard_map/convert_element_type | solution.py:120
  131.1 2.2 bitcast_convert_fusion
  133.3 59.7 %all_to_all.15 = bf16[8,192,768]{2,1,0:T(8,128)(2,1)S(1)} all-to-all(bf16[8,192,768]{2,1,0:T(8,128)(2,1)S(1)} %bitcast.201), channel_id=1, replica_groups=mesh['snp'=8,'sx'=2,'sc'=2] {'snp'}, dimensions={0} | all-to-all | bytes 4718592 | tf_op jit(solution)/shard_map/all_to_all | solution.py:91
  195.5 5.6 %collective-permute-done.14 = bf16[192,768]{1,0:T(8,128)(2,1)S(1)} collective-permute-done((bf16[192,768]{1,0:T(8,128)(2,1)S(1)}, bf16[192,768]{1,0:T(8,128)(2,1)S(1)}, u32[]{:S(2)}, u32[]{:S(2)}) %collective-permute-start.14) | collective-permute-done | bytes 294944 | tf_op jit(solution)/shard_map/ppermute | solution.py:102
  203.1 5.2 %collective-permute-done.15 = bf16[192,768]{1,0:T(8,128)(2,1)S(1)} collective-permute-done((bf16[192,768]{1,0:T(8,128)(2,1)S(1)}, bf16[192,768]{1,0:T(8,128)(2,1)S(1)}, u32[]{:S(2)}, u32[]{:S(2)}) %collective-permute-start.15) | collective-permute-done | bytes 294944 | tf_op jit(solution)/shard_map/ppermute | solution.py:102
  210.5 6.1 %collective-permute-done.16 = bf16[192,768]{1,0:T(8,128)(2,1)S(1)} collective-permute-done((bf16[192,768]{1,0:T(8,128)(2,1)S(1)}, bf16[192,768]{1,0:T(8,128)(2,1)S(1)}, u32[]{:S(2)}, u32[]{:S(2)}) %collective-permute-start.16) | collective-permute-done | bytes 294944 | tf_op jit(solution)/shard_map/ppermute | solution.py:102
  218.5 4.8 %collective-permute-done.17 = bf16[192,768]{1,0:T(8,128)(2,1)S(1)} collective-permute-done((bf16[192,768]{1,0:T(8,128)(2,1)S(1)}, bf16[192,768]{1,0:T(8,128)(2,1)S(1)}, u32[]{:S(2)}, u32[]{:S(2)}) %collective-permute-start.17) | collective-permute-done | bytes 294944 | tf_op jit(solution)/shard_map/ppermute | solution.py:102
  223.4 3.2 %fusion.9 = f32[48,5,32,128]{3,0,2,1:T(8,128)S(1)} fusion(bf16[768,5,128,1]{0,2,3,1:T(8,128)(2,1)S(1)} %bitcast.210, bf16[48,32,768]{2,1,0:T(8,128)(2,1)S(1)} %bitcast.213), kind=kOutput, calls=%fused_computation.18 | convolution fusion | flops 1509949440 | bytes 7274496 | tf_op jit(solution)/shard_map/jps,sbk->jbpk/dot_general | solution.py:110
  226.6 3.1 %copy.48 = f32[48,5,32,128]{3,2,1,0:T(8,128)} copy(f32[48,5,32,128]{3,0,2,1:T(8,128)S(1)} %fusion.9) | data formatting | bytes 7864320 | tf_op jit(solution)/shard_map/jps,sbk->jbpk/transpose | solution.py:110
  229.8 2.8 %gather_fusion.1 = f32[128,32,128]{2,1,0:T(8,128)S(1)} fusion(f32[240,32,128]{2,1,0:T(8,128)} %bitcast.185, s32[1024]{0:T(1024)S(1)} %pad_clamp_fusion), kind=kCustom, calls=%fused_computation.1 | custom fusion | bytes 4194816 | tf_op jit(solution)/shard_map/jit(_take)/gather | solution.py:113
  232.7 2.6 collective-permute-done.18
  236.0 2.0 collective-permute-start.19
  237.9 23.5 %collective-permute-done.19 = f32[64,32,128]{2,1,0:T(8,128)S(1)} collective-permute-done((f32[64,32,128]{2,1,0:T(8,128)S(1)}, f32[64,32,128]{2,1,0:T(8,128)S(1)}, u32[]{:S(2)}, u32[]{:S(2)}) %collective-permute-start.19) | collective-permute-done | bytes 1048608 | tf_op jit(solution)/shard_map/ppermute | solution.py:127
  261.9 4.1 %collective-permute-done.20 = f32[64,64,128]{2,1,0:T(8,128)S(1)} collective-permute-done((f32[64,64,128]{2,1,0:T(8,128)S(1)}, f32[64,64,128]{2,1,0:T(8,128)S(1)}, u32[]{:S(2)}, u32[]{:S(2)}) %collective-permute-start.20) | collective-permute-done | bytes 2097184 | tf_op jit(solution)/shard_map/ppermute | solution.py:133
  266.0 2.5 maximum_select_fusion
  (88 shorter events, 32.8 us)
Async XLA Ops:
  7.3 1.0 copy-start.6
  8.6 2.3 copy-start.1
  10.9 35.9 %all-to-all-start = ((bf16[8,192,384]{2,1,0:T(8,128)(2,1)}), bf16[8,192,384]{2,1,0:T(8,128)(2,1)S(1)}, u32[]{:S(2)}, u32[]{:S(2)}) async-start(bf16[8,192,384]{2,1,0:T(8,128)(2,1)} %bitcast.207), calls=%async_computation | async-start | bytes 2359296 | tf_op jit(solution)/shard_map/all_to_all | solution.py:91
  18.2 12.9 %collective-permute-start = (bf16[384,640]{0,1:T(8,128)(2,1)}, bf16[384,640]{0,1:T(8,128)(2,1)S(1)}, u32[]{:S(2)}, u32[]{:S(2)}) collective-permute-start(bf16[384,640]{0,1:T(8,128)(2,1)} %copy-done.1), channel_id=1, source_target_pairs={{0,2},{2,0},{1,3},{3,1},{4,6},{6,4},{5,7},{7,5},{8,10},{10,8},{9,1... | collective-permute-start | bytes 1474568 | tf_op jit(solution)/shard_map/ppermute | solution.py:34
  31.1 0.8 copy-start.7
  34.2 16.9 %copy-start.5 = (f32[384,384]{1,0:T(8,128)S(1)}, f32[384,384]{1,0:T(8,128)}, u32[]{:S(2)}) copy-start(f32[384,384]{1,0:T(8,128)} %param.9) | copy-start | bytes 1769476
  46.8 32.6 %all-to-all-start.1 = ((bf16[8,192,384]{2,1,0:T(8,128)(2,1)}), bf16[8,192,384]{2,1,0:T(8,128)(2,1)}, u32[]{:S(2)}, u32[]{:S(2)}) async-start(bf16[8,192,384]{2,1,0:T(8,128)(2,1)} %bitcast.206), calls=%async_computation.1 | async-start | bytes 2359296 | tf_op jit(solution)/shard_map/all_to_all | solution.py:91
  51.1 39.4 %copy-start.2 = (bf16[384,640]{0,1:T(8,128)(2,1)S(1)}, bf16[384,640]{0,1:T(8,128)(2,1)}, u32[]{:S(2)}) copy-start(bf16[384,640]{0,1:T(8,128)(2,1)} %copy-done.1) | copy-start | bytes 1474564
  51.1 29.7 %collective-permute-start.1 = (f32[6,32,384]{2,1,0:T(8,128)S(1)}, f32[6,32,384]{2,1,0:T(8,128)S(1)}, u32[]{:S(2)}, u32[]{:S(2)}) collective-permute-start(f32[6,32,384]{2,1,0:T(8,128)S(1)} %get-tuple-element.8), channel_id=1, source_target_pairs={{0,2},{2,0},{1,3},{3,1},{4,6},{6,4},{5,7},{7,5},{8,10},{10,8},{9,1... | collective-permute-start | bytes 884744 | tf_op jit(solution)/shard_map/ppermute | solution.py:40
  80.9 7.6 %collective-permute-start.5 = (bf16[192,768]{1,0:T(8,128)(2,1)S(1)}, bf16[192,768]{1,0:T(8,128)(2,1)S(1)}, u32[]{:S(2)}, u32[]{:S(2)}) collective-permute-start(bf16[192,768]{1,0:T(8,128)(2,1)S(1)} %fusion.19), channel_id=1, source_target_pairs={{0,8},{8,16},{16,24},{24,28},{28,20},{20,12},{12,4},{4,0},{1,9},{9... | collective-permute-start | bytes 884744 | tf_op jit(solution)/shard_map/ppermute | solution.py:102
  81.0 7.5 %collective-permute-start.2 = (bf16[192,768]{1,0:T(8,128)(2,1)S(1)}, bf16[192,768]{1,0:T(8,128)(2,1)S(1)}, u32[]{:S(2)}, u32[]{:S(2)}) collective-permute-start(bf16[192,768]{1,0:T(8,128)(2,1)S(1)} %fusion.19), channel_id=1, source_target_pairs={{0,4},{8,0},{16,8},{24,16},{28,24},{20,28},{12,20},{4,12},{1,5},{9... | collective-permute-start | bytes 884744 | tf_op jit(solution)/shard_map/ppermute | solution.py:106
  88.5 7.2 %collective-permute-start.6 = (bf16[192,768]{1,0:T(8,128)(2,1)S(1)}, bf16[192,768]{1,0:T(8,128)(2,1)S(1)}, u32[]{:S(2)}, u32[]{:S(2)}) collective-permute-start(bf16[192,768]{1,0:T(8,128)(2,1)S(1)} %collective-permute-done.5), channel_id=1, source_target_pairs={{0,8},{8,16},{16,24},{24,28},{28,20},{20,12},{12,4},{4,0},{1,9},{9... | collective-permute-start | bytes 884744 | tf_op jit(solution)/shard_map/ppermute | solution.py:102
  88.5 7.6 %collective-permute-start.3 = (bf16[192,768]{1,0:T(8,128)(2,1)S(1)}, bf16[192,768]{1,0:T(8,128)(2,1)S(1)}, u32[]{:S(2)}, u32[]{:S(2)}) collective-permute-start(bf16[192,768]{1,0:T(8,128)(2,1)S(1)} %collective-permute-done.2), channel_id=1, source_target_pairs={{0,4},{8,0},{16,8},{24,16},{28,24},{20,28},{12,20},{4,12},{1,5},{9... | collective-permute-start | bytes 884744 | tf_op jit(solution)/shard_map/ppermute | solution.py:106
  91.7 18.1 %copy-start.3 = (bf16[768,640]{0,1:T(8,128)(2,1)}, bf16[768,640]{0,1:T(8,128)(2,1)S(1)}, u32[]{:S(2)}) copy-start(bf16[768,640]{0,1:T(8,128)(2,1)S(1)} %pad_maximum_fusion) | copy-start | bytes 2949124
  95.7 6.7 %collective-permute-start.7 = (bf16[192,768]{1,0:T(8,128)(2,1)S(1)}, bf16[192,768]{1,0:T(8,128)(2,1)S(1)}, u32[]{:S(2)}, u32[]{:S(2)}) collective-permute-start(bf16[192,768]{1,0:T(8,128)(2,1)S(1)} %collective-permute-done.6), channel_id=1, source_target_pairs={{0,8},{8,16},{16,24},{24,28},{28,20},{20,12},{12,4},{4,0},{1,9},{9... | collective-permute-start | bytes 884744 | tf_op jit(solution)/shard_map/ppermute | solution.py:102
  96.1 7.0 %collective-permute-start.4 = (bf16[192,768]{1,0:T(8,128)(2,1)S(1)}, bf16[192,768]{1,0:T(8,128)(2,1)S(1)}, u32[]{:S(2)}, u32[]{:S(2)}) collective-permute-start(bf16[192,768]{1,0:T(8,128)(2,1)S(1)} %collective-permute-done.3), channel_id=1, source_target_pairs={{0,4},{8,0},{16,8},{24,16},{28,24},{20,28},{12,20},{4,12},{1,5},{9... | collective-permute-start | bytes 884744 | tf_op jit(solution)/shard_map/ppermute | solution.py:106
  102.4 7.2 %collective-permute-start.8 = (bf16[192,768]{1,0:T(8,128)(2,1)S(1)}, bf16[192,768]{1,0:T(8,128)(2,1)S(1)}, u32[]{:S(2)}, u32[]{:S(2)}) collective-permute-start(bf16[192,768]{1,0:T(8,128)(2,1)S(1)} %collective-permute-done.7), channel_id=1, source_target_pairs={{0,8},{8,16},{16,24},{24,28},{28,20},{20,12},{12,4},{4,0},{1,9},{9... | collective-permute-start | bytes 884744 | tf_op jit(solution)/shard_map/ppermute | solution.py:102
  116.1 3.9 %copy-start.8 = (f32[46]{0:T(128)S(1)}, f32[46]{0:T(128)}, u32[]{:S(2)}) copy-start(f32[46]{0:T(128)} %param.14) | copy-start | bytes 556
  120.0 3.0 %collective-permute-start.9 = (f32[64,32,128]{2,1,0:T(8,128)}, f32[64,32,128]{2,1,0:T(8,128)}, u32[]{:S(2)}, u32[]{:S(2)}) collective-permute-start(f32[64,32,128]{2,1,0:T(8,128)} %dynamic-slice_bitcast_fusion.1), channel_id=1, source_target_pairs={{0,1},{1,0},{2,3},{3,2},{4,5},{5,4},{6,7},{7,6},{8,9},{9,8},{10,11... | collective-permute-start | bytes 3145736 | tf_op jit(solution)/shard_map/ppermute | solution.py:117
  127.1 1.9 collective-permute-start.10
  129.9 1.2 copy-start.4
  193.4 7.7 %collective-permute-start.14 = (bf16[192,768]{1,0:T(8,128)(2,1)S(1)}, bf16[192,768]{1,0:T(8,128)(2,1)S(1)}, u32[]{:S(2)}, u32[]{:S(2)}) collective-permute-start(bf16[192,768]{1,0:T(8,128)(2,1)S(1)} %subtract_convert_fusion), channel_id=1, source_target_pairs={{0,8},{8,16},{16,24},{24,28},{28,20},{20,12},{12,4},{4,0},{1,9},{9... | collective-permute-start | bytes 884744 | tf_op jit(solution)/shard_map/ppermute | solution.py:102
  194.6 7.4 %collective-permute-start.11 = (bf16[192,768]{1,0:T(8,128)(2,1)S(1)}, bf16[192,768]{1,0:T(8,128)(2,1)S(1)}, u32[]{:S(2)}, u32[]{:S(2)}) collective-permute-start(bf16[192,768]{1,0:T(8,128)(2,1)S(1)} %subtract_convert_fusion), channel_id=1, source_target_pairs={{0,4},{8,0},{16,8},{24,16},{28,24},{20,28},{12,20},{4,12},{1,5},{9... | collective-permute-start | bytes 884744 | tf_op jit(solution)/shard_map/ppermute | solution.py:106
  201.1 7.2 %collective-permute-start.15 = (bf16[192,768]{1,0:T(8,128)(2,1)S(1)}, bf16[192,768]{1,0:T(8,128)(2,1)S(1)}, u32[]{:S(2)}, u32[]{:S(2)}) collective-permute-start(bf16[192,768]{1,0:T(8,128)(2,1)S(1)} %collective-permute-done.14), channel_id=1, source_target_pairs={{0,8},{8,16},{16,24},{24,28},{28,20},{20,12},{12,4},{4,0},{1,9},{9... | collective-permute-start | bytes 884744 | tf_op jit(solution)/shard_map/ppermute | solution.py:102
  202.0 7.8 %collective-permute-start.12 = (bf16[192,768]{1,0:T(8,128)(2,1)S(1)}, bf16[192,768]{1,0:T(8,128)(2,1)S(1)}, u32[]{:S(2)}, u32[]{:S(2)}) collective-permute-start(bf16[192,768]{1,0:T(8,128)(2,1)S(1)} %collective-permute-done.11), channel_id=1, source_target_pairs={{0,4},{8,0},{16,8},{24,16},{28,24},{20,28},{12,20},{4,12},{1,5},{9... | collective-permute-start | bytes 884744 | tf_op jit(solution)/shard_map/ppermute | solution.py:106
  208.3 8.3 %collective-permute-start.16 = (bf16[192,768]{1,0:T(8,128)(2,1)S(1)}, bf16[192,768]{1,0:T(8,128)(2,1)S(1)}, u32[]{:S(2)}, u32[]{:S(2)}) collective-permute-start(bf16[192,768]{1,0:T(8,128)(2,1)S(1)} %collective-permute-done.15), channel_id=1, source_target_pairs={{0,8},{8,16},{16,24},{24,28},{28,20},{20,12},{12,4},{4,0},{1,9},{9... | collective-permute-start | bytes 884744 | tf_op jit(solution)/shard_map/ppermute | solution.py:102
  209.7 8.7 %collective-permute-start.13 = (bf16[192,768]{1,0:T(8,128)(2,1)S(1)}, bf16[192,768]{1,0:T(8,128)(2,1)S(1)}, u32[]{:S(2)}, u32[]{:S(2)}) collective-permute-start(bf16[192,768]{1,0:T(8,128)(2,1)S(1)} %collective-permute-done.12), channel_id=1, source_target_pairs={{0,4},{8,0},{16,8},{24,16},{28,24},{20,28},{12,20},{4,12},{1,5},{9... | collective-permute-start | bytes 884744 | tf_op jit(solution)/shard_map/ppermute | solution.py:106
  216.6 6.7 %collective-permute-start.17 = (bf16[192,768]{1,0:T(8,128)(2,1)S(1)}, bf16[192,768]{1,0:T(8,128)(2,1)S(1)}, u32[]{:S(2)}, u32[]{:S(2)}) collective-permute-start(bf16[192,768]{1,0:T(8,128)(2,1)S(1)} %collective-permute-done.16), channel_id=1, source_target_pairs={{0,8},{8,16},{16,24},{24,28},{28,20},{20,12},{12,4},{4,0},{1,9},{9... | collective-permute-start | bytes 884744 | tf_op jit(solution)/shard_map/ppermute | solution.py:102
  232.6 2.8 %copy-start = (f32[64,32,128]{2,1,0:T(8,128)S(1)}, f32[64,32,128]{2,1,0:T(8,128)}, u32[]{:S(2)}) copy-start(f32[64,32,128]{2,1,0:T(8,128)} %get-tuple-element.6) | copy-start | bytes 3145732
  232.7 2.7 %collective-permute-start.18 = (f32[64,32,128]{2,1,0:T(8,128)S(1)}, f32[64,32,128]{2,1,0:T(8,128)S(1)}, u32[]{:S(2)}, u32[]{:S(2)}) collective-permute-start(f32[64,32,128]{2,1,0:T(8,128)S(1)} %dynamic-slice_bitcast_fusion), channel_id=1, source_target_pairs={{0,1},{1,0},{2,3},{3,2},{4,5},{5,4},{6,7},{7,6},{8,9},{9,8},{10,11... | collective-permute-start | bytes 3145736 | tf_op jit(solution)/shard_map/ppermute | solution.py:117
  236.0 25.4 %collective-permute-start.19 = (f32[64,32,128]{2,1,0:T(8,128)S(1)}, f32[64,32,128]{2,1,0:T(8,128)S(1)}, u32[]{:S(2)}, u32[]{:S(2)}) collective-permute-start(f32[64,32,128]{2,1,0:T(8,128)S(1)} %multiply_select_fusion), channel_id=1, source_target_pairs={{0,2},{2,0},{1,3},{3,1},{4,6},{6,4},{5,7},{7,5},{8,10},{10,8},{9,1... | collective-permute-start | bytes 3145736 | tf_op jit(solution)/shard_map/ppermute | solution.py:127
  261.8 4.2 %collective-permute-start.20 = (f32[64,64,128]{2,1,0:T(8,128)S(1)}, f32[64,64,128]{2,1,0:T(8,128)S(1)}, u32[]{:S(2)}, u32[]{:S(2)}) collective-permute-start(f32[64,64,128]{2,1,0:T(8,128)S(1)} %maximum_select_fusion.1), channel_id=1, source_target_pairs={{0,1},{1,0},{2,3},{3,2},{4,5},{5,4},{6,7},{7,6},{8,9},{9,8},{10,11... | collective-permute-start | bytes 6291464 | tf_op jit(solution)/shard_map/ppermute | solution.py:133

commit v11 on v10

--- a/solution.py
+++ b/solution.py
@@ -60,7 +60,7 @@
     ring_table = jnp.asarray(ring_pos, dtype=jnp.int32)
     here = ring_table[lax.axis_index("snp")]
     rel_owner = (ring_table[slot_ids // own_slots] - here) % owners
-    ring_cell = (rel_owner * own_slots + slot_ids % own_slots) * block_count + blk
+    ring_slot = rel_owner * own_slots + slot_ids % own_slots
     active = jnp.arange(entries, dtype=jnp.int32) < entry_count[0]
     w_half = lax.dynamic_slice_in_dim(weights, x * half_p, half_p, 1)
     weight_bf = jnp.where(active[:, None, None], w_half, jnp.float32(0.0)).astype(jnp.bfloat16)
@@ -108,9 +108,9 @@
         shard_rows = jnp.stack([received[d] for d in range(owners)])
         blocks = shard_rows.reshape(slot_total, half_p, sample_count)
         full = jnp.einsum(
-            "jps,sbk->jbpk", blocks, geno_blocks, preferred_element_type=jnp.float32
-        ).reshape(cells, half_p, block_width)
-        local_gradient = jnp.take(full, ring_cell, axis=0, mode="clip")
+            "jps,sbk->jpbk", blocks, geno_blocks, preferred_element_type=jnp.float32
+        )
+        local_gradient = full[ring_slot, :, blk, :]
         split = local_gradient.reshape(cores, share, half_p, block_width)
         keep = lax.dynamic_index_in_dim(split, c, 0, keepdims=False)
         give = lax.dynamic_index_in_dim(split, 1 - c, 0, keepdims=False)

time: 269 us -> 265 us (0.985)
  local copies, waits for them, and re-layouts: 18.7 us -> 14.7 us
    transpose x2 -> x0, local copies, waits for them, and re-layouts: 6.25 us -> none  [per_device(): jnp.einsum('jps,sbk->jbpk', blocks, geno_blocks, preferred_element_type=j...]
  transfers between devices with their start and end apart: 23 -> 23, of which waited for: 18 -> 18; matrix products, arithmetic and copies ran while one was open for 2% -> 3% of each run, Pallas kernels for 0% -> 0%
where the time goes in v11:
time: 265 us; the launch traced here: 264 us
  waiting for transfers between devices  128 us (48%)
  blocking collectives  59.4 us (22%)
  starting transfers between devices  30.1 us (11%)
  matrix products  16.2 us (6%)
  other arithmetic  15.1 us (6%)
  local copies, waits for them, and re-layouts  14.7 us (6%)
    all_to_all x1, blocking collectives, predict(): gathered = lax.all_to_all(partial, 'snp', 0, 0, tiled=False)  59.4 us
    ppermute x8, waiting for transfers between devices, per_device(): moving = lax.ppermute(moving, 'snp', forward)  41 us
    all_to_all x2, waiting for transfers between devices, predict(): gathered = lax.all_to_all(partial, 'snp', 0, 0, tiled=False)  39.1 us
    ppermute x1, waiting for transfers between devices, per_device(): other_half = lax.ppermute(own, 'sx', swap)  23.8 us
    all_to_all x2, starting transfers between devices, predict(): gathered = lax.all_to_all(partial, 'snp', 0, 0, tiled=False)  11.5 us
    ppermute x1, waiting for transfers between devices, per_device(): geno_peer = lax.ppermute(genotypes, 'sx', swap)  11.4 us
    ppermute x6, starting transfers between devices, per_device(): moving = lax.ppermute(moving, 'snp', backward)  8.11 us
    dot_general x2, matrix products, per_device(): jnp.einsum('jps,sbk->jpbk', blocks, geno_blocks, preferred_element_type=j...  7.99 us
  transfers between devices with their start and end apart: 23, of which 18 were waited for; matrix products, arithmetic and copies ran while one was open for 3% of the time, Pallas kernels for 0%

profile of v11, /device:TPU:0, one launch (start us, length us, event | category | flops | bytes accessed | tf_op | source)
XLA Modules:
  0.0 264.2 jit_solution(15496082920273471328)
XLA Ops:
  4.7 1.9 select_convert_fusion
  8.6 2.3 bitcast_convert_fusion.2
  10.9 7.3 %all-to-all-start = ((bf16[8,192,384]{2,1,0:T(8,128)(2,1)}), bf16[8,192,384]{2,1,0:T(8,128)(2,1)S(1)}, u32[]{:S(2)}, u32[]{:S(2)}) async-start(bf16[8,192,384]{2,1,0:T(8,128)(2,1)} %bitcast.206), calls=%async_computation | async-start | bytes 2359296 | tf_op jit(solution)/shard_map/all_to_all | solution.py:91
  19.7 11.4 %collective-permute-done.1 = bf16[384,640]{0,1:T(8,128)(2,1)S(1)} collective-permute-done((bf16[384,640]{0,1:T(8,128)(2,1)}, bf16[384,640]{0,1:T(8,128)(2,1)S(1)}, u32[]{:S(2)}, u32[]{:S(2)}) %collective-permute-start.1) | collective-permute-done | bytes 491552 | tf_op jit(solution)/shard_map/ppermute | solution.py:34
  31.9 2.3 bitcast_convert_fusion.1
  34.2 12.6 %all-to-all-done = bf16[8,192,384]{2,1,0:T(8,128)(2,1)S(1)} async-done(((bf16[8,192,384]{2,1,0:T(8,128)(2,1)}), bf16[8,192,384]{2,1,0:T(8,128)(2,1)S(1)}, u32[]{:S(2)}, u32[]{:S(2)}) %all-to-all-start) | async-done | bytes 1179680 | tf_op jit(solution)/shard_map/all_to_all | solution.py:91
  46.8 4.3 %all-to-all-start.1 = ((bf16[8,192,384]{2,1,0:T(8,128)(2,1)}), bf16[8,192,384]{2,1,0:T(8,128)(2,1)}, u32[]{:S(2)}, u32[]{:S(2)}) async-start(bf16[8,192,384]{2,1,0:T(8,128)(2,1)} %bitcast.205), calls=%async_computation.1 | async-start | bytes 2359296 | tf_op jit(solution)/shard_map/all_to_all | solution.py:91
  52.9 26.5 %all-to-all-done.1 = bf16[8,192,384]{2,1,0:T(8,128)(2,1)} async-done(((bf16[8,192,384]{2,1,0:T(8,128)(2,1)}), bf16[8,192,384]{2,1,0:T(8,128)(2,1)}, u32[]{:S(2)}, u32[]{:S(2)}) %all-to-all-start.1) | async-done | bytes 1179680 | tf_op jit(solution)/shard_map/all_to_all | solution.py:91
  81.0 2.0 collective-permute-start.2
  83.0 5.5 %collective-permute-done.5 = bf16[192,768]{1,0:T(8,128)(2,1)S(1)} collective-permute-done((bf16[192,768]{1,0:T(8,128)(2,1)S(1)}, bf16[192,768]{1,0:T(8,128)(2,1)S(1)}, u32[]{:S(2)}, u32[]{:S(2)}) %collective-permute-start.5) | collective-permute-done | bytes 294944 | tf_op jit(solution)/shard_map/ppermute | solution.py:102
  88.5 2.0 collective-permute-start.3
  91.7 4.0 %collective-permute-done.6 = bf16[192,768]{1,0:T(8,128)(2,1)S(1)} collective-permute-done((bf16[192,768]{1,0:T(8,128)(2,1)S(1)}, bf16[192,768]{1,0:T(8,128)(2,1)S(1)}, u32[]{:S(2)}, u32[]{:S(2)}) %collective-permute-start.6) | collective-permute-done | bytes 294944 | tf_op jit(solution)/shard_map/ppermute | solution.py:102
  98.8 3.6 %collective-permute-done.7 = bf16[192,768]{1,0:T(8,128)(2,1)S(1)} collective-permute-done((bf16[192,768]{1,0:T(8,128)(2,1)S(1)}, bf16[192,768]{1,0:T(8,128)(2,1)S(1)}, u32[]{:S(2)}, u32[]{:S(2)}) %collective-permute-start.7) | collective-permute-done | bytes 294944 | tf_op jit(solution)/shard_map/ppermute | solution.py:102
  103.8 6.4 %collective-permute-done.8 = bf16[192,768]{1,0:T(8,128)(2,1)S(1)} collective-permute-done((bf16[192,768]{1,0:T(8,128)(2,1)S(1)}, bf16[192,768]{1,0:T(8,128)(2,1)S(1)}, u32[]{:S(2)}, u32[]{:S(2)}) %collective-permute-start.8) | collective-permute-done | bytes 294944 | tf_op jit(solution)/shard_map/ppermute | solution.py:102
  110.3 4.0 %fusion.31 = f32[48,32,5,128]{3,1,2,0:T(8,128)} fusion(bf16[48,32,768,1]{2,1,3,0:T(8,128)(2,1)S(1)} %bitcast.213, bf16[768,5,128,1]{0,2,1,3:T(8,128)(2,1)S(1)} %bitcast.207), kind=kOutput, calls=%fused_computation.95 | convolution fusion | flops 1509949440 | bytes 7274496 | tf_op jit(solution)/shard_map/jps,sbk->jpbk/dot_general | solution.py:110
  114.3 3.0 %gather_fusion = f32[128,32,128]{2,1,0:T(8,128)S(1)} fusion(f32[48,32,5,128]{3,1,2,0:T(8,128)} %fusion.31, s32[128]{0:T(128)S(1)} %get-tuple-element.9), kind=kCustom, calls=%fused_computation | custom fusion | bytes 4195328 | tf_op jit(solution)/shard_map/gather | solution.py:113
  118.6 2.7 %collective-permute-done.9 = f32[64,32,128]{2,1,0:T(8,128)} collective-permute-done((f32[64,32,128]{2,1,0:T(8,128)}, f32[64,32,128]{2,1,0:T(8,128)}, u32[]{:S(2)}, u32[]{:S(2)}) %collective-permute-start.9) | collective-permute-done | bytes 1048608 | tf_op jit(solution)/shard_map/ppermute | solution.py:117
  121.4 4.2 %fusion.30 = (bf16[64,32,128]{2,1,0:T(8,128)(2,1)S(1)}, f32[64,32,128]{2,1,0:T(8,128)}) fusion(f32[64]{0:T(128)S(1)} %dynamic_slice.43, f32[64,32,128]{2,1,0:T(8,128)} %collective-permute-done.9, f32[2,64,32,128]{3,2,1,0:T(8,128)S(1)} %bitcast.189, s32[]{:T(128)S(6)} %select_n.157, f32[128,64,128]{2,1,0:T(8,128)} %param.10, s32[]{:T(128)S(6)} %select_n.142, ...), kind=kLoop, calls=%fused_computation.94 | loop fusion | flops 2883584 | bytes 4718924 | tf_op jit(solution)/shard_map/convert_element_type | solution.py:120
  125.7 1.8 collective-permute-done.10
  129.5 2.2 bitcast_convert_fusion
  131.7 59.4 %all_to_all.15 = bf16[8,192,768]{2,1,0:T(8,128)(2,1)S(1)} all-to-all(bf16[8,192,768]{2,1,0:T(8,128)(2,1)S(1)} %bitcast.200), channel_id=1, replica_groups=mesh['snp'=8,'sx'=2,'sc'=2] {'snp'}, dimensions={0} | all-to-all | bytes 4718592 | tf_op jit(solution)/shard_map/all_to_all | solution.py:91
  193.6 5.6 %collective-permute-done.14 = bf16[192,768]{1,0:T(8,128)(2,1)S(1)} collective-permute-done((bf16[192,768]{1,0:T(8,128)(2,1)S(1)}, bf16[192,768]{1,0:T(8,128)(2,1)S(1)}, u32[]{:S(2)}, u32[]{:S(2)}) %collective-permute-start.14) | collective-permute-done | bytes 294944 | tf_op jit(solution)/shard_map/ppermute | solution.py:102
  201.2 5.2 %collective-permute-done.15 = bf16[192,768]{1,0:T(8,128)(2,1)S(1)} collective-permute-done((bf16[192,768]{1,0:T(8,128)(2,1)S(1)}, bf16[192,768]{1,0:T(8,128)(2,1)S(1)}, u32[]{:S(2)}, u32[]{:S(2)}) %collective-permute-start.15) | collective-permute-done | bytes 294944 | tf_op jit(solution)/shard_map/ppermute | solution.py:102
  208.6 6.1 %collective-permute-done.16 = bf16[192,768]{1,0:T(8,128)(2,1)S(1)} collective-permute-done((bf16[192,768]{1,0:T(8,128)(2,1)S(1)}, bf16[192,768]{1,0:T(8,128)(2,1)S(1)}, u32[]{:S(2)}, u32[]{:S(2)}) %collective-permute-start.16) | collective-permute-done | bytes 294944 | tf_op jit(solution)/shard_map/ppermute | solution.py:102
  214.7 1.9 collective-permute-start.17
  216.6 4.7 %collective-permute-done.17 = bf16[192,768]{1,0:T(8,128)(2,1)S(1)} collective-permute-done((bf16[192,768]{1,0:T(8,128)(2,1)S(1)}, bf16[192,768]{1,0:T(8,128)(2,1)S(1)}, u32[]{:S(2)}, u32[]{:S(2)}) %collective-permute-start.17) | collective-permute-done | bytes 294944 | tf_op jit(solution)/shard_map/ppermute | solution.py:102
  221.5 4.0 %fusion.32 = f32[48,32,5,128]{3,1,2,0:T(8,128)} fusion(bf16[48,32,768,1]{2,1,3,0:T(8,128)(2,1)S(1)} %bitcast.212, bf16[768,5,128,1]{0,2,1,3:T(8,128)(2,1)S(1)} %bitcast.209), kind=kOutput, calls=%fused_computation.96 | convolution fusion | flops 1509949440 | bytes 7274496 | tf_op jit(solution)/shard_map/jps,sbk->jpbk/dot_general | solution.py:110
  225.5 3.0 %gather_fusion.1 = f32[128,32,128]{2,1,0:T(8,128)S(1)} fusion(f32[48,32,5,128]{3,1,2,0:T(8,128)} %fusion.32, s32[128]{0:T(128)S(1)} %get-tuple-element.9), kind=kCustom, calls=%fused_computation.1 | custom fusion | bytes 4195328 | tf_op jit(solution)/shard_map/gather | solution.py:113
  228.6 2.6 %collective-permute-done.18 = f32[64,32,128]{2,1,0:T(8,128)S(1)} collective-permute-done((f32[64,32,128]{2,1,0:T(8,128)S(1)}, f32[64,32,128]{2,1,0:T(8,128)S(1)}, u32[]{:S(2)}, u32[]{:S(2)}) %collective-permute-start.18) | collective-permute-done | bytes 1048608 | tf_op jit(solution)/shard_map/ppermute | solution.py:117
  233.3 23.8 %collective-permute-done.19 = f32[64,32,128]{2,1,0:T(8,128)S(1)} collective-permute-done((f32[64,32,128]{2,1,0:T(8,128)S(1)}, f32[64,32,128]{2,1,0:T(8,128)S(1)}, u32[]{:S(2)}, u32[]{:S(2)}) %collective-permute-start.19) | collective-permute-done | bytes 1048608 | tf_op jit(solution)/shard_map/ppermute | solution.py:127
  257.6 4.1 %collective-permute-done.20 = f32[64,64,128]{2,1,0:T(8,128)S(1)} collective-permute-done((f32[64,64,128]{2,1,0:T(8,128)S(1)}, f32[64,64,128]{2,1,0:T(8,128)S(1)}, u32[]{:S(2)}, u32[]{:S(2)}) %collective-permute-start.20) | collective-permute-done | bytes 2097184 | tf_op jit(solution)/shard_map/ppermute | solution.py:133
  261.7 2.5 maximum_select_fusion
  (85 shorter events, 30.4 us)
Async XLA Ops:
  7.3 1.0 copy-start.6
  8.6 2.3 copy-start.1
  10.9 35.9 %all-to-all-start = ((bf16[8,192,384]{2,1,0:T(8,128)(2,1)}), bf16[8,192,384]{2,1,0:T(8,128)(2,1)S(1)}, u32[]{:S(2)}, u32[]{:S(2)}) async-start(bf16[8,192,384]{2,1,0:T(8,128)(2,1)} %bitcast.206), calls=%async_computation | async-start | bytes 2359296 | tf_op jit(solution)/shard_map/all_to_all | solution.py:91
  18.2 12.9 %collective-permute-start.1 = (bf16[384,640]{0,1:T(8,128)(2,1)}, bf16[384,640]{0,1:T(8,128)(2,1)S(1)}, u32[]{:S(2)}, u32[]{:S(2)}) collective-permute-start(bf16[384,640]{0,1:T(8,128)(2,1)} %copy-done.1), channel_id=1, source_target_pairs={{0,2},{2,0},{1,3},{3,1},{4,6},{6,4},{5,7},{7,5},{8,10},{10,8},{9,1... | collective-permute-start | bytes 1474568 | tf_op jit(solution)/shard_map/ppermute | solution.py:34
  31.1 0.8 copy-start.7
  34.2 16.9 %copy-start.5 = (f32[384,384]{1,0:T(8,128)S(1)}, f32[384,384]{1,0:T(8,128)}, u32[]{:S(2)}) copy-start(f32[384,384]{1,0:T(8,128)} %param.9) | copy-start | bytes 1769476
  46.8 32.6 %all-to-all-start.1 = ((bf16[8,192,384]{2,1,0:T(8,128)(2,1)}), bf16[8,192,384]{2,1,0:T(8,128)(2,1)}, u32[]{:S(2)}, u32[]{:S(2)}) async-start(bf16[8,192,384]{2,1,0:T(8,128)(2,1)} %bitcast.205), calls=%async_computation.1 | async-start | bytes 2359296 | tf_op jit(solution)/shard_map/all_to_all | solution.py:91
  51.1 39.4 %copy-start.2 = (bf16[384,640]{0,1:T(8,128)(2,1)S(1)}, bf16[384,640]{0,1:T(8,128)(2,1)}, u32[]{:S(2)}) copy-start(bf16[384,640]{0,1:T(8,128)(2,1)} %copy-done.1) | copy-start | bytes 1474564
  51.1 29.7 %collective-permute-start = (f32[6,32,384]{2,1,0:T(8,128)S(1)}, f32[6,32,384]{2,1,0:T(8,128)S(1)}, u32[]{:S(2)}, u32[]{:S(2)}) collective-permute-start(f32[6,32,384]{2,1,0:T(8,128)S(1)} %get-tuple-element.8), channel_id=1, source_target_pairs={{0,2},{2,0},{1,3},{3,1},{4,6},{6,4},{5,7},{7,5},{8,10},{10,8},{9,1... | collective-permute-start | bytes 884744 | tf_op jit(solution)/shard_map/ppermute | solution.py:40
  80.9 7.6 %collective-permute-start.5 = (bf16[192,768]{1,0:T(8,128)(2,1)S(1)}, bf16[192,768]{1,0:T(8,128)(2,1)S(1)}, u32[]{:S(2)}, u32[]{:S(2)}) collective-permute-start(bf16[192,768]{1,0:T(8,128)(2,1)S(1)} %fusion.7), channel_id=1, source_target_pairs={{0,8},{8,16},{16,24},{24,28},{28,20},{20,12},{12,4},{4,0},{1,9},{9... | collective-permute-start | bytes 884744 | tf_op jit(solution)/shard_map/ppermute | solution.py:102
  81.0 7.5 %collective-permute-start.2 = (bf16[192,768]{1,0:T(8,128)(2,1)S(1)}, bf16[192,768]{1,0:T(8,128)(2,1)}, u32[]{:S(2)}, u32[]{:S(2)}) collective-permute-start(bf16[192,768]{1,0:T(8,128)(2,1)S(1)} %fusion.7), channel_id=1, source_target_pairs={{0,4},{8,0},{16,8},{24,16},{28,24},{20,28},{12,20},{4,12},{1,5},{9... | collective-permute-start | bytes 884744 | tf_op jit(solution)/shard_map/ppermute | solution.py:106
  88.5 7.1 %collective-permute-start.6 = (bf16[192,768]{1,0:T(8,128)(2,1)S(1)}, bf16[192,768]{1,0:T(8,128)(2,1)S(1)}, u32[]{:S(2)}, u32[]{:S(2)}) collective-permute-start(bf16[192,768]{1,0:T(8,128)(2,1)S(1)} %collective-permute-done.5), channel_id=1, source_target_pairs={{0,8},{8,16},{16,24},{24,28},{28,20},{20,12},{12,4},{4,0},{1,9},{9... | collective-permute-start | bytes 884744 | tf_op jit(solution)/shard_map/ppermute | solution.py:102
  88.5 8.0 %collective-permute-start.3 = (bf16[192,768]{1,0:T(8,128)(2,1)}, bf16[192,768]{1,0:T(8,128)(2,1)}, u32[]{:S(2)}, u32[]{:S(2)}) collective-permute-start(bf16[192,768]{1,0:T(8,128)(2,1)} %collective-permute-done.2), channel_id=1, source_target_pairs={{0,4},{8,0},{16,8},{24,16},{28,24},{20,28},{12,20},{4,12},{1,5},{9... | collective-permute-start | bytes 884744 | tf_op jit(solution)/shard_map/ppermute | solution.py:106
  91.7 18.6 %copy-start.3 = (bf16[768,640]{0,1:T(8,128)(2,1)}, bf16[768,640]{0,1:T(8,128)(2,1)S(1)}, u32[]{:S(2)}) copy-start(bf16[768,640]{0,1:T(8,128)(2,1)S(1)} %pad_maximum_fusion) | copy-start | bytes 2949124
  95.7 6.7 %collective-permute-start.7 = (bf16[192,768]{1,0:T(8,128)(2,1)S(1)}, bf16[192,768]{1,0:T(8,128)(2,1)S(1)}, u32[]{:S(2)}, u32[]{:S(2)}) collective-permute-start(bf16[192,768]{1,0:T(8,128)(2,1)S(1)} %collective-permute-done.6), channel_id=1, source_target_pairs={{0,8},{8,16},{16,24},{24,28},{28,20},{20,12},{12,4},{4,0},{1,9},{9... | collective-permute-start | bytes 884744 | tf_op jit(solution)/shard_map/ppermute | solution.py:102
  96.6 7.2 %collective-permute-start.4 = (bf16[192,768]{1,0:T(8,128)(2,1)}, bf16[192,768]{1,0:T(8,128)(2,1)S(1)}, u32[]{:S(2)}, u32[]{:S(2)}) collective-permute-start(bf16[192,768]{1,0:T(8,128)(2,1)} %collective-permute-done.3), channel_id=1, source_target_pairs={{0,4},{8,0},{16,8},{24,16},{28,24},{20,28},{12,20},{4,12},{1,5},{9... | collective-permute-start | bytes 884744 | tf_op jit(solution)/shard_map/ppermute | solution.py:106
  102.4 7.8 %collective-permute-start.8 = (bf16[192,768]{1,0:T(8,128)(2,1)S(1)}, bf16[192,768]{1,0:T(8,128)(2,1)S(1)}, u32[]{:S(2)}, u32[]{:S(2)}) collective-permute-start(bf16[192,768]{1,0:T(8,128)(2,1)S(1)} %collective-permute-done.7), channel_id=1, source_target_pairs={{0,8},{8,16},{16,24},{24,28},{28,20},{20,12},{12,4},{4,0},{1,9},{9... | collective-permute-start | bytes 884744 | tf_op jit(solution)/shard_map/ppermute | solution.py:102
  114.3 4.1 %copy-start.8 = (f32[46]{0:T(128)S(1)}, f32[46]{0:T(128)}, u32[]{:S(2)}) copy-start(f32[46]{0:T(128)} %param.14) | copy-start | bytes 556
  118.4 3.0 %collective-permute-start.9 = (f32[64,32,128]{2,1,0:T(8,128)}, f32[64,32,128]{2,1,0:T(8,128)}, u32[]{:S(2)}, u32[]{:S(2)}) collective-permute-start(f32[64,32,128]{2,1,0:T(8,128)} %dynamic-slice_bitcast_fusion.1), channel_id=1, source_target_pairs={{0,1},{1,0},{2,3},{3,2},{4,5},{5,4},{6,7},{7,6},{8,9},{9,8},{10,11... | collective-permute-start | bytes 3145736 | tf_op jit(solution)/shard_map/ppermute | solution.py:117
  125.5 1.9 collective-permute-start.10
  128.3 1.2 copy-start.4
  191.5 7.7 %collective-permute-start.14 = (bf16[192,768]{1,0:T(8,128)(2,1)S(1)}, bf16[192,768]{1,0:T(8,128)(2,1)S(1)}, u32[]{:S(2)}, u32[]{:S(2)}) collective-permute-start(bf16[192,768]{1,0:T(8,128)(2,1)S(1)} %subtract_convert_fusion), channel_id=1, source_target_pairs={{0,8},{8,16},{16,24},{24,28},{28,20},{20,12},{12,4},{4,0},{1,9},{9... | collective-permute-start | bytes 884744 | tf_op jit(solution)/shard_map/ppermute | solution.py:102
  192.7 7.4 %collective-permute-start.11 = (bf16[192,768]{1,0:T(8,128)(2,1)S(1)}, bf16[192,768]{1,0:T(8,128)(2,1)S(1)}, u32[]{:S(2)}, u32[]{:S(2)}) collective-permute-start(bf16[192,768]{1,0:T(8,128)(2,1)S(1)} %subtract_convert_fusion), channel_id=1, source_target_pairs={{0,4},{8,0},{16,8},{24,16},{28,24},{20,28},{12,20},{4,12},{1,5},{9... | collective-permute-start | bytes 884744 | tf_op jit(solution)/shard_map/ppermute | solution.py:106
  199.2 7.2 %collective-permute-start.15 = (bf16[192,768]{1,0:T(8,128)(2,1)S(1)}, bf16[192,768]{1,0:T(8,128)(2,1)S(1)}, u32[]{:S(2)}, u32[]{:S(2)}) collective-permute-start(bf16[192,768]{1,0:T(8,128)(2,1)S(1)} %collective-permute-done.14), channel_id=1, source_target_pairs={{0,8},{8,16},{16,24},{24,28},{28,20},{20,12},{12,4},{4,0},{1,9},{9... | collective-permute-start | bytes 884744 | tf_op jit(solution)/shard_map/ppermute | solution.py:102
  200.1 7.7 %collective-permute-start.12 = (bf16[192,768]{1,0:T(8,128)(2,1)S(1)}, bf16[192,768]{1,0:T(8,128)(2,1)S(1)}, u32[]{:S(2)}, u32[]{:S(2)}) collective-permute-start(bf16[192,768]{1,0:T(8,128)(2,1)S(1)} %collective-permute-done.11), channel_id=1, source_target_pairs={{0,4},{8,0},{16,8},{24,16},{28,24},{20,28},{12,20},{4,12},{1,5},{9... | collective-permute-start | bytes 884744 | tf_op jit(solution)/shard_map/ppermute | solution.py:106
  206.4 8.3 %collective-permute-start.16 = (bf16[192,768]{1,0:T(8,128)(2,1)S(1)}, bf16[192,768]{1,0:T(8,128)(2,1)S(1)}, u32[]{:S(2)}, u32[]{:S(2)}) collective-permute-start(bf16[192,768]{1,0:T(8,128)(2,1)S(1)} %collective-permute-done.15), channel_id=1, source_target_pairs={{0,8},{8,16},{16,24},{24,28},{28,20},{20,12},{12,4},{4,0},{1,9},{9... | collective-permute-start | bytes 884744 | tf_op jit(solution)/shard_map/ppermute | solution.py:102
  207.8 8.8 %collective-permute-start.13 = (bf16[192,768]{1,0:T(8,128)(2,1)S(1)}, bf16[192,768]{1,0:T(8,128)(2,1)S(1)}, u32[]{:S(2)}, u32[]{:S(2)}) collective-permute-start(bf16[192,768]{1,0:T(8,128)(2,1)S(1)} %collective-permute-done.12), channel_id=1, source_target_pairs={{0,4},{8,0},{16,8},{24,16},{28,24},{20,28},{12,20},{4,12},{1,5},{9... | collective-permute-start | bytes 884744 | tf_op jit(solution)/shard_map/ppermute | solution.py:106
  214.7 6.7 %collective-permute-start.17 = (bf16[192,768]{1,0:T(8,128)(2,1)S(1)}, bf16[192,768]{1,0:T(8,128)(2,1)S(1)}, u32[]{:S(2)}, u32[]{:S(2)}) collective-permute-start(bf16[192,768]{1,0:T(8,128)(2,1)S(1)} %collective-permute-done.16), channel_id=1, source_target_pairs={{0,8},{8,16},{16,24},{24,28},{28,20},{20,12},{12,4},{4,0},{1,9},{9... | collective-permute-start | bytes 884744 | tf_op jit(solution)/shard_map/ppermute | solution.py:102
  228.5 2.8 %copy-start = (f32[64,32,128]{2,1,0:T(8,128)S(1)}, f32[64,32,128]{2,1,0:T(8,128)}, u32[]{:S(2)}) copy-start(f32[64,32,128]{2,1,0:T(8,128)} %get-tuple-element.6) | copy-start | bytes 3145732
  228.5 2.7 %collective-permute-start.18 = (f32[64,32,128]{2,1,0:T(8,128)S(1)}, f32[64,32,128]{2,1,0:T(8,128)S(1)}, u32[]{:S(2)}, u32[]{:S(2)}) collective-permute-start(f32[64,32,128]{2,1,0:T(8,128)S(1)} %dynamic-slice_bitcast_fusion), channel_id=1, source_target_pairs={{0,1},{1,0},{2,3},{3,2},{4,5},{5,4},{6,7},{7,6},{8,9},{9,8},{10,11... | collective-permute-start | bytes 3145736 | tf_op jit(solution)/shard_map/ppermute | solution.py:117
  231.8 25.3 %collective-permute-start.19 = (f32[64,32,128]{2,1,0:T(8,128)S(1)}, f32[64,32,128]{2,1,0:T(8,128)S(1)}, u32[]{:S(2)}, u32[]{:S(2)}) collective-permute-start(f32[64,32,128]{2,1,0:T(8,128)S(1)} %multiply_select_fusion), channel_id=1, source_target_pairs={{0,2},{2,0},{1,3},{3,1},{4,6},{6,4},{5,7},{7,5},{8,10},{10,8},{9,1... | collective-permute-start | bytes 3145736 | tf_op jit(solution)/shard_map/ppermute | solution.py:127
  257.5 4.2 %collective-permute-start.20 = (f32[64,64,128]{2,1,0:T(8,128)S(1)}, f32[64,64,128]{2,1,0:T(8,128)S(1)}, u32[]{:S(2)}, u32[]{:S(2)}) collective-permute-start(f32[64,64,128]{2,1,0:T(8,128)S(1)} %maximum_select_fusion.1), channel_id=1, source_target_pairs={{0,1},{1,0},{2,3},{3,2},{4,5},{5,4},{6,7},{7,6},{8,9},{9,8},{10,11... | collective-permute-start | bytes 6291464 | tf_op jit(solution)/shard_map/ppermute | solution.py:133

commit v12 on v11

--- a/solution.py
+++ b/solution.py
@@ -58,6 +58,7 @@
     backward = [(ring[k], ring[(k - 1) % owners]) for k in range(owners)]
     forward_steps = owners // 2
     ring_table = jnp.asarray(ring_pos, dtype=jnp.int32)
+    ring_order = jnp.asarray(ring, dtype=jnp.int32)
     here = ring_table[lax.axis_index("snp")]
     rel_owner = (ring_table[slot_ids // own_slots] - here) % owners
     ring_slot = rel_owner * own_slots + slot_ids % own_slots
@@ -79,22 +80,27 @@
         ).astype(jnp.bfloat16)
         dense = dense.reshape(slot_total, block_count, half_p, block_width)
 
-        def predict(samples):
-            count = samples.shape[0]
-            partial = jnp.einsum(
-                "jbpk,sbk->jps",
-                dense,
-                samples.reshape(count, block_count, block_width),
-                preferred_element_type=jnp.float32,
-            ).astype(jnp.bfloat16)
-            partial = partial.reshape(owners, own_slots * half_p, count)
-            gathered = lax.all_to_all(partial, "snp", 0, 0, tiled=False)
-            return jnp.sum(gathered.astype(jnp.float32), axis=0)
+        partial = jnp.einsum(
+            "jbpk,sbk->jps", dense, geno_blocks, preferred_element_type=jnp.float32
+        ).astype(jnp.bfloat16)
+        partial = partial.reshape(owners, own_slots * half_p, sample_count)
 
-        if sweep == 0:
-            prediction = jnp.concatenate([predict(genotypes), predict(geno_peer)], axis=1)
-        else:
-            prediction = predict(geno)
+        def owner_block(distance):
+            owner = ring_order[(here + distance) % owners]
+            return lax.dynamic_index_in_dim(partial, owner, 0, keepdims=False)
+
+        ahead = lax.ppermute(owner_block(forward_steps), "snp", forward).astype(jnp.float32)
+        for step in range(2, forward_steps + 1):
+            carry = ahead + owner_block(forward_steps - step + 1).astype(jnp.float32)
+            ahead = lax.ppermute(carry, "snp", forward)
+        prediction = owner_block(0).astype(jnp.float32) + ahead
+        behind_steps = owners - 1 - forward_steps
+        if behind_steps > 0:
+            behind = lax.ppermute(owner_block(-behind_steps), "snp", backward).astype(jnp.float32)
+            for step in range(2, behind_steps + 1):
+                carry = behind + owner_block(step - behind_steps - 1).astype(jnp.float32)
+                behind = lax.ppermute(carry, "snp", backward)
+            prediction = prediction + behind
         residual = (resp - prediction).astype(jnp.bfloat16)
         received = {0: residual}
         moving = residual

time: 265 us -> 277 us (1.045)
  blocking collectives: 59.4 us -> 0 us
  waiting for transfers between devices: 128 us -> 162 us
  between operations: 1.02 us -> 22.3 us
  local copies, waits for them, and re-layouts: 14.7 us -> 22 us
  starting transfers between devices: 30.1 us -> 34.9 us
  other arithmetic: 15.1 us -> 18.3 us
    ppermute x0 -> x14, waiting for transfers between devices: none -> 71 us  [the longest x6 41.6 us: per_device(): ahead = lax.ppermute(carry, 'snp', forward)]
    all_to_all x1 -> x0, blocking collectives: 59.4 us -> none  [predict(): gathered = lax.all_to_all(partial, 'snp', 0, 0, tiled=False)]
    all_to_all x2 -> x0, waiting for transfers between devices: 39.1 us -> none  [predict(): gathered = lax.all_to_all(partial, 'snp', 0, 0, tiled=False)]
    ppermute x0 -> x14, starting transfers between devices: none -> 15.6 us  [the longest x6 9.62 us: per_device(): ahead = lax.ppermute(carry, 'snp', forward)]
    all_to_all x2 -> x0, starting transfers between devices: 11.5 us -> none  [predict(): gathered = lax.all_to_all(partial, 'snp', 0, 0, tiled=False)]
    ppermute x1, waiting for transfers between devices: 11.4 us -> 0.01 us  [per_device(): geno_peer = lax.ppermute(genotypes, 'sx', swap)]
    ppermute x8, waiting for transfers between devices: 41 us -> 50 us  [per_device(): moving = lax.ppermute(moving, 'snp', forward)]
    ppermute x8, starting transfers between devices: 5.63 us -> 10.7 us  [per_device(): moving = lax.ppermute(moving, 'snp', forward)]
  transfers between devices with their start and end apart: 23 -> 35, of which waited for: 18 -> 29; matrix products, arithmetic and copies ran while one was open for 3% -> 5% of each run, Pallas kernels for 0% -> 0%
where the time goes in v12:
time: 277 us; the launch traced here: 276 us
  waiting for transfers between devices  162 us (58%)
  starting transfers between devices  34.9 us (13%)
  between operations  22.3 us (8%)
  local copies, waits for them, and re-layouts  22 us (8%)
  other arithmetic  18.3 us (7%)
  matrix products  17.2 us (6%)
    ppermute x8, waiting for transfers between devices, per_device(): moving = lax.ppermute(moving, 'snp', forward)  50 us
    ppermute x6, waiting for transfers between devices, per_device(): ahead = lax.ppermute(carry, 'snp', forward)  41.6 us
    ppermute x1, waiting for transfers between devices, per_device(): other_half = lax.ppermute(own, 'sx', swap)  24.8 us
    ppermute x2, waiting for transfers between devices, per_device(): lax.ppermute(owner_block(forward_steps), 'snp', forward).astype(jnp.float32)  12.5 us
    ppermute x2, waiting for transfers between devices, per_device(): lax.ppermute(owner_block(-behind_steps), 'snp', backward)  11.1 us
    ppermute x8, starting transfers between devices, per_device(): moving = lax.ppermute(moving, 'snp', forward)  10.7 us
    ppermute x6, starting transfers between devices, per_device(): ahead = lax.ppermute(carry, 'snp', forward)  9.62 us
    dot_general x2, matrix products, per_device(): jnp.einsum('jps,sbk->jpbk', blocks, geno_blocks, preferred_element_type=j...  9.62 us
  transfers between devices with their start and end apart: 35, of which 29 were waited for; matrix products, arithmetic and copies ran while one was open for 5% of the time, Pallas kernels for 0%

profile of v12, /device:TPU:0, one launch (start us, length us, event | category | flops | bytes accessed | tf_op | source)
XLA Modules:
  0.0 276.2 jit_solution(10851023787029437357)
XLA Ops:
  1.3 3.0 %collective-permute-start.1 = (bf16[384,640]{0,1:T(8,128)(2,1)S(1)}, bf16[384,640]{0,1:T(8,128)(2,1)S(1)}, u32[]{:S(2)}, u32[]{:S(2)}) collective-permute-start(bf16[384,640]{0,1:T(8,128)(2,1)S(1)} %copy.27), channel_id=1, source_target_pairs={{0,2},{2,0},{1,3},{3,1},{4,6},{6,4},{5,7},{7,5},{8,10},{10,8},{9,1... | collective-permute-start | bytes 1474568 | tf_op jit(solution)/shard_map/ppermute | solution.py:34
  24.6 3.9 %bitcast_convert_fusion.1 = bf16[48,32,768]{2,1,0:T(8,128)(2,1)S(1)} fusion(bf16[48,5,32,128]{3,2,1,0:T(8,128)(2,1)} %bitcast.239, bf16[768,5,128,1]{0,2,1,3:T(8,128)(2,1)S(1)} %bitcast.243), kind=kOutput, calls=%fused_computation.3 | convolution fusion | flops 1511129088 | bytes 5308416 | tf_op jit(solution)/shard_map/jbpk,sbk->jps/dot_general | solution.py:83
  32.8 5.0 %collective-permute-done.2 = bf16[192,768]{1,0:T(8,128)(2,1)S(1)} collective-permute-done((bf16[192,768]{1,0:T(8,128)(2,1)S(1)}, bf16[192,768]{1,0:T(8,128)(2,1)S(1)}, u32[]{:S(2)}, u32[]{:S(2)}) %collective-permute-start.2) | collective-permute-done | bytes 294944 | tf_op jit(solution)/shard_map/ppermute | solution.py:92
  43.5 3.6 %collective-permute-done.6 = bf16[192,768]{1,0:T(8,128)(2,1)} collective-permute-done((bf16[192,768]{1,0:T(8,128)(2,1)}, bf16[192,768]{1,0:T(8,128)(2,1)}, u32[]{:S(2)}, u32[]{:S(2)}) %collective-permute-start.6) | collective-permute-done | bytes 294944 | tf_op jit(solution)/shard_map/ppermute | solution.py:99
  47.1 4.8 %collective-permute-done.3 = f32[192,768]{1,0:T(8,128)} collective-permute-done((f32[192,768]{1,0:T(8,128)S(1)}, f32[192,768]{1,0:T(8,128)}, u32[]{:S(2)}, u32[]{:S(2)}) %collective-permute-start.3) | collective-permute-done | bytes 589856 | tf_op jit(solution)/shard_map/ppermute | solution.py:95
  51.9 2.3 convert_add_fusion.9
  59.9 7.5 %collective-permute-done.4 = f32[192,768]{1,0:T(8,128)S(1)} collective-permute-done((f32[192,768]{1,0:T(8,128)}, f32[192,768]{1,0:T(8,128)S(1)}, u32[]{:S(2)}, u32[]{:S(2)}) %collective-permute-start.4) | collective-permute-done | bytes 589856 | tf_op jit(solution)/shard_map/ppermute | solution.py:95
  76.3 4.4 %collective-permute-done = f32[6,32,384]{2,1,0:T(8,128)S(1)} collective-permute-done((f32[6,32,384]{2,1,0:T(8,128)}, f32[6,32,384]{2,1,0:T(8,128)S(1)}, u32[]{:S(2)}, u32[]{:S(2)}) %collective-permute-start) | collective-permute-done | bytes 294944 | tf_op jit(solution)/shard_map/ppermute | solution.py:40
  80.7 2.3 collective-permute-done.5
  88.5 7.8 %collective-permute-done.12 = bf16[192,768]{1,0:T(8,128)(2,1)S(1)} collective-permute-done((bf16[192,768]{1,0:T(8,128)(2,1)S(1)}, bf16[192,768]{1,0:T(8,128)(2,1)S(1)}, u32[]{:S(2)}, u32[]{:S(2)}) %collective-permute-start.12) | collective-permute-done | bytes 294944 | tf_op jit(solution)/shard_map/ppermute | solution.py:108
  98.3 6.9 %collective-permute-done.13 = bf16[192,768]{1,0:T(8,128)(2,1)S(1)} collective-permute-done((bf16[192,768]{1,0:T(8,128)(2,1)S(1)}, bf16[192,768]{1,0:T(8,128)(2,1)S(1)}, u32[]{:S(2)}, u32[]{:S(2)}) %collective-permute-start.13) | collective-permute-done | bytes 294944 | tf_op jit(solution)/shard_map/ppermute | solution.py:108
  107.9 5.3 %collective-permute-done.14 = bf16[192,768]{1,0:T(8,128)(2,1)S(1)} collective-permute-done((bf16[192,768]{1,0:T(8,128)(2,1)S(1)}, bf16[192,768]{1,0:T(8,128)(2,1)S(1)}, u32[]{:S(2)}, u32[]{:S(2)}) %collective-permute-start.14) | collective-permute-done | bytes 294944 | tf_op jit(solution)/shard_map/ppermute | solution.py:108
  116.3 3.7 %collective-permute-done.15 = bf16[192,768]{1,0:T(8,128)(2,1)S(1)} collective-permute-done((bf16[192,768]{1,0:T(8,128)(2,1)S(1)}, bf16[192,768]{1,0:T(8,128)(2,1)S(1)}, u32[]{:S(2)}, u32[]{:S(2)}) %collective-permute-start.15) | collective-permute-done | bytes 294944 | tf_op jit(solution)/shard_map/ppermute | solution.py:108
  123.0 5.6 %fusion.35 = f32[48,32,5,128]{3,1,2,0:T(8,128)} fusion(bf16[48,32,768,1]{2,1,3,0:T(8,128)(2,1)} %bitcast.248, bf16[768,5,128,1]{0,2,1,3:T(8,128)(2,1)S(1)} %bitcast.244), kind=kOutput, calls=%fused_computation.106 | convolution fusion | flops 1509949440 | bytes 7274496 | tf_op jit(solution)/shard_map/jps,sbk->jpbk/dot_general | solution.py:116
  128.6 3.0 %gather_fusion = f32[128,32,128]{2,1,0:T(8,128)S(1)} fusion(f32[48,32,5,128]{3,1,2,0:T(8,128)} %fusion.35, s32[128]{0:T(128)S(1)} %get-tuple-element.25), kind=kCustom, calls=%fused_computation | custom fusion | bytes 4195328 | tf_op jit(solution)/shard_map/gather | solution.py:119
  132.9 2.7 collective-permute-done.16
  135.7 4.2 %fusion.32 = (bf16[64,32,128]{2,1,0:T(8,128)(2,1)S(1)}, f32[64,32,128]{2,1,0:T(8,128)}) fusion(f32[64]{0:T(128)S(1)} %dynamic_slice.140, f32[64,32,128]{2,1,0:T(8,128)} %collective-permute-done.16, f32[2,64,32,128]{3,2,1,0:T(8,128)S(1)} %bitcast.226, s32[]{:T(128)S(6)} %select_n.296, f32[128,64,128]{2,1,0:T(8,128)} %param.11, s32[]{:T(128)S(6)} %select_n.257, ...), kind=kLoop, calls=%fused_computation.104 | loop fusion | flops 2883584 | bytes 4718924 | tf_op jit(solution)/shard_map/convert_element_type | solution.py:126
  147.7 7.5 %collective-permute-done.18 = bf16[192,768]{1,0:T(8,128)(2,1)S(1)} collective-permute-done((bf16[192,768]{1,0:T(8,128)(2,1)S(1)}, bf16[192,768]{1,0:T(8,128)(2,1)S(1)}, u32[]{:S(2)}, u32[]{:S(2)}) %collective-permute-start.18) | collective-permute-done | bytes 294944 | tf_op jit(solution)/shard_map/ppermute | solution.py:92
  157.4 7.5 %collective-permute-done.22 = bf16[192,768]{1,0:T(8,128)(2,1)S(1)} collective-permute-done((bf16[192,768]{1,0:T(8,128)(2,1)S(1)}, bf16[192,768]{1,0:T(8,128)(2,1)S(1)}, u32[]{:S(2)}, u32[]{:S(2)}) %collective-permute-start.22) | collective-permute-done | bytes 294944 | tf_op jit(solution)/shard_map/ppermute | solution.py:99
  164.8 5.0 %collective-permute-done.19 = f32[192,768]{1,0:T(8,128)S(1)} collective-permute-done((f32[192,768]{1,0:T(8,128)S(1)}, f32[192,768]{1,0:T(8,128)S(1)}, u32[]{:S(2)}, u32[]{:S(2)}) %collective-permute-start.19) | collective-permute-done | bytes 589856 | tf_op jit(solution)/shard_map/ppermute | solution.py:95
  172.1 11.6 %collective-permute-done.20 = f32[192,768]{1,0:T(8,128)S(1)} collective-permute-done((f32[192,768]{1,0:T(8,128)S(1)}, f32[192,768]{1,0:T(8,128)S(1)}, u32[]{:S(2)}, u32[]{:S(2)}) %collective-permute-start.20) | collective-permute-done | bytes 589856 | tf_op jit(solution)/shard_map/ppermute | solution.py:95
  187.1 10.4 %collective-permute-done.21 = f32[192,768]{1,0:T(8,128)S(1)} collective-permute-done((f32[192,768]{1,0:T(8,128)S(1)}, f32[192,768]{1,0:T(8,128)S(1)}, u32[]{:S(2)}, u32[]{:S(2)}) %collective-permute-start.21) | collective-permute-done | bytes 589856 | tf_op jit(solution)/shard_map/ppermute | solution.py:95
  201.6 7.8 %collective-permute-done.28 = bf16[192,768]{1,0:T(8,128)(2,1)S(1)} collective-permute-done((bf16[192,768]{1,0:T(8,128)(2,1)S(1)}, bf16[192,768]{1,0:T(8,128)(2,1)S(1)}, u32[]{:S(2)}, u32[]{:S(2)}) %collective-permute-start.28) | collective-permute-done | bytes 294944 | tf_op jit(solution)/shard_map/ppermute | solution.py:108
  211.5 7.0 %collective-permute-done.29 = bf16[192,768]{1,0:T(8,128)(2,1)S(1)} collective-permute-done((bf16[192,768]{1,0:T(8,128)(2,1)S(1)}, bf16[192,768]{1,0:T(8,128)(2,1)S(1)}, u32[]{:S(2)}, u32[]{:S(2)}) %collective-permute-start.29) | collective-permute-done | bytes 294944 | tf_op jit(solution)/shard_map/ppermute | solution.py:108
  220.5 6.2 %collective-permute-done.30 = bf16[192,768]{1,0:T(8,128)(2,1)S(1)} collective-permute-done((bf16[192,768]{1,0:T(8,128)(2,1)S(1)}, bf16[192,768]{1,0:T(8,128)(2,1)S(1)}, u32[]{:S(2)}, u32[]{:S(2)}) %collective-permute-start.30) | collective-permute-done | bytes 294944 | tf_op jit(solution)/shard_map/ppermute | solution.py:108
  228.2 5.2 %collective-permute-done.31 = bf16[192,768]{1,0:T(8,128)(2,1)S(1)} collective-permute-done((bf16[192,768]{1,0:T(8,128)(2,1)S(1)}, bf16[192,768]{1,0:T(8,128)(2,1)S(1)}, u32[]{:S(2)}, u32[]{:S(2)}) %collective-permute-start.31) | collective-permute-done | bytes 294944 | tf_op jit(solution)/shard_map/ppermute | solution.py:108
  233.5 4.0 %fusion.36 = f32[48,32,5,128]{3,1,2,0:T(8,128)} fusion(bf16[48,32,768,1]{2,1,3,0:T(8,128)(2,1)S(1)} %bitcast.249, bf16[768,5,128,1]{0,2,1,3:T(8,128)(2,1)S(1)} %bitcast.246), kind=kOutput, calls=%fused_computation.107 | convolution fusion | flops 1509949440 | bytes 7274496 | tf_op jit(solution)/shard_map/jps,sbk->jpbk/dot_general | solution.py:116
  237.5 3.0 %gather_fusion.1 = f32[128,32,128]{2,1,0:T(8,128)S(1)} fusion(f32[48,32,5,128]{3,1,2,0:T(8,128)} %fusion.36, s32[128]{0:T(128)S(1)} %get-tuple-element.25), kind=kCustom, calls=%fused_computation.1 | custom fusion | bytes 4195328 | tf_op jit(solution)/shard_map/gather | solution.py:119
  240.7 2.6 collective-permute-done.32
  244.3 24.8 %collective-permute-done.33 = f32[64,32,128]{2,1,0:T(8,128)S(1)} collective-permute-done((f32[64,32,128]{2,1,0:T(8,128)S(1)}, f32[64,32,128]{2,1,0:T(8,128)S(1)}, u32[]{:S(2)}, u32[]{:S(2)}) %collective-permute-start.33) | collective-permute-done | bytes 1048608 | tf_op jit(solution)/shard_map/ppermute | solution.py:133
  269.6 4.1 %collective-permute-done.34 = f32[64,64,128]{2,1,0:T(8,128)S(1)} collective-permute-done((f32[64,64,128]{2,1,0:T(8,128)S(1)}, f32[64,64,128]{2,1,0:T(8,128)S(1)}, u32[]{:S(2)}, u32[]{:S(2)}) %collective-permute-start.34) | collective-permute-done | bytes 2097184 | tf_op jit(solution)/shard_map/ppermute | solution.py:139
  273.8 2.5 maximum_select_fusion
  (107 shorter events, 68.7 us)
Async XLA Ops:
  1.3 23.2 %collective-permute-start.1 = (bf16[384,640]{0,1:T(8,128)(2,1)S(1)}, bf16[384,640]{0,1:T(8,128)(2,1)S(1)}, u32[]{:S(2)}, u32[]{:S(2)}) collective-permute-start(bf16[384,640]{0,1:T(8,128)(2,1)S(1)} %copy.27), channel_id=1, source_target_pairs={{0,2},{2,0},{1,3},{3,1},{4,6},{6,4},{5,7},{7,5},{8,10},{10,8},{9,1... | collective-permute-start | bytes 1474568 | tf_op jit(solution)/shard_map/ppermute | solution.py:34
  29.4 8.5 %collective-permute-start.2 = (bf16[192,768]{1,0:T(8,128)(2,1)S(1)}, bf16[192,768]{1,0:T(8,128)(2,1)S(1)}, u32[]{:S(2)}, u32[]{:S(2)}) collective-permute-start(bf16[192,768]{1,0:T(8,128)(2,1)S(1)} %get-tuple-element.21), channel_id=1, source_target_pairs={{0,8},{8,16},{16,24},{24,28},{28,20},{20,12},{12,4},{4,0},{1,9},{9... | collective-permute-start | bytes 884744 | tf_op jit(solution)/shard_map/ppermute | solution.py:92
  37.9 14.0 %collective-permute-start.3 = (f32[192,768]{1,0:T(8,128)S(1)}, f32[192,768]{1,0:T(8,128)}, u32[]{:S(2)}, u32[]{:S(2)}) collective-permute-start(f32[192,768]{1,0:T(8,128)S(1)} %convert_add_fusion.10), channel_id=1, source_target_pairs={{0,8},{8,16},{16,24},{24,28},{28,20},{20,12},{12,4},{4,0},{1,9},{9... | collective-permute-start | bytes 1769480 | tf_op jit(solution)/shard_map/ppermute | solution.py:95
  39.5 7.6 %collective-permute-start.6 = (bf16[192,768]{1,0:T(8,128)(2,1)}, bf16[192,768]{1,0:T(8,128)(2,1)}, u32[]{:S(2)}, u32[]{:S(2)}) collective-permute-start(bf16[192,768]{1,0:T(8,128)(2,1)} %get-tuple-element.22), channel_id=1, source_target_pairs={{0,4},{8,0},{16,8},{24,16},{28,24},{20,28},{12,20},{4,12},{1,5},{9... | collective-permute-start | bytes 884744 | tf_op jit(solution)/shard_map/ppermute | solution.py:99
  54.2 13.2 %collective-permute-start.4 = (f32[192,768]{1,0:T(8,128)}, f32[192,768]{1,0:T(8,128)S(1)}, u32[]{:S(2)}, u32[]{:S(2)}) collective-permute-start(f32[192,768]{1,0:T(8,128)} %get-tuple-element.19), channel_id=1, source_target_pairs={{0,8},{8,16},{16,24},{24,28},{28,20},{20,12},{12,4},{4,0},{1,9},{9... | collective-permute-start | bytes 1769480 | tf_op jit(solution)/shard_map/ppermute | solution.py:95
  55.8 13.0 %collective-permute-start.7 = (f32[192,768]{1,0:T(8,128)}, f32[192,768]{1,0:T(8,128)}, u32[]{:S(2)}, u32[]{:S(2)}) collective-permute-start(f32[192,768]{1,0:T(8,128)} %get-tuple-element.20), channel_id=1, source_target_pairs={{0,4},{8,0},{16,8},{24,16},{28,24},{20,28},{12,20},{4,12},{1,5},{9... | collective-permute-start | bytes 1769480 | tf_op jit(solution)/shard_map/ppermute | solution.py:102
  70.9 12.1 %collective-permute-start.5 = (f32[192,768]{1,0:T(8,128)}, f32[192,768]{1,0:T(8,128)}, u32[]{:S(2)}, u32[]{:S(2)}) collective-permute-start(f32[192,768]{1,0:T(8,128)} %get-tuple-element.17), channel_id=1, source_target_pairs={{0,8},{8,16},{16,24},{24,28},{28,20},{20,12},{12,4},{4,0},{1,9},{9... | collective-permute-start | bytes 1769480 | tf_op jit(solution)/shard_map/ppermute | solution.py:95
  72.5 11.8 %collective-permute-start.8 = (f32[192,768]{1,0:T(8,128)}, f32[192,768]{1,0:T(8,128)}, u32[]{:S(2)}, u32[]{:S(2)}) collective-permute-start(f32[192,768]{1,0:T(8,128)} %get-tuple-element.18), channel_id=1, source_target_pairs={{0,4},{8,0},{16,8},{24,16},{28,24},{20,28},{12,20},{4,12},{1,5},{9... | collective-permute-start | bytes 1769480 | tf_op jit(solution)/shard_map/ppermute | solution.py:102
  73.7 6.9 %collective-permute-start = (f32[6,32,384]{2,1,0:T(8,128)}, f32[6,32,384]{2,1,0:T(8,128)S(1)}, u32[]{:S(2)}, u32[]{:S(2)}) collective-permute-start(f32[6,32,384]{2,1,0:T(8,128)} %get-tuple-element.24), channel_id=1, source_target_pairs={{0,2},{2,0},{1,3},{3,1},{4,6},{6,4},{5,7},{7,5},{8,10},{10,8},{9,1... | collective-permute-start | bytes 884744 | tf_op jit(solution)/shard_map/ppermute | solution.py:40
  86.4 9.8 %collective-permute-start.12 = (bf16[192,768]{1,0:T(8,128)(2,1)S(1)}, bf16[192,768]{1,0:T(8,128)(2,1)S(1)}, u32[]{:S(2)}, u32[]{:S(2)}) collective-permute-start(bf16[192,768]{1,0:T(8,128)(2,1)S(1)} %get-tuple-element.10), channel_id=1, source_target_pairs={{0,8},{8,16},{16,24},{24,28},{28,20},{20,12},{12,4},{4,0},{1,9},{9... | collective-permute-start | bytes 884744 | tf_op jit(solution)/shard_map/ppermute | solution.py:108
  88.0 9.8 %collective-permute-start.9 = (bf16[192,768]{1,0:T(8,128)(2,1)S(1)}, bf16[192,768]{1,0:T(8,128)(2,1)S(1)}, u32[]{:S(2)}, u32[]{:S(2)}) collective-permute-start(bf16[192,768]{1,0:T(8,128)(2,1)S(1)} %get-tuple-element.10), channel_id=1, source_target_pairs={{0,4},{8,0},{16,8},{24,16},{28,24},{20,28},{12,20},{4,12},{1,5},{9... | collective-permute-start | bytes 884744 | tf_op jit(solution)/shard_map/ppermute | solution.py:112
  96.2 9.0 %collective-permute-start.13 = (bf16[192,768]{1,0:T(8,128)(2,1)S(1)}, bf16[192,768]{1,0:T(8,128)(2,1)S(1)}, u32[]{:S(2)}, u32[]{:S(2)}) collective-permute-start(bf16[192,768]{1,0:T(8,128)(2,1)S(1)} %collective-permute-done.12), channel_id=1, source_target_pairs={{0,8},{8,16},{16,24},{24,28},{28,20},{20,12},{12,4},{4,0},{1,9},{9... | collective-permute-start | bytes 884744 | tf_op jit(solution)/shard_map/ppermute | solution.py:108
  97.8 9.0 %collective-permute-start.10 = (bf16[192,768]{1,0:T(8,128)(2,1)S(1)}, bf16[192,768]{1,0:T(8,128)(2,1)S(1)}, u32[]{:S(2)}, u32[]{:S(2)}) collective-permute-start(bf16[192,768]{1,0:T(8,128)(2,1)S(1)} %collective-permute-done.9), channel_id=1, source_target_pairs={{0,4},{8,0},{16,8},{24,16},{28,24},{20,28},{12,20},{4,12},{1,5},{9... | collective-permute-start | bytes 884744 | tf_op jit(solution)/shard_map/ppermute | solution.py:112
  105.2 8.1 %collective-permute-start.14 = (bf16[192,768]{1,0:T(8,128)(2,1)S(1)}, bf16[192,768]{1,0:T(8,128)(2,1)S(1)}, u32[]{:S(2)}, u32[]{:S(2)}) collective-permute-start(bf16[192,768]{1,0:T(8,128)(2,1)S(1)} %collective-permute-done.13), channel_id=1, source_target_pairs={{0,8},{8,16},{16,24},{24,28},{28,20},{20,12},{12,4},{4,0},{1,9},{9... | collective-permute-start | bytes 884744 | tf_op jit(solution)/shard_map/ppermute | solution.py:108
  106.8 8.8 %collective-permute-start.11 = (bf16[192,768]{1,0:T(8,128)(2,1)S(1)}, bf16[192,768]{1,0:T(8,128)(2,1)S(1)}, u32[]{:S(2)}, u32[]{:S(2)}) collective-permute-start(bf16[192,768]{1,0:T(8,128)(2,1)S(1)} %collective-permute-done.10), channel_id=1, source_target_pairs={{0,4},{8,0},{16,8},{24,16},{28,24},{20,28},{12,20},{4,12},{1,5},{9... | collective-permute-start | bytes 884744 | tf_op jit(solution)/shard_map/ppermute | solution.py:112
  113.3 6.7 %collective-permute-start.15 = (bf16[192,768]{1,0:T(8,128)(2,1)S(1)}, bf16[192,768]{1,0:T(8,128)(2,1)S(1)}, u32[]{:S(2)}, u32[]{:S(2)}) collective-permute-start(bf16[192,768]{1,0:T(8,128)(2,1)S(1)} %collective-permute-done.14), channel_id=1, source_target_pairs={{0,8},{8,16},{16,24},{24,28},{28,20},{20,12},{12,4},{4,0},{1,9},{9... | collective-permute-start | bytes 884744 | tf_op jit(solution)/shard_map/ppermute | solution.py:108
  146.1 9.1 %collective-permute-start.18 = (bf16[192,768]{1,0:T(8,128)(2,1)S(1)}, bf16[192,768]{1,0:T(8,128)(2,1)S(1)}, u32[]{:S(2)}, u32[]{:S(2)}) collective-permute-start(bf16[192,768]{1,0:T(8,128)(2,1)S(1)} %get-tuple-element.15), channel_id=1, source_target_pairs={{0,8},{8,16},{16,24},{24,28},{28,20},{20,12},{12,4},{4,0},{1,9},{9... | collective-permute-start | bytes 884744 | tf_op jit(solution)/shard_map/ppermute | solution.py:92
  155.3 14.6 %collective-permute-start.19 = (f32[192,768]{1,0:T(8,128)S(1)}, f32[192,768]{1,0:T(8,128)S(1)}, u32[]{:S(2)}, u32[]{:S(2)}) collective-permute-start(f32[192,768]{1,0:T(8,128)S(1)} %convert_add_fusion.4), channel_id=1, source_target_pairs={{0,8},{8,16},{16,24},{24,28},{28,20},{20,12},{12,4},{4,0},{1,9},{9... | collective-permute-start | bytes 1769480 | tf_op jit(solution)/shard_map/ppermute | solution.py:95
  156.9 7.9 %collective-permute-start.22 = (bf16[192,768]{1,0:T(8,128)(2,1)S(1)}, bf16[192,768]{1,0:T(8,128)(2,1)S(1)}, u32[]{:S(2)}, u32[]{:S(2)}) collective-permute-start(bf16[192,768]{1,0:T(8,128)(2,1)S(1)} %get-tuple-element.16), channel_id=1, source_target_pairs={{0,4},{8,0},{16,8},{24,16},{28,24},{20,28},{12,20},{4,12},{1,5},{9... | collective-permute-start | bytes 884744 | tf_op jit(solution)/shard_map/ppermute | solution.py:99
  170.0 13.7 %collective-permute-start.20 = (f32[192,768]{1,0:T(8,128)S(1)}, f32[192,768]{1,0:T(8,128)S(1)}, u32[]{:S(2)}, u32[]{:S(2)}) collective-permute-start(f32[192,768]{1,0:T(8,128)S(1)} %get-tuple-element.13), channel_id=1, source_target_pairs={{0,8},{8,16},{16,24},{24,28},{28,20},{20,12},{12,4},{4,0},{1,9},{9... | collective-permute-start | bytes 1769480 | tf_op jit(solution)/shard_map/ppermute | solution.py:95
  171.6 13.3 %collective-permute-start.23 = (f32[192,768]{1,0:T(8,128)S(1)}, f32[192,768]{1,0:T(8,128)S(1)}, u32[]{:S(2)}, u32[]{:S(2)}) collective-permute-start(f32[192,768]{1,0:T(8,128)S(1)} %get-tuple-element.14), channel_id=1, source_target_pairs={{0,4},{8,0},{16,8},{24,16},{28,24},{20,28},{12,20},{4,12},{1,5},{9... | collective-permute-start | bytes 1769480 | tf_op jit(solution)/shard_map/ppermute | solution.py:102
  185.0 12.5 %collective-permute-start.21 = (f32[192,768]{1,0:T(8,128)S(1)}, f32[192,768]{1,0:T(8,128)S(1)}, u32[]{:S(2)}, u32[]{:S(2)}) collective-permute-start(f32[192,768]{1,0:T(8,128)S(1)} %get-tuple-element.11), channel_id=1, source_target_pairs={{0,8},{8,16},{16,24},{24,28},{28,20},{20,12},{12,4},{4,0},{1,9},{9... | collective-permute-start | bytes 1769480 | tf_op jit(solution)/shard_map/ppermute | solution.py:95
  186.6 12.7 %collective-permute-start.24 = (f32[192,768]{1,0:T(8,128)S(1)}, f32[192,768]{1,0:T(8,128)S(1)}, u32[]{:S(2)}, u32[]{:S(2)}) collective-permute-start(f32[192,768]{1,0:T(8,128)S(1)} %get-tuple-element.12), channel_id=1, source_target_pairs={{0,4},{8,0},{16,8},{24,16},{28,24},{20,28},{12,20},{4,12},{1,5},{9... | collective-permute-start | bytes 1769480 | tf_op jit(solution)/shard_map/ppermute | solution.py:102
  199.5 9.9 %collective-permute-start.28 = (bf16[192,768]{1,0:T(8,128)(2,1)S(1)}, bf16[192,768]{1,0:T(8,128)(2,1)S(1)}, u32[]{:S(2)}, u32[]{:S(2)}) collective-permute-start(bf16[192,768]{1,0:T(8,128)(2,1)S(1)} %get-tuple-element.6), channel_id=1, source_target_pairs={{0,8},{8,16},{16,24},{24,28},{28,20},{20,12},{12,4},{4,0},{1,9},{9... | collective-permute-start | bytes 884744 | tf_op jit(solution)/shard_map/ppermute | solution.py:108
  200.6 9.7 %collective-permute-start.25 = (bf16[192,768]{1,0:T(8,128)(2,1)S(1)}, bf16[192,768]{1,0:T(8,128)(2,1)S(1)}, u32[]{:S(2)}, u32[]{:S(2)}) collective-permute-start(bf16[192,768]{1,0:T(8,128)(2,1)S(1)} %get-tuple-element.6), channel_id=1, source_target_pairs={{0,4},{8,0},{16,8},{24,16},{28,24},{20,28},{12,20},{4,12},{1,5},{9... | collective-permute-start | bytes 884744 | tf_op jit(solution)/shard_map/ppermute | solution.py:112
  209.4 9.0 %collective-permute-start.29 = (bf16[192,768]{1,0:T(8,128)(2,1)S(1)}, bf16[192,768]{1,0:T(8,128)(2,1)S(1)}, u32[]{:S(2)}, u32[]{:S(2)}) collective-permute-start(bf16[192,768]{1,0:T(8,128)(2,1)S(1)} %collective-permute-done.28), channel_id=1, source_target_pairs={{0,8},{8,16},{16,24},{24,28},{28,20},{20,12},{12,4},{4,0},{1,9},{9... | collective-permute-start | bytes 884744 | tf_op jit(solution)/shard_map/ppermute | solution.py:108
  210.4 9.2 %collective-permute-start.26 = (bf16[192,768]{1,0:T(8,128)(2,1)S(1)}, bf16[192,768]{1,0:T(8,128)(2,1)S(1)}, u32[]{:S(2)}, u32[]{:S(2)}) collective-permute-start(bf16[192,768]{1,0:T(8,128)(2,1)S(1)} %collective-permute-done.25), channel_id=1, source_target_pairs={{0,4},{8,0},{16,8},{24,16},{28,24},{20,28},{12,20},{4,12},{1,5},{9... | collective-permute-start | bytes 884744 | tf_op jit(solution)/shard_map/ppermute | solution.py:112
  218.5 8.2 %collective-permute-start.30 = (bf16[192,768]{1,0:T(8,128)(2,1)S(1)}, bf16[192,768]{1,0:T(8,128)(2,1)S(1)}, u32[]{:S(2)}, u32[]{:S(2)}) collective-permute-start(bf16[192,768]{1,0:T(8,128)(2,1)S(1)} %collective-permute-done.29), channel_id=1, source_target_pairs={{0,8},{8,16},{16,24},{24,28},{28,20},{20,12},{12,4},{4,0},{1,9},{9... | collective-permute-start | bytes 884744 | tf_op jit(solution)/shard_map/ppermute | solution.py:108
  219.6 8.6 %collective-permute-start.27 = (bf16[192,768]{1,0:T(8,128)(2,1)S(1)}, bf16[192,768]{1,0:T(8,128)(2,1)S(1)}, u32[]{:S(2)}, u32[]{:S(2)}) collective-permute-start(bf16[192,768]{1,0:T(8,128)(2,1)S(1)} %collective-permute-done.26), channel_id=1, source_target_pairs={{0,4},{8,0},{16,8},{24,16},{28,24},{20,28},{12,20},{4,12},{1,5},{9... | collective-permute-start | bytes 884744 | tf_op jit(solution)/shard_map/ppermute | solution.py:112
  226.7 6.7 %collective-permute-start.31 = (bf16[192,768]{1,0:T(8,128)(2,1)S(1)}, bf16[192,768]{1,0:T(8,128)(2,1)S(1)}, u32[]{:S(2)}, u32[]{:S(2)}) collective-permute-start(bf16[192,768]{1,0:T(8,128)(2,1)S(1)} %collective-permute-done.30), channel_id=1, source_target_pairs={{0,8},{8,16},{16,24},{24,28},{28,20},{20,12},{12,4},{4,0},{1,9},{9... | collective-permute-start | bytes 884744 | tf_op jit(solution)/shard_map/ppermute | solution.py:108
  243.9 25.3 %collective-permute-start.33 = (f32[64,32,128]{2,1,0:T(8,128)S(1)}, f32[64,32,128]{2,1,0:T(8,128)S(1)}, u32[]{:S(2)}, u32[]{:S(2)}) collective-permute-start(f32[64,32,128]{2,1,0:T(8,128)S(1)} %multiply_select_fusion), channel_id=1, source_target_pairs={{0,2},{2,0},{1,3},{3,1},{4,6},{6,4},{5,7},{7,5},{8,10},{10,8},{9,1... | collective-permute-start | bytes 3145736 | tf_op jit(solution)/shard_map/ppermute | solution.py:133
  269.6 4.2 %collective-permute-start.34 = (f32[64,64,128]{2,1,0:T(8,128)S(1)}, f32[64,64,128]{2,1,0:T(8,128)S(1)}, u32[]{:S(2)}, u32[]{:S(2)}) collective-permute-start(f32[64,64,128]{2,1,0:T(8,128)S(1)} %maximum_select_fusion.1), channel_id=1, source_target_pairs={{0,1},{1,0},{2,3},{3,2},{4,5},{5,4},{6,7},{7,6},{8,9},{9,8},{10,11... | collective-permute-start | bytes 6291464 | tf_op jit(solution)/shard_map/ppermute | solution.py:139
  (10 other events, 105.9 us)

commit v13 on v11

--- a/solution.py
+++ b/solution.py
@@ -58,6 +58,7 @@
     backward = [(ring[k], ring[(k - 1) % owners]) for k in range(owners)]
     forward_steps = owners // 2
     ring_table = jnp.asarray(ring_pos, dtype=jnp.int32)
+    ring_order = jnp.asarray(ring, dtype=jnp.int32)
     here = ring_table[lax.axis_index("snp")]
     rel_owner = (ring_table[slot_ids // own_slots] - here) % owners
     ring_slot = rel_owner * own_slots + slot_ids % own_slots
@@ -73,6 +74,30 @@
         lax.dynamic_slice_in_dim(w_half, start, share, 0),
         jnp.float32(0.0),
     )
+    def ring_predict(dense):
+        partial = jnp.einsum(
+            "jbpk,sbk->jps", dense, geno_blocks, preferred_element_type=jnp.float32
+        ).astype(jnp.bfloat16)
+        partial = partial.reshape(owners, own_slots * half_p, sample_count)
+
+        def owner_block(distance):
+            owner = ring_order[(here + distance) % owners]
+            return lax.dynamic_index_in_dim(partial, owner, 0, keepdims=False)
+
+        ahead = lax.ppermute(owner_block(forward_steps), "snp", forward).astype(jnp.float32)
+        for step in range(2, forward_steps + 1):
+            carry = ahead + owner_block(forward_steps - step + 1).astype(jnp.float32)
+            ahead = lax.ppermute(carry, "snp", forward)
+        prediction = owner_block(0).astype(jnp.float32) + ahead
+        behind_steps = owners - 1 - forward_steps
+        if behind_steps > 0:
+            behind = lax.ppermute(owner_block(-behind_steps), "snp", backward).astype(jnp.float32)
+            for step in range(2, behind_steps + 1):
+                carry = behind + owner_block(step - behind_steps - 1).astype(jnp.float32)
+                behind = lax.ppermute(carry, "snp", backward)
+            prediction = prediction + behind
+        return prediction
+
     for sweep in range(ITERS):
         dense = jnp.einsum(
             "ec,epk->cpk", cell_hot, weight_bf, preferred_element_type=jnp.float32
@@ -94,7 +119,7 @@
         if sweep == 0:
             prediction = jnp.concatenate([predict(genotypes), predict(geno_peer)], axis=1)
         else:
-            prediction = predict(geno)
+            prediction = ring_predict(dense)
         residual = (resp - prediction).astype(jnp.bfloat16)
         received = {0: residual}
         moving = residual

time: 265 us -> 280 us (1.057)
  blocking collectives: 59.4 us -> 0 us
  waiting for transfers between devices: 128 us -> 168 us
  between operations: 1.02 us -> 24 us
  starting transfers between devices: 30.1 us -> 35.9 us
  other arithmetic: 15.1 us -> 20.2 us
    all_to_all x1 -> x0, blocking collectives: 59.4 us -> none  [predict(): gathered = lax.all_to_all(partial, 'snp', 0, 0, tiled=False)]
    ppermute x0 -> x7, waiting for transfers between devices: none -> 36.2 us  [the longest x3 23.9 us: ring_predict(): ahead = lax.ppermute(carry, 'snp', forward)]
    ppermute x0 -> x7, starting transfers between devices: none -> 6.13 us  [the longest x3 2.12 us: ring_predict(): ahead = lax.ppermute(carry, 'snp', forward)]
    add x0 -> x3, other arithmetic: none -> 5.47 us  [ring_predict(): carry = ahead + owner_block(forward_steps - step + 1).astype(jnp.float32)]
    ppermute x8, waiting for transfers between devices: 41 us -> 45.5 us  [per_device(): moving = lax.ppermute(moving, 'snp', forward)]
    dot_general x3 -> x2, matrix products: 6.82 us -> 4.62 us  [predict(): jnp.einsum('jbpk,sbk->jps', dense, samples.reshape(count, block_count, bl...]
  transfers between devices with their start and end apart: 23 -> 30, of which waited for: 18 -> 25; matrix products, arithmetic and copies ran while one was open for 3% -> 2% of each run, Pallas kernels for 0% -> 0%
where the time goes in v13:
time: 280 us; the launch traced here: 279 us
  waiting for transfers between devices  168 us (60%)
  starting transfers between devices  35.9 us (13%)
  between operations  24 us (9%)
  other arithmetic  20.2 us (7%)
  matrix products  16.2 us (6%)
  local copies, waits for them, and re-layouts  14.9 us (5%)
    ppermute x8, waiting for transfers between devices, per_device(): moving = lax.ppermute(moving, 'snp', forward)  45.5 us
    all_to_all x2, waiting for transfers between devices, predict(): gathered = lax.all_to_all(partial, 'snp', 0, 0, tiled=False)  39.6 us
    ppermute x3, waiting for transfers between devices, ring_predict(): ahead = lax.ppermute(carry, 'snp', forward)  23.9 us
    ppermute x1, waiting for transfers between devices, per_device(): other_half = lax.ppermute(own, 'sx', swap)  23.8 us
    ppermute x1, waiting for transfers between devices, per_device(): geno_peer = lax.ppermute(genotypes, 'sx', swap)  11.4 us
    all_to_all x2, starting transfers between devices, predict(): gathered = lax.all_to_all(partial, 'snp', 0, 0, tiled=False)  10.9 us
    ppermute x8, starting transfers between devices, per_device(): moving = lax.ppermute(moving, 'snp', forward)  8.29 us
    dot_general x2, matrix products, per_device(): jnp.einsum('jps,sbk->jpbk', blocks, geno_blocks, preferred_element_type=j...  7.99 us
  transfers between devices with their start and end apart: 30, of which 25 were waited for; matrix products, arithmetic and copies ran while one was open for 2% of the time, Pallas kernels for 0%

profile of v13, /device:TPU:0, one launch (start us, length us, event | category | flops | bytes accessed | tf_op | source)
XLA Modules:
  0.0 279.4 jit_solution(15357653159146458035)
XLA Ops:
  9.3 2.3 bitcast_convert_fusion.2
  11.6 7.3 %all-to-all-start = ((bf16[8,192,384]{2,1,0:T(8,128)(2,1)}), bf16[8,192,384]{2,1,0:T(8,128)(2,1)S(1)}, u32[]{:S(2)}, u32[]{:S(2)}) async-start(bf16[8,192,384]{2,1,0:T(8,128)(2,1)} %bitcast.235), calls=%async_computation | async-start | bytes 2359296 | tf_op jit(solution)/shard_map/all_to_all | solution.py:116
  20.4 11.4 %collective-permute-done.1 = bf16[384,640]{0,1:T(8,128)(2,1)S(1)} collective-permute-done((bf16[384,640]{0,1:T(8,128)(2,1)}, bf16[384,640]{0,1:T(8,128)(2,1)S(1)}, u32[]{:S(2)}, u32[]{:S(2)}) %collective-permute-start.1) | collective-permute-done | bytes 491552 | tf_op jit(solution)/shard_map/ppermute | solution.py:34
  32.6 2.3 bitcast_convert_fusion.1
  34.9 12.6 %all-to-all-done = bf16[8,192,384]{2,1,0:T(8,128)(2,1)S(1)} async-done(((bf16[8,192,384]{2,1,0:T(8,128)(2,1)}), bf16[8,192,384]{2,1,0:T(8,128)(2,1)S(1)}, u32[]{:S(2)}, u32[]{:S(2)}) %all-to-all-start) | async-done | bytes 1179680 | tf_op jit(solution)/shard_map/all_to_all | solution.py:116
  47.5 3.6 %all-to-all-start.1 = ((bf16[8,192,384]{2,1,0:T(8,128)(2,1)}), bf16[8,192,384]{2,1,0:T(8,128)(2,1)S(1)}, u32[]{:S(2)}, u32[]{:S(2)}) async-start(bf16[8,192,384]{2,1,0:T(8,128)(2,1)} %bitcast.234), calls=%async_computation.1 | async-start | bytes 2359296 | tf_op jit(solution)/shard_map/all_to_all | solution.py:116
  52.9 27.0 %all-to-all-done.1 = bf16[8,192,384]{2,1,0:T(8,128)(2,1)S(1)} async-done(((bf16[8,192,384]{2,1,0:T(8,128)(2,1)}), bf16[8,192,384]{2,1,0:T(8,128)(2,1)S(1)}, u32[]{:S(2)}, u32[]{:S(2)}) %all-to-all-start.1) | async-done | bytes 1179680 | tf_op jit(solution)/shard_map/all_to_all | solution.py:116
  82.2 5.8 %collective-permute-done.5 = bf16[192,768]{1,0:T(8,128)(2,1)S(1)} collective-permute-done((bf16[192,768]{1,0:T(8,128)(2,1)S(1)}, bf16[192,768]{1,0:T(8,128)(2,1)S(1)}, u32[]{:S(2)}, u32[]{:S(2)}) %collective-permute-start.5) | collective-permute-done | bytes 294944 | tf_op jit(solution)/shard_map/ppermute | solution.py:127
  91.3 3.7 %collective-permute-done.6 = bf16[192,768]{1,0:T(8,128)(2,1)S(1)} collective-permute-done((bf16[192,768]{1,0:T(8,128)(2,1)S(1)}, bf16[192,768]{1,0:T(8,128)(2,1)S(1)}, u32[]{:S(2)}, u32[]{:S(2)}) %collective-permute-start.6) | collective-permute-done | bytes 294944 | tf_op jit(solution)/shard_map/ppermute | solution.py:127
  97.2 4.6 %collective-permute-done.7 = bf16[192,768]{1,0:T(8,128)(2,1)S(1)} collective-permute-done((bf16[192,768]{1,0:T(8,128)(2,1)S(1)}, bf16[192,768]{1,0:T(8,128)(2,1)S(1)}, u32[]{:S(2)}, u32[]{:S(2)}) %collective-permute-start.7) | collective-permute-done | bytes 294944 | tf_op jit(solution)/shard_map/ppermute | solution.py:127
  103.4 5.5 %collective-permute-done.8 = bf16[192,768]{1,0:T(8,128)(2,1)S(1)} collective-permute-done((bf16[192,768]{1,0:T(8,128)(2,1)S(1)}, bf16[192,768]{1,0:T(8,128)(2,1)S(1)}, u32[]{:S(2)}, u32[]{:S(2)}) %collective-permute-start.8) | collective-permute-done | bytes 294944 | tf_op jit(solution)/shard_map/ppermute | solution.py:127
  109.0 4.0 %fusion.34 = f32[48,32,5,128]{3,1,2,0:T(8,128)} fusion(bf16[48,32,768,1]{2,1,3,0:T(8,128)(2,1)S(1)} %bitcast.242, bf16[768,5,128,1]{0,2,1,3:T(8,128)(2,1)S(1)} %bitcast.236), kind=kOutput, calls=%fused_computation.102 | convolution fusion | flops 1509949440 | bytes 7274496 | tf_op jit(solution)/shard_map/jps,sbk->jpbk/dot_general | solution.py:135
  113.0 3.0 %gather_fusion = f32[128,32,128]{2,1,0:T(8,128)S(1)} fusion(f32[48,32,5,128]{3,1,2,0:T(8,128)} %fusion.34, s32[128]{0:T(128)S(1)} %get-tuple-element.17), kind=kCustom, calls=%fused_computation | custom fusion | bytes 4195328 | tf_op jit(solution)/shard_map/gather | solution.py:138
  117.3 2.7 collective-permute-done.9
  120.1 4.1 %fusion.32 = (bf16[64,32,128]{2,1,0:T(8,128)(2,1)S(1)}, f32[64,32,128]{2,1,0:T(8,128)}) fusion(f32[64]{0:T(128)S(1)} %dynamic_slice.92, f32[64,32,128]{2,1,0:T(8,128)} %collective-permute-done.9, f32[2,64,32,128]{3,2,1,0:T(8,128)S(1)} %bitcast.216, s32[]{:T(128)S(6)} %select_n.240, f32[128,64,128]{2,1,0:T(8,128)} %param.11, s32[]{:T(128)S(6)} %select_n.225, ...), kind=kLoop, calls=%fused_computation.100 | loop fusion | flops 2883584 | bytes 4718924 | tf_op jit(solution)/shard_map/convert_element_type | solution.py:145
  138.2 2.2 bitcast_convert_fusion
  142.9 8.0 %collective-permute-done.11 = bf16[192,768]{1,0:T(8,128)(2,1)} collective-permute-done((bf16[192,768]{1,0:T(8,128)(2,1)S(1)}, bf16[192,768]{1,0:T(8,128)(2,1)}, u32[]{:S(2)}, u32[]{:S(2)}) %collective-permute-start.11) | collective-permute-done | bytes 294944 | tf_op jit(solution)/shard_map/ppermute | solution.py:87
  158.1 3.0 %collective-permute-done.15 = bf16[192,768]{1,0:T(8,128)(2,1)} collective-permute-done((bf16[192,768]{1,0:T(8,128)(2,1)}, bf16[192,768]{1,0:T(8,128)(2,1)}, u32[]{:S(2)}, u32[]{:S(2)}) %collective-permute-start.15) | collective-permute-done | bytes 294944 | tf_op jit(solution)/shard_map/ppermute | solution.py:94
  161.1 6.0 %collective-permute-done.12 = f32[192,768]{1,0:T(8,128)} collective-permute-done((f32[192,768]{1,0:T(8,128)S(1)}, f32[192,768]{1,0:T(8,128)}, u32[]{:S(2)}, u32[]{:S(2)}) %collective-permute-start.12) | collective-permute-done | bytes 589856 | tf_op jit(solution)/shard_map/ppermute | solution.py:90
  175.2 8.5 %collective-permute-done.13 = f32[192,768]{1,0:T(8,128)} collective-permute-done((f32[192,768]{1,0:T(8,128)}, f32[192,768]{1,0:T(8,128)}, u32[]{:S(2)}, u32[]{:S(2)}) %collective-permute-start.13) | collective-permute-done | bytes 589856 | tf_op jit(solution)/shard_map/ppermute | solution.py:90
  183.8 2.4 convert_add_fusion.2
  190.3 9.4 %collective-permute-done.14 = f32[192,768]{1,0:T(8,128)S(1)} collective-permute-done((f32[192,768]{1,0:T(8,128)}, f32[192,768]{1,0:T(8,128)S(1)}, u32[]{:S(2)}, u32[]{:S(2)}) %collective-permute-start.14) | collective-permute-done | bytes 589856 | tf_op jit(solution)/shard_map/ppermute | solution.py:90
  204.2 6.7 %collective-permute-done.21 = bf16[192,768]{1,0:T(8,128)(2,1)S(1)} collective-permute-done((bf16[192,768]{1,0:T(8,128)(2,1)S(1)}, bf16[192,768]{1,0:T(8,128)(2,1)S(1)}, u32[]{:S(2)}, u32[]{:S(2)}) %collective-permute-start.21) | collective-permute-done | bytes 294944 | tf_op jit(solution)/shard_map/ppermute | solution.py:127
  213.3 7.2 %collective-permute-done.22 = bf16[192,768]{1,0:T(8,128)(2,1)S(1)} collective-permute-done((bf16[192,768]{1,0:T(8,128)(2,1)S(1)}, bf16[192,768]{1,0:T(8,128)(2,1)S(1)}, u32[]{:S(2)}, u32[]{:S(2)}) %collective-permute-start.22) | collective-permute-done | bytes 294944 | tf_op jit(solution)/shard_map/ppermute | solution.py:127
  222.9 7.0 %collective-permute-done.23 = bf16[192,768]{1,0:T(8,128)(2,1)S(1)} collective-permute-done((bf16[192,768]{1,0:T(8,128)(2,1)S(1)}, bf16[192,768]{1,0:T(8,128)(2,1)S(1)}, u32[]{:S(2)}, u32[]{:S(2)}) %collective-permute-start.23) | collective-permute-done | bytes 294944 | tf_op jit(solution)/shard_map/ppermute | solution.py:127
  231.7 4.9 %collective-permute-done.24 = bf16[192,768]{1,0:T(8,128)(2,1)S(1)} collective-permute-done((bf16[192,768]{1,0:T(8,128)(2,1)S(1)}, bf16[192,768]{1,0:T(8,128)(2,1)S(1)}, u32[]{:S(2)}, u32[]{:S(2)}) %collective-permute-start.24) | collective-permute-done | bytes 294944 | tf_op jit(solution)/shard_map/ppermute | solution.py:127
  236.7 4.0 %fusion.35 = f32[48,32,5,128]{3,1,2,0:T(8,128)} fusion(bf16[48,32,768,1]{2,1,3,0:T(8,128)(2,1)S(1)} %bitcast.241, bf16[768,5,128,1]{0,2,1,3:T(8,128)(2,1)S(1)} %bitcast.238), kind=kOutput, calls=%fused_computation.103 | convolution fusion | flops 1509949440 | bytes 7274496 | tf_op jit(solution)/shard_map/jps,sbk->jpbk/dot_general | solution.py:135
  240.7 3.0 %gather_fusion.1 = f32[128,32,128]{2,1,0:T(8,128)S(1)} fusion(f32[48,32,5,128]{3,1,2,0:T(8,128)} %fusion.35, s32[128]{0:T(128)S(1)} %get-tuple-element.17), kind=kCustom, calls=%fused_computation.1 | custom fusion | bytes 4195328 | tf_op jit(solution)/shard_map/gather | solution.py:138
  243.9 2.6 collective-permute-done.25
  248.6 23.8 %collective-permute-done.26 = f32[64,32,128]{2,1,0:T(8,128)S(1)} collective-permute-done((f32[64,32,128]{2,1,0:T(8,128)S(1)}, f32[64,32,128]{2,1,0:T(8,128)S(1)}, u32[]{:S(2)}, u32[]{:S(2)}) %collective-permute-start.26) | collective-permute-done | bytes 1048608 | tf_op jit(solution)/shard_map/ppermute | solution.py:152
  272.8 4.1 %collective-permute-done.27 = f32[64,64,128]{2,1,0:T(8,128)S(1)} collective-permute-done((f32[64,64,128]{2,1,0:T(8,128)S(1)}, f32[64,64,128]{2,1,0:T(8,128)S(1)}, u32[]{:S(2)}, u32[]{:S(2)}) %collective-permute-start.27) | collective-permute-done | bytes 2097184 | tf_op jit(solution)/shard_map/ppermute | solution.py:158
  277.0 2.5 maximum_select_fusion
  (105 shorter events, 50.2 us)
Async XLA Ops:
  11.6 35.9 %all-to-all-start = ((bf16[8,192,384]{2,1,0:T(8,128)(2,1)}), bf16[8,192,384]{2,1,0:T(8,128)(2,1)S(1)}, u32[]{:S(2)}, u32[]{:S(2)}) async-start(bf16[8,192,384]{2,1,0:T(8,128)(2,1)} %bitcast.235), calls=%async_computation | async-start | bytes 2359296 | tf_op jit(solution)/shard_map/all_to_all | solution.py:116
  18.9 12.9 %collective-permute-start.1 = (bf16[384,640]{0,1:T(8,128)(2,1)}, bf16[384,640]{0,1:T(8,128)(2,1)S(1)}, u32[]{:S(2)}, u32[]{:S(2)}) collective-permute-start(bf16[384,640]{0,1:T(8,128)(2,1)} %copy-done.1), channel_id=1, source_target_pairs={{0,2},{2,0},{1,3},{3,1},{4,6},{6,4},{5,7},{7,5},{8,10},{10,8},{9,1... | collective-permute-start | bytes 1474568 | tf_op jit(solution)/shard_map/ppermute | solution.py:34
  47.5 32.4 %all-to-all-start.1 = ((bf16[8,192,384]{2,1,0:T(8,128)(2,1)}), bf16[8,192,384]{2,1,0:T(8,128)(2,1)S(1)}, u32[]{:S(2)}, u32[]{:S(2)}) async-start(bf16[8,192,384]{2,1,0:T(8,128)(2,1)} %bitcast.234), calls=%async_computation.1 | async-start | bytes 2359296 | tf_op jit(solution)/shard_map/all_to_all | solution.py:116
  51.1 28.9 %collective-permute-start = (f32[6,32,384]{2,1,0:T(8,128)S(1)}, f32[6,32,384]{2,1,0:T(8,128)S(1)}, u32[]{:S(2)}, u32[]{:S(2)}) collective-permute-start(f32[6,32,384]{2,1,0:T(8,128)S(1)} %get-tuple-element.16), channel_id=1, source_target_pairs={{0,2},{2,0},{1,3},{3,1},{4,6},{6,4},{5,7},{7,5},{8,10},{10,8},{9,1... | collective-permute-start | bytes 884744 | tf_op jit(solution)/shard_map/ppermute | solution.py:40
  80.1 7.9 %collective-permute-start.5 = (bf16[192,768]{1,0:T(8,128)(2,1)S(1)}, bf16[192,768]{1,0:T(8,128)(2,1)S(1)}, u32[]{:S(2)}, u32[]{:S(2)}) collective-permute-start(bf16[192,768]{1,0:T(8,128)(2,1)S(1)} %fusion.7), channel_id=1, source_target_pairs={{0,8},{8,16},{16,24},{24,28},{28,20},{20,12},{12,4},{4,0},{1,9},{9... | collective-permute-start | bytes 884744 | tf_op jit(solution)/shard_map/ppermute | solution.py:127
  80.2 8.1 %collective-permute-start.2 = (bf16[192,768]{1,0:T(8,128)(2,1)S(1)}, bf16[192,768]{1,0:T(8,128)(2,1)S(1)}, u32[]{:S(2)}, u32[]{:S(2)}) collective-permute-start(bf16[192,768]{1,0:T(8,128)(2,1)S(1)} %fusion.7), channel_id=1, source_target_pairs={{0,4},{8,0},{16,8},{24,16},{28,24},{20,28},{12,20},{4,12},{1,5},{9... | collective-permute-start | bytes 884744 | tf_op jit(solution)/shard_map/ppermute | solution.py:131
  88.0 7.0 %collective-permute-start.6 = (bf16[192,768]{1,0:T(8,128)(2,1)S(1)}, bf16[192,768]{1,0:T(8,128)(2,1)S(1)}, u32[]{:S(2)}, u32[]{:S(2)}) collective-permute-start(bf16[192,768]{1,0:T(8,128)(2,1)S(1)} %collective-permute-done.5), channel_id=1, source_target_pairs={{0,8},{8,16},{16,24},{24,28},{28,20},{20,12},{12,4},{4,0},{1,9},{9... | collective-permute-start | bytes 884744 | tf_op jit(solution)/shard_map/ppermute | solution.py:127
  88.2 8.0 %collective-permute-start.3 = (bf16[192,768]{1,0:T(8,128)(2,1)S(1)}, bf16[192,768]{1,0:T(8,128)(2,1)S(1)}, u32[]{:S(2)}, u32[]{:S(2)}) collective-permute-start(bf16[192,768]{1,0:T(8,128)(2,1)S(1)} %collective-permute-done.2), channel_id=1, source_target_pairs={{0,4},{8,0},{16,8},{24,16},{28,24},{20,28},{12,20},{4,12},{1,5},{9... | collective-permute-start | bytes 884744 | tf_op jit(solution)/shard_map/ppermute | solution.py:131
  91.2 17.8 %copy-start.2 = (bf16[768,640]{0,1:T(8,128)(2,1)}, bf16[768,640]{0,1:T(8,128)(2,1)S(1)}, u32[]{:S(2)}) copy-start(bf16[768,640]{0,1:T(8,128)(2,1)S(1)} %pad_maximum_fusion) | copy-start | bytes 2949124
  95.0 6.7 %collective-permute-start.7 = (bf16[192,768]{1,0:T(8,128)(2,1)S(1)}, bf16[192,768]{1,0:T(8,128)(2,1)S(1)}, u32[]{:S(2)}, u32[]{:S(2)}) collective-permute-start(bf16[192,768]{1,0:T(8,128)(2,1)S(1)} %collective-permute-done.6), channel_id=1, source_target_pairs={{0,8},{8,16},{16,24},{24,28},{28,20},{20,12},{12,4},{4,0},{1,9},{9... | collective-permute-start | bytes 884744 | tf_op jit(solution)/shard_map/ppermute | solution.py:127
  96.2 7.2 %collective-permute-start.4 = (bf16[192,768]{1,0:T(8,128)(2,1)S(1)}, bf16[192,768]{1,0:T(8,128)(2,1)S(1)}, u32[]{:S(2)}, u32[]{:S(2)}) collective-permute-start(bf16[192,768]{1,0:T(8,128)(2,1)S(1)} %collective-permute-done.3), channel_id=1, source_target_pairs={{0,4},{8,0},{16,8},{24,16},{28,24},{20,28},{12,20},{4,12},{1,5},{9... | collective-permute-start | bytes 884744 | tf_op jit(solution)/shard_map/ppermute | solution.py:131
  101.7 7.2 %collective-permute-start.8 = (bf16[192,768]{1,0:T(8,128)(2,1)S(1)}, bf16[192,768]{1,0:T(8,128)(2,1)S(1)}, u32[]{:S(2)}, u32[]{:S(2)}) collective-permute-start(bf16[192,768]{1,0:T(8,128)(2,1)S(1)} %collective-permute-done.7), channel_id=1, source_target_pairs={{0,8},{8,16},{16,24},{24,28},{28,20},{20,12},{12,4},{4,0},{1,9},{9... | collective-permute-start | bytes 884744 | tf_op jit(solution)/shard_map/ppermute | solution.py:127
  117.1 3.0 %collective-permute-start.9 = (f32[64,32,128]{2,1,0:T(8,128)}, f32[64,32,128]{2,1,0:T(8,128)}, u32[]{:S(2)}, u32[]{:S(2)}) collective-permute-start(f32[64,32,128]{2,1,0:T(8,128)} %dynamic-slice_bitcast_fusion.1), channel_id=1, source_target_pairs={{0,1},{1,0},{2,3},{3,2},{4,5},{5,4},{6,7},{7,6},{8,9},{9,8},{10,11... | collective-permute-start | bytes 3145736 | tf_op jit(solution)/shard_map/ppermute | solution.py:142
  124.2 11.9 %collective-permute-start.10 = (bf16[64,32,128]{2,1,0:T(8,128)(2,1)S(1)}, bf16[64,32,128]{2,1,0:T(8,128)(2,1)S(1)}, u32[]{:S(2)}, u32[]{:S(2)}) collective-permute-start(bf16[64,32,128]{2,1,0:T(8,128)(2,1)S(1)} %get-tuple-element.7), channel_id=1, source_target_pairs={{0,1},{1,0},{2,3},{3,2},{4,5},{5,4},{6,7},{7,6},{8,9},{9,8},{10,11... | collective-permute-start | bytes 1572872 | tf_op jit(solution)/shard_map/ppermute | solution.py:146
  141.2 9.7 %collective-permute-start.11 = (bf16[192,768]{1,0:T(8,128)(2,1)S(1)}, bf16[192,768]{1,0:T(8,128)(2,1)}, u32[]{:S(2)}, u32[]{:S(2)}) collective-permute-start(bf16[192,768]{1,0:T(8,128)(2,1)S(1)} %get-tuple-element.13), channel_id=1, source_target_pairs={{0,8},{8,16},{16,24},{24,28},{28,20},{20,12},{12,4},{4,0},{1,9},{9... | collective-permute-start | bytes 884744 | tf_op jit(solution)/shard_map/ppermute | solution.py:87
  152.0 15.2 %collective-permute-start.12 = (f32[192,768]{1,0:T(8,128)S(1)}, f32[192,768]{1,0:T(8,128)}, u32[]{:S(2)}, u32[]{:S(2)}) collective-permute-start(f32[192,768]{1,0:T(8,128)S(1)} %convert_add_fusion.4), channel_id=1, source_target_pairs={{0,8},{8,16},{16,24},{24,28},{28,20},{20,12},{12,4},{4,0},{1,9},{9... | collective-permute-start | bytes 1769480 | tf_op jit(solution)/shard_map/ppermute | solution.py:90
  152.0 9.1 %collective-permute-start.15 = (bf16[192,768]{1,0:T(8,128)(2,1)}, bf16[192,768]{1,0:T(8,128)(2,1)}, u32[]{:S(2)}, u32[]{:S(2)}) collective-permute-start(bf16[192,768]{1,0:T(8,128)(2,1)} %get-tuple-element.14), channel_id=1, source_target_pairs={{0,4},{8,0},{16,8},{24,16},{28,24},{20,28},{12,20},{4,12},{1,5},{9... | collective-permute-start | bytes 884744 | tf_op jit(solution)/shard_map/ppermute | solution.py:94
  169.2 14.5 %collective-permute-start.13 = (f32[192,768]{1,0:T(8,128)}, f32[192,768]{1,0:T(8,128)}, u32[]{:S(2)}, u32[]{:S(2)}) collective-permute-start(f32[192,768]{1,0:T(8,128)} %get-tuple-element.11), channel_id=1, source_target_pairs={{0,8},{8,16},{16,24},{24,28},{28,20},{20,12},{12,4},{4,0},{1,9},{9... | collective-permute-start | bytes 1769480 | tf_op jit(solution)/shard_map/ppermute | solution.py:90
  169.5 14.3 %collective-permute-start.16 = (f32[192,768]{1,0:T(8,128)S(1)}, f32[192,768]{1,0:T(8,128)}, u32[]{:S(2)}, u32[]{:S(2)}) collective-permute-start(f32[192,768]{1,0:T(8,128)S(1)} %get-tuple-element.12), channel_id=1, source_target_pairs={{0,4},{8,0},{16,8},{24,16},{28,24},{20,28},{12,20},{4,12},{1,5},{9... | collective-permute-start | bytes 1769480 | tf_op jit(solution)/shard_map/ppermute | solution.py:97
  186.2 13.5 %collective-permute-start.14 = (f32[192,768]{1,0:T(8,128)}, f32[192,768]{1,0:T(8,128)S(1)}, u32[]{:S(2)}, u32[]{:S(2)}) collective-permute-start(f32[192,768]{1,0:T(8,128)} %get-tuple-element.9), channel_id=1, source_target_pairs={{0,8},{8,16},{16,24},{24,28},{28,20},{20,12},{12,4},{4,0},{1,9},{9... | collective-permute-start | bytes 1769480 | tf_op jit(solution)/shard_map/ppermute | solution.py:90
  187.9 13.0 %collective-permute-start.17 = (f32[192,768]{1,0:T(8,128)}, f32[192,768]{1,0:T(8,128)}, u32[]{:S(2)}, u32[]{:S(2)}) collective-permute-start(f32[192,768]{1,0:T(8,128)} %get-tuple-element.10), channel_id=1, source_target_pairs={{0,4},{8,0},{16,8},{24,16},{28,24},{20,28},{12,20},{4,12},{1,5},{9... | collective-permute-start | bytes 1769480 | tf_op jit(solution)/shard_map/ppermute | solution.py:97
  202.2 34.6 %copy-start.4 = (bf16[768,640]{0,1:T(8,128)(2,1)S(1)}, bf16[768,640]{0,1:T(8,128)(2,1)}, u32[]{:S(2)}) copy-start(bf16[768,640]{0,1:T(8,128)(2,1)} %copy-done.2) | copy-start | bytes 2949124
  202.2 8.8 %collective-permute-start.21 = (bf16[192,768]{1,0:T(8,128)(2,1)S(1)}, bf16[192,768]{1,0:T(8,128)(2,1)S(1)}, u32[]{:S(2)}, u32[]{:S(2)}) collective-permute-start(bf16[192,768]{1,0:T(8,128)(2,1)S(1)} %get-tuple-element.6), channel_id=1, source_target_pairs={{0,8},{8,16},{16,24},{24,28},{28,20},{20,12},{12,4},{4,0},{1,9},{9... | collective-permute-start | bytes 884744 | tf_op jit(solution)/shard_map/ppermute | solution.py:127
  203.7 9.4 %collective-permute-start.18 = (bf16[192,768]{1,0:T(8,128)(2,1)S(1)}, bf16[192,768]{1,0:T(8,128)(2,1)S(1)}, u32[]{:S(2)}, u32[]{:S(2)}) collective-permute-start(bf16[192,768]{1,0:T(8,128)(2,1)S(1)} %get-tuple-element.6), channel_id=1, source_target_pairs={{0,4},{8,0},{16,8},{24,16},{28,24},{20,28},{12,20},{4,12},{1,5},{9... | collective-permute-start | bytes 884744 | tf_op jit(solution)/shard_map/ppermute | solution.py:131
  211.0 9.6 %collective-permute-start.22 = (bf16[192,768]{1,0:T(8,128)(2,1)S(1)}, bf16[192,768]{1,0:T(8,128)(2,1)S(1)}, u32[]{:S(2)}, u32[]{:S(2)}) collective-permute-start(bf16[192,768]{1,0:T(8,128)(2,1)S(1)} %collective-permute-done.21), channel_id=1, source_target_pairs={{0,8},{8,16},{16,24},{24,28},{28,20},{20,12},{12,4},{4,0},{1,9},{9... | collective-permute-start | bytes 884744 | tf_op jit(solution)/shard_map/ppermute | solution.py:127
  213.1 9.5 %collective-permute-start.19 = (bf16[192,768]{1,0:T(8,128)(2,1)S(1)}, bf16[192,768]{1,0:T(8,128)(2,1)S(1)}, u32[]{:S(2)}, u32[]{:S(2)}) collective-permute-start(bf16[192,768]{1,0:T(8,128)(2,1)S(1)} %collective-permute-done.18), channel_id=1, source_target_pairs={{0,4},{8,0},{16,8},{24,16},{28,24},{20,28},{12,20},{4,12},{1,5},{9... | collective-permute-start | bytes 884744 | tf_op jit(solution)/shard_map/ppermute | solution.py:131
  220.5 9.3 %collective-permute-start.23 = (bf16[192,768]{1,0:T(8,128)(2,1)S(1)}, bf16[192,768]{1,0:T(8,128)(2,1)S(1)}, u32[]{:S(2)}, u32[]{:S(2)}) collective-permute-start(bf16[192,768]{1,0:T(8,128)(2,1)S(1)} %collective-permute-done.22), channel_id=1, source_target_pairs={{0,8},{8,16},{16,24},{24,28},{28,20},{20,12},{12,4},{4,0},{1,9},{9... | collective-permute-start | bytes 884744 | tf_op jit(solution)/shard_map/ppermute | solution.py:127
  222.6 9.0 %collective-permute-start.20 = (bf16[192,768]{1,0:T(8,128)(2,1)S(1)}, bf16[192,768]{1,0:T(8,128)(2,1)S(1)}, u32[]{:S(2)}, u32[]{:S(2)}) collective-permute-start(bf16[192,768]{1,0:T(8,128)(2,1)S(1)} %collective-permute-done.19), channel_id=1, source_target_pairs={{0,4},{8,0},{16,8},{24,16},{28,24},{20,28},{12,20},{4,12},{1,5},{9... | collective-permute-start | bytes 884744 | tf_op jit(solution)/shard_map/ppermute | solution.py:131
  229.9 6.7 %collective-permute-start.24 = (bf16[192,768]{1,0:T(8,128)(2,1)S(1)}, bf16[192,768]{1,0:T(8,128)(2,1)S(1)}, u32[]{:S(2)}, u32[]{:S(2)}) collective-permute-start(bf16[192,768]{1,0:T(8,128)(2,1)S(1)} %collective-permute-done.23), channel_id=1, source_target_pairs={{0,8},{8,16},{16,24},{24,28},{28,20},{20,12},{12,4},{4,0},{1,9},{9... | collective-permute-start | bytes 884744 | tf_op jit(solution)/shard_map/ppermute | solution.py:127
  243.8 2.7 collective-permute-start.25
  247.1 25.3 %collective-permute-start.26 = (f32[64,32,128]{2,1,0:T(8,128)S(1)}, f32[64,32,128]{2,1,0:T(8,128)S(1)}, u32[]{:S(2)}, u32[]{:S(2)}) collective-permute-start(f32[64,32,128]{2,1,0:T(8,128)S(1)} %multiply_select_fusion), channel_id=1, source_target_pairs={{0,2},{2,0},{1,3},{3,1},{4,6},{6,4},{5,7},{7,5},{8,10},{10,8},{9,1... | collective-permute-start | bytes 3145736 | tf_op jit(solution)/shard_map/ppermute | solution.py:152
  272.8 4.2 %collective-permute-start.27 = (f32[64,64,128]{2,1,0:T(8,128)S(1)}, f32[64,64,128]{2,1,0:T(8,128)S(1)}, u32[]{:S(2)}, u32[]{:S(2)}) collective-permute-start(f32[64,64,128]{2,1,0:T(8,128)S(1)} %maximum_select_fusion.1), channel_id=1, source_target_pairs={{0,1},{1,0},{2,3},{3,2},{4,5},{5,4},{6,7},{7,6},{8,9},{9,8},{10,11... | collective-permute-start | bytes 6291464 | tf_op jit(solution)/shard_map/ppermute | solution.py:158
  (9 other events, 55.7 us)

commit v14 on v11

--- a/solution.py
+++ b/solution.py
@@ -97,14 +97,24 @@
             prediction = predict(geno)
         residual = (resp - prediction).astype(jnp.bfloat16)
         received = {0: residual}
-        moving = residual
-        for step in range(1, forward_steps + 1):
-            moving = lax.ppermute(moving, "snp", forward)
-            received[owners - step] = moving
-        moving = residual
-        for step in range(1, owners - forward_steps):
-            moving = lax.ppermute(moving, "snp", backward)
-            received[step] = moving
+        full_steps = owners - 1 - forward_steps
+        split_far = owners % 2 == 0 and full_steps > 0
+        ahead_moving = residual
+        behind_moving = residual
+        for step in range(1, full_steps + 1):
+            ahead_moving = lax.ppermute(ahead_moving, "snp", forward)
+            received[owners - step] = ahead_moving
+            behind_moving = lax.ppermute(behind_moving, "snp", backward)
+            received[step] = behind_moving
+        if split_far:
+            half_rows = residual.shape[0] // 2
+            first = lax.ppermute(ahead_moving[:half_rows], "snp", forward)
+            second = lax.ppermute(behind_moving[half_rows:], "snp", backward)
+            received[forward_steps] = jnp.concatenate([first, second], axis=0)
+        else:
+            for step in range(full_steps + 1, forward_steps + 1):
+                ahead_moving = lax.ppermute(ahead_moving, "snp", forward)
+                received[owners - step] = ahead_moving
         shard_rows = jnp.stack([received[d] for d in range(owners)])
         blocks = shard_rows.reshape(slot_total, half_p, sample_count)
         full = jnp.einsum(

time: 265 us -> 266 us (level)
  starting transfers between devices: 30.1 us -> 33.5 us
  waiting for transfers between devices: 128 us -> 125 us
    ppermute x14 -> x16, starting transfers between devices: 13.7 us -> 17.2 us  [the longest x6 10.5 us: per_device(): behind_moving = lax.ppermute(behind_moving, 'snp', backward)]
    ppermute x14 -> x16, waiting for transfers between devices: 42 us -> 39.5 us  [the longest x6 19.8 us: per_device(): behind_moving = lax.ppermute(behind_moving, 'snp', backward)]
  transfers between devices with their start and end apart: 23 -> 25, of which waited for: 18 -> 19; matrix products, arithmetic and copies ran while one was open for 3% -> 3% of each run, Pallas kernels for 0% -> 0%
where the time goes in v14:
time: 266 us
  waiting for transfers between devices  125 us (47%)
  blocking collectives  59.9 us (23%)
  starting transfers between devices  33.5 us (13%)
  matrix products  16.2 us (6%)
  other arithmetic  15.2 us (6%)
  local copies, waits for them, and re-layouts  14.7 us (6%)
    all_to_all x1, blocking collectives, predict(): gathered = lax.all_to_all(partial, 'snp', 0, 0, tiled=False)  59.9 us
    all_to_all x2, waiting for transfers between devices, predict(): gathered = lax.all_to_all(partial, 'snp', 0, 0, tiled=False)  39.1 us
    ppermute x1, waiting for transfers between devices, per_device(): other_half = lax.ppermute(own, 'sx', swap)  23.8 us
    ppermute x6, waiting for transfers between devices, per_device(): behind_moving = lax.ppermute(behind_moving, 'snp', backward)  19.8 us
    ppermute x6, waiting for transfers between devices, per_device(): ahead_moving = lax.ppermute(ahead_moving, 'snp', forward)  12.8 us
    all_to_all x2, starting transfers between devices, predict(): gathered = lax.all_to_all(partial, 'snp', 0, 0, tiled=False)  11.5 us
    ppermute x1, waiting for transfers between devices, per_device(): geno_peer = lax.ppermute(genotypes, 'sx', swap)  11.4 us
    ppermute x6, starting transfers between devices, per_device(): behind_moving = lax.ppermute(behind_moving, 'snp', backward)  10.5 us
  transfers between devices with their start and end apart: 25, of which 19 were waited for; matrix products, arithmetic and copies ran while one was open for 3% of the time, Pallas kernels for 0%

profile of v14, /device:TPU:0, one launch (start us, length us, event | category | flops | bytes accessed | tf_op | source)
XLA Modules:
  0.0 265.7 jit_solution(2954338057753694092)
XLA Ops:
  4.7 1.9 select_convert_fusion
  8.6 2.3 bitcast_convert_fusion.2
  10.9 7.3 %all-to-all-start = ((bf16[8,192,384]{2,1,0:T(8,128)(2,1)}), bf16[8,192,384]{2,1,0:T(8,128)(2,1)S(1)}, u32[]{:S(2)}, u32[]{:S(2)}) async-start(bf16[8,192,384]{2,1,0:T(8,128)(2,1)} %bitcast.210), calls=%async_computation | async-start | bytes 2359296 | tf_op jit(solution)/shard_map/all_to_all | solution.py:91
  19.7 11.4 %collective-permute-done.1 = bf16[384,640]{0,1:T(8,128)(2,1)S(1)} collective-permute-done((bf16[384,640]{0,1:T(8,128)(2,1)}, bf16[384,640]{0,1:T(8,128)(2,1)S(1)}, u32[]{:S(2)}, u32[]{:S(2)}) %collective-permute-start.1) | collective-permute-done | bytes 491552 | tf_op jit(solution)/shard_map/ppermute | solution.py:34
  31.9 2.3 bitcast_convert_fusion.1
  34.2 12.6 %all-to-all-done = bf16[8,192,384]{2,1,0:T(8,128)(2,1)S(1)} async-done(((bf16[8,192,384]{2,1,0:T(8,128)(2,1)}), bf16[8,192,384]{2,1,0:T(8,128)(2,1)S(1)}, u32[]{:S(2)}, u32[]{:S(2)}) %all-to-all-start) | async-done | bytes 1179680 | tf_op jit(solution)/shard_map/all_to_all | solution.py:91
  46.8 4.2 %all-to-all-start.1 = ((bf16[8,192,384]{2,1,0:T(8,128)(2,1)}), bf16[8,192,384]{2,1,0:T(8,128)(2,1)}, u32[]{:S(2)}, u32[]{:S(2)}) async-start(bf16[8,192,384]{2,1,0:T(8,128)(2,1)} %bitcast.209), calls=%async_computation.1 | async-start | bytes 2359296 | tf_op jit(solution)/shard_map/all_to_all | solution.py:91
  52.8 26.5 %all-to-all-done.1 = bf16[8,192,384]{2,1,0:T(8,128)(2,1)} async-done(((bf16[8,192,384]{2,1,0:T(8,128)(2,1)}), bf16[8,192,384]{2,1,0:T(8,128)(2,1)}, u32[]{:S(2)}, u32[]{:S(2)}) %all-to-all-start.1) | async-done | bytes 1179680 | tf_op jit(solution)/shard_map/all_to_all | solution.py:91
  83.0 5.1 %collective-permute-done.2 = bf16[192,768]{1,0:T(8,128)(2,1)} collective-permute-done((bf16[192,768]{1,0:T(8,128)(2,1)S(1)}, bf16[192,768]{1,0:T(8,128)(2,1)}, u32[]{:S(2)}, u32[]{:S(2)}) %collective-permute-start.2) | collective-permute-done | bytes 294944 | tf_op jit(solution)/shard_map/ppermute | solution.py:107
  88.2 2.2 collective-permute-start.3
  91.6 3.7 %collective-permute-done.3 = bf16[192,768]{1,0:T(8,128)(2,1)} collective-permute-done((bf16[192,768]{1,0:T(8,128)(2,1)}, bf16[192,768]{1,0:T(8,128)(2,1)}, u32[]{:S(2)}, u32[]{:S(2)}) %collective-permute-start.3) | collective-permute-done | bytes 294944 | tf_op jit(solution)/shard_map/ppermute | solution.py:107
  95.2 2.5 collective-permute-start.4
  99.7 5.3 %collective-permute-done.7 = bf16[192,768]{1,0:T(8,128)(2,1)S(1)} collective-permute-done((bf16[192,768]{1,0:T(8,128)(2,1)S(1)}, bf16[192,768]{1,0:T(8,128)(2,1)S(1)}, u32[]{:S(2)}, u32[]{:S(2)}) %collective-permute-start.7) | collective-permute-done | bytes 294944 | tf_op jit(solution)/shard_map/ppermute | solution.py:105
  105.1 2.2 collective-permute-start.9
  107.4 2.8 %collective-permute-done.8 = bf16[96,768]{1,0:T(8,128)(2,1)S(1)} collective-permute-done((bf16[96,768]{1,0:T(8,128)(2,1)S(1)}, bf16[96,768]{1,0:T(8,128)(2,1)S(1)}, u32[]{:S(2)}, u32[]{:S(2)}) %collective-permute-start.8) | collective-permute-done | bytes 147488 | tf_op jit(solution)/shard_map/ppermute | solution.py:111
  110.6 4.0 %fusion.33 = f32[48,32,5,128]{3,1,2,0:T(8,128)} fusion(bf16[48,32,768,1]{2,1,3,0:T(8,128)(2,1)S(1)} %bitcast.217, bf16[768,5,128,1]{0,2,1,3:T(8,128)(2,1)S(1)} %bitcast.211), kind=kOutput, calls=%fused_computation.97 | convolution fusion | flops 1509949440 | bytes 7274496 | tf_op jit(solution)/shard_map/jps,sbk->jpbk/dot_general | solution.py:120
  114.6 3.0 %gather_fusion = f32[128,32,128]{2,1,0:T(8,128)S(1)} fusion(f32[48,32,5,128]{3,1,2,0:T(8,128)} %fusion.33, s32[128]{0:T(128)S(1)} %get-tuple-element.9), kind=kCustom, calls=%fused_computation | custom fusion | bytes 4195328 | tf_op jit(solution)/shard_map/gather | solution.py:123
  118.9 2.7 %collective-permute-done.10 = f32[64,32,128]{2,1,0:T(8,128)} collective-permute-done((f32[64,32,128]{2,1,0:T(8,128)}, f32[64,32,128]{2,1,0:T(8,128)}, u32[]{:S(2)}, u32[]{:S(2)}) %collective-permute-start.10) | collective-permute-done | bytes 1048608 | tf_op jit(solution)/shard_map/ppermute | solution.py:127
  121.6 4.2 %fusion.32 = (bf16[64,32,128]{2,1,0:T(8,128)(2,1)S(1)}, f32[64,32,128]{2,1,0:T(8,128)}) fusion(f32[64]{0:T(128)S(1)} %dynamic_slice.43, f32[64,32,128]{2,1,0:T(8,128)} %collective-permute-done.10, f32[2,64,32,128]{3,2,1,0:T(8,128)S(1)} %bitcast.193, s32[]{:T(128)S(6)} %select_n.157, f32[128,64,128]{2,1,0:T(8,128)} %param.10, s32[]{:T(128)S(6)} %select_n.142, ...), kind=kLoop, calls=%fused_computation.96 | loop fusion | flops 2883584 | bytes 4718924 | tf_op jit(solution)/shard_map/convert_element_type | solution.py:130
  125.9 1.8 collective-permute-done.11
  129.8 2.2 bitcast_convert_fusion
  132.0 59.9 %all_to_all.15 = bf16[8,192,768]{2,1,0:T(8,128)(2,1)S(1)} all-to-all(bf16[8,192,768]{2,1,0:T(8,128)(2,1)S(1)} %bitcast.204), channel_id=1, replica_groups=mesh['snp'=8,'sx'=2,'sc'=2] {'snp'}, dimensions={0} | all-to-all | bytes 4718592 | tf_op jit(solution)/shard_map/all_to_all | solution.py:91
  194.4 5.6 %collective-permute-done.12 = bf16[192,768]{1,0:T(8,128)(2,1)S(1)} collective-permute-done((bf16[192,768]{1,0:T(8,128)(2,1)S(1)}, bf16[192,768]{1,0:T(8,128)(2,1)S(1)}, u32[]{:S(2)}, u32[]{:S(2)}) %collective-permute-start.12) | collective-permute-done | bytes 294944 | tf_op jit(solution)/shard_map/ppermute | solution.py:107
  202.1 5.3 %collective-permute-done.13 = bf16[192,768]{1,0:T(8,128)(2,1)S(1)} collective-permute-done((bf16[192,768]{1,0:T(8,128)(2,1)S(1)}, bf16[192,768]{1,0:T(8,128)(2,1)S(1)}, u32[]{:S(2)}, u32[]{:S(2)}) %collective-permute-start.13) | collective-permute-done | bytes 294944 | tf_op jit(solution)/shard_map/ppermute | solution.py:107
  209.5 7.4 %collective-permute-done.17 = bf16[192,768]{1,0:T(8,128)(2,1)S(1)} collective-permute-done((bf16[192,768]{1,0:T(8,128)(2,1)S(1)}, bf16[192,768]{1,0:T(8,128)(2,1)S(1)}, u32[]{:S(2)}, u32[]{:S(2)}) %collective-permute-start.17) | collective-permute-done | bytes 294944 | tf_op jit(solution)/shard_map/ppermute | solution.py:105
  219.1 3.0 %collective-permute-done.18 = bf16[96,768]{1,0:T(8,128)(2,1)S(1)} collective-permute-done((bf16[96,768]{1,0:T(8,128)(2,1)S(1)}, bf16[96,768]{1,0:T(8,128)(2,1)S(1)}, u32[]{:S(2)}, u32[]{:S(2)}) %collective-permute-start.18) | collective-permute-done | bytes 147488 | tf_op jit(solution)/shard_map/ppermute | solution.py:111
  223.0 4.0 %fusion.34 = f32[48,32,5,128]{3,1,2,0:T(8,128)} fusion(bf16[48,32,768,1]{2,1,3,0:T(8,128)(2,1)S(1)} %bitcast.216, bf16[768,5,128,1]{0,2,1,3:T(8,128)(2,1)S(1)} %bitcast.213), kind=kOutput, calls=%fused_computation.98 | convolution fusion | flops 1509949440 | bytes 7274496 | tf_op jit(solution)/shard_map/jps,sbk->jpbk/dot_general | solution.py:120
  227.0 3.0 %gather_fusion.1 = f32[128,32,128]{2,1,0:T(8,128)S(1)} fusion(f32[48,32,5,128]{3,1,2,0:T(8,128)} %fusion.34, s32[128]{0:T(128)S(1)} %get-tuple-element.9), kind=kCustom, calls=%fused_computation.1 | custom fusion | bytes 4195328 | tf_op jit(solution)/shard_map/gather | solution.py:123
  230.2 2.6 collective-permute-done.20
  234.8 23.8 %collective-permute-done.21 = f32[64,32,128]{2,1,0:T(8,128)S(1)} collective-permute-done((f32[64,32,128]{2,1,0:T(8,128)S(1)}, f32[64,32,128]{2,1,0:T(8,128)S(1)}, u32[]{:S(2)}, u32[]{:S(2)}) %collective-permute-start.21) | collective-permute-done | bytes 1048608 | tf_op jit(solution)/shard_map/ppermute | solution.py:137
  259.1 4.1 %collective-permute-done.22 = f32[64,64,128]{2,1,0:T(8,128)S(1)} collective-permute-done((f32[64,64,128]{2,1,0:T(8,128)S(1)}, f32[64,64,128]{2,1,0:T(8,128)S(1)}, u32[]{:S(2)}, u32[]{:S(2)}) %collective-permute-start.22) | collective-permute-done | bytes 2097184 | tf_op jit(solution)/shard_map/ppermute | solution.py:143
  263.3 2.5 maximum_select_fusion
  (93 shorter events, 33.1 us)
Async XLA Ops:
  8.6 2.3 copy-start.1
  10.9 35.9 %all-to-all-start = ((bf16[8,192,384]{2,1,0:T(8,128)(2,1)}), bf16[8,192,384]{2,1,0:T(8,128)(2,1)S(1)}, u32[]{:S(2)}, u32[]{:S(2)}) async-start(bf16[8,192,384]{2,1,0:T(8,128)(2,1)} %bitcast.210), calls=%async_computation | async-start | bytes 2359296 | tf_op jit(solution)/shard_map/all_to_all | solution.py:91
  18.2 12.9 %collective-permute-start.1 = (bf16[384,640]{0,1:T(8,128)(2,1)}, bf16[384,640]{0,1:T(8,128)(2,1)S(1)}, u32[]{:S(2)}, u32[]{:S(2)}) collective-permute-start(bf16[384,640]{0,1:T(8,128)(2,1)} %copy-done.1), channel_id=1, source_target_pairs={{0,2},{2,0},{1,3},{3,1},{4,6},{6,4},{5,7},{7,5},{8,10},{10,8},{9,1... | collective-permute-start | bytes 1474568 | tf_op jit(solution)/shard_map/ppermute | solution.py:34
  34.2 16.9 %copy-start.5 = (f32[384,384]{1,0:T(8,128)S(1)}, f32[384,384]{1,0:T(8,128)}, u32[]{:S(2)}) copy-start(f32[384,384]{1,0:T(8,128)} %param.9) | copy-start | bytes 1769476
  46.8 32.6 %all-to-all-start.1 = ((bf16[8,192,384]{2,1,0:T(8,128)(2,1)}), bf16[8,192,384]{2,1,0:T(8,128)(2,1)}, u32[]{:S(2)}, u32[]{:S(2)}) async-start(bf16[8,192,384]{2,1,0:T(8,128)(2,1)} %bitcast.209), calls=%async_computation.1 | async-start | bytes 2359296 | tf_op jit(solution)/shard_map/all_to_all | solution.py:91
  51.1 39.3 %copy-start.2 = (bf16[384,640]{0,1:T(8,128)(2,1)S(1)}, bf16[384,640]{0,1:T(8,128)(2,1)}, u32[]{:S(2)}) copy-start(bf16[384,640]{0,1:T(8,128)(2,1)} %copy-done.1) | copy-start | bytes 1474564
  51.1 29.7 %collective-permute-start = (f32[6,32,384]{2,1,0:T(8,128)S(1)}, f32[6,32,384]{2,1,0:T(8,128)S(1)}, u32[]{:S(2)}, u32[]{:S(2)}) collective-permute-start(f32[6,32,384]{2,1,0:T(8,128)S(1)} %get-tuple-element.8), channel_id=1, source_target_pairs={{0,2},{2,0},{1,3},{3,1},{4,6},{6,4},{5,7},{7,5},{8,10},{10,8},{9,1... | collective-permute-start | bytes 884744 | tf_op jit(solution)/shard_map/ppermute | solution.py:40
  80.9 7.2 %collective-permute-start.2 = (bf16[192,768]{1,0:T(8,128)(2,1)S(1)}, bf16[192,768]{1,0:T(8,128)(2,1)}, u32[]{:S(2)}, u32[]{:S(2)}) collective-permute-start(bf16[192,768]{1,0:T(8,128)(2,1)S(1)} %fusion.7), channel_id=1, source_target_pairs={{0,4},{8,0},{16,8},{24,16},{28,24},{20,28},{12,20},{4,12},{1,5},{9... | collective-permute-start | bytes 884744 | tf_op jit(solution)/shard_map/ppermute | solution.py:107
  82.3 8.1 %collective-permute-start.5 = (bf16[192,768]{1,0:T(8,128)(2,1)S(1)}, bf16[192,768]{1,0:T(8,128)(2,1)S(1)}, u32[]{:S(2)}, u32[]{:S(2)}) collective-permute-start(bf16[192,768]{1,0:T(8,128)(2,1)S(1)} %fusion.7), channel_id=1, source_target_pairs={{0,8},{8,16},{16,24},{24,28},{28,20},{20,12},{12,4},{4,0},{1,9},{9... | collective-permute-start | bytes 884744 | tf_op jit(solution)/shard_map/ppermute | solution.py:105
  88.2 7.1 %collective-permute-start.3 = (bf16[192,768]{1,0:T(8,128)(2,1)}, bf16[192,768]{1,0:T(8,128)(2,1)}, u32[]{:S(2)}, u32[]{:S(2)}) collective-permute-start(bf16[192,768]{1,0:T(8,128)(2,1)} %collective-permute-done.2), channel_id=1, source_target_pairs={{0,4},{8,0},{16,8},{24,16},{28,24},{20,28},{12,20},{4,12},{1,5},{9... | collective-permute-start | bytes 884744 | tf_op jit(solution)/shard_map/ppermute | solution.py:107
  90.4 7.4 %collective-permute-start.6 = (bf16[192,768]{1,0:T(8,128)(2,1)S(1)}, bf16[192,768]{1,0:T(8,128)(2,1)S(1)}, u32[]{:S(2)}, u32[]{:S(2)}) collective-permute-start(bf16[192,768]{1,0:T(8,128)(2,1)S(1)} %collective-permute-done.5), channel_id=1, source_target_pairs={{0,8},{8,16},{16,24},{24,28},{28,20},{20,12},{12,4},{4,0},{1,9},{9... | collective-permute-start | bytes 884744 | tf_op jit(solution)/shard_map/ppermute | solution.py:105
  91.5 19.1 %copy-start.3 = (bf16[768,640]{0,1:T(8,128)(2,1)}, bf16[768,640]{0,1:T(8,128)(2,1)S(1)}, u32[]{:S(2)}) copy-start(bf16[768,640]{0,1:T(8,128)(2,1)S(1)} %pad_maximum_fusion) | copy-start | bytes 2949124
  95.2 9.8 %collective-permute-start.4 = (bf16[192,768]{1,0:T(8,128)(2,1)}, bf16[192,768]{1,0:T(8,128)(2,1)S(1)}, u32[]{:S(2)}, u32[]{:S(2)}) collective-permute-start(bf16[192,768]{1,0:T(8,128)(2,1)} %collective-permute-done.3), channel_id=1, source_target_pairs={{0,4},{8,0},{16,8},{24,16},{28,24},{20,28},{12,20},{4,12},{1,5},{9... | collective-permute-start | bytes 884744 | tf_op jit(solution)/shard_map/ppermute | solution.py:107
  97.7 7.3 %collective-permute-start.7 = (bf16[192,768]{1,0:T(8,128)(2,1)S(1)}, bf16[192,768]{1,0:T(8,128)(2,1)S(1)}, u32[]{:S(2)}, u32[]{:S(2)}) collective-permute-start(bf16[192,768]{1,0:T(8,128)(2,1)S(1)} %collective-permute-done.6), channel_id=1, source_target_pairs={{0,8},{8,16},{16,24},{24,28},{28,20},{20,12},{12,4},{4,0},{1,9},{9... | collective-permute-start | bytes 884744 | tf_op jit(solution)/shard_map/ppermute | solution.py:105
  105.0 5.2 %collective-permute-start.8 = (bf16[96,768]{1,0:T(8,128)(2,1)S(1)}, bf16[96,768]{1,0:T(8,128)(2,1)S(1)}, u32[]{:S(2)}, u32[]{:S(2)}) collective-permute-start(bf16[96,768]{1,0:T(8,128)(2,1)S(1)} %slice.37), channel_id=1, source_target_pairs={{0,8},{8,16},{16,24},{24,28},{28,20},{20,12},{12,4},{4,0},{1,9},{9... | collective-permute-start | bytes 442376 | tf_op jit(solution)/shard_map/ppermute | solution.py:111
  105.1 5.4 %collective-permute-start.9 = (bf16[96,768]{1,0:T(8,128)(2,1)S(1)}, bf16[96,768]{1,0:T(8,128)(2,1)S(1)}, u32[]{:S(2)}, u32[]{:S(2)}) collective-permute-start(bf16[96,768]{1,0:T(8,128)(2,1)S(1)} %slice.38), channel_id=1, source_target_pairs={{0,4},{8,0},{16,8},{24,16},{28,24},{20,28},{12,20},{4,12},{1,5},{9... | collective-permute-start | bytes 442376 | tf_op jit(solution)/shard_map/ppermute | solution.py:112
  114.6 4.1 %copy-start.8 = (f32[46]{0:T(128)S(1)}, f32[46]{0:T(128)}, u32[]{:S(2)}) copy-start(f32[46]{0:T(128)} %param.14) | copy-start | bytes 556
  118.6 3.0 %collective-permute-start.10 = (f32[64,32,128]{2,1,0:T(8,128)}, f32[64,32,128]{2,1,0:T(8,128)}, u32[]{:S(2)}, u32[]{:S(2)}) collective-permute-start(f32[64,32,128]{2,1,0:T(8,128)} %dynamic-slice_bitcast_fusion.1), channel_id=1, source_target_pairs={{0,1},{1,0},{2,3},{3,2},{4,5},{5,4},{6,7},{7,6},{8,9},{9,8},{10,11... | collective-permute-start | bytes 3145736 | tf_op jit(solution)/shard_map/ppermute | solution.py:127
  125.8 1.9 collective-permute-start.11
  128.6 1.2 copy-start.4
  192.3 7.7 %collective-permute-start.12 = (bf16[192,768]{1,0:T(8,128)(2,1)S(1)}, bf16[192,768]{1,0:T(8,128)(2,1)S(1)}, u32[]{:S(2)}, u32[]{:S(2)}) collective-permute-start(bf16[192,768]{1,0:T(8,128)(2,1)S(1)} %subtract_convert_fusion), channel_id=1, source_target_pairs={{0,4},{8,0},{16,8},{24,16},{28,24},{20,28},{12,20},{4,12},{1,5},{9... | collective-permute-start | bytes 884744 | tf_op jit(solution)/shard_map/ppermute | solution.py:107
  193.8 7.7 %collective-permute-start.15 = (bf16[192,768]{1,0:T(8,128)(2,1)S(1)}, bf16[192,768]{1,0:T(8,128)(2,1)S(1)}, u32[]{:S(2)}, u32[]{:S(2)}) collective-permute-start(bf16[192,768]{1,0:T(8,128)(2,1)S(1)} %subtract_convert_fusion), channel_id=1, source_target_pairs={{0,8},{8,16},{16,24},{24,28},{28,20},{20,12},{12,4},{4,0},{1,9},{9... | collective-permute-start | bytes 884744 | tf_op jit(solution)/shard_map/ppermute | solution.py:105
  200.0 7.4 %collective-permute-start.13 = (bf16[192,768]{1,0:T(8,128)(2,1)S(1)}, bf16[192,768]{1,0:T(8,128)(2,1)S(1)}, u32[]{:S(2)}, u32[]{:S(2)}) collective-permute-start(bf16[192,768]{1,0:T(8,128)(2,1)S(1)} %collective-permute-done.12), channel_id=1, source_target_pairs={{0,4},{8,0},{16,8},{24,16},{28,24},{20,28},{12,20},{4,12},{1,5},{9... | collective-permute-start | bytes 884744 | tf_op jit(solution)/shard_map/ppermute | solution.py:107
  201.6 7.3 %collective-permute-start.16 = (bf16[192,768]{1,0:T(8,128)(2,1)S(1)}, bf16[192,768]{1,0:T(8,128)(2,1)S(1)}, u32[]{:S(2)}, u32[]{:S(2)}) collective-permute-start(bf16[192,768]{1,0:T(8,128)(2,1)S(1)} %collective-permute-done.15), channel_id=1, source_target_pairs={{0,8},{8,16},{16,24},{24,28},{28,20},{20,12},{12,4},{4,0},{1,9},{9... | collective-permute-start | bytes 884744 | tf_op jit(solution)/shard_map/ppermute | solution.py:105
  207.4 10.3 %collective-permute-start.14 = (bf16[192,768]{1,0:T(8,128)(2,1)S(1)}, bf16[192,768]{1,0:T(8,128)(2,1)S(1)}, u32[]{:S(2)}, u32[]{:S(2)}) collective-permute-start(bf16[192,768]{1,0:T(8,128)(2,1)S(1)} %collective-permute-done.13), channel_id=1, source_target_pairs={{0,4},{8,0},{16,8},{24,16},{28,24},{20,28},{12,20},{4,12},{1,5},{9... | collective-permute-start | bytes 884744 | tf_op jit(solution)/shard_map/ppermute | solution.py:107
  208.9 8.0 %collective-permute-start.17 = (bf16[192,768]{1,0:T(8,128)(2,1)S(1)}, bf16[192,768]{1,0:T(8,128)(2,1)S(1)}, u32[]{:S(2)}, u32[]{:S(2)}) collective-permute-start(bf16[192,768]{1,0:T(8,128)(2,1)S(1)} %collective-permute-done.16), channel_id=1, source_target_pairs={{0,8},{8,16},{16,24},{24,28},{28,20},{20,12},{12,4},{4,0},{1,9},{9... | collective-permute-start | bytes 884744 | tf_op jit(solution)/shard_map/ppermute | solution.py:105
  216.9 5.2 %collective-permute-start.18 = (bf16[96,768]{1,0:T(8,128)(2,1)S(1)}, bf16[96,768]{1,0:T(8,128)(2,1)S(1)}, u32[]{:S(2)}, u32[]{:S(2)}) collective-permute-start(bf16[96,768]{1,0:T(8,128)(2,1)S(1)} %slice.39), channel_id=1, source_target_pairs={{0,8},{8,16},{16,24},{24,28},{28,20},{20,12},{12,4},{4,0},{1,9},{9... | collective-permute-start | bytes 442376 | tf_op jit(solution)/shard_map/ppermute | solution.py:111
  217.7 5.2 %collective-permute-start.19 = (bf16[96,768]{1,0:T(8,128)(2,1)S(1)}, bf16[96,768]{1,0:T(8,128)(2,1)S(1)}, u32[]{:S(2)}, u32[]{:S(2)}) collective-permute-start(bf16[96,768]{1,0:T(8,128)(2,1)S(1)} %slice.40), channel_id=1, source_target_pairs={{0,4},{8,0},{16,8},{24,16},{28,24},{20,28},{12,20},{4,12},{1,5},{9... | collective-permute-start | bytes 442376 | tf_op jit(solution)/shard_map/ppermute | solution.py:112
  230.0 2.8 %copy-start = (f32[64,32,128]{2,1,0:T(8,128)S(1)}, f32[64,32,128]{2,1,0:T(8,128)}, u32[]{:S(2)}) copy-start(f32[64,32,128]{2,1,0:T(8,128)} %get-tuple-element.6) | copy-start | bytes 3145732
  230.1 2.7 %collective-permute-start.20 = (f32[64,32,128]{2,1,0:T(8,128)S(1)}, f32[64,32,128]{2,1,0:T(8,128)S(1)}, u32[]{:S(2)}, u32[]{:S(2)}) collective-permute-start(f32[64,32,128]{2,1,0:T(8,128)S(1)} %dynamic-slice_bitcast_fusion), channel_id=1, source_target_pairs={{0,1},{1,0},{2,3},{3,2},{4,5},{5,4},{6,7},{7,6},{8,9},{9,8},{10,11... | collective-permute-start | bytes 3145736 | tf_op jit(solution)/shard_map/ppermute | solution.py:127
  233.4 25.3 %collective-permute-start.21 = (f32[64,32,128]{2,1,0:T(8,128)S(1)}, f32[64,32,128]{2,1,0:T(8,128)S(1)}, u32[]{:S(2)}, u32[]{:S(2)}) collective-permute-start(f32[64,32,128]{2,1,0:T(8,128)S(1)} %multiply_select_fusion), channel_id=1, source_target_pairs={{0,2},{2,0},{1,3},{3,1},{4,6},{6,4},{5,7},{7,5},{8,10},{10,8},{9,1... | collective-permute-start | bytes 3145736 | tf_op jit(solution)/shard_map/ppermute | solution.py:137
  259.0 4.2 %collective-permute-start.22 = (f32[64,64,128]{2,1,0:T(8,128)S(1)}, f32[64,64,128]{2,1,0:T(8,128)S(1)}, u32[]{:S(2)}, u32[]{:S(2)}) collective-permute-start(f32[64,64,128]{2,1,0:T(8,128)S(1)} %maximum_select_fusion.1), channel_id=1, source_target_pairs={{0,1},{1,0},{2,3},{3,2},{4,5},{5,4},{6,7},{7,6},{8,9},{9,8},{10,11... | collective-permute-start | bytes 6291464 | tf_op jit(solution)/shard_map/ppermute | solution.py:143
  (2 other events, 1.8 us)

commit v15 on v11

--- a/solution.py
+++ b/solution.py
@@ -91,21 +91,26 @@
             gathered = lax.all_to_all(partial, "snp", 0, 0, tiled=False)
             return jnp.sum(gathered.astype(jnp.float32), axis=0)
 
+        def ring_gather(residual):
+            received = {0: residual}
+            moving = residual
+            for step in range(1, forward_steps + 1):
+                moving = lax.ppermute(moving, "snp", forward)
+                received[owners - step] = moving
+            moving = residual
+            for step in range(1, owners - forward_steps):
+                moving = lax.ppermute(moving, "snp", backward)
+                received[step] = moving
+            return jnp.stack([received[d] for d in range(owners)])
+
         if sweep == 0:
-            prediction = jnp.concatenate([predict(genotypes), predict(geno_peer)], axis=1)
+            first = (resp[:, :quarter] - predict(genotypes)).astype(jnp.bfloat16)
+            first_rows = ring_gather(first)
+            second = (resp[:, quarter:] - predict(geno_peer)).astype(jnp.bfloat16)
+            shard_rows = jnp.concatenate([first_rows, ring_gather(second)], axis=2)
         else:
-            prediction = predict(geno)
-        residual = (resp - prediction).astype(jnp.bfloat16)
-        received = {0: residual}
-        moving = residual
-        for step in range(1, forward_steps + 1):
-            moving = lax.ppermute(moving, "snp", forward)
-            received[owners - step] = moving
-        moving = residual
-        for step in range(1, owners - forward_steps):
-            moving = lax.ppermute(moving, "snp", backward)
-            received[step] = moving
-        shard_rows = jnp.stack([received[d] for d in range(owners)])
+            residual = (resp - predict(geno)).astype(jnp.bfloat16)
+            shard_rows = ring_gather(residual)
         blocks = shard_rows.reshape(slot_total, half_p, sample_count)
         full = jnp.einsum(
             "jps,sbk->jpbk", blocks, geno_blocks, preferred_element_type=jnp.float32

time: 265 us -> 276 us (1.042)
  starting transfers between devices: 30.1 us -> 48.9 us
  waiting for transfers between devices: 128 us -> 115 us
  local copies, waits for them, and re-layouts: 14.7 us -> 19.1 us
    all_to_all x2, waiting for transfers between devices: 39.1 us -> 12.6 us  [predict(): gathered = lax.all_to_all(partial, 'snp', 0, 0, tiled=False)]
    ppermute x14 -> x21, starting transfers between devices: 13.7 us -> 33.2 us  [the longest x12 20.2 us: ring_gather(): moving = lax.ppermute(moving, 'snp', forward)]
    ppermute x14 -> x21, waiting for transfers between devices: 42 us -> 56.1 us  [the longest x12 36.6 us: ring_gather(): moving = lax.ppermute(moving, 'snp', forward)]
    unnamed x31 -> x43, local copies, waits for them, and re-layouts: 4.45 us -> 8.18 us
  transfers between devices with their start and end apart: 23 -> 30, of which waited for: 18 -> 20; matrix products, arithmetic and copies ran while one was open for 3% -> 4% of each run, Pallas kernels for 0% -> 0%
where the time goes in v15:
time: 276 us; the launch traced here: 275 us
  waiting for transfers between devices  115 us (42%)
  blocking collectives  58.7 us (21%)
  starting transfers between devices  48.9 us (18%)
  local copies, waits for them, and re-layouts  19.1 us (7%)
  matrix products  16.2 us (6%)
  other arithmetic  16 us (6%)
    all_to_all x1, blocking collectives, predict(): gathered = lax.all_to_all(partial, 'snp', 0, 0, tiled=False)  58.7 us
    ppermute x12, waiting for transfers between devices, ring_gather(): moving = lax.ppermute(moving, 'snp', forward)  36.6 us
    ppermute x1, waiting for transfers between devices, per_device(): other_half = lax.ppermute(own, 'sx', swap)  23.8 us
    ppermute x12, starting transfers between devices, ring_gather(): moving = lax.ppermute(moving, 'snp', forward)  20.2 us
    ppermute x9, waiting for transfers between devices, ring_gather(): moving = lax.ppermute(moving, 'snp', backward)  19.5 us
    ppermute x9, starting transfers between devices, ring_gather(): moving = lax.ppermute(moving, 'snp', backward)  13 us
    all_to_all x2, waiting for transfers between devices, predict(): gathered = lax.all_to_all(partial, 'snp', 0, 0, tiled=False)  12.6 us
    ppermute x1, waiting for transfers between devices, per_device(): geno_peer = lax.ppermute(genotypes, 'sx', swap)  11.4 us
  transfers between devices with their start and end apart: 30, of which 20 were waited for; matrix products, arithmetic and copies ran while one was open for 4% of the time, Pallas kernels for 0%

profile of v15, /device:TPU:0, one launch (start us, length us, event | category | flops | bytes accessed | tf_op | source)
XLA Modules:
  0.0 275.1 jit_solution(665275881806268860)
XLA Ops:
  8.6 2.3 bitcast_convert_fusion.2
  10.9 7.3 %all-to-all-start = ((bf16[8,192,384]{2,1,0:T(8,128)(2,1)}), bf16[8,192,384]{2,1,0:T(8,128)(2,1)S(1)}, u32[]{:S(2)}, u32[]{:S(2)}) async-start(bf16[8,192,384]{2,1,0:T(8,128)(2,1)} %bitcast.229), calls=%async_computation | async-start | bytes 2359296 | tf_op jit(solution)/shard_map/all_to_all | solution.py:91
  19.7 11.4 %collective-permute-done.8 = bf16[384,640]{0,1:T(8,128)(2,1)S(1)} collective-permute-done((bf16[384,640]{0,1:T(8,128)(2,1)}, bf16[384,640]{0,1:T(8,128)(2,1)S(1)}, u32[]{:S(2)}, u32[]{:S(2)}) %collective-permute-start.8) | collective-permute-done | bytes 491552 | tf_op jit(solution)/shard_map/ppermute | solution.py:34
  31.9 2.3 bitcast_convert_fusion.1
  34.2 12.6 %all-to-all-done = bf16[8,192,384]{2,1,0:T(8,128)(2,1)S(1)} async-done(((bf16[8,192,384]{2,1,0:T(8,128)(2,1)}), bf16[8,192,384]{2,1,0:T(8,128)(2,1)S(1)}, u32[]{:S(2)}, u32[]{:S(2)}) %all-to-all-start) | async-done | bytes 1179680 | tf_op jit(solution)/shard_map/all_to_all | solution.py:91
  47.8 3.6 %all-to-all-start.1 = ((bf16[8,192,384]{2,1,0:T(8,128)(2,1)}), bf16[8,192,384]{2,1,0:T(8,128)(2,1)S(1)}, u32[]{:S(2)}, u32[]{:S(2)}) async-start(bf16[8,192,384]{2,1,0:T(8,128)(2,1)} %bitcast.228), calls=%async_computation.1 | async-start | bytes 2359296 | tf_op jit(solution)/shard_map/all_to_all | solution.py:91
  54.9 2.1 collective-permute-start
  57.7 13.2 %collective-permute-done = bf16[192,384]{1,0:T(8,128)(2,1)S(1)} collective-permute-done((bf16[192,384]{1,0:T(8,128)(2,1)S(1)}, bf16[192,384]{1,0:T(8,128)(2,1)S(1)}, u32[]{:S(2)}, u32[]{:S(2)}) %collective-permute-start) | collective-permute-done | bytes 147488 | tf_op jit(solution)/shard_map/ppermute | solution.py:102
  70.9 4.7 %collective-permute-start.1 = (bf16[192,384]{1,0:T(8,128)(2,1)S(1)}, bf16[192,384]{1,0:T(8,128)(2,1)S(1)}, u32[]{:S(2)}, u32[]{:S(2)}) collective-permute-start(bf16[192,384]{1,0:T(8,128)(2,1)S(1)} %collective-permute-done), channel_id=1, source_target_pairs={{0,4},{8,0},{16,8},{24,16},{28,24},{20,28},{12,20},{4,12},{1,5},{9... | collective-permute-start | bytes 442376 | tf_op jit(solution)/shard_map/ppermute | solution.py:102
  75.7 8.2 %collective-permute-start.4 = (bf16[192,384]{1,0:T(8,128)(2,1)S(1)}, bf16[192,384]{1,0:T(8,128)(2,1)S(1)}, u32[]{:S(2)}, u32[]{:S(2)}) collective-permute-start(bf16[192,384]{1,0:T(8,128)(2,1)S(1)} %collective-permute-done.3), channel_id=1, source_target_pairs={{0,8},{8,16},{16,24},{24,28},{28,20},{20,12},{12,4},{4,0},{1,9},{9... | collective-permute-start | bytes 442376 | tf_op jit(solution)/shard_map/ppermute | solution.py:98
  84.6 2.4 collective-permute-done.1
  89.7 3.2 %collective-permute-done.5 = bf16[192,384]{1,0:T(8,128)(2,1)S(1)} collective-permute-done((bf16[192,384]{1,0:T(8,128)(2,1)S(1)}, bf16[192,384]{1,0:T(8,128)(2,1)S(1)}, u32[]{:S(2)}, u32[]{:S(2)}) %collective-permute-start.5) | collective-permute-done | bytes 147488 | tf_op jit(solution)/shard_map/ppermute | solution.py:98
  95.9 2.0 collective-permute-start.12
  104.4 3.8 %collective-permute-done.10 = bf16[192,384]{1,0:T(8,128)(2,1)S(1)} collective-permute-done((bf16[192,384]{1,0:T(8,128)(2,1)S(1)}, bf16[192,384]{1,0:T(8,128)(2,1)S(1)}, u32[]{:S(2)}, u32[]{:S(2)}) %collective-permute-start.10) | collective-permute-done | bytes 147488 | tf_op jit(solution)/shard_map/ppermute | solution.py:102
  110.3 4.3 %collective-permute-done.14 = bf16[192,384]{1,0:T(8,128)(2,1)S(1)} collective-permute-done((bf16[192,384]{1,0:T(8,128)(2,1)S(1)}, bf16[192,384]{1,0:T(8,128)(2,1)S(1)}, u32[]{:S(2)}, u32[]{:S(2)}) %collective-permute-start.14) | collective-permute-done | bytes 147488 | tf_op jit(solution)/shard_map/ppermute | solution.py:98
  115.4 4.3 %collective-permute-done.15 = bf16[192,384]{1,0:T(8,128)(2,1)S(1)} collective-permute-done((bf16[192,384]{1,0:T(8,128)(2,1)S(1)}, bf16[192,384]{1,0:T(8,128)(2,1)S(1)}, u32[]{:S(2)}, u32[]{:S(2)}) %collective-permute-start.15) | collective-permute-done | bytes 147488 | tf_op jit(solution)/shard_map/ppermute | solution.py:98
  121.5 4.0 %fusion.33 = f32[48,32,5,128]{3,1,2,0:T(8,128)} fusion(bf16[48,32,768,1]{2,1,3,0:T(8,128)(2,1)S(1)} %bitcast.222, bf16[768,5,128,1]{0,2,1,3:T(8,128)(2,1)S(1)} %bitcast.230), kind=kOutput, calls=%fused_computation.105 | convolution fusion | flops 1509949440 | bytes 7274496 | tf_op jit(solution)/shard_map/jps,sbk->jpbk/dot_general | solution.py:115
  125.4 3.0 %gather_fusion = f32[128,32,128]{2,1,0:T(8,128)S(1)} fusion(f32[48,32,5,128]{3,1,2,0:T(8,128)} %fusion.33, s32[128]{0:T(128)S(1)} %get-tuple-element.9), kind=kCustom, calls=%fused_computation | custom fusion | bytes 4195328 | tf_op jit(solution)/shard_map/gather | solution.py:118
  129.7 2.7 collective-permute-done.16
  132.5 4.2 %fusion.32 = (bf16[64,32,128]{2,1,0:T(8,128)(2,1)S(1)}, f32[64,32,128]{2,1,0:T(8,128)}) fusion(f32[64]{0:T(128)S(1)} %dynamic_slice.43, f32[64,32,128]{2,1,0:T(8,128)} %collective-permute-done.16, f32[2,64,32,128]{3,2,1,0:T(8,128)S(1)} %bitcast.215, s32[]{:T(128)S(6)} %select_n.157, f32[128,64,128]{2,1,0:T(8,128)} %param.10, s32[]{:T(128)S(6)} %select_n.142, ...), kind=kLoop, calls=%fused_computation.104 | loop fusion | flops 2883584 | bytes 4718924 | tf_op jit(solution)/shard_map/convert_element_type | solution.py:125
  140.6 2.2 bitcast_convert_fusion
  142.8 58.7 %all_to_all.15 = bf16[8,192,768]{2,1,0:T(8,128)(2,1)S(1)} all-to-all(bf16[8,192,768]{2,1,0:T(8,128)(2,1)S(1)} %bitcast.223), channel_id=1, replica_groups=mesh['snp'=8,'sx'=2,'sc'=2] {'snp'}, dimensions={0} | all-to-all | bytes 4718592 | tf_op jit(solution)/shard_map/all_to_all | solution.py:91
  204.0 5.6 %collective-permute-done.21 = bf16[192,768]{1,0:T(8,128)(2,1)S(1)} collective-permute-done((bf16[192,768]{1,0:T(8,128)(2,1)S(1)}, bf16[192,768]{1,0:T(8,128)(2,1)S(1)}, u32[]{:S(2)}, u32[]{:S(2)}) %collective-permute-start.21) | collective-permute-done | bytes 294944 | tf_op jit(solution)/shard_map/ppermute | solution.py:98
  211.6 5.4 %collective-permute-done.22 = bf16[192,768]{1,0:T(8,128)(2,1)S(1)} collective-permute-done((bf16[192,768]{1,0:T(8,128)(2,1)S(1)}, bf16[192,768]{1,0:T(8,128)(2,1)S(1)}, u32[]{:S(2)}, u32[]{:S(2)}) %collective-permute-start.22) | collective-permute-done | bytes 294944 | tf_op jit(solution)/shard_map/ppermute | solution.py:98
  219.2 6.4 %collective-permute-done.23 = bf16[192,768]{1,0:T(8,128)(2,1)S(1)} collective-permute-done((bf16[192,768]{1,0:T(8,128)(2,1)S(1)}, bf16[192,768]{1,0:T(8,128)(2,1)S(1)}, u32[]{:S(2)}, u32[]{:S(2)}) %collective-permute-start.23) | collective-permute-done | bytes 294944 | tf_op jit(solution)/shard_map/ppermute | solution.py:98
  227.0 5.3 %collective-permute-done.24 = bf16[192,768]{1,0:T(8,128)(2,1)S(1)} collective-permute-done((bf16[192,768]{1,0:T(8,128)(2,1)S(1)}, bf16[192,768]{1,0:T(8,128)(2,1)S(1)}, u32[]{:S(2)}, u32[]{:S(2)}) %collective-permute-start.24) | collective-permute-done | bytes 294944 | tf_op jit(solution)/shard_map/ppermute | solution.py:98
  232.4 4.0 %fusion.34 = f32[48,32,5,128]{3,1,2,0:T(8,128)} fusion(bf16[48,32,768,1]{2,1,3,0:T(8,128)(2,1)S(1)} %bitcast.235, bf16[768,5,128,1]{0,2,1,3:T(8,128)(2,1)S(1)} %bitcast.232), kind=kOutput, calls=%fused_computation.106 | convolution fusion | flops 1509949440 | bytes 7274496 | tf_op jit(solution)/shard_map/jps,sbk->jpbk/dot_general | solution.py:115
  236.4 3.0 %gather_fusion.1 = f32[128,32,128]{2,1,0:T(8,128)S(1)} fusion(f32[48,32,5,128]{3,1,2,0:T(8,128)} %fusion.34, s32[128]{0:T(128)S(1)} %get-tuple-element.9), kind=kCustom, calls=%fused_computation.1 | custom fusion | bytes 4195328 | tf_op jit(solution)/shard_map/gather | solution.py:118
  239.5 2.6 collective-permute-done.25
  244.2 23.8 %collective-permute-done.26 = f32[64,32,128]{2,1,0:T(8,128)S(1)} collective-permute-done((f32[64,32,128]{2,1,0:T(8,128)S(1)}, f32[64,32,128]{2,1,0:T(8,128)S(1)}, u32[]{:S(2)}, u32[]{:S(2)}) %collective-permute-start.26) | collective-permute-done | bytes 1048608 | tf_op jit(solution)/shard_map/ppermute | solution.py:132
  268.5 4.1 %collective-permute-done.27 = f32[64,64,128]{2,1,0:T(8,128)S(1)} collective-permute-done((f32[64,64,128]{2,1,0:T(8,128)S(1)}, f32[64,64,128]{2,1,0:T(8,128)S(1)}, u32[]{:S(2)}, u32[]{:S(2)}) %collective-permute-start.27) | collective-permute-done | bytes 2097184 | tf_op jit(solution)/shard_map/ppermute | solution.py:138
  272.6 2.5 maximum_select_fusion
  (115 shorter events, 48.8 us)
Async XLA Ops:
  10.9 35.9 %all-to-all-start = ((bf16[8,192,384]{2,1,0:T(8,128)(2,1)}), bf16[8,192,384]{2,1,0:T(8,128)(2,1)S(1)}, u32[]{:S(2)}, u32[]{:S(2)}) async-start(bf16[8,192,384]{2,1,0:T(8,128)(2,1)} %bitcast.229), calls=%async_computation | async-start | bytes 2359296 | tf_op jit(solution)/shard_map/all_to_all | solution.py:91
  18.2 12.9 %collective-permute-start.8 = (bf16[384,640]{0,1:T(8,128)(2,1)}, bf16[384,640]{0,1:T(8,128)(2,1)S(1)}, u32[]{:S(2)}, u32[]{:S(2)}) collective-permute-start(bf16[384,640]{0,1:T(8,128)(2,1)} %copy-done.3), channel_id=1, source_target_pairs={{0,2},{2,0},{1,3},{3,1},{4,6},{6,4},{5,7},{7,5},{8,10},{10,8},{9,1... | collective-permute-start | bytes 1474568 | tf_op jit(solution)/shard_map/ppermute | solution.py:34
  34.2 18.9 %copy-start.4 = (bf16[384,640]{0,1:T(8,128)(2,1)S(1)}, bf16[384,640]{0,1:T(8,128)(2,1)}, u32[]{:S(2)}) copy-start(bf16[384,640]{0,1:T(8,128)(2,1)} %copy-done.3) | copy-start | bytes 1474564
  34.2 18.9 %copy-start.10 = (bf16[384,640]{0,1:T(8,128)(2,1)S(1)}, bf16[384,640]{0,1:T(8,128)(2,1)}, u32[]{:S(2)}) copy-start(bf16[384,640]{0,1:T(8,128)(2,1)} %copy-done.9) | copy-start | bytes 1474564
  47.8 47.3 %all-to-all-start.1 = ((bf16[8,192,384]{2,1,0:T(8,128)(2,1)}), bf16[8,192,384]{2,1,0:T(8,128)(2,1)S(1)}, u32[]{:S(2)}, u32[]{:S(2)}) async-start(bf16[8,192,384]{2,1,0:T(8,128)(2,1)} %bitcast.228), calls=%async_computation.1 | async-start | bytes 2359296 | tf_op jit(solution)/shard_map/all_to_all | solution.py:91
  51.5 43.8 %collective-permute-start.7 = (f32[6,32,384]{2,1,0:T(8,128)S(1)}, f32[6,32,384]{2,1,0:T(8,128)S(1)}, u32[]{:S(2)}, u32[]{:S(2)}) collective-permute-start(f32[6,32,384]{2,1,0:T(8,128)S(1)} %get-tuple-element.8), channel_id=1, source_target_pairs={{0,2},{2,0},{1,3},{3,1},{4,6},{6,4},{5,7},{7,5},{8,10},{10,8},{9,1... | collective-permute-start | bytes 884744 | tf_op jit(solution)/shard_map/ppermute | solution.py:40
  54.9 16.0 %collective-permute-start = (bf16[192,384]{1,0:T(8,128)(2,1)S(1)}, bf16[192,384]{1,0:T(8,128)(2,1)S(1)}, u32[]{:S(2)}, u32[]{:S(2)}) collective-permute-start(bf16[192,384]{1,0:T(8,128)(2,1)S(1)} %subtract_convert_fusion.1), channel_id=1, source_target_pairs={{0,4},{8,0},{16,8},{24,16},{28,24},{20,28},{12,20},{4,12},{1,5},{9... | collective-permute-start | bytes 442376 | tf_op jit(solution)/shard_map/ppermute | solution.py:102
  56.9 18.7 %collective-permute-start.3 = (bf16[192,384]{1,0:T(8,128)(2,1)S(1)}, bf16[192,384]{1,0:T(8,128)(2,1)S(1)}, u32[]{:S(2)}, u32[]{:S(2)}) collective-permute-start(bf16[192,384]{1,0:T(8,128)(2,1)S(1)} %subtract_convert_fusion.1), channel_id=1, source_target_pairs={{0,8},{8,16},{16,24},{24,28},{28,20},{20,12},{12,4},{4,0},{1,9},{9... | collective-permute-start | bytes 442376 | tf_op jit(solution)/shard_map/ppermute | solution.py:98
  70.9 16.1 %collective-permute-start.1 = (bf16[192,384]{1,0:T(8,128)(2,1)S(1)}, bf16[192,384]{1,0:T(8,128)(2,1)S(1)}, u32[]{:S(2)}, u32[]{:S(2)}) collective-permute-start(bf16[192,384]{1,0:T(8,128)(2,1)S(1)} %collective-permute-done), channel_id=1, source_target_pairs={{0,4},{8,0},{16,8},{24,16},{28,24},{20,28},{12,20},{4,12},{1,5},{9... | collective-permute-start | bytes 442376 | tf_op jit(solution)/shard_map/ppermute | solution.py:102
  75.7 11.6 %collective-permute-start.4 = (bf16[192,384]{1,0:T(8,128)(2,1)S(1)}, bf16[192,384]{1,0:T(8,128)(2,1)S(1)}, u32[]{:S(2)}, u32[]{:S(2)}) collective-permute-start(bf16[192,384]{1,0:T(8,128)(2,1)S(1)} %collective-permute-done.3), channel_id=1, source_target_pairs={{0,8},{8,16},{16,24},{24,28},{28,20},{20,12},{12,4},{4,0},{1,9},{9... | collective-permute-start | bytes 442376 | tf_op jit(solution)/shard_map/ppermute | solution.py:98
  87.0 7.4 %collective-permute-start.2 = (bf16[192,384]{1,0:T(8,128)(2,1)S(1)}, bf16[192,384]{1,0:T(8,128)(2,1)S(1)}, u32[]{:S(2)}, u32[]{:S(2)}) collective-permute-start(bf16[192,384]{1,0:T(8,128)(2,1)S(1)} %collective-permute-done.1), channel_id=1, source_target_pairs={{0,4},{8,0},{16,8},{24,16},{28,24},{20,28},{12,20},{4,12},{1,5},{9... | collective-permute-start | bytes 442376 | tf_op jit(solution)/shard_map/ppermute | solution.py:102
  87.3 5.7 %collective-permute-start.5 = (bf16[192,384]{1,0:T(8,128)(2,1)S(1)}, bf16[192,384]{1,0:T(8,128)(2,1)S(1)}, u32[]{:S(2)}, u32[]{:S(2)}) collective-permute-start(bf16[192,384]{1,0:T(8,128)(2,1)S(1)} %collective-permute-done.4), channel_id=1, source_target_pairs={{0,8},{8,16},{16,24},{24,28},{28,20},{20,12},{12,4},{4,0},{1,9},{9... | collective-permute-start | bytes 442376 | tf_op jit(solution)/shard_map/ppermute | solution.py:98
  92.9 6.7 %collective-permute-start.6 = (bf16[192,384]{1,0:T(8,128)(2,1)S(1)}, bf16[192,384]{1,0:T(8,128)(2,1)S(1)}, u32[]{:S(2)}, u32[]{:S(2)}) collective-permute-start(bf16[192,384]{1,0:T(8,128)(2,1)S(1)} %collective-permute-done.5), channel_id=1, source_target_pairs={{0,8},{8,16},{16,24},{24,28},{28,20},{20,12},{12,4},{4,0},{1,9},{9... | collective-permute-start | bytes 442376 | tf_op jit(solution)/shard_map/ppermute | solution.py:98
  95.3 7.0 %collective-permute-start.9 = (bf16[192,384]{1,0:T(8,128)(2,1)S(1)}, bf16[192,384]{1,0:T(8,128)(2,1)S(1)}, u32[]{:S(2)}, u32[]{:S(2)}) collective-permute-start(bf16[192,384]{1,0:T(8,128)(2,1)S(1)} %subtract_convert_fusion), channel_id=1, source_target_pairs={{0,4},{8,0},{16,8},{24,16},{28,24},{20,28},{12,20},{4,12},{1,5},{9... | collective-permute-start | bytes 442376 | tf_op jit(solution)/shard_map/ppermute | solution.py:102
  95.9 7.9 %collective-permute-start.12 = (bf16[192,384]{1,0:T(8,128)(2,1)S(1)}, bf16[192,384]{1,0:T(8,128)(2,1)S(1)}, u32[]{:S(2)}, u32[]{:S(2)}) collective-permute-start(bf16[192,384]{1,0:T(8,128)(2,1)S(1)} %subtract_convert_fusion), channel_id=1, source_target_pairs={{0,8},{8,16},{16,24},{24,28},{28,20},{20,12},{12,4},{4,0},{1,9},{9... | collective-permute-start | bytes 442376 | tf_op jit(solution)/shard_map/ppermute | solution.py:98
  102.3 5.9 %collective-permute-start.10 = (bf16[192,384]{1,0:T(8,128)(2,1)S(1)}, bf16[192,384]{1,0:T(8,128)(2,1)S(1)}, u32[]{:S(2)}, u32[]{:S(2)}) collective-permute-start(bf16[192,384]{1,0:T(8,128)(2,1)S(1)} %collective-permute-done.9), channel_id=1, source_target_pairs={{0,4},{8,0},{16,8},{24,16},{28,24},{20,28},{12,20},{4,12},{1,5},{9... | collective-permute-start | bytes 442376 | tf_op jit(solution)/shard_map/ppermute | solution.py:102
  103.8 5.7 %collective-permute-start.13 = (bf16[192,384]{1,0:T(8,128)(2,1)S(1)}, bf16[192,384]{1,0:T(8,128)(2,1)S(1)}, u32[]{:S(2)}, u32[]{:S(2)}) collective-permute-start(bf16[192,384]{1,0:T(8,128)(2,1)S(1)} %collective-permute-done.12), channel_id=1, source_target_pairs={{0,8},{8,16},{16,24},{24,28},{28,20},{20,12},{12,4},{4,0},{1,9},{9... | collective-permute-start | bytes 442376 | tf_op jit(solution)/shard_map/ppermute | solution.py:98
  108.2 7.2 %collective-permute-start.11 = (bf16[192,384]{1,0:T(8,128)(2,1)S(1)}, bf16[192,384]{1,0:T(8,128)(2,1)S(1)}, u32[]{:S(2)}, u32[]{:S(2)}) collective-permute-start(bf16[192,384]{1,0:T(8,128)(2,1)S(1)} %collective-permute-done.10), channel_id=1, source_target_pairs={{0,4},{8,0},{16,8},{24,16},{28,24},{20,28},{12,20},{4,12},{1,5},{9... | collective-permute-start | bytes 442376 | tf_op jit(solution)/shard_map/ppermute | solution.py:102
  109.5 5.1 %collective-permute-start.14 = (bf16[192,384]{1,0:T(8,128)(2,1)S(1)}, bf16[192,384]{1,0:T(8,128)(2,1)S(1)}, u32[]{:S(2)}, u32[]{:S(2)}) collective-permute-start(bf16[192,384]{1,0:T(8,128)(2,1)S(1)} %collective-permute-done.13), channel_id=1, source_target_pairs={{0,8},{8,16},{16,24},{24,28},{28,20},{20,12},{12,4},{4,0},{1,9},{9... | collective-permute-start | bytes 442376 | tf_op jit(solution)/shard_map/ppermute | solution.py:98
  114.6 5.1 %collective-permute-start.15 = (bf16[192,384]{1,0:T(8,128)(2,1)S(1)}, bf16[192,384]{1,0:T(8,128)(2,1)S(1)}, u32[]{:S(2)}, u32[]{:S(2)}) collective-permute-start(bf16[192,384]{1,0:T(8,128)(2,1)S(1)} %collective-permute-done.14), channel_id=1, source_target_pairs={{0,8},{8,16},{16,24},{24,28},{28,20},{20,12},{12,4},{4,0},{1,9},{9... | collective-permute-start | bytes 442376 | tf_op jit(solution)/shard_map/ppermute | solution.py:98
  129.5 3.0 %collective-permute-start.16 = (f32[64,32,128]{2,1,0:T(8,128)}, f32[64,32,128]{2,1,0:T(8,128)}, u32[]{:S(2)}, u32[]{:S(2)}) collective-permute-start(f32[64,32,128]{2,1,0:T(8,128)} %dynamic-slice_bitcast_fusion.1), channel_id=1, source_target_pairs={{0,1},{1,0},{2,3},{3,2},{4,5},{5,4},{6,7},{7,6},{8,9},{9,8},{10,11... | collective-permute-start | bytes 3145736 | tf_op jit(solution)/shard_map/ppermute | solution.py:122
  136.6 1.9 collective-permute-start.17
  201.9 7.7 %collective-permute-start.21 = (bf16[192,768]{1,0:T(8,128)(2,1)S(1)}, bf16[192,768]{1,0:T(8,128)(2,1)S(1)}, u32[]{:S(2)}, u32[]{:S(2)}) collective-permute-start(bf16[192,768]{1,0:T(8,128)(2,1)S(1)} %fusion.7), channel_id=1, source_target_pairs={{0,8},{8,16},{16,24},{24,28},{28,20},{20,12},{12,4},{4,0},{1,9},{9... | collective-permute-start | bytes 884744 | tf_op jit(solution)/shard_map/ppermute | solution.py:98
  203.1 7.4 %collective-permute-start.18 = (bf16[192,768]{1,0:T(8,128)(2,1)S(1)}, bf16[192,768]{1,0:T(8,128)(2,1)S(1)}, u32[]{:S(2)}, u32[]{:S(2)}) collective-permute-start(bf16[192,768]{1,0:T(8,128)(2,1)S(1)} %fusion.7), channel_id=1, source_target_pairs={{0,4},{8,0},{16,8},{24,16},{28,24},{20,28},{12,20},{4,12},{1,5},{9... | collective-permute-start | bytes 884744 | tf_op jit(solution)/shard_map/ppermute | solution.py:102
  209.5 7.4 %collective-permute-start.22 = (bf16[192,768]{1,0:T(8,128)(2,1)S(1)}, bf16[192,768]{1,0:T(8,128)(2,1)S(1)}, u32[]{:S(2)}, u32[]{:S(2)}) collective-permute-start(bf16[192,768]{1,0:T(8,128)(2,1)S(1)} %collective-permute-done.21), channel_id=1, source_target_pairs={{0,8},{8,16},{16,24},{24,28},{28,20},{20,12},{12,4},{4,0},{1,9},{9... | collective-permute-start | bytes 884744 | tf_op jit(solution)/shard_map/ppermute | solution.py:98
  210.4 7.7 %collective-permute-start.19 = (bf16[192,768]{1,0:T(8,128)(2,1)S(1)}, bf16[192,768]{1,0:T(8,128)(2,1)S(1)}, u32[]{:S(2)}, u32[]{:S(2)}) collective-permute-start(bf16[192,768]{1,0:T(8,128)(2,1)S(1)} %collective-permute-done.18), channel_id=1, source_target_pairs={{0,4},{8,0},{16,8},{24,16},{28,24},{20,28},{12,20},{4,12},{1,5},{9... | collective-permute-start | bytes 884744 | tf_op jit(solution)/shard_map/ppermute | solution.py:102
  217.0 8.6 %collective-permute-start.23 = (bf16[192,768]{1,0:T(8,128)(2,1)S(1)}, bf16[192,768]{1,0:T(8,128)(2,1)S(1)}, u32[]{:S(2)}, u32[]{:S(2)}) collective-permute-start(bf16[192,768]{1,0:T(8,128)(2,1)S(1)} %collective-permute-done.22), channel_id=1, source_target_pairs={{0,8},{8,16},{16,24},{24,28},{28,20},{20,12},{12,4},{4,0},{1,9},{9... | collective-permute-start | bytes 884744 | tf_op jit(solution)/shard_map/ppermute | solution.py:98
  218.2 8.8 %collective-permute-start.20 = (bf16[192,768]{1,0:T(8,128)(2,1)S(1)}, bf16[192,768]{1,0:T(8,128)(2,1)S(1)}, u32[]{:S(2)}, u32[]{:S(2)}) collective-permute-start(bf16[192,768]{1,0:T(8,128)(2,1)S(1)} %collective-permute-done.19), channel_id=1, source_target_pairs={{0,4},{8,0},{16,8},{24,16},{28,24},{20,28},{12,20},{4,12},{1,5},{9... | collective-permute-start | bytes 884744 | tf_op jit(solution)/shard_map/ppermute | solution.py:102
  225.5 6.7 %collective-permute-start.24 = (bf16[192,768]{1,0:T(8,128)(2,1)S(1)}, bf16[192,768]{1,0:T(8,128)(2,1)S(1)}, u32[]{:S(2)}, u32[]{:S(2)}) collective-permute-start(bf16[192,768]{1,0:T(8,128)(2,1)S(1)} %collective-permute-done.23), channel_id=1, source_target_pairs={{0,8},{8,16},{16,24},{24,28},{28,20},{20,12},{12,4},{4,0},{1,9},{9... | collective-permute-start | bytes 884744 | tf_op jit(solution)/shard_map/ppermute | solution.py:98
  239.4 2.7 collective-permute-start.25
  242.7 25.3 %collective-permute-start.26 = (f32[64,32,128]{2,1,0:T(8,128)S(1)}, f32[64,32,128]{2,1,0:T(8,128)S(1)}, u32[]{:S(2)}, u32[]{:S(2)}) collective-permute-start(f32[64,32,128]{2,1,0:T(8,128)S(1)} %multiply_select_fusion), channel_id=1, source_target_pairs={{0,2},{2,0},{1,3},{3,1},{4,6},{6,4},{5,7},{7,5},{8,10},{10,8},{9,1... | collective-permute-start | bytes 3145736 | tf_op jit(solution)/shard_map/ppermute | solution.py:132
  268.4 4.2 %collective-permute-start.27 = (f32[64,64,128]{2,1,0:T(8,128)S(1)}, f32[64,64,128]{2,1,0:T(8,128)S(1)}, u32[]{:S(2)}, u32[]{:S(2)}) collective-permute-start(f32[64,64,128]{2,1,0:T(8,128)S(1)} %maximum_select_fusion.1), channel_id=1, source_target_pairs={{0,1},{1,0},{2,3},{3,2},{4,5},{5,4},{6,7},{7,6},{8,9},{9,8},{10,11... | collective-permute-start | bytes 6291464 | tf_op jit(solution)/shard_map/ppermute | solution.py:138
  (10 other events, 30.8 us)

commit v16 on v11

--- a/solution.py
+++ b/solution.py
@@ -125,12 +125,18 @@
                 jnp.concatenate([other_bf, own_bf], axis=0),
             )
     other_half = lax.ppermute(own, "sx", swap)
+    core_own = lax.ppermute(own, "sc", swap)
+    core_other = lax.ppermute(other_half, "sc", swap)
     mine = jnp.where(
         x == 0,
         jnp.concatenate([own, other_half], axis=1),
         jnp.concatenate([other_half, own], axis=1),
     )
-    other_entries = lax.ppermute(mine, "sc", swap)
+    other_entries = jnp.where(
+        x == 0,
+        jnp.concatenate([core_own, core_other], axis=1),
+        jnp.concatenate([core_other, core_own], axis=1),
+    )
     return jnp.where(
         c == 0,
         jnp.concatenate([mine, other_entries], axis=0),

time: 265 us -> 265 us (level)
  transfers between devices with their start and end apart: 23 -> 24, of which waited for: 18 -> 18; matrix products, arithmetic and copies ran while one was open for 3% -> 3% of each run, Pallas kernels for 0% -> 0%
where the time goes in v16:
time: 265 us; the launch traced here: 264 us
  waiting for transfers between devices  126 us (48%)
  blocking collectives  59.4 us (22%)
  starting transfers between devices  29.9 us (11%)
  other arithmetic  17.1 us (6%)
  matrix products  16.2 us (6%)
  local copies, waits for them, and re-layouts  14.7 us (6%)
    all_to_all x1, blocking collectives, predict(): gathered = lax.all_to_all(partial, 'snp', 0, 0, tiled=False)  59.4 us
    ppermute x8, waiting for transfers between devices, per_device(): moving = lax.ppermute(moving, 'snp', forward)  41 us
    all_to_all x2, waiting for transfers between devices, predict(): gathered = lax.all_to_all(partial, 'snp', 0, 0, tiled=False)  39.1 us
    ppermute x1, waiting for transfers between devices, per_device(): other_half = lax.ppermute(own, 'sx', swap)  23.8 us
    all_to_all x2, starting transfers between devices, predict(): gathered = lax.all_to_all(partial, 'snp', 0, 0, tiled=False)  11.5 us
    ppermute x1, waiting for transfers between devices, per_device(): geno_peer = lax.ppermute(genotypes, 'sx', swap)  11.4 us
    ppermute x6, starting transfers between devices, per_device(): moving = lax.ppermute(moving, 'snp', backward)  8.1 us
    dot_general x2, matrix products, per_device(): jnp.einsum('jps,sbk->jpbk', blocks, geno_blocks, preferred_element_type=j...  7.99 us
  transfers between devices with their start and end apart: 24, of which 18 were waited for; matrix products, arithmetic and copies ran while one was open for 3% of the time, Pallas kernels for 0%

profile of v16, /device:TPU:0, one launch (start us, length us, event | category | flops | bytes accessed | tf_op | source)
XLA Modules:
  0.0 264.3 jit_solution(12782607409798107588)
XLA Ops:
  4.7 1.9 select_convert_fusion
  8.6 2.3 bitcast_convert_fusion.2
  10.9 7.3 %all-to-all-start = ((bf16[8,192,384]{2,1,0:T(8,128)(2,1)}), bf16[8,192,384]{2,1,0:T(8,128)(2,1)S(1)}, u32[]{:S(2)}, u32[]{:S(2)}) async-start(bf16[8,192,384]{2,1,0:T(8,128)(2,1)} %bitcast.206), calls=%async_computation | async-start | bytes 2359296 | tf_op jit(solution)/shard_map/all_to_all | solution.py:91
  19.7 11.4 %collective-permute-done.1 = bf16[384,640]{0,1:T(8,128)(2,1)S(1)} collective-permute-done((bf16[384,640]{0,1:T(8,128)(2,1)}, bf16[384,640]{0,1:T(8,128)(2,1)S(1)}, u32[]{:S(2)}, u32[]{:S(2)}) %collective-permute-start.1) | collective-permute-done | bytes 491552 | tf_op jit(solution)/shard_map/ppermute | solution.py:34
  31.9 2.3 bitcast_convert_fusion.1
  34.2 12.6 %all-to-all-done = bf16[8,192,384]{2,1,0:T(8,128)(2,1)S(1)} async-done(((bf16[8,192,384]{2,1,0:T(8,128)(2,1)}), bf16[8,192,384]{2,1,0:T(8,128)(2,1)S(1)}, u32[]{:S(2)}, u32[]{:S(2)}) %all-to-all-start) | async-done | bytes 1179680 | tf_op jit(solution)/shard_map/all_to_all | solution.py:91
  46.8 4.2 %all-to-all-start.1 = ((bf16[8,192,384]{2,1,0:T(8,128)(2,1)}), bf16[8,192,384]{2,1,0:T(8,128)(2,1)}, u32[]{:S(2)}, u32[]{:S(2)}) async-start(bf16[8,192,384]{2,1,0:T(8,128)(2,1)} %bitcast.205), calls=%async_computation.1 | async-start | bytes 2359296 | tf_op jit(solution)/shard_map/all_to_all | solution.py:91
  52.8 26.5 %all-to-all-done.1 = bf16[8,192,384]{2,1,0:T(8,128)(2,1)} async-done(((bf16[8,192,384]{2,1,0:T(8,128)(2,1)}), bf16[8,192,384]{2,1,0:T(8,128)(2,1)}, u32[]{:S(2)}, u32[]{:S(2)}) %all-to-all-start.1) | async-done | bytes 1179680 | tf_op jit(solution)/shard_map/all_to_all | solution.py:91
  81.0 2.0 collective-permute-start.2
  83.0 5.5 %collective-permute-done.5 = bf16[192,768]{1,0:T(8,128)(2,1)S(1)} collective-permute-done((bf16[192,768]{1,0:T(8,128)(2,1)S(1)}, bf16[192,768]{1,0:T(8,128)(2,1)S(1)}, u32[]{:S(2)}, u32[]{:S(2)}) %collective-permute-start.5) | collective-permute-done | bytes 294944 | tf_op jit(solution)/shard_map/ppermute | solution.py:102
  88.5 2.0 collective-permute-start.3
  91.7 4.0 %collective-permute-done.6 = bf16[192,768]{1,0:T(8,128)(2,1)S(1)} collective-permute-done((bf16[192,768]{1,0:T(8,128)(2,1)S(1)}, bf16[192,768]{1,0:T(8,128)(2,1)S(1)}, u32[]{:S(2)}, u32[]{:S(2)}) %collective-permute-start.6) | collective-permute-done | bytes 294944 | tf_op jit(solution)/shard_map/ppermute | solution.py:102
  98.8 3.6 %collective-permute-done.7 = bf16[192,768]{1,0:T(8,128)(2,1)S(1)} collective-permute-done((bf16[192,768]{1,0:T(8,128)(2,1)S(1)}, bf16[192,768]{1,0:T(8,128)(2,1)S(1)}, u32[]{:S(2)}, u32[]{:S(2)}) %collective-permute-start.7) | collective-permute-done | bytes 294944 | tf_op jit(solution)/shard_map/ppermute | solution.py:102
  103.9 6.3 %collective-permute-done.8 = bf16[192,768]{1,0:T(8,128)(2,1)S(1)} collective-permute-done((bf16[192,768]{1,0:T(8,128)(2,1)S(1)}, bf16[192,768]{1,0:T(8,128)(2,1)S(1)}, u32[]{:S(2)}, u32[]{:S(2)}) %collective-permute-start.8) | collective-permute-done | bytes 294944 | tf_op jit(solution)/shard_map/ppermute | solution.py:102
  110.3 4.0 %fusion.31 = f32[48,32,5,128]{3,1,2,0:T(8,128)} fusion(bf16[48,32,768,1]{2,1,3,0:T(8,128)(2,1)S(1)} %bitcast.213, bf16[768,5,128,1]{0,2,1,3:T(8,128)(2,1)S(1)} %bitcast.207), kind=kOutput, calls=%fused_computation.96 | convolution fusion | flops 1509949440 | bytes 7274496 | tf_op jit(solution)/shard_map/jps,sbk->jpbk/dot_general | solution.py:110
  114.3 3.0 %gather_fusion = f32[128,32,128]{2,1,0:T(8,128)S(1)} fusion(f32[48,32,5,128]{3,1,2,0:T(8,128)} %fusion.31, s32[128]{0:T(128)S(1)} %get-tuple-element.9), kind=kCustom, calls=%fused_computation | custom fusion | bytes 4195328 | tf_op jit(solution)/shard_map/gather | solution.py:113
  118.6 2.7 %collective-permute-done.9 = f32[64,32,128]{2,1,0:T(8,128)} collective-permute-done((f32[64,32,128]{2,1,0:T(8,128)}, f32[64,32,128]{2,1,0:T(8,128)}, u32[]{:S(2)}, u32[]{:S(2)}) %collective-permute-start.9) | collective-permute-done | bytes 1048608 | tf_op jit(solution)/shard_map/ppermute | solution.py:117
  121.3 4.2 %fusion.30 = (bf16[64,32,128]{2,1,0:T(8,128)(2,1)S(1)}, f32[64,32,128]{2,1,0:T(8,128)}) fusion(f32[64]{0:T(128)S(1)} %dynamic_slice.43, f32[64,32,128]{2,1,0:T(8,128)} %collective-permute-done.9, f32[2,64,32,128]{3,2,1,0:T(8,128)S(1)} %bitcast.189, s32[]{:T(128)S(6)} %select_n.161, f32[128,64,128]{2,1,0:T(8,128)} %param.10, s32[]{:T(128)S(6)} %select_n.146, ...), kind=kLoop, calls=%fused_computation.95 | loop fusion | flops 2883584 | bytes 4718924 | tf_op jit(solution)/shard_map/convert_element_type | solution.py:120
  129.5 2.2 bitcast_convert_fusion
  131.7 59.4 %all_to_all.15 = bf16[8,192,768]{2,1,0:T(8,128)(2,1)S(1)} all-to-all(bf16[8,192,768]{2,1,0:T(8,128)(2,1)S(1)} %bitcast.200), channel_id=1, replica_groups=mesh['snp'=8,'sx'=2,'sc'=2] {'snp'}, dimensions={0} | all-to-all | bytes 4718592 | tf_op jit(solution)/shard_map/all_to_all | solution.py:91
  193.6 5.6 %collective-permute-done.14 = bf16[192,768]{1,0:T(8,128)(2,1)S(1)} collective-permute-done((bf16[192,768]{1,0:T(8,128)(2,1)S(1)}, bf16[192,768]{1,0:T(8,128)(2,1)S(1)}, u32[]{:S(2)}, u32[]{:S(2)}) %collective-permute-start.14) | collective-permute-done | bytes 294944 | tf_op jit(solution)/shard_map/ppermute | solution.py:102
  201.2 5.2 %collective-permute-done.15 = bf16[192,768]{1,0:T(8,128)(2,1)S(1)} collective-permute-done((bf16[192,768]{1,0:T(8,128)(2,1)S(1)}, bf16[192,768]{1,0:T(8,128)(2,1)S(1)}, u32[]{:S(2)}, u32[]{:S(2)}) %collective-permute-start.15) | collective-permute-done | bytes 294944 | tf_op jit(solution)/shard_map/ppermute | solution.py:102
  208.6 6.1 %collective-permute-done.16 = bf16[192,768]{1,0:T(8,128)(2,1)S(1)} collective-permute-done((bf16[192,768]{1,0:T(8,128)(2,1)S(1)}, bf16[192,768]{1,0:T(8,128)(2,1)S(1)}, u32[]{:S(2)}, u32[]{:S(2)}) %collective-permute-start.16) | collective-permute-done | bytes 294944 | tf_op jit(solution)/shard_map/ppermute | solution.py:102
  214.7 1.9 collective-permute-start.17
  216.6 4.8 %collective-permute-done.17 = bf16[192,768]{1,0:T(8,128)(2,1)S(1)} collective-permute-done((bf16[192,768]{1,0:T(8,128)(2,1)S(1)}, bf16[192,768]{1,0:T(8,128)(2,1)S(1)}, u32[]{:S(2)}, u32[]{:S(2)}) %collective-permute-start.17) | collective-permute-done | bytes 294944 | tf_op jit(solution)/shard_map/ppermute | solution.py:102
  221.5 4.0 %fusion.32 = f32[48,32,5,128]{3,1,2,0:T(8,128)} fusion(bf16[48,32,768,1]{2,1,3,0:T(8,128)(2,1)S(1)} %bitcast.212, bf16[768,5,128,1]{0,2,1,3:T(8,128)(2,1)S(1)} %bitcast.209), kind=kOutput, calls=%fused_computation.97 | convolution fusion | flops 1509949440 | bytes 7274496 | tf_op jit(solution)/shard_map/jps,sbk->jpbk/dot_general | solution.py:110
  225.5 3.0 %gather_fusion.1 = f32[128,32,128]{2,1,0:T(8,128)S(1)} fusion(f32[48,32,5,128]{3,1,2,0:T(8,128)} %fusion.32, s32[128]{0:T(128)S(1)} %get-tuple-element.9), kind=kCustom, calls=%fused_computation.1 | custom fusion | bytes 4195328 | tf_op jit(solution)/shard_map/gather | solution.py:113
  228.6 2.6 %collective-permute-done.18 = f32[64,32,128]{2,1,0:T(8,128)S(1)} collective-permute-done((f32[64,32,128]{2,1,0:T(8,128)S(1)}, f32[64,32,128]{2,1,0:T(8,128)S(1)}, u32[]{:S(2)}, u32[]{:S(2)}) %collective-permute-start.18) | collective-permute-done | bytes 1048608 | tf_op jit(solution)/shard_map/ppermute | solution.py:117
  233.3 23.8 %collective-permute-done.19 = f32[64,32,128]{2,1,0:T(8,128)S(1)} collective-permute-done((f32[64,32,128]{2,1,0:T(8,128)S(1)}, f32[64,32,128]{2,1,0:T(8,128)S(1)}, u32[]{:S(2)}, u32[]{:S(2)}) %collective-permute-start.19) | collective-permute-done | bytes 1048608 | tf_op jit(solution)/shard_map/ppermute | solution.py:127
  257.5 2.4 collective-permute-done.21
  259.9 1.9 maximum_select_fusion.2
  261.9 2.5 maximum_select_fusion
  (88 shorter events, 32.1 us)
Async XLA Ops:
  7.3 1.0 copy-start.6
  8.6 2.3 copy-start.1
  10.9 35.9 %all-to-all-start = ((bf16[8,192,384]{2,1,0:T(8,128)(2,1)}), bf16[8,192,384]{2,1,0:T(8,128)(2,1)S(1)}, u32[]{:S(2)}, u32[]{:S(2)}) async-start(bf16[8,192,384]{2,1,0:T(8,128)(2,1)} %bitcast.206), calls=%async_computation | async-start | bytes 2359296 | tf_op jit(solution)/shard_map/all_to_all | solution.py:91
  18.2 12.9 %collective-permute-start.1 = (bf16[384,640]{0,1:T(8,128)(2,1)}, bf16[384,640]{0,1:T(8,128)(2,1)S(1)}, u32[]{:S(2)}, u32[]{:S(2)}) collective-permute-start(bf16[384,640]{0,1:T(8,128)(2,1)} %copy-done.1), channel_id=1, source_target_pairs={{0,2},{2,0},{1,3},{3,1},{4,6},{6,4},{5,7},{7,5},{8,10},{10,8},{9,1... | collective-permute-start | bytes 1474568 | tf_op jit(solution)/shard_map/ppermute | solution.py:34
  34.2 16.9 %copy-start.5 = (f32[384,384]{1,0:T(8,128)S(1)}, f32[384,384]{1,0:T(8,128)}, u32[]{:S(2)}) copy-start(f32[384,384]{1,0:T(8,128)} %param.9) | copy-start | bytes 1769476
  46.8 32.6 %all-to-all-start.1 = ((bf16[8,192,384]{2,1,0:T(8,128)(2,1)}), bf16[8,192,384]{2,1,0:T(8,128)(2,1)}, u32[]{:S(2)}, u32[]{:S(2)}) async-start(bf16[8,192,384]{2,1,0:T(8,128)(2,1)} %bitcast.205), calls=%async_computation.1 | async-start | bytes 2359296 | tf_op jit(solution)/shard_map/all_to_all | solution.py:91
  51.1 39.4 %copy-start.2 = (bf16[384,640]{0,1:T(8,128)(2,1)S(1)}, bf16[384,640]{0,1:T(8,128)(2,1)}, u32[]{:S(2)}) copy-start(bf16[384,640]{0,1:T(8,128)(2,1)} %copy-done.1) | copy-start | bytes 1474564
  51.1 29.7 %collective-permute-start = (f32[6,32,384]{2,1,0:T(8,128)S(1)}, f32[6,32,384]{2,1,0:T(8,128)S(1)}, u32[]{:S(2)}, u32[]{:S(2)}) collective-permute-start(f32[6,32,384]{2,1,0:T(8,128)S(1)} %get-tuple-element.8), channel_id=1, source_target_pairs={{0,2},{2,0},{1,3},{3,1},{4,6},{6,4},{5,7},{7,5},{8,10},{10,8},{9,1... | collective-permute-start | bytes 884744 | tf_op jit(solution)/shard_map/ppermute | solution.py:40
  80.9 7.6 %collective-permute-start.5 = (bf16[192,768]{1,0:T(8,128)(2,1)S(1)}, bf16[192,768]{1,0:T(8,128)(2,1)S(1)}, u32[]{:S(2)}, u32[]{:S(2)}) collective-permute-start(bf16[192,768]{1,0:T(8,128)(2,1)S(1)} %fusion.7), channel_id=1, source_target_pairs={{0,8},{8,16},{16,24},{24,28},{28,20},{20,12},{12,4},{4,0},{1,9},{9... | collective-permute-start | bytes 884744 | tf_op jit(solution)/shard_map/ppermute | solution.py:102
  81.0 7.5 %collective-permute-start.2 = (bf16[192,768]{1,0:T(8,128)(2,1)S(1)}, bf16[192,768]{1,0:T(8,128)(2,1)}, u32[]{:S(2)}, u32[]{:S(2)}) collective-permute-start(bf16[192,768]{1,0:T(8,128)(2,1)S(1)} %fusion.7), channel_id=1, source_target_pairs={{0,4},{8,0},{16,8},{24,16},{28,24},{20,28},{12,20},{4,12},{1,5},{9... | collective-permute-start | bytes 884744 | tf_op jit(solution)/shard_map/ppermute | solution.py:106
  88.5 7.1 %collective-permute-start.6 = (bf16[192,768]{1,0:T(8,128)(2,1)S(1)}, bf16[192,768]{1,0:T(8,128)(2,1)S(1)}, u32[]{:S(2)}, u32[]{:S(2)}) collective-permute-start(bf16[192,768]{1,0:T(8,128)(2,1)S(1)} %collective-permute-done.5), channel_id=1, source_target_pairs={{0,8},{8,16},{16,24},{24,28},{28,20},{20,12},{12,4},{4,0},{1,9},{9... | collective-permute-start | bytes 884744 | tf_op jit(solution)/shard_map/ppermute | solution.py:102
  88.5 8.1 %collective-permute-start.3 = (bf16[192,768]{1,0:T(8,128)(2,1)}, bf16[192,768]{1,0:T(8,128)(2,1)}, u32[]{:S(2)}, u32[]{:S(2)}) collective-permute-start(bf16[192,768]{1,0:T(8,128)(2,1)} %collective-permute-done.2), channel_id=1, source_target_pairs={{0,4},{8,0},{16,8},{24,16},{28,24},{20,28},{12,20},{4,12},{1,5},{9... | collective-permute-start | bytes 884744 | tf_op jit(solution)/shard_map/ppermute | solution.py:106
  91.7 18.6 %copy-start.3 = (bf16[768,640]{0,1:T(8,128)(2,1)}, bf16[768,640]{0,1:T(8,128)(2,1)S(1)}, u32[]{:S(2)}) copy-start(bf16[768,640]{0,1:T(8,128)(2,1)S(1)} %pad_maximum_fusion) | copy-start | bytes 2949124
  95.7 6.7 %collective-permute-start.7 = (bf16[192,768]{1,0:T(8,128)(2,1)S(1)}, bf16[192,768]{1,0:T(8,128)(2,1)S(1)}, u32[]{:S(2)}, u32[]{:S(2)}) collective-permute-start(bf16[192,768]{1,0:T(8,128)(2,1)S(1)} %collective-permute-done.6), channel_id=1, source_target_pairs={{0,8},{8,16},{16,24},{24,28},{28,20},{20,12},{12,4},{4,0},{1,9},{9... | collective-permute-start | bytes 884744 | tf_op jit(solution)/shard_map/ppermute | solution.py:102
  96.6 7.3 %collective-permute-start.4 = (bf16[192,768]{1,0:T(8,128)(2,1)}, bf16[192,768]{1,0:T(8,128)(2,1)S(1)}, u32[]{:S(2)}, u32[]{:S(2)}) collective-permute-start(bf16[192,768]{1,0:T(8,128)(2,1)} %collective-permute-done.3), channel_id=1, source_target_pairs={{0,4},{8,0},{16,8},{24,16},{28,24},{20,28},{12,20},{4,12},{1,5},{9... | collective-permute-start | bytes 884744 | tf_op jit(solution)/shard_map/ppermute | solution.py:106
  102.4 7.8 %collective-permute-start.8 = (bf16[192,768]{1,0:T(8,128)(2,1)S(1)}, bf16[192,768]{1,0:T(8,128)(2,1)S(1)}, u32[]{:S(2)}, u32[]{:S(2)}) collective-permute-start(bf16[192,768]{1,0:T(8,128)(2,1)S(1)} %collective-permute-done.7), channel_id=1, source_target_pairs={{0,8},{8,16},{16,24},{24,28},{28,20},{20,12},{12,4},{4,0},{1,9},{9... | collective-permute-start | bytes 884744 | tf_op jit(solution)/shard_map/ppermute | solution.py:102
  114.3 4.1 %copy-start.8 = (f32[46]{0:T(128)S(1)}, f32[46]{0:T(128)}, u32[]{:S(2)}) copy-start(f32[46]{0:T(128)} %param.14) | copy-start | bytes 556
  118.3 3.0 %collective-permute-start.9 = (f32[64,32,128]{2,1,0:T(8,128)}, f32[64,32,128]{2,1,0:T(8,128)}, u32[]{:S(2)}, u32[]{:S(2)}) collective-permute-start(f32[64,32,128]{2,1,0:T(8,128)} %dynamic-slice_bitcast_fusion.1), channel_id=1, source_target_pairs={{0,1},{1,0},{2,3},{3,2},{4,5},{5,4},{6,7},{7,6},{8,9},{9,8},{10,11... | collective-permute-start | bytes 3145736 | tf_op jit(solution)/shard_map/ppermute | solution.py:117
  125.5 1.9 collective-permute-start.10
  128.3 1.2 copy-start.4
  191.5 7.7 %collective-permute-start.14 = (bf16[192,768]{1,0:T(8,128)(2,1)S(1)}, bf16[192,768]{1,0:T(8,128)(2,1)S(1)}, u32[]{:S(2)}, u32[]{:S(2)}) collective-permute-start(bf16[192,768]{1,0:T(8,128)(2,1)S(1)} %subtract_convert_fusion), channel_id=1, source_target_pairs={{0,8},{8,16},{16,24},{24,28},{28,20},{20,12},{12,4},{4,0},{1,9},{9... | collective-permute-start | bytes 884744 | tf_op jit(solution)/shard_map/ppermute | solution.py:102
  192.7 7.4 %collective-permute-start.11 = (bf16[192,768]{1,0:T(8,128)(2,1)S(1)}, bf16[192,768]{1,0:T(8,128)(2,1)S(1)}, u32[]{:S(2)}, u32[]{:S(2)}) collective-permute-start(bf16[192,768]{1,0:T(8,128)(2,1)S(1)} %subtract_convert_fusion), channel_id=1, source_target_pairs={{0,4},{8,0},{16,8},{24,16},{28,24},{20,28},{12,20},{4,12},{1,5},{9... | collective-permute-start | bytes 884744 | tf_op jit(solution)/shard_map/ppermute | solution.py:106
  199.2 7.2 %collective-permute-start.15 = (bf16[192,768]{1,0:T(8,128)(2,1)S(1)}, bf16[192,768]{1,0:T(8,128)(2,1)S(1)}, u32[]{:S(2)}, u32[]{:S(2)}) collective-permute-start(bf16[192,768]{1,0:T(8,128)(2,1)S(1)} %collective-permute-done.14), channel_id=1, source_target_pairs={{0,8},{8,16},{16,24},{24,28},{28,20},{20,12},{12,4},{4,0},{1,9},{9... | collective-permute-start | bytes 884744 | tf_op jit(solution)/shard_map/ppermute | solution.py:102
  200.1 7.7 %collective-permute-start.12 = (bf16[192,768]{1,0:T(8,128)(2,1)S(1)}, bf16[192,768]{1,0:T(8,128)(2,1)S(1)}, u32[]{:S(2)}, u32[]{:S(2)}) collective-permute-start(bf16[192,768]{1,0:T(8,128)(2,1)S(1)} %collective-permute-done.11), channel_id=1, source_target_pairs={{0,4},{8,0},{16,8},{24,16},{28,24},{20,28},{12,20},{4,12},{1,5},{9... | collective-permute-start | bytes 884744 | tf_op jit(solution)/shard_map/ppermute | solution.py:106
  206.4 8.3 %collective-permute-start.16 = (bf16[192,768]{1,0:T(8,128)(2,1)S(1)}, bf16[192,768]{1,0:T(8,128)(2,1)S(1)}, u32[]{:S(2)}, u32[]{:S(2)}) collective-permute-start(bf16[192,768]{1,0:T(8,128)(2,1)S(1)} %collective-permute-done.15), channel_id=1, source_target_pairs={{0,8},{8,16},{16,24},{24,28},{28,20},{20,12},{12,4},{4,0},{1,9},{9... | collective-permute-start | bytes 884744 | tf_op jit(solution)/shard_map/ppermute | solution.py:102
  207.8 8.8 %collective-permute-start.13 = (bf16[192,768]{1,0:T(8,128)(2,1)S(1)}, bf16[192,768]{1,0:T(8,128)(2,1)S(1)}, u32[]{:S(2)}, u32[]{:S(2)}) collective-permute-start(bf16[192,768]{1,0:T(8,128)(2,1)S(1)} %collective-permute-done.12), channel_id=1, source_target_pairs={{0,4},{8,0},{16,8},{24,16},{28,24},{20,28},{12,20},{4,12},{1,5},{9... | collective-permute-start | bytes 884744 | tf_op jit(solution)/shard_map/ppermute | solution.py:106
  214.7 6.7 %collective-permute-start.17 = (bf16[192,768]{1,0:T(8,128)(2,1)S(1)}, bf16[192,768]{1,0:T(8,128)(2,1)S(1)}, u32[]{:S(2)}, u32[]{:S(2)}) collective-permute-start(bf16[192,768]{1,0:T(8,128)(2,1)S(1)} %collective-permute-done.16), channel_id=1, source_target_pairs={{0,8},{8,16},{16,24},{24,28},{28,20},{20,12},{12,4},{4,0},{1,9},{9... | collective-permute-start | bytes 884744 | tf_op jit(solution)/shard_map/ppermute | solution.py:102
  228.5 2.8 %copy-start = (f32[64,32,128]{2,1,0:T(8,128)S(1)}, f32[64,32,128]{2,1,0:T(8,128)}, u32[]{:S(2)}) copy-start(f32[64,32,128]{2,1,0:T(8,128)} %get-tuple-element.6) | copy-start | bytes 3145732
  228.6 2.7 %collective-permute-start.18 = (f32[64,32,128]{2,1,0:T(8,128)S(1)}, f32[64,32,128]{2,1,0:T(8,128)S(1)}, u32[]{:S(2)}, u32[]{:S(2)}) collective-permute-start(f32[64,32,128]{2,1,0:T(8,128)S(1)} %dynamic-slice_bitcast_fusion), channel_id=1, source_target_pairs={{0,1},{1,0},{2,3},{3,2},{4,5},{5,4},{6,7},{7,6},{8,9},{9,8},{10,11... | collective-permute-start | bytes 3145736 | tf_op jit(solution)/shard_map/ppermute | solution.py:117
  231.8 25.3 %collective-permute-start.19 = (f32[64,32,128]{2,1,0:T(8,128)S(1)}, f32[64,32,128]{2,1,0:T(8,128)S(1)}, u32[]{:S(2)}, u32[]{:S(2)}) collective-permute-start(f32[64,32,128]{2,1,0:T(8,128)S(1)} %multiply_select_fusion), channel_id=1, source_target_pairs={{0,2},{2,0},{1,3},{3,1},{4,6},{6,4},{5,7},{7,5},{8,10},{10,8},{9,1... | collective-permute-start | bytes 3145736 | tf_op jit(solution)/shard_map/ppermute | solution.py:127
  233.3 24.2 %collective-permute-start.20 = (f32[64,32,128]{2,1,0:T(8,128)S(1)}, f32[64,32,128]{2,1,0:T(8,128)S(1)}, u32[]{:S(2)}, u32[]{:S(2)}) collective-permute-start(f32[64,32,128]{2,1,0:T(8,128)S(1)} %multiply_select_fusion), channel_id=1, source_target_pairs={{0,1},{1,0},{2,3},{3,2},{4,5},{5,4},{6,7},{7,6},{8,9},{9,8},{10,11... | collective-permute-start | bytes 3145736 | tf_op jit(solution)/shard_map/ppermute | solution.py:128
  257.1 2.8 %collective-permute-start.21 = (f32[64,32,128]{2,1,0:T(8,128)S(1)}, f32[64,32,128]{2,1,0:T(8,128)}, u32[]{:S(2)}, u32[]{:S(2)}) collective-permute-start(f32[64,32,128]{2,1,0:T(8,128)S(1)} %collective-permute-done.19), channel_id=1, source_target_pairs={{0,1},{1,0},{2,3},{3,2},{4,5},{5,4},{6,7},{7,6},{8,9},{9,8},{10,11... | collective-permute-start | bytes 3145736 | tf_op jit(solution)/shard_map/ppermute | solution.py:129
  (1 other events, 0.8 us)

commit v17 on v11

--- a/solution.py
+++ b/solution.py
@@ -125,17 +125,15 @@
                 jnp.concatenate([other_bf, own_bf], axis=0),
             )
     other_half = lax.ppermute(own, "sx", swap)
-    mine = jnp.where(
-        x == 0,
-        jnp.concatenate([own, other_half], axis=1),
-        jnp.concatenate([other_half, own], axis=1),
-    )
-    other_entries = lax.ppermute(mine, "sc", swap)
-    return jnp.where(
-        c == 0,
-        jnp.concatenate([mine, other_entries], axis=0),
-        jnp.concatenate([other_entries, mine], axis=0),
-    )
+    core_own = lax.ppermute(own, "sc", swap)
+    core_other = lax.ppermute(other_half, "sc", swap)
+    result = jnp.zeros(weights.shape, jnp.float32)
+    zero = jnp.int32(0)
+    other_start = (1 - c) * share
+    result = lax.dynamic_update_slice(result, own, (start, x * half_p, zero))
+    result = lax.dynamic_update_slice(result, other_half, (start, (1 - x) * half_p, zero))
+    result = lax.dynamic_update_slice(result, core_own, (other_start, x * half_p, zero))
+    return lax.dynamic_update_slice(result, core_other, (other_start, (1 - x) * half_p, zero))
 
 
 def solution(mesh):

time: 265 us -> 267 us (level)
  local copies, waits for them, and re-layouts: 14.7 us -> 21.4 us
  waiting for transfers between devices: 128 us -> 124 us
  other arithmetic: 15.1 us -> 11.3 us
    dynamic_update_slice x0 -> x3, local copies, waits for them, and re-layouts: none -> 4.34 us  [the longest x1 2.26 us: per_device(): lax.dynamic_update_slice(result, core_other, (other_start, (1 - x) * half...]
    ppermute x1 -> x2, waiting for transfers between devices: 4.15 us -> 0.71 us  [the longest x1 0.71 us: per_device(): core_other = lax.ppermute(other_half, 'sc', swap)]
    select_n x3 -> x0, other arithmetic: 3.42 us -> none  [the longest x1 2.46 us: per_device(): jnp.where(c == 0, jnp.concatenate([mine, other_entries], axis=0), jnp.con...]
  transfers between devices with their start and end apart: 23 -> 24, of which waited for: 18 -> 18; matrix products, arithmetic and copies ran while one was open for 3% -> 3% of each run, Pallas kernels for 0% -> 0%
where the time goes in v17:
time: 267 us; the launch traced here: 266 us
  waiting for transfers between devices  124 us (46%)
  blocking collectives  59.7 us (22%)
  starting transfers between devices  31.2 us (12%)
  local copies, waits for them, and re-layouts  21.4 us (8%)
  matrix products  17.8 us (7%)
  other arithmetic  11.3 us (4%)
    all_to_all x1, blocking collectives, predict(): gathered = lax.all_to_all(partial, 'snp', 0, 0, tiled=False)  59.7 us
    ppermute x8, waiting for transfers between devices, per_device(): moving = lax.ppermute(moving, 'snp', forward)  43.1 us
    all_to_all x2, waiting for transfers between devices, predict(): gathered = lax.all_to_all(partial, 'snp', 0, 0, tiled=False)  37.7 us
    ppermute x1, waiting for transfers between devices, per_device(): other_half = lax.ppermute(own, 'sx', swap)  23.5 us
    all_to_all x2, starting transfers between devices, predict(): gathered = lax.all_to_all(partial, 'snp', 0, 0, tiled=False)  11.5 us
    ppermute x1, waiting for transfers between devices, per_device(): geno_peer = lax.ppermute(genotypes, 'sx', swap)  11.2 us
    ppermute x6, starting transfers between devices, per_device(): moving = lax.ppermute(moving, 'snp', backward)  8.53 us
    dot_general x3, matrix products, predict(): jnp.einsum('jbpk,sbk->jps', dense, samples.reshape(count, block_count, bl...  8.41 us
  transfers between devices with their start and end apart: 24, of which 18 were waited for; matrix products, arithmetic and copies ran while one was open for 3% of the time, Pallas kernels for 0%

profile of v17, /device:TPU:0, one launch (start us, length us, event | category | flops | bytes accessed | tf_op | source)
XLA Modules:
  0.0 266.3 jit_solution(2003079075227502617)
XLA Ops:
  6.0 1.9 select_convert_fusion
  10.4 2.3 bitcast_convert_fusion.2
  12.7 7.3 %all-to-all-start = ((bf16[8,192,384]{2,1,0:T(8,128)(2,1)}), bf16[8,192,384]{2,1,0:T(8,128)(2,1)S(1)}, u32[]{:S(2)}, u32[]{:S(2)}) async-start(bf16[8,192,384]{2,1,0:T(8,128)(2,1)} %bitcast.207), calls=%async_computation | async-start | bytes 2359296 | tf_op jit(solution)/shard_map/all_to_all | solution.py:91
  21.4 11.2 %collective-permute-done.1 = bf16[384,640]{0,1:T(8,128)(2,1)S(1)} collective-permute-done((bf16[384,640]{0,1:T(8,128)(2,1)S(1)}, bf16[384,640]{0,1:T(8,128)(2,1)S(1)}, u32[]{:S(2)}, u32[]{:S(2)}) %collective-permute-start.1) | collective-permute-done | bytes 491552 | tf_op jit(solution)/shard_map/ppermute | solution.py:34
  33.4 3.9 %bitcast_convert_fusion.1 = bf16[48,32,384]{2,1,0:T(8,128)(2,1)} fusion(bf16[48,5,32,128]{3,2,1,0:T(8,128)(2,1)} %bitcast.203, bf16[384,5,128,1]{0,2,1,3:T(8,128)(2,1)S(1)} %bitcast.212), kind=kOutput, calls=%fused_computation.4 | convolution fusion | flops 755564544 | bytes 3637248 | tf_op jit(solution)/shard_map/jbpk,sbk->jps/dot_general | solution.py:84
  37.3 11.2 %all-to-all-done = bf16[8,192,384]{2,1,0:T(8,128)(2,1)S(1)} async-done(((bf16[8,192,384]{2,1,0:T(8,128)(2,1)}), bf16[8,192,384]{2,1,0:T(8,128)(2,1)S(1)}, u32[]{:S(2)}, u32[]{:S(2)}) %all-to-all-start) | async-done | bytes 1179680 | tf_op jit(solution)/shard_map/all_to_all | solution.py:91
  48.5 4.3 %all-to-all-start.1 = ((bf16[8,192,384]{2,1,0:T(8,128)(2,1)}), bf16[8,192,384]{2,1,0:T(8,128)(2,1)}, u32[]{:S(2)}, u32[]{:S(2)}) async-start(bf16[8,192,384]{2,1,0:T(8,128)(2,1)} %bitcast.206), calls=%async_computation.1 | async-start | bytes 2359296 | tf_op jit(solution)/shard_map/all_to_all | solution.py:91
  54.6 26.5 %all-to-all-done.1 = bf16[8,192,384]{2,1,0:T(8,128)(2,1)} async-done(((bf16[8,192,384]{2,1,0:T(8,128)(2,1)}), bf16[8,192,384]{2,1,0:T(8,128)(2,1)}, u32[]{:S(2)}, u32[]{:S(2)}) %all-to-all-start.1) | async-done | bytes 1179680 | tf_op jit(solution)/shard_map/all_to_all | solution.py:91
  82.7 2.0 collective-permute-start.2
  84.8 5.5 %collective-permute-done.5 = bf16[192,768]{1,0:T(8,128)(2,1)S(1)} collective-permute-done((bf16[192,768]{1,0:T(8,128)(2,1)S(1)}, bf16[192,768]{1,0:T(8,128)(2,1)S(1)}, u32[]{:S(2)}, u32[]{:S(2)}) %collective-permute-start.5) | collective-permute-done | bytes 294944 | tf_op jit(solution)/shard_map/ppermute | solution.py:102
  90.3 2.0 collective-permute-start.3
  92.4 5.0 %collective-permute-done.6 = bf16[192,768]{1,0:T(8,128)(2,1)S(1)} collective-permute-done((bf16[192,768]{1,0:T(8,128)(2,1)S(1)}, bf16[192,768]{1,0:T(8,128)(2,1)S(1)}, u32[]{:S(2)}, u32[]{:S(2)}) %collective-permute-start.6) | collective-permute-done | bytes 294944 | tf_op jit(solution)/shard_map/ppermute | solution.py:102
  99.6 4.6 %collective-permute-done.7 = bf16[192,768]{1,0:T(8,128)(2,1)S(1)} collective-permute-done((bf16[192,768]{1,0:T(8,128)(2,1)S(1)}, bf16[192,768]{1,0:T(8,128)(2,1)S(1)}, u32[]{:S(2)}, u32[]{:S(2)}) %collective-permute-start.7) | collective-permute-done | bytes 294944 | tf_op jit(solution)/shard_map/ppermute | solution.py:102
  104.9 6.4 %collective-permute-done.8 = bf16[192,768]{1,0:T(8,128)(2,1)S(1)} collective-permute-done((bf16[192,768]{1,0:T(8,128)(2,1)S(1)}, bf16[192,768]{1,0:T(8,128)(2,1)S(1)}, u32[]{:S(2)}, u32[]{:S(2)}) %collective-permute-start.8) | collective-permute-done | bytes 294944 | tf_op jit(solution)/shard_map/ppermute | solution.py:102
  111.5 4.0 %fusion.31 = f32[48,32,5,128]{3,1,2,0:T(8,128)} fusion(bf16[48,32,768,1]{2,1,3,0:T(8,128)(2,1)S(1)} %bitcast.214, bf16[768,5,128,1]{0,2,1,3:T(8,128)(2,1)S(1)} %bitcast.208), kind=kOutput, calls=%fused_computation.97 | convolution fusion | flops 1509949440 | bytes 7274496 | tf_op jit(solution)/shard_map/jps,sbk->jpbk/dot_general | solution.py:110
  115.5 3.0 %gather_fusion = f32[128,32,128]{2,1,0:T(8,128)S(1)} fusion(f32[48,32,5,128]{3,1,2,0:T(8,128)} %fusion.31, s32[128]{0:T(128)S(1)} %get-tuple-element.11), kind=kCustom, calls=%fused_computation | custom fusion | bytes 4195328 | tf_op jit(solution)/shard_map/gather | solution.py:113
  119.8 2.7 %collective-permute-done.9 = f32[64,32,128]{2,1,0:T(8,128)} collective-permute-done((f32[64,32,128]{2,1,0:T(8,128)}, f32[64,32,128]{2,1,0:T(8,128)}, u32[]{:S(2)}, u32[]{:S(2)}) %collective-permute-start.9) | collective-permute-done | bytes 1048608 | tf_op jit(solution)/shard_map/ppermute | solution.py:117
  122.5 4.2 %fusion.30 = (bf16[64,32,128]{2,1,0:T(8,128)(2,1)S(1)}, f32[64,32,128]{2,1,0:T(8,128)}) fusion(f32[64]{0:T(128)S(1)} %dynamic_slice.43, f32[64,32,128]{2,1,0:T(8,128)} %collective-permute-done.9, f32[2,64,32,128]{3,2,1,0:T(8,128)S(1)} %bitcast.190, s32[]{:T(128)S(6)} %select_n.151, f32[128,64,128]{2,1,0:T(8,128)} %param.10, s32[]{:T(128)S(6)} %select_n.136, ...), kind=kLoop, calls=%fused_computation.96 | loop fusion | flops 2883584 | bytes 4718924 | tf_op jit(solution)/shard_map/convert_element_type | solution.py:120
  130.7 2.2 bitcast_convert_fusion
  132.9 59.7 %all_to_all.15 = bf16[8,192,768]{2,1,0:T(8,128)(2,1)S(1)} all-to-all(bf16[8,192,768]{2,1,0:T(8,128)(2,1)S(1)} %bitcast.201), channel_id=1, replica_groups=mesh['snp'=8,'sx'=2,'sc'=2] {'snp'}, dimensions={0} | all-to-all | bytes 4718592 | tf_op jit(solution)/shard_map/all_to_all | solution.py:91
  195.0 5.6 %collective-permute-done.14 = bf16[192,768]{1,0:T(8,128)(2,1)S(1)} collective-permute-done((bf16[192,768]{1,0:T(8,128)(2,1)S(1)}, bf16[192,768]{1,0:T(8,128)(2,1)S(1)}, u32[]{:S(2)}, u32[]{:S(2)}) %collective-permute-start.14) | collective-permute-done | bytes 294944 | tf_op jit(solution)/shard_map/ppermute | solution.py:102
  202.7 5.2 %collective-permute-done.15 = bf16[192,768]{1,0:T(8,128)(2,1)S(1)} collective-permute-done((bf16[192,768]{1,0:T(8,128)(2,1)S(1)}, bf16[192,768]{1,0:T(8,128)(2,1)S(1)}, u32[]{:S(2)}, u32[]{:S(2)}) %collective-permute-start.15) | collective-permute-done | bytes 294944 | tf_op jit(solution)/shard_map/ppermute | solution.py:102
  210.0 6.1 %collective-permute-done.16 = bf16[192,768]{1,0:T(8,128)(2,1)S(1)} collective-permute-done((bf16[192,768]{1,0:T(8,128)(2,1)S(1)}, bf16[192,768]{1,0:T(8,128)(2,1)S(1)}, u32[]{:S(2)}, u32[]{:S(2)}) %collective-permute-start.16) | collective-permute-done | bytes 294944 | tf_op jit(solution)/shard_map/ppermute | solution.py:102
  216.1 1.9 collective-permute-start.17
  218.1 4.8 %collective-permute-done.17 = bf16[192,768]{1,0:T(8,128)(2,1)S(1)} collective-permute-done((bf16[192,768]{1,0:T(8,128)(2,1)S(1)}, bf16[192,768]{1,0:T(8,128)(2,1)S(1)}, u32[]{:S(2)}, u32[]{:S(2)}) %collective-permute-start.17) | collective-permute-done | bytes 294944 | tf_op jit(solution)/shard_map/ppermute | solution.py:102
  222.9 4.0 %fusion.32 = f32[48,32,5,128]{3,1,2,0:T(8,128)} fusion(bf16[48,32,768,1]{2,1,3,0:T(8,128)(2,1)S(1)} %bitcast.213, bf16[768,5,128,1]{0,2,1,3:T(8,128)(2,1)S(1)} %bitcast.210), kind=kOutput, calls=%fused_computation.98 | convolution fusion | flops 1509949440 | bytes 7274496 | tf_op jit(solution)/shard_map/jps,sbk->jpbk/dot_general | solution.py:110
  226.9 3.0 %gather_fusion.1 = f32[128,32,128]{2,1,0:T(8,128)S(1)} fusion(f32[48,32,5,128]{3,1,2,0:T(8,128)} %fusion.32, s32[128]{0:T(128)S(1)} %get-tuple-element.11), kind=kCustom, calls=%fused_computation.1 | custom fusion | bytes 4195328 | tf_op jit(solution)/shard_map/gather | solution.py:113
  230.1 2.6 collective-permute-done.18
  233.8 2.0 copy-done
  235.8 1.9 collective-permute-start.19
  237.7 23.5 %collective-permute-done.19 = f32[64,32,128]{2,1,0:T(8,128)S(1)} collective-permute-done((f32[64,32,128]{2,1,0:T(8,128)S(1)}, f32[64,32,128]{2,1,0:T(8,128)S(1)}, u32[]{:S(2)}, u32[]{:S(2)}) %collective-permute-start.19) | collective-permute-done | bytes 1048608 | tf_op jit(solution)/shard_map/ppermute | solution.py:127
  264.0 2.3 constant_dynamic-update-slice_fusion.3
  (89 shorter events, 32.7 us)
Async XLA Ops:
  9.1 1.3 copy-start.2
  12.7 35.9 %all-to-all-start = ((bf16[8,192,384]{2,1,0:T(8,128)(2,1)}), bf16[8,192,384]{2,1,0:T(8,128)(2,1)S(1)}, u32[]{:S(2)}, u32[]{:S(2)}) async-start(bf16[8,192,384]{2,1,0:T(8,128)(2,1)} %bitcast.207), calls=%async_computation | async-start | bytes 2359296 | tf_op jit(solution)/shard_map/all_to_all | solution.py:91
  20.0 12.7 %collective-permute-start.1 = (bf16[384,640]{0,1:T(8,128)(2,1)S(1)}, bf16[384,640]{0,1:T(8,128)(2,1)S(1)}, u32[]{:S(2)}, u32[]{:S(2)}) collective-permute-start(bf16[384,640]{0,1:T(8,128)(2,1)S(1)} %copy.29), channel_id=1, source_target_pairs={{0,2},{2,0},{1,3},{3,1},{4,6},{6,4},{5,7},{7,5},{8,10},{10,8},{9,1... | collective-permute-start | bytes 1474568 | tf_op jit(solution)/shard_map/ppermute | solution.py:34
  33.4 19.4 %copy-start.5 = (f32[384,384]{1,0:T(8,128)S(1)}, f32[384,384]{1,0:T(8,128)}, u32[]{:S(2)}) copy-start(f32[384,384]{1,0:T(8,128)} %param.9) | copy-start | bytes 1769476
  48.5 32.6 %all-to-all-start.1 = ((bf16[8,192,384]{2,1,0:T(8,128)(2,1)}), bf16[8,192,384]{2,1,0:T(8,128)(2,1)}, u32[]{:S(2)}, u32[]{:S(2)}) async-start(bf16[8,192,384]{2,1,0:T(8,128)(2,1)} %bitcast.206), calls=%async_computation.1 | async-start | bytes 2359296 | tf_op jit(solution)/shard_map/all_to_all | solution.py:91
  52.9 39.4 %copy-start.7 = (bf16[384,640]{0,1:T(8,128)(2,1)S(1)}, bf16[384,640]{0,1:T(8,128)(2,1)}, u32[]{:S(2)}) copy-start(bf16[384,640]{0,1:T(8,128)(2,1)} %copy-done.6) | copy-start | bytes 1474564
  52.9 29.7 %collective-permute-start = (f32[6,32,384]{2,1,0:T(8,128)S(1)}, f32[6,32,384]{2,1,0:T(8,128)S(1)}, u32[]{:S(2)}, u32[]{:S(2)}) collective-permute-start(f32[6,32,384]{2,1,0:T(8,128)S(1)} %get-tuple-element.10), channel_id=1, source_target_pairs={{0,2},{2,0},{1,3},{3,1},{4,6},{6,4},{5,7},{7,5},{8,10},{10,8},{9,1... | collective-permute-start | bytes 884744 | tf_op jit(solution)/shard_map/ppermute | solution.py:40
  82.7 7.6 %collective-permute-start.5 = (bf16[192,768]{1,0:T(8,128)(2,1)S(1)}, bf16[192,768]{1,0:T(8,128)(2,1)S(1)}, u32[]{:S(2)}, u32[]{:S(2)}) collective-permute-start(bf16[192,768]{1,0:T(8,128)(2,1)S(1)} %fusion.7), channel_id=1, source_target_pairs={{0,8},{8,16},{16,24},{24,28},{28,20},{20,12},{12,4},{4,0},{1,9},{9... | collective-permute-start | bytes 884744 | tf_op jit(solution)/shard_map/ppermute | solution.py:102
  82.7 7.5 %collective-permute-start.2 = (bf16[192,768]{1,0:T(8,128)(2,1)S(1)}, bf16[192,768]{1,0:T(8,128)(2,1)S(1)}, u32[]{:S(2)}, u32[]{:S(2)}) collective-permute-start(bf16[192,768]{1,0:T(8,128)(2,1)S(1)} %fusion.7), channel_id=1, source_target_pairs={{0,4},{8,0},{16,8},{24,16},{28,24},{20,28},{12,20},{4,12},{1,5},{9... | collective-permute-start | bytes 884744 | tf_op jit(solution)/shard_map/ppermute | solution.py:106
  90.3 7.2 %collective-permute-start.6 = (bf16[192,768]{1,0:T(8,128)(2,1)S(1)}, bf16[192,768]{1,0:T(8,128)(2,1)S(1)}, u32[]{:S(2)}, u32[]{:S(2)}) collective-permute-start(bf16[192,768]{1,0:T(8,128)(2,1)S(1)} %collective-permute-done.5), channel_id=1, source_target_pairs={{0,8},{8,16},{16,24},{24,28},{28,20},{20,12},{12,4},{4,0},{1,9},{9... | collective-permute-start | bytes 884744 | tf_op jit(solution)/shard_map/ppermute | solution.py:102
  90.3 7.6 %collective-permute-start.3 = (bf16[192,768]{1,0:T(8,128)(2,1)S(1)}, bf16[192,768]{1,0:T(8,128)(2,1)S(1)}, u32[]{:S(2)}, u32[]{:S(2)}) collective-permute-start(bf16[192,768]{1,0:T(8,128)(2,1)S(1)} %collective-permute-done.2), channel_id=1, source_target_pairs={{0,4},{8,0},{16,8},{24,16},{28,24},{20,28},{12,20},{4,12},{1,5},{9... | collective-permute-start | bytes 884744 | tf_op jit(solution)/shard_map/ppermute | solution.py:106
  92.4 19.1 %copy-start.3 = (bf16[768,640]{0,1:T(8,128)(2,1)}, bf16[768,640]{0,1:T(8,128)(2,1)S(1)}, u32[]{:S(2)}) copy-start(bf16[768,640]{0,1:T(8,128)(2,1)S(1)} %pad_maximum_fusion) | copy-start | bytes 2949124
  97.4 6.7 %collective-permute-start.7 = (bf16[192,768]{1,0:T(8,128)(2,1)S(1)}, bf16[192,768]{1,0:T(8,128)(2,1)S(1)}, u32[]{:S(2)}, u32[]{:S(2)}) collective-permute-start(bf16[192,768]{1,0:T(8,128)(2,1)S(1)} %collective-permute-done.6), channel_id=1, source_target_pairs={{0,8},{8,16},{16,24},{24,28},{28,20},{20,12},{12,4},{4,0},{1,9},{9... | collective-permute-start | bytes 884744 | tf_op jit(solution)/shard_map/ppermute | solution.py:102
  97.9 7.0 %collective-permute-start.4 = (bf16[192,768]{1,0:T(8,128)(2,1)S(1)}, bf16[192,768]{1,0:T(8,128)(2,1)S(1)}, u32[]{:S(2)}, u32[]{:S(2)}) collective-permute-start(bf16[192,768]{1,0:T(8,128)(2,1)S(1)} %collective-permute-done.3), channel_id=1, source_target_pairs={{0,4},{8,0},{16,8},{24,16},{28,24},{20,28},{12,20},{4,12},{1,5},{9... | collective-permute-start | bytes 884744 | tf_op jit(solution)/shard_map/ppermute | solution.py:106
  104.2 7.2 %collective-permute-start.8 = (bf16[192,768]{1,0:T(8,128)(2,1)S(1)}, bf16[192,768]{1,0:T(8,128)(2,1)S(1)}, u32[]{:S(2)}, u32[]{:S(2)}) collective-permute-start(bf16[192,768]{1,0:T(8,128)(2,1)S(1)} %collective-permute-done.7), channel_id=1, source_target_pairs={{0,8},{8,16},{16,24},{24,28},{28,20},{20,12},{12,4},{4,0},{1,9},{9... | collective-permute-start | bytes 884744 | tf_op jit(solution)/shard_map/ppermute | solution.py:102
  115.5 4.1 %copy-start.8 = (f32[46]{0:T(128)S(1)}, f32[46]{0:T(128)}, u32[]{:S(2)}) copy-start(f32[46]{0:T(128)} %param.14) | copy-start | bytes 556
  119.5 3.0 %collective-permute-start.9 = (f32[64,32,128]{2,1,0:T(8,128)}, f32[64,32,128]{2,1,0:T(8,128)}, u32[]{:S(2)}, u32[]{:S(2)}) collective-permute-start(f32[64,32,128]{2,1,0:T(8,128)} %dynamic-slice_bitcast_fusion.1), channel_id=1, source_target_pairs={{0,1},{1,0},{2,3},{3,2},{4,5},{5,4},{6,7},{7,6},{8,9},{9,8},{10,11... | collective-permute-start | bytes 3145736 | tf_op jit(solution)/shard_map/ppermute | solution.py:117
  126.7 1.9 collective-permute-start.10
  129.5 1.2 copy-start.4
  193.0 7.7 %collective-permute-start.14 = (bf16[192,768]{1,0:T(8,128)(2,1)S(1)}, bf16[192,768]{1,0:T(8,128)(2,1)S(1)}, u32[]{:S(2)}, u32[]{:S(2)}) collective-permute-start(bf16[192,768]{1,0:T(8,128)(2,1)S(1)} %subtract_convert_fusion), channel_id=1, source_target_pairs={{0,8},{8,16},{16,24},{24,28},{28,20},{20,12},{12,4},{4,0},{1,9},{9... | collective-permute-start | bytes 884744 | tf_op jit(solution)/shard_map/ppermute | solution.py:102
  194.1 7.4 %collective-permute-start.11 = (bf16[192,768]{1,0:T(8,128)(2,1)S(1)}, bf16[192,768]{1,0:T(8,128)(2,1)S(1)}, u32[]{:S(2)}, u32[]{:S(2)}) collective-permute-start(bf16[192,768]{1,0:T(8,128)(2,1)S(1)} %subtract_convert_fusion), channel_id=1, source_target_pairs={{0,4},{8,0},{16,8},{24,16},{28,24},{20,28},{12,20},{4,12},{1,5},{9... | collective-permute-start | bytes 884744 | tf_op jit(solution)/shard_map/ppermute | solution.py:106
  200.6 7.2 %collective-permute-start.15 = (bf16[192,768]{1,0:T(8,128)(2,1)S(1)}, bf16[192,768]{1,0:T(8,128)(2,1)S(1)}, u32[]{:S(2)}, u32[]{:S(2)}) collective-permute-start(bf16[192,768]{1,0:T(8,128)(2,1)S(1)} %collective-permute-done.14), channel_id=1, source_target_pairs={{0,8},{8,16},{16,24},{24,28},{28,20},{20,12},{12,4},{4,0},{1,9},{9... | collective-permute-start | bytes 884744 | tf_op jit(solution)/shard_map/ppermute | solution.py:102
  201.5 7.8 %collective-permute-start.12 = (bf16[192,768]{1,0:T(8,128)(2,1)S(1)}, bf16[192,768]{1,0:T(8,128)(2,1)S(1)}, u32[]{:S(2)}, u32[]{:S(2)}) collective-permute-start(bf16[192,768]{1,0:T(8,128)(2,1)S(1)} %collective-permute-done.11), channel_id=1, source_target_pairs={{0,4},{8,0},{16,8},{24,16},{28,24},{20,28},{12,20},{4,12},{1,5},{9... | collective-permute-start | bytes 884744 | tf_op jit(solution)/shard_map/ppermute | solution.py:106
  207.8 8.3 %collective-permute-start.16 = (bf16[192,768]{1,0:T(8,128)(2,1)S(1)}, bf16[192,768]{1,0:T(8,128)(2,1)S(1)}, u32[]{:S(2)}, u32[]{:S(2)}) collective-permute-start(bf16[192,768]{1,0:T(8,128)(2,1)S(1)} %collective-permute-done.15), channel_id=1, source_target_pairs={{0,8},{8,16},{16,24},{24,28},{28,20},{20,12},{12,4},{4,0},{1,9},{9... | collective-permute-start | bytes 884744 | tf_op jit(solution)/shard_map/ppermute | solution.py:102
  209.3 8.7 %collective-permute-start.13 = (bf16[192,768]{1,0:T(8,128)(2,1)S(1)}, bf16[192,768]{1,0:T(8,128)(2,1)S(1)}, u32[]{:S(2)}, u32[]{:S(2)}) collective-permute-start(bf16[192,768]{1,0:T(8,128)(2,1)S(1)} %collective-permute-done.12), channel_id=1, source_target_pairs={{0,4},{8,0},{16,8},{24,16},{28,24},{20,28},{12,20},{4,12},{1,5},{9... | collective-permute-start | bytes 884744 | tf_op jit(solution)/shard_map/ppermute | solution.py:106
  216.1 6.7 %collective-permute-start.17 = (bf16[192,768]{1,0:T(8,128)(2,1)S(1)}, bf16[192,768]{1,0:T(8,128)(2,1)S(1)}, u32[]{:S(2)}, u32[]{:S(2)}) collective-permute-start(bf16[192,768]{1,0:T(8,128)(2,1)S(1)} %collective-permute-done.16), channel_id=1, source_target_pairs={{0,8},{8,16},{16,24},{24,28},{28,20},{20,12},{12,4},{4,0},{1,9},{9... | collective-permute-start | bytes 884744 | tf_op jit(solution)/shard_map/ppermute | solution.py:102
  230.0 3.3 %copy-start.1 = (f32[64,32,128]{2,1,0:T(8,128)S(1)}, f32[64,32,128]{2,1,0:T(8,128)}, u32[]{:S(2)}) copy-start(f32[64,32,128]{2,1,0:T(8,128)} %get-tuple-element.8) | copy-start | bytes 3145732
  230.0 2.7 %collective-permute-start.18 = (f32[64,32,128]{2,1,0:T(8,128)S(1)}, f32[64,32,128]{2,1,0:T(8,128)S(1)}, u32[]{:S(2)}, u32[]{:S(2)}) collective-permute-start(f32[64,32,128]{2,1,0:T(8,128)S(1)} %dynamic-slice_bitcast_fusion), channel_id=1, source_target_pairs={{0,1},{1,0},{2,3},{3,2},{4,5},{5,4},{6,7},{7,6},{8,9},{9,8},{10,11... | collective-permute-start | bytes 3145736 | tf_op jit(solution)/shard_map/ppermute | solution.py:117
  233.8 2.0 copy-start
  235.8 25.4 %collective-permute-start.19 = (f32[64,32,128]{2,1,0:T(8,128)S(1)}, f32[64,32,128]{2,1,0:T(8,128)S(1)}, u32[]{:S(2)}, u32[]{:S(2)}) collective-permute-start(f32[64,32,128]{2,1,0:T(8,128)S(1)} %get-tuple-element.6), channel_id=1, source_target_pairs={{0,2},{2,0},{1,3},{3,1},{4,6},{6,4},{5,7},{7,5},{8,10},{10,8},{9,1... | collective-permute-start | bytes 3145736 | tf_op jit(solution)/shard_map/ppermute | solution.py:127
  237.7 24.5 %collective-permute-start.20 = (f32[64,32,128]{2,1,0:T(8,128)S(1)}, f32[64,32,128]{2,1,0:T(8,128)S(1)}, u32[]{:S(2)}, u32[]{:S(2)}) collective-permute-start(f32[64,32,128]{2,1,0:T(8,128)S(1)} %get-tuple-element.6), channel_id=1, source_target_pairs={{0,1},{1,0},{2,3},{3,2},{4,5},{5,4},{6,7},{7,6},{8,9},{9,8},{10,11... | collective-permute-start | bytes 3145736 | tf_op jit(solution)/shard_map/ppermute | solution.py:128
  261.2 2.8 %collective-permute-start.21 = (f32[64,32,128]{2,1,0:T(8,128)S(1)}, f32[64,32,128]{2,1,0:T(8,128)}, u32[]{:S(2)}, u32[]{:S(2)}) collective-permute-start(f32[64,32,128]{2,1,0:T(8,128)S(1)} %collective-permute-done.19), channel_id=1, source_target_pairs={{0,1},{1,0},{2,3},{3,2},{4,5},{5,4},{6,7},{7,6},{8,9},{9,8},{10,11... | collective-permute-start | bytes 3145736 | tf_op jit(solution)/shard_map/ppermute | solution.py:129
  (1 other events, 0.8 us)

commit v18 on v11

--- a/solution.py
+++ b/solution.py
@@ -119,10 +119,10 @@
         if sweep + 1 < ITERS:
             own_bf = own.astype(jnp.bfloat16)
             other_bf = lax.ppermute(own_bf, "sc", swap)
-            weight_bf = jnp.where(
-                c == 0,
-                jnp.concatenate([own_bf, other_bf], axis=0),
-                jnp.concatenate([other_bf, own_bf], axis=0),
+            zero = jnp.int32(0)
+            weight_bf = lax.dynamic_update_slice(weight_bf, own_bf, (start, zero, zero))
+            weight_bf = lax.dynamic_update_slice(
+                weight_bf, other_bf, ((1 - c) * share, zero, zero)
             )
     other_half = lax.ppermute(own, "sx", swap)
     mine = jnp.where(

time: 265 us -> 271 us (1.023)
  other arithmetic: 15.1 us -> 19.6 us
    dynamic_update_slice x0 -> x1, other arithmetic: none -> 4.38 us  [per_device(): weight_bf = lax.dynamic_update_slice(weight_bf, own_bf, (start, zero, zero))]
    convert_element_type x1 -> x0, other arithmetic: 4.18 us -> none  [per_device(): own_bf = own.astype(jnp.bfloat16)]
    select_n x1, other arithmetic: 2.46 us -> 5.19 us  [per_device(): jnp.where(c == 0, jnp.concatenate([mine, other_entries], axis=0), jnp.con...]
where the time goes in v18:
time: 271 us; the launch traced here: 270 us
  waiting for transfers between devices  127 us (47%)
  blocking collectives  59.7 us (22%)
  starting transfers between devices  30.8 us (11%)
  other arithmetic  19.6 us (7%)
  matrix products  17.8 us (7%)
  local copies, waits for them, and re-layouts  14.3 us (5%)
    all_to_all x1, blocking collectives, predict(): gathered = lax.all_to_all(partial, 'snp', 0, 0, tiled=False)  59.7 us
    ppermute x8, waiting for transfers between devices, per_device(): moving = lax.ppermute(moving, 'snp', forward)  41.9 us
    all_to_all x2, waiting for transfers between devices, predict(): gathered = lax.all_to_all(partial, 'snp', 0, 0, tiled=False)  37.5 us
    ppermute x1, waiting for transfers between devices, per_device(): other_half = lax.ppermute(own, 'sx', swap)  23.9 us
    all_to_all x2, starting transfers between devices, predict(): gathered = lax.all_to_all(partial, 'snp', 0, 0, tiled=False)  11.5 us
    ppermute x1, waiting for transfers between devices, per_device(): geno_peer = lax.ppermute(genotypes, 'sx', swap)  11.4 us
    ppermute x6, starting transfers between devices, per_device(): moving = lax.ppermute(moving, 'snp', backward)  8.56 us
    dot_general x3, matrix products, predict(): jnp.einsum('jbpk,sbk->jps', dense, samples.reshape(count, block_count, bl...  8.43 us
  transfers between devices with their start and end apart: 23, of which 18 were waited for; matrix products, arithmetic and copies ran while one was open for 3% of the time, Pallas kernels for 0%

profile of v18, /device:TPU:0, one launch (start us, length us, event | category | flops | bytes accessed | tf_op | source)
XLA Modules:
  0.0 270.2 jit_solution(5419834055433453160)
XLA Ops:
  9.5 2.3 bitcast_convert_fusion.2
  11.8 7.3 %all-to-all-start = ((bf16[8,192,384]{2,1,0:T(8,128)(2,1)}), bf16[8,192,384]{2,1,0:T(8,128)(2,1)S(1)}, u32[]{:S(2)}, u32[]{:S(2)}) async-start(bf16[8,192,384]{2,1,0:T(8,128)(2,1)} %bitcast.206), calls=%async_computation | async-start | bytes 2359296 | tf_op jit(solution)/shard_map/all_to_all | solution.py:91
  20.6 11.4 %collective-permute-done.1 = bf16[384,640]{0,1:T(8,128)(2,1)S(1)} collective-permute-done((bf16[384,640]{0,1:T(8,128)(2,1)}, bf16[384,640]{0,1:T(8,128)(2,1)S(1)}, u32[]{:S(2)}, u32[]{:S(2)}) %collective-permute-start.1) | collective-permute-done | bytes 491552 | tf_op jit(solution)/shard_map/ppermute | solution.py:34
  32.8 3.9 %bitcast_convert_fusion.1 = bf16[48,32,384]{2,1,0:T(8,128)(2,1)} fusion(bf16[48,5,32,128]{3,2,1,0:T(8,128)(2,1)} %bitcast.202, bf16[384,5,128,1]{0,2,1,3:T(8,128)(2,1)S(1)} %bitcast.211), kind=kOutput, calls=%fused_computation.5 | convolution fusion | flops 755564544 | bytes 3637248 | tf_op jit(solution)/shard_map/jbpk,sbk->jps/dot_general | solution.py:84
  36.7 11.0 %all-to-all-done = bf16[8,192,384]{2,1,0:T(8,128)(2,1)S(1)} async-done(((bf16[8,192,384]{2,1,0:T(8,128)(2,1)}), bf16[8,192,384]{2,1,0:T(8,128)(2,1)S(1)}, u32[]{:S(2)}, u32[]{:S(2)}) %all-to-all-start) | async-done | bytes 1179680 | tf_op jit(solution)/shard_map/all_to_all | solution.py:91
  47.7 4.2 %all-to-all-start.1 = ((bf16[8,192,384]{2,1,0:T(8,128)(2,1)}), bf16[8,192,384]{2,1,0:T(8,128)(2,1)}, u32[]{:S(2)}, u32[]{:S(2)}) async-start(bf16[8,192,384]{2,1,0:T(8,128)(2,1)} %bitcast.205), calls=%async_computation.1 | async-start | bytes 2359296 | tf_op jit(solution)/shard_map/all_to_all | solution.py:91
  53.7 26.5 %all-to-all-done.1 = bf16[8,192,384]{2,1,0:T(8,128)(2,1)} async-done(((bf16[8,192,384]{2,1,0:T(8,128)(2,1)}), bf16[8,192,384]{2,1,0:T(8,128)(2,1)}, u32[]{:S(2)}, u32[]{:S(2)}) %all-to-all-start.1) | async-done | bytes 1179680 | tf_op jit(solution)/shard_map/all_to_all | solution.py:91
  81.9 2.0 collective-permute-start.2
  83.9 5.5 %collective-permute-done.5 = bf16[192,768]{1,0:T(8,128)(2,1)S(1)} collective-permute-done((bf16[192,768]{1,0:T(8,128)(2,1)S(1)}, bf16[192,768]{1,0:T(8,128)(2,1)S(1)}, u32[]{:S(2)}, u32[]{:S(2)}) %collective-permute-start.5) | collective-permute-done | bytes 294944 | tf_op jit(solution)/shard_map/ppermute | solution.py:102
  89.4 2.0 collective-permute-start.3
  92.7 3.9 %collective-permute-done.6 = bf16[192,768]{1,0:T(8,128)(2,1)S(1)} collective-permute-done((bf16[192,768]{1,0:T(8,128)(2,1)S(1)}, bf16[192,768]{1,0:T(8,128)(2,1)S(1)}, u32[]{:S(2)}, u32[]{:S(2)}) %collective-permute-start.6) | collective-permute-done | bytes 294944 | tf_op jit(solution)/shard_map/ppermute | solution.py:102
  98.7 4.5 %collective-permute-done.7 = bf16[192,768]{1,0:T(8,128)(2,1)S(1)} collective-permute-done((bf16[192,768]{1,0:T(8,128)(2,1)S(1)}, bf16[192,768]{1,0:T(8,128)(2,1)S(1)}, u32[]{:S(2)}, u32[]{:S(2)}) %collective-permute-start.7) | collective-permute-done | bytes 294944 | tf_op jit(solution)/shard_map/ppermute | solution.py:102
  104.1 6.4 %collective-permute-done.8 = bf16[192,768]{1,0:T(8,128)(2,1)S(1)} collective-permute-done((bf16[192,768]{1,0:T(8,128)(2,1)S(1)}, bf16[192,768]{1,0:T(8,128)(2,1)S(1)}, u32[]{:S(2)}, u32[]{:S(2)}) %collective-permute-start.8) | collective-permute-done | bytes 294944 | tf_op jit(solution)/shard_map/ppermute | solution.py:102
  110.6 4.0 %fusion.30 = f32[48,32,5,128]{3,1,2,0:T(8,128)} fusion(bf16[48,32,768,1]{2,1,3,0:T(8,128)(2,1)S(1)} %bitcast.213, bf16[768,5,128,1]{0,2,1,3:T(8,128)(2,1)S(1)} %bitcast.207), kind=kOutput, calls=%fused_computation.95 | convolution fusion | flops 1509949440 | bytes 7274496 | tf_op jit(solution)/shard_map/jps,sbk->jpbk/dot_general | solution.py:110
  114.6 3.0 %gather_fusion = f32[128,32,128]{2,1,0:T(8,128)S(1)} fusion(f32[48,32,5,128]{3,1,2,0:T(8,128)} %fusion.30, s32[128]{0:T(128)S(1)} %get-tuple-element.10), kind=kCustom, calls=%fused_computation | custom fusion | bytes 4195328 | tf_op jit(solution)/shard_map/gather | solution.py:113
  118.9 2.7 %collective-permute-done.9 = f32[64,32,128]{2,1,0:T(8,128)} collective-permute-done((f32[64,32,128]{2,1,0:T(8,128)}, f32[64,32,128]{2,1,0:T(8,128)}, u32[]{:S(2)}, u32[]{:S(2)}) %collective-permute-start.9) | collective-permute-done | bytes 1048608 | tf_op jit(solution)/shard_map/ppermute | solution.py:117
  121.7 4.4 %constant_dynamic-update-slice_fusion.1 = (bf16[128,32,128]{2,1,0:T(8,128)(2,1)S(1)}, bf16[64,32,128]{2,1,0:T(8,128)(2,1)}, f32[64,32,128]{2,1,0:T(8,128)}) fusion(bf16[128,32,128]{2,1,0:T(8,128)(2,1)S(1)} %select_convert_fusion, s32[]{:T(128)S(6)} %select_n.137, f32[64]{0:T(128)S(1)} %dynamic_slice.43, f32[64,32,128]{2,1,0:T(8,128)} %collective-permute-done.9, ...), kind=kLoop, calls=%fused_computation.63 | loop fusion | flops 2883584 | bytes 5243920 | tf_op jit(solution)/shard_map/dynamic_update_slice | solution.py:123
  126.2 2.0 collective-permute-done.10
  130.2 2.2 bitcast_convert_fusion
  132.4 59.7 %all_to_all.15 = bf16[8,192,768]{2,1,0:T(8,128)(2,1)S(1)} all-to-all(bf16[8,192,768]{2,1,0:T(8,128)(2,1)S(1)} %bitcast.200), channel_id=1, replica_groups=mesh['snp'=8,'sx'=2,'sc'=2] {'snp'}, dimensions={0} | all-to-all | bytes 4718592 | tf_op jit(solution)/shard_map/all_to_all | solution.py:91
  195.1 5.6 %collective-permute-done.14 = bf16[192,768]{1,0:T(8,128)(2,1)S(1)} collective-permute-done((bf16[192,768]{1,0:T(8,128)(2,1)S(1)}, bf16[192,768]{1,0:T(8,128)(2,1)S(1)}, u32[]{:S(2)}, u32[]{:S(2)}) %collective-permute-start.14) | collective-permute-done | bytes 294944 | tf_op jit(solution)/shard_map/ppermute | solution.py:102
  202.7 5.2 %collective-permute-done.15 = bf16[192,768]{1,0:T(8,128)(2,1)S(1)} collective-permute-done((bf16[192,768]{1,0:T(8,128)(2,1)S(1)}, bf16[192,768]{1,0:T(8,128)(2,1)S(1)}, u32[]{:S(2)}, u32[]{:S(2)}) %collective-permute-start.15) | collective-permute-done | bytes 294944 | tf_op jit(solution)/shard_map/ppermute | solution.py:102
  210.1 6.1 %collective-permute-done.16 = bf16[192,768]{1,0:T(8,128)(2,1)S(1)} collective-permute-done((bf16[192,768]{1,0:T(8,128)(2,1)S(1)}, bf16[192,768]{1,0:T(8,128)(2,1)S(1)}, u32[]{:S(2)}, u32[]{:S(2)}) %collective-permute-start.16) | collective-permute-done | bytes 294944 | tf_op jit(solution)/shard_map/ppermute | solution.py:102
  216.2 1.9 collective-permute-start.17
  218.1 4.8 %collective-permute-done.17 = bf16[192,768]{1,0:T(8,128)(2,1)S(1)} collective-permute-done((bf16[192,768]{1,0:T(8,128)(2,1)S(1)}, bf16[192,768]{1,0:T(8,128)(2,1)S(1)}, u32[]{:S(2)}, u32[]{:S(2)}) %collective-permute-start.17) | collective-permute-done | bytes 294944 | tf_op jit(solution)/shard_map/ppermute | solution.py:102
  223.0 4.0 %fusion.31 = f32[48,32,5,128]{3,1,2,0:T(8,128)} fusion(bf16[48,32,768,1]{2,1,3,0:T(8,128)(2,1)S(1)} %bitcast.212, bf16[768,5,128,1]{0,2,1,3:T(8,128)(2,1)S(1)} %bitcast.209), kind=kOutput, calls=%fused_computation.96 | convolution fusion | flops 1509949440 | bytes 7274496 | tf_op jit(solution)/shard_map/jps,sbk->jpbk/dot_general | solution.py:110
  227.0 3.0 %gather_fusion.1 = f32[128,32,128]{2,1,0:T(8,128)S(1)} fusion(f32[48,32,5,128]{3,1,2,0:T(8,128)} %fusion.31, s32[128]{0:T(128)S(1)} %get-tuple-element.10), kind=kCustom, calls=%fused_computation.1 | custom fusion | bytes 4195328 | tf_op jit(solution)/shard_map/gather | solution.py:113
  230.2 2.6 collective-permute-done.18
  234.8 23.9 %collective-permute-done.19 = f32[64,32,128]{2,1,0:T(8,128)} collective-permute-done((f32[64,32,128]{2,1,0:T(8,128)S(1)}, f32[64,32,128]{2,1,0:T(8,128)}, u32[]{:S(2)}, u32[]{:S(2)}) %collective-permute-start.19) | collective-permute-done | bytes 1048608 | tf_op jit(solution)/shard_map/ppermute | solution.py:127
  258.7 2.0 maximum_select_fusion.1
  260.8 4.3 %collective-permute-done.20 = f32[64,64,128]{2,1,0:T(8,128)} collective-permute-done((f32[64,64,128]{2,1,0:T(8,128)S(1)}, f32[64,64,128]{2,1,0:T(8,128)}, u32[]{:S(2)}, u32[]{:S(2)}) %collective-permute-start.20) | collective-permute-done | bytes 2097184 | tf_op jit(solution)/shard_map/ppermute | solution.py:133
  265.1 5.2 %maximum_select_fusion = f32[128,64,128]{2,1,0:T(8,128)} fusion(f32[64,64,128]{2,1,0:T(8,128)} %collective-permute-done.20, f32[64,64,128]{2,1,0:T(8,128)S(1)} %maximum_select_fusion.1, pred[]{:T(512)S(6)} %eq.39), kind=kLoop, calls=%fused_computation.4 | loop fusion | flops 3145728 | bytes 8388609 | tf_op jit(solution)/shard_map/jit(_where)/select_n | solution.py:134
  (87 shorter events, 31.8 us)
Async XLA Ops:
  7.8 4.0 %copy-start.3 = (bf16[240,32,128]{2,1,0:T(8,128)(2,1)}, bf16[240,32,128]{2,1,0:T(8,128)(2,1)S(1)}, u32[]{:S(2)}) copy-start(bf16[240,32,128]{2,1,0:T(8,128)(2,1)S(1)} %copy.28) | copy-start | bytes 5898244
  9.5 2.3 copy-start.4
  11.8 35.9 %all-to-all-start = ((bf16[8,192,384]{2,1,0:T(8,128)(2,1)}), bf16[8,192,384]{2,1,0:T(8,128)(2,1)S(1)}, u32[]{:S(2)}, u32[]{:S(2)}) async-start(bf16[8,192,384]{2,1,0:T(8,128)(2,1)} %bitcast.206), calls=%async_computation | async-start | bytes 2359296 | tf_op jit(solution)/shard_map/all_to_all | solution.py:91
  19.1 12.9 %collective-permute-start.1 = (bf16[384,640]{0,1:T(8,128)(2,1)}, bf16[384,640]{0,1:T(8,128)(2,1)S(1)}, u32[]{:S(2)}, u32[]{:S(2)}) collective-permute-start(bf16[384,640]{0,1:T(8,128)(2,1)} %copy-done.4), channel_id=1, source_target_pairs={{0,2},{2,0},{1,3},{3,1},{4,6},{6,4},{5,7},{7,5},{8,10},{10,8},{9,1... | collective-permute-start | bytes 1474568 | tf_op jit(solution)/shard_map/ppermute | solution.py:34
  32.8 19.2 %copy-start.7 = (f32[384,384]{1,0:T(8,128)S(1)}, f32[384,384]{1,0:T(8,128)}, u32[]{:S(2)}) copy-start(f32[384,384]{1,0:T(8,128)} %param.9) | copy-start | bytes 1769476
  47.7 32.6 %all-to-all-start.1 = ((bf16[8,192,384]{2,1,0:T(8,128)(2,1)}), bf16[8,192,384]{2,1,0:T(8,128)(2,1)}, u32[]{:S(2)}, u32[]{:S(2)}) async-start(bf16[8,192,384]{2,1,0:T(8,128)(2,1)} %bitcast.205), calls=%async_computation.1 | async-start | bytes 2359296 | tf_op jit(solution)/shard_map/all_to_all | solution.py:91
  52.0 29.7 %collective-permute-start = (f32[6,32,384]{2,1,0:T(8,128)S(1)}, f32[6,32,384]{2,1,0:T(8,128)S(1)}, u32[]{:S(2)}, u32[]{:S(2)}) collective-permute-start(f32[6,32,384]{2,1,0:T(8,128)S(1)} %get-tuple-element.9), channel_id=1, source_target_pairs={{0,2},{2,0},{1,3},{3,1},{4,6},{6,4},{5,7},{7,5},{8,10},{10,8},{9,1... | collective-permute-start | bytes 884744 | tf_op jit(solution)/shard_map/ppermute | solution.py:40
  81.7 14.9 %copy-start = (f32[6,32,384]{2,1,0:T(8,128)}, f32[6,32,384]{2,1,0:T(8,128)S(1)}, u32[]{:S(2)}) copy-start(f32[6,32,384]{2,1,0:T(8,128)S(1)} %collective-permute-done) | copy-start | bytes 884740
  81.8 7.6 %collective-permute-start.5 = (bf16[192,768]{1,0:T(8,128)(2,1)S(1)}, bf16[192,768]{1,0:T(8,128)(2,1)S(1)}, u32[]{:S(2)}, u32[]{:S(2)}) collective-permute-start(bf16[192,768]{1,0:T(8,128)(2,1)S(1)} %fusion.7), channel_id=1, source_target_pairs={{0,8},{8,16},{16,24},{24,28},{28,20},{20,12},{12,4},{4,0},{1,9},{9... | collective-permute-start | bytes 884744 | tf_op jit(solution)/shard_map/ppermute | solution.py:102
  81.9 7.5 %collective-permute-start.2 = (bf16[192,768]{1,0:T(8,128)(2,1)S(1)}, bf16[192,768]{1,0:T(8,128)(2,1)S(1)}, u32[]{:S(2)}, u32[]{:S(2)}) collective-permute-start(bf16[192,768]{1,0:T(8,128)(2,1)S(1)} %fusion.7), channel_id=1, source_target_pairs={{0,4},{8,0},{16,8},{24,16},{28,24},{20,28},{12,20},{4,12},{1,5},{9... | collective-permute-start | bytes 884744 | tf_op jit(solution)/shard_map/ppermute | solution.py:106
  89.4 7.2 %collective-permute-start.6 = (bf16[192,768]{1,0:T(8,128)(2,1)S(1)}, bf16[192,768]{1,0:T(8,128)(2,1)S(1)}, u32[]{:S(2)}, u32[]{:S(2)}) collective-permute-start(bf16[192,768]{1,0:T(8,128)(2,1)S(1)} %collective-permute-done.5), channel_id=1, source_target_pairs={{0,8},{8,16},{16,24},{24,28},{28,20},{20,12},{12,4},{4,0},{1,9},{9... | collective-permute-start | bytes 884744 | tf_op jit(solution)/shard_map/ppermute | solution.py:102
  89.4 7.6 %collective-permute-start.3 = (bf16[192,768]{1,0:T(8,128)(2,1)S(1)}, bf16[192,768]{1,0:T(8,128)(2,1)S(1)}, u32[]{:S(2)}, u32[]{:S(2)}) collective-permute-start(bf16[192,768]{1,0:T(8,128)(2,1)S(1)} %collective-permute-done.2), channel_id=1, source_target_pairs={{0,4},{8,0},{16,8},{24,16},{28,24},{20,28},{12,20},{4,12},{1,5},{9... | collective-permute-start | bytes 884744 | tf_op jit(solution)/shard_map/ppermute | solution.py:106
  92.7 17.9 %copy-start.5 = (bf16[768,640]{0,1:T(8,128)(2,1)}, bf16[768,640]{0,1:T(8,128)(2,1)S(1)}, u32[]{:S(2)}) copy-start(bf16[768,640]{0,1:T(8,128)(2,1)S(1)} %pad_maximum_fusion) | copy-start | bytes 2949124
  96.6 6.7 %collective-permute-start.7 = (bf16[192,768]{1,0:T(8,128)(2,1)S(1)}, bf16[192,768]{1,0:T(8,128)(2,1)S(1)}, u32[]{:S(2)}, u32[]{:S(2)}) collective-permute-start(bf16[192,768]{1,0:T(8,128)(2,1)S(1)} %collective-permute-done.6), channel_id=1, source_target_pairs={{0,8},{8,16},{16,24},{24,28},{28,20},{20,12},{12,4},{4,0},{1,9},{9... | collective-permute-start | bytes 884744 | tf_op jit(solution)/shard_map/ppermute | solution.py:102
  97.0 7.0 %collective-permute-start.4 = (bf16[192,768]{1,0:T(8,128)(2,1)S(1)}, bf16[192,768]{1,0:T(8,128)(2,1)S(1)}, u32[]{:S(2)}, u32[]{:S(2)}) collective-permute-start(bf16[192,768]{1,0:T(8,128)(2,1)S(1)} %collective-permute-done.3), channel_id=1, source_target_pairs={{0,4},{8,0},{16,8},{24,16},{28,24},{20,28},{12,20},{4,12},{1,5},{9... | collective-permute-start | bytes 884744 | tf_op jit(solution)/shard_map/ppermute | solution.py:106
  103.3 7.2 %collective-permute-start.8 = (bf16[192,768]{1,0:T(8,128)(2,1)S(1)}, bf16[192,768]{1,0:T(8,128)(2,1)S(1)}, u32[]{:S(2)}, u32[]{:S(2)}) collective-permute-start(bf16[192,768]{1,0:T(8,128)(2,1)S(1)} %collective-permute-done.7), channel_id=1, source_target_pairs={{0,8},{8,16},{16,24},{24,28},{28,20},{20,12},{12,4},{4,0},{1,9},{9... | collective-permute-start | bytes 884744 | tf_op jit(solution)/shard_map/ppermute | solution.py:102
  114.6 4.1 %copy-start.9 = (f32[46]{0:T(128)S(1)}, f32[46]{0:T(128)}, u32[]{:S(2)}) copy-start(f32[46]{0:T(128)} %param.14) | copy-start | bytes 556
  118.7 3.0 %collective-permute-start.9 = (f32[64,32,128]{2,1,0:T(8,128)}, f32[64,32,128]{2,1,0:T(8,128)}, u32[]{:S(2)}, u32[]{:S(2)}) collective-permute-start(f32[64,32,128]{2,1,0:T(8,128)} %dynamic-slice_bitcast_fusion.1), channel_id=1, source_target_pairs={{0,1},{1,0},{2,3},{3,2},{4,5},{5,4},{6,7},{7,6},{8,9},{9,8},{10,11... | collective-permute-start | bytes 3145736 | tf_op jit(solution)/shard_map/ppermute | solution.py:117
  126.0 2.1 collective-permute-start.10
  129.0 1.2 copy-start.6
  192.0 1.0 copy-start.1
  193.1 7.7 %collective-permute-start.14 = (bf16[192,768]{1,0:T(8,128)(2,1)S(1)}, bf16[192,768]{1,0:T(8,128)(2,1)S(1)}, u32[]{:S(2)}, u32[]{:S(2)}) collective-permute-start(bf16[192,768]{1,0:T(8,128)(2,1)S(1)} %subtract_convert_fusion), channel_id=1, source_target_pairs={{0,8},{8,16},{16,24},{24,28},{28,20},{20,12},{12,4},{4,0},{1,9},{9... | collective-permute-start | bytes 884744 | tf_op jit(solution)/shard_map/ppermute | solution.py:102
  194.2 7.4 %collective-permute-start.11 = (bf16[192,768]{1,0:T(8,128)(2,1)S(1)}, bf16[192,768]{1,0:T(8,128)(2,1)S(1)}, u32[]{:S(2)}, u32[]{:S(2)}) collective-permute-start(bf16[192,768]{1,0:T(8,128)(2,1)S(1)} %subtract_convert_fusion), channel_id=1, source_target_pairs={{0,4},{8,0},{16,8},{24,16},{28,24},{20,28},{12,20},{4,12},{1,5},{9... | collective-permute-start | bytes 884744 | tf_op jit(solution)/shard_map/ppermute | solution.py:106
  200.7 7.2 %collective-permute-start.15 = (bf16[192,768]{1,0:T(8,128)(2,1)S(1)}, bf16[192,768]{1,0:T(8,128)(2,1)S(1)}, u32[]{:S(2)}, u32[]{:S(2)}) collective-permute-start(bf16[192,768]{1,0:T(8,128)(2,1)S(1)} %collective-permute-done.14), channel_id=1, source_target_pairs={{0,8},{8,16},{16,24},{24,28},{28,20},{20,12},{12,4},{4,0},{1,9},{9... | collective-permute-start | bytes 884744 | tf_op jit(solution)/shard_map/ppermute | solution.py:102
  201.6 7.7 %collective-permute-start.12 = (bf16[192,768]{1,0:T(8,128)(2,1)S(1)}, bf16[192,768]{1,0:T(8,128)(2,1)S(1)}, u32[]{:S(2)}, u32[]{:S(2)}) collective-permute-start(bf16[192,768]{1,0:T(8,128)(2,1)S(1)} %collective-permute-done.11), channel_id=1, source_target_pairs={{0,4},{8,0},{16,8},{24,16},{28,24},{20,28},{12,20},{4,12},{1,5},{9... | collective-permute-start | bytes 884744 | tf_op jit(solution)/shard_map/ppermute | solution.py:106
  207.9 8.3 %collective-permute-start.16 = (bf16[192,768]{1,0:T(8,128)(2,1)S(1)}, bf16[192,768]{1,0:T(8,128)(2,1)S(1)}, u32[]{:S(2)}, u32[]{:S(2)}) collective-permute-start(bf16[192,768]{1,0:T(8,128)(2,1)S(1)} %collective-permute-done.15), channel_id=1, source_target_pairs={{0,8},{8,16},{16,24},{24,28},{28,20},{20,12},{12,4},{4,0},{1,9},{9... | collective-permute-start | bytes 884744 | tf_op jit(solution)/shard_map/ppermute | solution.py:102
  209.3 8.8 %collective-permute-start.13 = (bf16[192,768]{1,0:T(8,128)(2,1)S(1)}, bf16[192,768]{1,0:T(8,128)(2,1)S(1)}, u32[]{:S(2)}, u32[]{:S(2)}) collective-permute-start(bf16[192,768]{1,0:T(8,128)(2,1)S(1)} %collective-permute-done.12), channel_id=1, source_target_pairs={{0,4},{8,0},{16,8},{24,16},{28,24},{20,28},{12,20},{4,12},{1,5},{9... | collective-permute-start | bytes 884744 | tf_op jit(solution)/shard_map/ppermute | solution.py:106
  216.2 6.7 %collective-permute-start.17 = (bf16[192,768]{1,0:T(8,128)(2,1)S(1)}, bf16[192,768]{1,0:T(8,128)(2,1)S(1)}, u32[]{:S(2)}, u32[]{:S(2)}) collective-permute-start(bf16[192,768]{1,0:T(8,128)(2,1)S(1)} %collective-permute-done.16), channel_id=1, source_target_pairs={{0,8},{8,16},{16,24},{24,28},{28,20},{20,12},{12,4},{4,0},{1,9},{9... | collective-permute-start | bytes 884744 | tf_op jit(solution)/shard_map/ppermute | solution.py:102
  230.0 2.8 %copy-start.2 = (f32[64,32,128]{2,1,0:T(8,128)S(1)}, f32[64,32,128]{2,1,0:T(8,128)}, u32[]{:S(2)}) copy-start(f32[64,32,128]{2,1,0:T(8,128)} %get-tuple-element.7) | copy-start | bytes 3145732
  230.1 2.7 %collective-permute-start.18 = (f32[64,32,128]{2,1,0:T(8,128)S(1)}, f32[64,32,128]{2,1,0:T(8,128)S(1)}, u32[]{:S(2)}, u32[]{:S(2)}) collective-permute-start(f32[64,32,128]{2,1,0:T(8,128)S(1)} %dynamic-slice_bitcast_fusion), channel_id=1, source_target_pairs={{0,1},{1,0},{2,3},{3,2},{4,5},{5,4},{6,7},{7,6},{8,9},{9,8},{10,11... | collective-permute-start | bytes 3145736 | tf_op jit(solution)/shard_map/ppermute | solution.py:117
  233.4 25.4 %collective-permute-start.19 = (f32[64,32,128]{2,1,0:T(8,128)S(1)}, f32[64,32,128]{2,1,0:T(8,128)}, u32[]{:S(2)}, u32[]{:S(2)}) collective-permute-start(f32[64,32,128]{2,1,0:T(8,128)S(1)} %multiply_select_fusion), channel_id=1, source_target_pairs={{0,2},{2,0},{1,3},{3,1},{4,6},{6,4},{5,7},{7,5},{8,10},{10,8},{9,1... | collective-permute-start | bytes 3145736 | tf_op jit(solution)/shard_map/ppermute | solution.py:127
  260.7 4.4 %collective-permute-start.20 = (f32[64,64,128]{2,1,0:T(8,128)S(1)}, f32[64,64,128]{2,1,0:T(8,128)}, u32[]{:S(2)}, u32[]{:S(2)}) collective-permute-start(f32[64,64,128]{2,1,0:T(8,128)S(1)} %maximum_select_fusion.1), channel_id=1, source_target_pairs={{0,1},{1,0},{2,3},{3,2},{4,5},{5,4},{6,7},{7,6},{8,9},{9,8},{10,11... | collective-permute-start | bytes 6291464 | tf_op jit(solution)/shard_map/ppermute | solution.py:133
  (1 other events, 0.8 us)
